TPU v7x, 32 devices: a whole 2x2x4 slice. The times are simulated.
32 devices in a mesh: dom: 2 (over y), blk: 16 (over z, x, core).
Axes of the slice: x: 2, y: 2, z: 4, core: 2. Of those that a mesh axis runs over, the one named last changes fastest.
Arguments:
- right_side: float32 [2, 4, 2, 8192], P(None, None, 'dom', 'blk')
- near_blocks: bfloat16 [2, 32, 4, 2, 256, 256], P('dom', 'blk'), may hold values from -0.125 to 0.125
- near_cols: int32 [2, 32, 4], P('dom', 'blk'), may hold values from 0 to 5
- partner: int32 [2, 32], P('dom', 'blk'), may hold values from 0 to 3, as said below
- source_basis: bfloat16 [2, 2, 64, 8192], P('dom', None, None, 'blk'), may hold values from -0.25 to 0.25
- target_basis: bfloat16 [2, 2, 64, 8192], P('dom', None, None, 'blk'), may hold values from -0.75 to 0.75
- coupling: float32 [2, 16, 16, 2, 64, 64], P('dom', 'blk'), as said below
- far_ranks: int32 [2, 16, 16], P('dom', 'blk'), may hold values from 32 to 64, as said below
Outputs:
- second_basis: float32 [2, 4, 2, 8192], P(None, None, 'dom', 'blk')
- third_basis: float32 [2, 4, 2, 8192], P(None, None, 'dom', 'blk')
- hessenberg: float32 [4, 9], replicated
Inputs may be any that keep to these rules, and one draw needn't show every extreme that they name: partner[d, c * 2 + i] = e * 2 + j names block j of cluster c in subdomain e; the named block names the first one back, and no block names itself. coupling[d, c, s, a, k, l] equals coupling[d, s, c, a, l, k]. far_ranks[d, c, s] equals far_ranks[d, s, c].
All inputs are finite; a program needn't handle non-finite values.
Results may differ from a plain program's by a relative error of at most 0.0065.
Values may be sent and summed in bfloat16 or wider, within the bound.
No kernel may reach another device: no remote copies, remote signals or barrier semaphores. Data moves between devices by JAX's collectives and lax.ppermute only.
A program may use at most 64 MiB of HBM per device.

v0:
```python
import jax
import jax.numpy as jnp
from jax import lax
from jax.sharding import PartitionSpec as P

EPSILON = 1e-06


def extended(cells, sides, width):
    for axis, dim in sides:
        count = lax.axis_size(axis)
        ends = count - 1
        head = lax.slice_in_dim(cells, 0, width, axis=dim)
        tail = lax.slice_in_dim(cells, cells.shape[dim] - width, cells.shape[dim], axis=dim)
        cells = jnp.concatenate(
            [
                lax.ppermute(tail, axis, [(i, (i + 1) % count) for i in range(ends)]),
                cells,
                lax.ppermute(head, axis, [((i + 1) % count, i) for i in range(ends)]),
            ],
            axis=dim,
        )
    return cells


def complex_mix(products):
    return jnp.stack([products[0, 0] - products[1, 1], products[0, 1] + products[1, 0]])


def apply_operator(
    vector, near_blocks, near_cols, partner, source_basis, target_basis, coupling, far_ranks
):
    nrhs = vector.shape[1]
    rows = vector.shape[3]
    blocks_dev = near_blocks.shape[1]
    slots = near_blocks.shape[2]
    width = near_blocks.shape[4]
    rank_cap = source_basis.shape[2]
    rounded = vector.astype(jnp.bfloat16)
    window = extended(rounded, (("blk", 3),), rows)
    window = window.reshape(2, nrhs, 3 * blocks_dev, width)
    chosen = jnp.take(window, near_cols[0].reshape(-1), axis=2).reshape(
        2, nrhs, blocks_dev, slots, width
    )
    near_prod = jnp.einsum(
        "ikarc,pqikc->apqir", near_blocks[0], chosen, preferred_element_type=jnp.float32
    )
    near_part = complex_mix(near_prod).reshape(2, nrhs, 1, rows)
    coef_prod = jnp.einsum(
        "akr,pqr->apqk", source_basis[0], rounded[:, :, 0], preferred_element_type=jnp.float32
    )
    coeffs = jnp.stack([coef_prod[0, 0] + coef_prod[1, 1], coef_prod[0, 1] - coef_prod[1, 0]])
    row_coupling = coupling[0, 0]
    row_ranks = far_ranks[0, 0]
    levels = jnp.arange(rank_cap, dtype=jnp.int32)
    limit = row_ranks[:, None, None]
    keep = (levels[None, :, None] < limit) & (levels[None, None, :] < limit)
    weights = row_coupling * keep[:, None].astype(jnp.float32)
    inner = jnp.einsum(
        "sakl,spql->apqk",
        weights,
        lax.all_gather(coeffs[None], "blk", axis=0, tiled=True),
        precision=lax.Precision.HIGHEST,
    )
    far_coef = complex_mix(inner)
    rounded_coef = far_coef.astype(jnp.bfloat16)
    outward = jnp.einsum(
        "akr,pqk->apqr", target_basis[0], rounded_coef, preferred_element_type=jnp.float32
    )
    far_part = complex_mix(outward).reshape(2, nrhs, 1, rows)
    every = lax.all_gather(vector, "dom", axis=2, tiled=True)
    every = every.reshape(2, nrhs, -1, width)
    mates = jnp.take(every, partner[0], axis=2).reshape(2, nrhs, 1, rows)
    return vector + near_part + far_part - mates


def local_products(vectors, image):
    stacked = []
    for basis in vectors:
        real_part = jnp.sum(basis[0] * image[0] + basis[1] * image[1], axis=(1, 2))
        imag_part = jnp.sum(basis[0] * image[1] - basis[1] * image[0], axis=(1, 2))
        stacked.append(jnp.stack([real_part, imag_part]))
    return jnp.stack(stacked)


def local_squares(field):
    return jnp.sum(field[0] * field[0] + field[1] * field[1], axis=(1, 2))


def scaled(factor, field):
    real_f = factor[0][:, None, None]
    imag_f = factor[1][:, None, None]
    return jnp.stack([real_f * field[0] - imag_f * field[1], real_f * field[1] + imag_f * field[0]])


def shards(
    right_side, near_blocks, near_cols, partner, source_basis, target_basis, coupling, far_ranks
):
    rows = right_side.shape[3]
    total = float(rows * lax.axis_size("dom") * lax.axis_size("blk"))

    def operator(field):
        return apply_operator(
            field, near_blocks, near_cols, partner, source_basis, target_basis, coupling, far_ranks
        )

    start_sum = lax.psum(local_squares(right_side), ("dom", "blk"))
    beta = jnp.sqrt(start_sum / total + EPSILON)
    first_vec = right_side / beta[None, :, None, None]
    image_one = operator(first_vec)

    def projections(vectors, image):
        return lax.psum(local_products(vectors, image), ("dom", "blk")) / total

    def lengths(field):
        return lax.psum(local_squares(field), ("dom", "blk")) / total

    h_one_one = projections([first_vec], image_one)[0]
    rest_one = image_one - scaled(h_one_one, first_vec)
    h_two_one = jnp.sqrt(lengths(rest_one) + EPSILON)
    second_basis = rest_one / h_two_one[None, :, None, None]
    image_two = operator(second_basis)
    both = projections([first_vec, second_basis], image_two)
    h_one_two = both[0]
    h_two_two = both[1]
    rest_two = image_two - scaled(h_one_two, first_vec) - scaled(h_two_two, second_basis)
    h_three_two = jnp.sqrt(lengths(rest_two) + EPSILON)
    third_basis = rest_two / h_three_two[None, :, None, None]
    hessenberg = jnp.stack(
        [
            beta,
            h_one_one[0],
            h_one_one[1],
            h_two_one,
            h_one_two[0],
            h_one_two[1],
            h_two_two[0],
            h_two_two[1],
            h_three_two,
        ],
        axis=1,
    )
    return (second_basis, third_basis, hessenberg)


def solution(mesh):
    return jax.shard_map(
        shards,
        mesh=mesh,
        in_specs=(
            P(None, None, "dom", "blk"),
            P("dom", "blk", None, None, None, None),
            P("dom", "blk", None),
            P("dom", "blk"),
            P("dom", None, None, "blk"),
            P("dom", None, None, "blk"),
            P("dom", "blk", None, None, None, None),
            P("dom", "blk", None),
        ),
        out_specs=(P(None, None, "dom", "blk"), P(None, None, "dom", "blk"), P()),
        check_vma=False,
    )
```

profile of v0, /device:TPU:0, one launch (start us, length us, event | category | flops | bytes accessed | tf_op | source)
XLA Modules:
  0.0 278.6 jit_solution(17837477689193010791)
XLA Ops:
  0.6 0.0 copy-start
  0.6 0.0 copy-start.2
  0.7 0.0 copy-start.3
  0.7 0.0 copy-start.4
  0.7 1.0 add_reduce_fusion.3
  1.7 42.0 %psum.35 = f32[4]{0:T(128)S(1)} all-reduce(f32[4]{0:T(128)S(1)} %add_reduce_fusion.3), channel_id=1, replica_groups=mesh['dom'=2,'blk'=16] {'dom','blk'}, use_global_device_ids=true, to_apply=%region_1.0 | all-reduce | flops 4 | bytes 32 | tf_op jit(solution)/shard_map/psum | solution.py:107
  43.7 0.8 fusion.64
  44.5 1.3 collective-permute-start
  45.8 1.3 collective-permute-start.1
  47.1 1.1 convolution_bitcast_fusion.3
  48.2 24.1 %all-gather = f32[32,4,64]{2,1,0:T(4,128)S(1)} all-gather(f32[2,4,64]{2,1,0:T(4,128)S(1)} %pad_maximum_fusion.2), channel_id=2, replica_groups=mesh['dom'=2,'blk'=16] {'blk'}, dimensions={0}, use_global_device_ids=true | all-gather | bytes 34816 | tf_op jit(solution)/shard_map/all_gather | solution.py:62
  72.3 0.7 iota_compare_fusion
  73.0 0.2 and_convert_fusion
  73.2 2.6 fusion.12
  75.9 0.0 copy-start.1
  75.9 0.1 convolution_bitcast_fusion.1
  76.1 0.1 reshape_squeeze.4
  76.2 4.4 %all_gather.13 = f32[2,4,2,512]{3,1,0,2:T(4,128)S(1)} all-gather(f32[2,4,1,512]{3,1,0,2:T(4,128)S(1)} %get-tuple-element.28), channel_id=1, replica_groups=mesh['dom'=2,'blk'=16] {'dom'}, dimensions={2}, use_global_device_ids=true | all-gather | bytes 49152 | tf_op jit(solution)/shard_map/all_gather | solution.py:71
  80.7 0.6 gather_fusion.1
  81.3 0.1 select_bitcast_fusion.1
  81.5 0.0 collective-permute-done
  81.5 0.0 collective-permute-done.1
  81.5 0.6 gather_fusion
  82.1 0.1 broadcast_select_fusion.1
  82.2 0.7 fusion.4
  82.9 0.1 add_reduce_fusion.2
  83.1 36.9 %psum.36 = f32[1,2,4]{2,1,0:T(2,128)S(1)} all-reduce(f32[1,2,4]{2,1,0:T(2,128)S(1)} %maximum_bitcast_fusion.6), channel_id=1, replica_groups=mesh['dom'=2,'blk'=16] {'dom','blk'}, use_global_device_ids=true, to_apply=%region_4.7 | all-reduce | flops 8 | bytes 64 | tf_op jit(solution)/shard_map/psum | solution.py:113
  120.0 0.1 multiply_subtract_fusion.2
  120.1 0.1 fusion.34
  120.2 0.1 copy.136
  120.3 41.3 %psum.37 = f32[4]{0:T(128)S(1)} all-reduce(f32[4]{0:T(128)S(1)} %fusion.34), channel_id=1, replica_groups=mesh['dom'=2,'blk'=16] {'dom','blk'}, use_global_device_ids=true, to_apply=%region_6.9 | all-reduce | flops 4 | bytes 32 | tf_op jit(solution)/shard_map/psum | solution.py:116
  161.6 0.1 fusion.63
  161.7 0.1 convolution_bitcast_fusion.2
  161.9 20.6 %all-gather.1 = f32[32,4,64]{2,1,0:T(4,128)S(1)} all-gather(f32[2,4,64]{2,1,0:T(4,128)S(1)} %pad_maximum_fusion.3), channel_id=3, replica_groups=mesh['dom'=2,'blk'=16] {'blk'}, dimensions={0}, use_global_device_ids=true | all-gather | bytes 34816 | tf_op jit(solution)/shard_map/all_gather | solution.py:62
  182.5 2.6 fusion.10
  185.1 2.2 collective-permute-start.2
  187.4 1.3 collective-permute-start.3
  188.7 4.4 %all_gather.15 = f32[2,4,2,512]{3,1,0,2:T(4,128)S(1)} all-gather(f32[2,4,1,512]{3,1,0,2:T(4,128)S(1)} %get-tuple-element.26), channel_id=1, replica_groups=mesh['dom'=2,'blk'=16] {'dom'}, dimensions={2}, use_global_device_ids=true | all-gather | bytes 49152 | tf_op jit(solution)/shard_map/all_gather | solution.py:71
  193.2 0.6 gather_fusion.3
  193.8 0.1 select_bitcast_fusion
  193.9 0.1 convolution_bitcast_fusion
  194.0 0.6 copy.145
  194.7 0.1 copy.139
  194.8 0.0 collective-permute-done.2
  194.8 0.0 collective-permute-done.3
  194.8 0.6 gather_fusion.2
  195.4 0.1 broadcast_select_fusion
  195.5 0.7 fusion.7
  196.2 0.2 add_reduce_fusion.1
  196.4 0.1 copy.137
  196.5 39.3 %psum.38 = f32[2,2,4]{2,1,0:T(2,128)S(1)} all-reduce(f32[2,2,4]{2,1,0:T(2,128)S(1)} %pad_maximum_fusion.4), channel_id=1, replica_groups=mesh['dom'=2,'blk'=16] {'dom','blk'}, use_global_device_ids=true, to_apply=%region_11.14 | all-reduce | flops 16 | bytes 128 | tf_op jit(solution)/shard_map/psum | solution.py:113
  235.8 0.1 multiply_subtract_fusion
  235.9 0.1 multiply_subtract_fusion.1
  236.0 0.1 fusion.30
  236.1 0.1 copy.138
  236.2 40.5 %psum.39 = f32[4]{0:T(128)S(1)} all-reduce(f32[4]{0:T(128)S(1)} %fusion.30), channel_id=1, replica_groups=mesh['dom'=2,'blk'=16] {'dom','blk'}, use_global_device_ids=true, to_apply=%region_13.16 | all-reduce | flops 4 | bytes 32 | tf_op jit(solution)/shard_map/psum | solution.py:116
  276.7 0.1 copy.144
  276.8 0.1 copy.140
  276.9 0.1 copy.141
  277.0 0.1 copy.142
  277.1 0.1 copy.143
  277.2 0.1 broadcast_divide_fusion
  277.3 0.6 copy.146
  277.9 0.7 stack.135
  (56 shorter events, 0.5 us)
Async XLA Ops:
  0.6 81.5 %copy-start = (bf16[1,2,4,2,256,256]{5,4,3,2,1,0:T(8,128)(2,1)S(1)}, bf16[1,2,4,2,256,256]{5,4,3,2,1,0:T(8,128)(2,1)}, u32[]{:S(2)}) copy-start(bf16[1,2,4,2,256,256]{5,4,3,2,1,0:T(8,128)(2,1)} %param.13) | copy-start | bytes 6291460
  0.6 75.3 %copy-start.2 = (bf16[1,2,64,512]{3,2,1,0:T(8,128)(2,1)S(1)}, bf16[1,2,64,512]{3,2,1,0:T(8,128)(2,1)}, u32[]{:S(2)}) copy-start(bf16[1,2,64,512]{3,2,1,0:T(8,128)(2,1)} %param.17) | copy-start | bytes 393220
  0.7 75.4 %copy-start.3 = (s32[1,2,4]{2,1,0:T(2,128)S(1)}, s32[1,2,4]{2,1,0:T(2,128)}, u32[]{:S(2)}) copy-start(s32[1,2,4]{2,1,0:T(2,128)} %param.14) | copy-start | bytes 100
  0.7 75.5 %copy-start.4 = (s32[1,2]{1,0:T(1,128)S(1)}, s32[1,2]{1,0:T(1,128)}, u32[]{:S(2)}) copy-start(s32[1,2]{1,0:T(1,128)} %param.15) | copy-start | bytes 28
  44.5 37.0 %collective-permute-start = (bf16[2,4,1,512]{3,1,0,2:T(4,128)(2,1)S(1)}, bf16[2,4,1,512]{3,1,0,2:T(4,128)(2,1)S(1)}, u32[]{:S(2)}, u32[]{:S(2)}) collective-permute-start(bf16[2,4,1,512]{3,1,0,2:T(4,128)(2,1)S(1)} %get-tuple-element.27), channel_id=1, source_target_pairs={{0,1},{1,2},{2,3},{3,4},{4,5},{5,6},{6,7},{7,8},{8,9},{9,10},{10,1... | collective-permute-start | bytes 24584 | tf_op jit(solution)/shard_map/ppermute | solution.py:17
  45.8 35.7 %collective-permute-start.1 = (bf16[2,4,1,512]{3,1,0,2:T(4,128)(2,1)S(1)}, bf16[2,4,1,512]{3,1,0,2:T(4,128)(2,1)S(1)}, u32[]{:S(2)}, u32[]{:S(2)}) collective-permute-start(bf16[2,4,1,512]{3,1,0,2:T(4,128)(2,1)S(1)} %get-tuple-element.27), channel_id=1, source_target_pairs={{1,0},{2,1},{3,2},{4,3},{5,4},{6,5},{7,6},{8,7},{9,8},{10,9},{11,1... | collective-permute-start | bytes 24584 | tf_op jit(solution)/shard_map/ppermute | solution.py:19
  75.9 85.8 %copy-start.1 = (bf16[1,2,64,512]{3,2,1,0:T(8,128)(2,1)S(1)}, bf16[1,2,64,512]{3,2,1,0:T(8,128)(2,1)}, u32[]{:S(2)}) copy-start(bf16[1,2,64,512]{3,2,1,0:T(8,128)(2,1)} %param.16) | copy-start | bytes 393220
  185.1 9.7 %collective-permute-start.2 = (bf16[2,4,1,512]{3,1,0,2:T(4,128)(2,1)S(1)}, bf16[2,4,1,512]{3,1,0,2:T(4,128)(2,1)S(1)}, u32[]{:S(2)}, u32[]{:S(2)}) collective-permute-start(bf16[2,4,1,512]{3,1,0,2:T(4,128)(2,1)S(1)} %get-tuple-element.25), channel_id=1, source_target_pairs={{0,1},{1,2},{2,3},{3,4},{4,5},{5,6},{6,7},{7,8},{8,9},{9,10},{10,1... | collective-permute-start | bytes 24584 | tf_op jit(solution)/shard_map/ppermute | solution.py:17
  187.4 7.4 %collective-permute-start.3 = (bf16[2,4,1,512]{3,1,0,2:T(4,128)(2,1)S(1)}, bf16[2,4,1,512]{3,1,0,2:T(4,128)(2,1)S(1)}, u32[]{:S(2)}, u32[]{:S(2)}) collective-permute-start(bf16[2,4,1,512]{3,1,0,2:T(4,128)(2,1)S(1)} %get-tuple-element.25), channel_id=1, source_target_pairs={{1,0},{2,1},{3,2},{4,3},{5,4},{6,5},{7,6},{8,7},{9,8},{10,9},{11,1... | collective-permute-start | bytes 24584 | tf_op jit(solution)/shard_map/ppermute | solution.py:19
where the time goes:
time: 280 us; the launch traced here: 279 us
  blocking collectives  254 us (91%)
  matrix products  8.05 us (3%)
  starting transfers between devices  6.11 us (2%)
  local copies, waits for them, and re-layouts  5.44 us (2%)
  other arithmetic  4.26 us (2%)
    psum x2, blocking collectives, lengths(): return lax.psum(local_squares(field), ('dom', 'blk')) / total  81.9 us
    psum x2, blocking collectives, projections(): return lax.psum(local_products(vectors, image), ('dom', 'blk')) / total  76.2 us
    all_gather x2, blocking collectives, apply_operator(): lax.all_gather(coeffs[None], 'blk', axis=0, tiled=True)  44.7 us
    psum x1, blocking collectives, shards(): start_sum = lax.psum(local_squares(right_side), ('dom', 'blk'))  42 us
    all_gather x2, blocking collectives, apply_operator(): every = lax.all_gather(vector, 'dom', axis=2, tiled=True)  8.85 us
  transfers between devices with their start and end apart: 4, of which 0 were waited for; matrix products, arithmetic and copies ran while one was open for 3% of the time, Pallas kernels for 0%

commit v1 on v0

--- a/solution.py
+++ b/solution.py
@@ -4,6 +4,38 @@
 from jax.sharding import PartitionSpec as P
 
 EPSILON = 1e-06
+
+
+def _pow2(n):
+    return n > 0 and (n & (n - 1)) == 0
+
+
+def tree_sum(x, axes):
+    for axis in axes:
+        n = lax.axis_size(axis)
+        if not _pow2(n):
+            x = lax.psum(x, axis)
+            continue
+        k = 1
+        while k < n:
+            x = x + lax.ppermute(x, axis, [(i, i ^ k) for i in range(n)])
+            k *= 2
+    return x
+
+
+def tree_gather(x, axis):
+    n = lax.axis_size(axis)
+    if not _pow2(n):
+        return lax.all_gather(x, axis, axis=0)
+    idx = lax.axis_index(axis)
+    buf = x[None]
+    k = 1
+    while k < n:
+        other = lax.ppermute(buf, axis, [(i, i ^ k) for i in range(n)])
+        low = (idx // k) % 2 == 0
+        buf = jnp.where(low, jnp.concatenate([buf, other]), jnp.concatenate([other, buf]))
+        k *= 2
+    return buf
 
 
 def extended(cells, sides, width):
@@ -59,7 +91,7 @@
     inner = jnp.einsum(
         "sakl,spql->apqk",
         weights,
-        lax.all_gather(coeffs[None], "blk", axis=0, tiled=True),
+        tree_gather(coeffs, "blk"),
         precision=lax.Precision.HIGHEST,
     )
     far_coef = complex_mix(inner)
@@ -68,7 +100,7 @@
         "akr,pqk->apqr", target_basis[0], rounded_coef, preferred_element_type=jnp.float32
     )
     far_part = complex_mix(outward).reshape(2, nrhs, 1, rows)
-    every = lax.all_gather(vector, "dom", axis=2, tiled=True)
+    every = jnp.moveaxis(tree_gather(vector[:, :, 0], "dom"), 0, 2)
     every = every.reshape(2, nrhs, -1, width)
     mates = jnp.take(every, partner[0], axis=2).reshape(2, nrhs, 1, rows)
     return vector + near_part + far_part - mates
@@ -98,22 +130,23 @@
 ):
     rows = right_side.shape[3]
     total = float(rows * lax.axis_size("dom") * lax.axis_size("blk"))
+    everyone = ("dom", "blk")
 
     def operator(field):
         return apply_operator(
             field, near_blocks, near_cols, partner, source_basis, target_basis, coupling, far_ranks
         )
 
-    start_sum = lax.psum(local_squares(right_side), ("dom", "blk"))
+    start_sum = tree_sum(local_squares(right_side), everyone)
     beta = jnp.sqrt(start_sum / total + EPSILON)
     first_vec = right_side / beta[None, :, None, None]
     image_one = operator(first_vec)
 
     def projections(vectors, image):
-        return lax.psum(local_products(vectors, image), ("dom", "blk")) / total
+        return tree_sum(local_products(vectors, image), everyone) / total
 
     def lengths(field):
-        return lax.psum(local_squares(field), ("dom", "blk")) / total
+        return tree_sum(local_squares(field), everyone) / total
 
     h_one_one = projections([first_vec], image_one)[0]
     rest_one = image_one - scaled(h_one_one, first_vec)

time: 280 us -> 133 us (0.47)
  blocking collectives: 254 us -> 0 us
  starting transfers between devices: 6.11 us -> 61.8 us
  waiting for transfers between devices: 0.01 us -> 49.9 us
    psum x5 -> x0, blocking collectives: 200 us -> none  [the longest x2 81.9 us: lengths(): return lax.psum(local_squares(field), ('dom', 'blk')) / total]
    ppermute x0 -> x35, starting transfers between devices: none -> 55.3 us  [the longest x25 35 us: tree_sum(): x = x + lax.ppermute(x, axis, [(i, i ^ k) for i in range(n)])]
    all_gather x4 -> x0, blocking collectives: 53.6 us -> none  [the longest x2 44.7 us: apply_operator(): lax.all_gather(coeffs[None], 'blk', axis=0, tiled=True)]
    ppermute x0 -> x35, waiting for transfers between devices: none -> 49.9 us  [the longest x25 44.8 us: tree_sum(): x = x + lax.ppermute(x, axis, [(i, i ^ k) for i in range(n)])]
  transfers between devices with their start and end apart: 4 -> 39, of which waited for: 0 -> 30; matrix products, arithmetic and copies ran while one was open for 3% -> 7% of each run, Pallas kernels for 0% -> 0%
where the time goes in v1:
time: 133 us
  starting transfers between devices  61.8 us (46%)
  waiting for transfers between devices  49.9 us (38%)
  matrix products  8.04 us (6%)
  local copies, waits for them, and re-layouts  6.09 us (5%)
  other arithmetic  5.73 us (4%)
    ppermute x25, waiting for transfers between devices, tree_sum(): x = x + lax.ppermute(x, axis, [(i, i ^ k) for i in range(n)])  44.8 us
    ppermute x25, starting transfers between devices, tree_sum(): x = x + lax.ppermute(x, axis, [(i, i ^ k) for i in range(n)])  35 us
    ppermute x10, starting transfers between devices, tree_gather(): other = lax.ppermute(buf, axis, [(i, i ^ k) for i in range(n)])  20.3 us
    dot_general x2, matrix products, apply_operator(): jnp.einsum('sakl,spql->apqk', weights, tree_gather(coeffs, 'blk'), precis...  5.23 us
    ppermute x10, waiting for transfers between devices, tree_gather(): other = lax.ppermute(buf, axis, [(i, i ^ k) for i in range(n)])  5.08 us
    ppermute x2, starting transfers between devices, extended(): lax.ppermute(tail, axis, [(i, (i + 1) % count) for i in range(ends)])  3.85 us
  transfers between devices with their start and end apart: 39, of which 30 were waited for; matrix products, arithmetic and copies ran while one was open for 7% of the time, Pallas kernels for 0%

profile of v1, /device:TPU:0, one launch (start us, length us, event | category | flops | bytes accessed | tf_op | source)
XLA Modules:
  0.0 132.6 jit_solution(15560113585439301118)
XLA Ops:
  0.6 1.0 add_reduce_fusion.3
  1.6 3.0 %collective-permute-start = (f32[4]{0:T(128)S(1)}, f32[4]{0:T(128)S(1)}, u32[]{:S(2)}, u32[]{:S(2)}) collective-permute-start(f32[4]{0:T(128)S(1)} %add_reduce_fusion.3), channel_id=1, source_target_pairs={{0,16},{16,0},{1,17},{17,1},{2,18},{18,2},{3,19},{19,3},{4,20},{20... | collective-permute-start | bytes 56 | tf_op jit(solution)/shard_map/ppermute | solution.py:21
  6.0 0.8 reshape_squeeze.4
  6.7 0.7 iota_compare_fusion
  7.8 1.1 collective-permute-done.1
  8.9 1.5 %collective-permute-start.2 = (f32[4]{0:T(128)S(1)}, f32[4]{0:T(128)S(1)}, u32[]{:S(2)}, u32[]{:S(2)}) collective-permute-start(f32[4]{0:T(128)S(1)} %add.326), channel_id=1, source_target_pairs={{0,2},{1,3},{2,0},{3,1},{4,6},{5,7},{6,4},{7,5},{8,10},{9,11},{10,... | collective-permute-start | bytes 56 | tf_op jit(solution)/shard_map/ppermute | solution.py:21
  10.4 2.0 %collective-permute-done.2 = f32[4]{0:T(128)S(1)} collective-permute-done((f32[4]{0:T(128)S(1)}, f32[4]{0:T(128)S(1)}, u32[]{:S(2)}, u32[]{:S(2)}) %collective-permute-start.2) | collective-permute-done | bytes 48 | tf_op jit(solution)/shard_map/ppermute | solution.py:21
  12.4 1.6 %collective-permute-start.3 = (f32[4]{0:T(128)S(1)}, f32[4]{0:T(128)S(1)}, u32[]{:S(2)}, u32[]{:S(2)}) collective-permute-start(f32[4]{0:T(128)S(1)} %add.327), channel_id=1, source_target_pairs={{0,4},{1,5},{2,6},{3,7},{4,0},{5,1},{6,2},{7,3},{8,12},{9,13},{10,... | collective-permute-start | bytes 56 | tf_op jit(solution)/shard_map/ppermute | solution.py:21
  14.0 2.0 %collective-permute-done.3 = f32[4]{0:T(128)S(1)} collective-permute-done((f32[4]{0:T(128)S(1)}, f32[4]{0:T(128)S(1)}, u32[]{:S(2)}, u32[]{:S(2)}) %collective-permute-start.3) | collective-permute-done | bytes 48 | tf_op jit(solution)/shard_map/ppermute | solution.py:21
  16.0 2.6 %collective-permute-start.4 = (f32[4]{0:T(128)S(1)}, f32[4]{0:T(128)S(1)}, u32[]{:S(2)}, u32[]{:S(2)}) collective-permute-start(f32[4]{0:T(128)S(1)} %add.328), channel_id=1, source_target_pairs={{0,8},{1,9},{2,10},{3,11},{4,12},{5,13},{6,14},{7,15},{8,0},{9,1},... | collective-permute-start | bytes 56 | tf_op jit(solution)/shard_map/ppermute | solution.py:21
  18.6 1.9 %collective-permute-done.4 = f32[4]{0:T(128)S(1)} collective-permute-done((f32[4]{0:T(128)S(1)}, f32[4]{0:T(128)S(1)}, u32[]{:S(2)}, u32[]{:S(2)}) %collective-permute-start.4) | collective-permute-done | bytes 48 | tf_op jit(solution)/shard_map/ppermute | solution.py:21
  20.4 0.8 fusion.66
  21.2 1.1 convolution_bitcast_fusion.5
  22.4 1.1 collective-permute-done.7
  23.6 1.5 %collective-permute-start.8 = (f32[2,2,4,64]{3,2,1,0:T(4,128)S(1)}, f32[2,2,4,64]{3,2,1,0:T(4,128)S(1)}, u32[]{:S(2)}, u32[]{:S(2)}) collective-permute-start(f32[2,2,4,64]{3,2,1,0:T(4,128)S(1)} %maximum_select_fusion.8), channel_id=1, source_target_pairs={{0,2},{1,3},{2,0},{3,1},{4,6},{5,7},{6,4},{7,5},{8,10},{9,11},{10,... | collective-permute-start | bytes 12296 | tf_op jit(solution)/shard_map/ppermute | solution.py:34
  25.1 1.8 %collective-permute-start.5 = (bf16[2,4,1,512]{3,1,0,2:T(4,128)(2,1)S(1)}, bf16[2,4,1,512]{3,1,0,2:T(4,128)(2,1)S(1)}, u32[]{:S(2)}, u32[]{:S(2)}) collective-permute-start(bf16[2,4,1,512]{3,1,0,2:T(4,128)(2,1)S(1)} %get-tuple-element.24), channel_id=1, source_target_pairs={{0,1},{1,2},{2,3},{3,4},{4,5},{5,6},{6,7},{7,8},{8,9},{9,10},{10,1... | collective-permute-start | bytes 24584 | tf_op jit(solution)/shard_map/ppermute | solution.py:49
  26.9 1.3 collective-permute-start.6
  28.7 5.0 %collective-permute-start.9 = (f32[4,2,4,64]{3,2,1,0:T(4,128)S(1)}, f32[4,2,4,64]{3,2,1,0:T(4,128)S(1)}, u32[]{:S(2)}, u32[]{:S(2)}) collective-permute-start(f32[4,2,4,64]{3,2,1,0:T(4,128)S(1)} %maximum_select_fusion.6), channel_id=1, source_target_pairs={{0,4},{1,5},{2,6},{3,7},{4,0},{5,1},{6,2},{7,3},{8,12},{9,13},{10,... | collective-permute-start | bytes 24584 | tf_op jit(solution)/shard_map/ppermute | solution.py:34
  35.5 3.1 %collective-permute-start.10 = (f32[8,2,4,64]{3,2,1,0:T(4,128)S(1)}, f32[8,2,4,64]{3,2,1,0:T(4,128)S(1)}, u32[]{:S(2)}, u32[]{:S(2)}) collective-permute-start(f32[8,2,4,64]{3,2,1,0:T(4,128)S(1)} %maximum_select_fusion.2), channel_id=1, source_target_pairs={{0,8},{1,9},{2,10},{3,11},{4,12},{5,13},{6,14},{7,15},{8,0},{9,1},... | collective-permute-start | bytes 49160 | tf_op jit(solution)/shard_map/ppermute | solution.py:34
  39.4 1.1 collective-permute-done.10
  40.5 2.6 %convolution_bitcast_fusion.4 = f32[2,2,4,64]{3,2,0,1:T(4,128)S(1)} fusion(f32[1,1,16,2,64,64]{5,4,3,2,1,0:T(8,128)} %param.18, f32[16,64,64]{2,1,0:T(8,128)S(1)} %and_convert_fusion, f32[8,2,4,64]{3,2,1,0:T(4,128)S(1)} %collective-permute-done.10, f32[8,2,4,64]{3,2,1,0:T(4,128)S(1)} %maximum_select_fusion.2, pred[]{:T(512)S(6)} %eq.31), kind=kOutput, calls=%fused_computation.14 | convolution fusion | flops 12738560 | bytes 823297 | tf_op jit(solution)/shard_map/sakl,spql->apqk/dot_general | solution.py:91
  43.5 1.8 %collective-permute-start.12 = (f32[1,2,4]{2,1,0:T(2,128)S(1)}, f32[1,2,4]{2,1,0:T(2,128)S(1)}, u32[]{:S(2)}, u32[]{:S(2)}) collective-permute-start(f32[1,2,4]{2,1,0:T(2,128)S(1)} %maximum_bitcast_fusion.8), channel_id=1, source_target_pairs={{0,16},{16,0},{1,17},{17,1},{2,18},{18,2},{3,19},{19,3},{4,20},{20... | collective-permute-start | bytes 104 | tf_op jit(solution)/shard_map/ppermute | solution.py:21
  45.2 1.9 %collective-permute-done.12 = f32[1,2,4]{2,1,0:T(2,128)S(1)} collective-permute-done((f32[1,2,4]{2,1,0:T(2,128)S(1)}, f32[1,2,4]{2,1,0:T(2,128)S(1)}, u32[]{:S(2)}, u32[]{:S(2)}) %collective-permute-start.12) | collective-permute-done | bytes 64 | tf_op jit(solution)/shard_map/ppermute | solution.py:21
  47.2 1.1 collective-permute-done.13
  48.4 3.6 %collective-permute-done.14 = f32[1,2,4]{2,1,0:T(2,128)S(1)} collective-permute-done((f32[1,2,4]{2,1,0:T(2,128)S(1)}, f32[1,2,4]{2,1,0:T(2,128)S(1)}, u32[]{:S(2)}, u32[]{:S(2)}) %collective-permute-start.14) | collective-permute-done | bytes 64 | tf_op jit(solution)/shard_map/ppermute | solution.py:21
  52.0 1.9 %collective-permute-start.15 = (f32[1,2,4]{2,1,0:T(2,128)S(1)}, f32[1,2,4]{2,1,0:T(2,128)S(1)}, u32[]{:S(2)}, u32[]{:S(2)}) collective-permute-start(f32[1,2,4]{2,1,0:T(2,128)S(1)} %add.349), channel_id=1, source_target_pairs={{0,4},{1,5},{2,6},{3,7},{4,0},{5,1},{6,2},{7,3},{8,12},{9,13},{10,... | collective-permute-start | bytes 104 | tf_op jit(solution)/shard_map/ppermute | solution.py:21
  53.9 1.7 %collective-permute-done.15 = f32[1,2,4]{2,1,0:T(2,128)S(1)} collective-permute-done((f32[1,2,4]{2,1,0:T(2,128)S(1)}, f32[1,2,4]{2,1,0:T(2,128)S(1)}, u32[]{:S(2)}, u32[]{:S(2)}) %collective-permute-start.15) | collective-permute-done | bytes 64 | tf_op jit(solution)/shard_map/ppermute | solution.py:21
  55.6 2.9 %collective-permute-start.16 = (f32[1,2,4]{2,1,0:T(2,128)S(1)}, f32[1,2,4]{2,1,0:T(2,128)S(1)}, u32[]{:S(2)}, u32[]{:S(2)}) collective-permute-start(f32[1,2,4]{2,1,0:T(2,128)S(1)} %add.350), channel_id=1, source_target_pairs={{0,8},{1,9},{2,10},{3,11},{4,12},{5,13},{6,14},{7,15},{8,0},{9,1},... | collective-permute-start | bytes 104 | tf_op jit(solution)/shard_map/ppermute | solution.py:21
  58.5 1.5 %collective-permute-done.16 = f32[1,2,4]{2,1,0:T(2,128)S(1)} collective-permute-done((f32[1,2,4]{2,1,0:T(2,128)S(1)}, f32[1,2,4]{2,1,0:T(2,128)S(1)}, u32[]{:S(2)}, u32[]{:S(2)}) %collective-permute-start.16) | collective-permute-done | bytes 64 | tf_op jit(solution)/shard_map/ppermute | solution.py:21
  60.3 1.8 %collective-permute-start.17 = (f32[4]{0:T(128)S(1)}, f32[4]{0:T(128)S(1)}, u32[]{:S(2)}, u32[]{:S(2)}) collective-permute-start(f32[4]{0:T(128)S(1)} %fusion.36), channel_id=1, source_target_pairs={{0,16},{16,0},{1,17},{17,1},{2,18},{18,2},{3,19},{19,3},{4,20},{20... | collective-permute-start | bytes 56 | tf_op jit(solution)/shard_map/ppermute | solution.py:21
  62.1 1.8 %collective-permute-done.17 = f32[4]{0:T(128)S(1)} collective-permute-done((f32[4]{0:T(128)S(1)}, f32[4]{0:T(128)S(1)}, u32[]{:S(2)}, u32[]{:S(2)}) %collective-permute-start.17) | collective-permute-done | bytes 48 | tf_op jit(solution)/shard_map/ppermute | solution.py:21
  63.9 1.1 collective-permute-done.18
  65.0 3.5 %collective-permute-done.19 = f32[4]{0:T(128)S(1)} collective-permute-done((f32[4]{0:T(128)S(1)}, f32[4]{0:T(128)S(1)}, u32[]{:S(2)}, u32[]{:S(2)}) %collective-permute-start.19) | collective-permute-done | bytes 48 | tf_op jit(solution)/shard_map/ppermute | solution.py:21
  68.5 1.9 %collective-permute-start.20 = (f32[4]{0:T(128)S(1)}, f32[4]{0:T(128)S(1)}, u32[]{:S(2)}, u32[]{:S(2)}) collective-permute-start(f32[4]{0:T(128)S(1)} %add.356), channel_id=1, source_target_pairs={{0,4},{1,5},{2,6},{3,7},{4,0},{5,1},{6,2},{7,3},{8,12},{9,13},{10,... | collective-permute-start | bytes 56 | tf_op jit(solution)/shard_map/ppermute | solution.py:21
  70.4 1.7 %collective-permute-done.20 = f32[4]{0:T(128)S(1)} collective-permute-done((f32[4]{0:T(128)S(1)}, f32[4]{0:T(128)S(1)}, u32[]{:S(2)}, u32[]{:S(2)}) %collective-permute-start.20) | collective-permute-done | bytes 48 | tf_op jit(solution)/shard_map/ppermute | solution.py:21
  72.1 2.9 %collective-permute-start.21 = (f32[4]{0:T(128)S(1)}, f32[4]{0:T(128)S(1)}, u32[]{:S(2)}, u32[]{:S(2)}) collective-permute-start(f32[4]{0:T(128)S(1)} %add.357), channel_id=1, source_target_pairs={{0,8},{1,9},{2,10},{3,11},{4,12},{5,13},{6,14},{7,15},{8,0},{9,1},... | collective-permute-start | bytes 56 | tf_op jit(solution)/shard_map/ppermute | solution.py:21
  75.0 1.5 %collective-permute-done.21 = f32[4]{0:T(128)S(1)} collective-permute-done((f32[4]{0:T(128)S(1)}, f32[4]{0:T(128)S(1)}, u32[]{:S(2)}, u32[]{:S(2)}) %collective-permute-start.21) | collective-permute-done | bytes 48 | tf_op jit(solution)/shard_map/ppermute | solution.py:21
  76.9 1.2 collective-permute-done.24
  78.1 2.1 %collective-permute-start.22 = (bf16[2,4,1,512]{3,1,0,2:T(4,128)(2,1)S(1)}, bf16[2,4,1,512]{3,1,0,2:T(4,128)(2,1)S(1)}, u32[]{:S(2)}, u32[]{:S(2)}) collective-permute-start(bf16[2,4,1,512]{3,1,0,2:T(4,128)(2,1)S(1)} %get-tuple-element.22), channel_id=1, source_target_pairs={{0,1},{1,2},{2,3},{3,4},{4,5},{5,6},{6,7},{7,8},{8,9},{9,10},{10,1... | collective-permute-start | bytes 24584 | tf_op jit(solution)/shard_map/ppermute | solution.py:49
  80.1 1.3 collective-permute-start.23
  81.4 1.8 %collective-permute-start.28 = (f32[1,2,4,512]{3,2,1,0:T(4,128)S(1)}, f32[1,2,4,512]{3,2,1,0:T(4,128)S(1)}, u32[]{:S(2)}, u32[]{:S(2)}) collective-permute-start(f32[1,2,4,512]{3,2,1,0:T(4,128)S(1)} %bitcast.252), channel_id=1, source_target_pairs={{0,16},{16,0},{1,17},{17,1},{2,18},{18,2},{3,19},{19,3},{4,20},{20... | collective-permute-start | bytes 49160 | tf_op jit(solution)/shard_map/ppermute | solution.py:34
  83.3 4.8 %collective-permute-start.26 = (f32[4,2,4,64]{3,2,1,0:T(4,128)S(1)}, f32[4,2,4,64]{3,2,1,0:T(4,128)S(1)}, u32[]{:S(2)}, u32[]{:S(2)}) collective-permute-start(f32[4,2,4,64]{3,2,1,0:T(4,128)S(1)} %maximum_select_fusion.7), channel_id=1, source_target_pairs={{0,4},{1,5},{2,6},{3,7},{4,0},{5,1},{6,2},{7,3},{8,12},{9,13},{10,... | collective-permute-start | bytes 24584 | tf_op jit(solution)/shard_map/ppermute | solution.py:34
  88.8 0.7 fusion.7
  89.8 3.4 %collective-permute-start.27 = (f32[8,2,4,64]{3,2,1,0:T(4,128)S(1)}, f32[8,2,4,64]{3,2,1,0:T(4,128)S(1)}, u32[]{:S(2)}, u32[]{:S(2)}) collective-permute-start(f32[8,2,4,64]{3,2,1,0:T(4,128)S(1)} %maximum_select_fusion.4), channel_id=1, source_target_pairs={{0,8},{1,9},{2,10},{3,11},{4,12},{5,13},{6,14},{7,15},{8,0},{9,1},... | collective-permute-start | bytes 49160 | tf_op jit(solution)/shard_map/ppermute | solution.py:34
  94.0 1.1 collective-permute-done.27
  95.1 2.6 %convolution_bitcast_fusion.2 = f32[2,2,4,64]{3,2,0,1:T(4,128)S(1)} fusion(f32[1,1,16,2,64,64]{5,4,3,2,1,0:T(8,128)} %param.18, f32[16,64,64]{2,1,0:T(8,128)S(1)} %and_convert_fusion, f32[8,2,4,64]{3,2,1,0:T(4,128)S(1)} %collective-permute-done.27, f32[8,2,4,64]{3,2,1,0:T(4,128)S(1)} %maximum_select_fusion.4, pred[]{:T(512)S(6)} %eq.31), kind=kOutput, calls=%fused_computation.12 | convolution fusion | flops 12738560 | bytes 823297 | tf_op jit(solution)/shard_map/sakl,spql->apqk/dot_general | solution.py:91
  98.1 0.7 collective-permute-start.29
  98.9 2.9 %collective-permute-done.29 = f32[2,2,4]{2,1,0:T(2,128)S(1)} collective-permute-done((f32[2,2,4]{2,1,0:T(2,128)S(1)}, f32[2,2,4]{2,1,0:T(2,128)S(1)}, u32[]{:S(2)}, u32[]{:S(2)}) %collective-permute-start.29) | collective-permute-done | bytes 96 | tf_op jit(solution)/shard_map/ppermute | solution.py:21
  101.8 1.1 collective-permute-done.30
  102.9 1.1 collective-permute-start.31
  104.1 2.4 %collective-permute-done.31 = f32[2,2,4]{2,1,0:T(2,128)S(1)} collective-permute-done((f32[2,2,4]{2,1,0:T(2,128)S(1)}, f32[2,2,4]{2,1,0:T(2,128)S(1)}, u32[]{:S(2)}, u32[]{:S(2)}) %collective-permute-start.31) | collective-permute-done | bytes 96 | tf_op jit(solution)/shard_map/ppermute | solution.py:21
  106.5 1.7 %collective-permute-start.32 = (f32[2,2,4]{2,1,0:T(2,128)S(1)}, f32[2,2,4]{2,1,0:T(2,128)S(1)}, u32[]{:S(2)}, u32[]{:S(2)}) collective-permute-start(f32[2,2,4]{2,1,0:T(2,128)S(1)} %add.374), channel_id=1, source_target_pairs={{0,4},{1,5},{2,6},{3,7},{4,0},{5,1},{6,2},{7,3},{8,12},{9,13},{10,... | collective-permute-start | bytes 200 | tf_op jit(solution)/shard_map/ppermute | solution.py:21
  108.8 1.3 collective-permute-done.32
  110.1 2.9 %collective-permute-start.33 = (f32[2,2,4]{2,1,0:T(2,128)S(1)}, f32[2,2,4]{2,1,0:T(2,128)S(1)}, u32[]{:S(2)}, u32[]{:S(2)}) collective-permute-start(f32[2,2,4]{2,1,0:T(2,128)S(1)} %add.375), channel_id=1, source_target_pairs={{0,8},{1,9},{2,10},{3,11},{4,12},{5,13},{6,14},{7,15},{8,0},{9,1},... | collective-permute-start | bytes 200 | tf_op jit(solution)/shard_map/ppermute | solution.py:21
  113.1 1.5 %collective-permute-done.33 = f32[2,2,4]{2,1,0:T(2,128)S(1)} collective-permute-done((f32[2,2,4]{2,1,0:T(2,128)S(1)}, f32[2,2,4]{2,1,0:T(2,128)S(1)}, u32[]{:S(2)}, u32[]{:S(2)}) %collective-permute-start.33) | collective-permute-done | bytes 96 | tf_op jit(solution)/shard_map/ppermute | solution.py:21
  115.9 2.6 %collective-permute-done.34 = f32[4]{0:T(128)S(1)} collective-permute-done((f32[4]{0:T(128)S(1)}, f32[4]{0:T(128)S(1)}, u32[]{:S(2)}, u32[]{:S(2)}) %collective-permute-start.34) | collective-permute-done | bytes 48 | tf_op jit(solution)/shard_map/ppermute | solution.py:21
  118.5 1.1 collective-permute-done.35
  119.6 1.1 collective-permute-start.36
  120.7 2.4 %collective-permute-done.36 = f32[4]{0:T(128)S(1)} collective-permute-done((f32[4]{0:T(128)S(1)}, f32[4]{0:T(128)S(1)}, u32[]{:S(2)}, u32[]{:S(2)}) %collective-permute-start.36) | collective-permute-done | bytes 48 | tf_op jit(solution)/shard_map/ppermute | solution.py:21
  123.2 1.8 %collective-permute-start.37 = (f32[4]{0:T(128)S(1)}, f32[4]{0:T(128)S(1)}, u32[]{:S(2)}, u32[]{:S(2)}) collective-permute-start(f32[4]{0:T(128)S(1)} %add.382), channel_id=1, source_target_pairs={{0,4},{1,5},{2,6},{3,7},{4,0},{5,1},{6,2},{7,3},{8,12},{9,13},{10,... | collective-permute-start | bytes 56 | tf_op jit(solution)/shard_map/ppermute | solution.py:21
  125.0 1.7 %collective-permute-done.37 = f32[4]{0:T(128)S(1)} collective-permute-done((f32[4]{0:T(128)S(1)}, f32[4]{0:T(128)S(1)}, u32[]{:S(2)}, u32[]{:S(2)}) %collective-permute-start.37) | collective-permute-done | bytes 48 | tf_op jit(solution)/shard_map/ppermute | solution.py:21
  126.7 2.9 %collective-permute-start.38 = (f32[4]{0:T(128)S(1)}, f32[4]{0:T(128)S(1)}, u32[]{:S(2)}, u32[]{:S(2)}) collective-permute-start(f32[4]{0:T(128)S(1)} %add.383), channel_id=1, source_target_pairs={{0,8},{1,9},{2,10},{3,11},{4,12},{5,13},{6,14},{7,15},{8,0},{9,1},... | collective-permute-start | bytes 56 | tf_op jit(solution)/shard_map/ppermute | solution.py:21
  129.6 1.5 %collective-permute-done.38 = f32[4]{0:T(128)S(1)} collective-permute-done((f32[4]{0:T(128)S(1)}, f32[4]{0:T(128)S(1)}, u32[]{:S(2)}, u32[]{:S(2)}) %collective-permute-start.38) | collective-permute-done | bytes 48 | tf_op jit(solution)/shard_map/ppermute | solution.py:21
  132.0 0.7 stack.135
  (136 shorter events, 11.2 us)
Async XLA Ops:
  0.6 33.8 %copy-start = (bf16[1,2,4,2,256,256]{5,4,3,2,1,0:T(8,128)(2,1)S(1)}, bf16[1,2,4,2,256,256]{5,4,3,2,1,0:T(8,128)(2,1)}, u32[]{:S(2)}) copy-start(bf16[1,2,4,2,256,256]{5,4,3,2,1,0:T(8,128)(2,1)} %param.13) | copy-start | bytes 6291460
  1.6 6.1 %collective-permute-start = (f32[4]{0:T(128)S(1)}, f32[4]{0:T(128)S(1)}, u32[]{:S(2)}, u32[]{:S(2)}) collective-permute-start(f32[4]{0:T(128)S(1)} %add_reduce_fusion.3), channel_id=1, source_target_pairs={{0,16},{16,0},{1,17},{17,1},{2,18},{18,2},{3,19},{19,3},{4,20},{20... | collective-permute-start | bytes 56 | tf_op jit(solution)/shard_map/ppermute | solution.py:21
  7.7 1.2 collective-permute-start.1
  8.9 3.5 %collective-permute-start.2 = (f32[4]{0:T(128)S(1)}, f32[4]{0:T(128)S(1)}, u32[]{:S(2)}, u32[]{:S(2)}) collective-permute-start(f32[4]{0:T(128)S(1)} %add.326), channel_id=1, source_target_pairs={{0,2},{1,3},{2,0},{3,1},{4,6},{5,7},{6,4},{7,5},{8,10},{9,11},{10,... | collective-permute-start | bytes 56 | tf_op jit(solution)/shard_map/ppermute | solution.py:21
  12.4 3.5 %collective-permute-start.3 = (f32[4]{0:T(128)S(1)}, f32[4]{0:T(128)S(1)}, u32[]{:S(2)}, u32[]{:S(2)}) collective-permute-start(f32[4]{0:T(128)S(1)} %add.327), channel_id=1, source_target_pairs={{0,4},{1,5},{2,6},{3,7},{4,0},{5,1},{6,2},{7,3},{8,12},{9,13},{10,... | collective-permute-start | bytes 56 | tf_op jit(solution)/shard_map/ppermute | solution.py:21
  16.0 4.4 %collective-permute-start.4 = (f32[4]{0:T(128)S(1)}, f32[4]{0:T(128)S(1)}, u32[]{:S(2)}, u32[]{:S(2)}) collective-permute-start(f32[4]{0:T(128)S(1)} %add.328), channel_id=1, source_target_pairs={{0,8},{1,9},{2,10},{3,11},{4,12},{5,13},{6,14},{7,15},{8,0},{9,1},... | collective-permute-start | bytes 56 | tf_op jit(solution)/shard_map/ppermute | solution.py:21
  22.3 1.2 collective-permute-start.7
  23.6 5.2 %collective-permute-start.8 = (f32[2,2,4,64]{3,2,1,0:T(4,128)S(1)}, f32[2,2,4,64]{3,2,1,0:T(4,128)S(1)}, u32[]{:S(2)}, u32[]{:S(2)}) collective-permute-start(f32[2,2,4,64]{3,2,1,0:T(4,128)S(1)} %maximum_select_fusion.8), channel_id=1, source_target_pairs={{0,2},{1,3},{2,0},{3,1},{4,6},{5,7},{6,4},{7,5},{8,10},{9,11},{10,... | collective-permute-start | bytes 12296 | tf_op jit(solution)/shard_map/ppermute | solution.py:34
  25.1 8.7 %collective-permute-start.5 = (bf16[2,4,1,512]{3,1,0,2:T(4,128)(2,1)S(1)}, bf16[2,4,1,512]{3,1,0,2:T(4,128)(2,1)S(1)}, u32[]{:S(2)}, u32[]{:S(2)}) collective-permute-start(bf16[2,4,1,512]{3,1,0,2:T(4,128)(2,1)S(1)} %get-tuple-element.24), channel_id=1, source_target_pairs={{0,1},{1,2},{2,3},{3,4},{4,5},{5,6},{6,7},{7,8},{8,9},{9,10},{10,1... | collective-permute-start | bytes 24584 | tf_op jit(solution)/shard_map/ppermute | solution.py:49
  26.9 6.9 %collective-permute-start.6 = (bf16[2,4,1,512]{3,1,0,2:T(4,128)(2,1)S(1)}, bf16[2,4,1,512]{3,1,0,2:T(4,128)(2,1)S(1)}, u32[]{:S(2)}, u32[]{:S(2)}) collective-permute-start(bf16[2,4,1,512]{3,1,0,2:T(4,128)(2,1)S(1)} %get-tuple-element.24), channel_id=1, source_target_pairs={{1,0},{2,1},{3,2},{4,3},{5,4},{6,5},{7,6},{8,7},{9,8},{10,9},{11,1... | collective-permute-start | bytes 24584 | tf_op jit(solution)/shard_map/ppermute | solution.py:51
  28.1 10.4 %collective-permute-start.11 = (f32[1,2,4,512]{3,2,1,0:T(4,128)S(1)}, f32[1,2,4,512]{3,2,1,0:T(4,128)S(1)}, u32[]{:S(2)}, u32[]{:S(2)}) collective-permute-start(f32[1,2,4,512]{3,2,1,0:T(4,128)S(1)} %bitcast.250), channel_id=1, source_target_pairs={{0,16},{16,0},{1,17},{17,1},{2,18},{18,2},{3,19},{19,3},{4,20},{20... | collective-permute-start | bytes 49160 | tf_op jit(solution)/shard_map/ppermute | solution.py:34
  28.7 6.7 %collective-permute-start.9 = (f32[4,2,4,64]{3,2,1,0:T(4,128)S(1)}, f32[4,2,4,64]{3,2,1,0:T(4,128)S(1)}, u32[]{:S(2)}, u32[]{:S(2)}) collective-permute-start(f32[4,2,4,64]{3,2,1,0:T(4,128)S(1)} %maximum_select_fusion.6), channel_id=1, source_target_pairs={{0,4},{1,5},{2,6},{3,7},{4,0},{5,1},{6,2},{7,3},{8,12},{9,13},{10,... | collective-permute-start | bytes 24584 | tf_op jit(solution)/shard_map/ppermute | solution.py:34
  34.5 8.7 %copy-start.2 = (bf16[1,2,64,512]{3,2,1,0:T(8,128)(2,1)S(1)}, bf16[1,2,64,512]{3,2,1,0:T(8,128)(2,1)}, u32[]{:S(2)}) copy-start(bf16[1,2,64,512]{3,2,1,0:T(8,128)(2,1)} %param.17) | copy-start | bytes 393220
  34.5 42.1 %copy-start.1 = (bf16[1,2,64,512]{3,2,1,0:T(8,128)(2,1)S(1)}, bf16[1,2,64,512]{3,2,1,0:T(8,128)(2,1)}, u32[]{:S(2)}) copy-start(bf16[1,2,64,512]{3,2,1,0:T(8,128)(2,1)} %param.16) | copy-start | bytes 393220
  35.5 5.0 %collective-permute-start.10 = (f32[8,2,4,64]{3,2,1,0:T(4,128)S(1)}, f32[8,2,4,64]{3,2,1,0:T(4,128)S(1)}, u32[]{:S(2)}, u32[]{:S(2)}) collective-permute-start(f32[8,2,4,64]{3,2,1,0:T(4,128)S(1)} %maximum_select_fusion.2), channel_id=1, source_target_pairs={{0,8},{1,9},{2,10},{3,11},{4,12},{5,13},{6,14},{7,15},{8,0},{9,1},... | collective-permute-start | bytes 49160 | tf_op jit(solution)/shard_map/ppermute | solution.py:34
  43.5 3.6 %collective-permute-start.12 = (f32[1,2,4]{2,1,0:T(2,128)S(1)}, f32[1,2,4]{2,1,0:T(2,128)S(1)}, u32[]{:S(2)}, u32[]{:S(2)}) collective-permute-start(f32[1,2,4]{2,1,0:T(2,128)S(1)} %maximum_bitcast_fusion.8), channel_id=1, source_target_pairs={{0,16},{16,0},{1,17},{17,1},{2,18},{18,2},{3,19},{19,3},{4,20},{20... | collective-permute-start | bytes 104 | tf_op jit(solution)/shard_map/ppermute | solution.py:21
  47.1 1.2 collective-permute-start.13
  48.3 3.6 %collective-permute-start.14 = (f32[1,2,4]{2,1,0:T(2,128)S(1)}, f32[1,2,4]{2,1,0:T(2,128)S(1)}, u32[]{:S(2)}, u32[]{:S(2)}) collective-permute-start(f32[1,2,4]{2,1,0:T(2,128)S(1)} %fusion.68), channel_id=1, source_target_pairs={{0,2},{1,3},{2,0},{3,1},{4,6},{5,7},{6,4},{7,5},{8,10},{9,11},{10,... | collective-permute-start | bytes 104 | tf_op jit(solution)/shard_map/ppermute | solution.py:21
  52.0 3.6 %collective-permute-start.15 = (f32[1,2,4]{2,1,0:T(2,128)S(1)}, f32[1,2,4]{2,1,0:T(2,128)S(1)}, u32[]{:S(2)}, u32[]{:S(2)}) collective-permute-start(f32[1,2,4]{2,1,0:T(2,128)S(1)} %add.349), channel_id=1, source_target_pairs={{0,4},{1,5},{2,6},{3,7},{4,0},{5,1},{6,2},{7,3},{8,12},{9,13},{10,... | collective-permute-start | bytes 104 | tf_op jit(solution)/shard_map/ppermute | solution.py:21
  55.6 4.5 %collective-permute-start.16 = (f32[1,2,4]{2,1,0:T(2,128)S(1)}, f32[1,2,4]{2,1,0:T(2,128)S(1)}, u32[]{:S(2)}, u32[]{:S(2)}) collective-permute-start(f32[1,2,4]{2,1,0:T(2,128)S(1)} %add.350), channel_id=1, source_target_pairs={{0,8},{1,9},{2,10},{3,11},{4,12},{5,13},{6,14},{7,15},{8,0},{9,1},... | collective-permute-start | bytes 104 | tf_op jit(solution)/shard_map/ppermute | solution.py:21
  60.3 3.6 %collective-permute-start.17 = (f32[4]{0:T(128)S(1)}, f32[4]{0:T(128)S(1)}, u32[]{:S(2)}, u32[]{:S(2)}) collective-permute-start(f32[4]{0:T(128)S(1)} %fusion.36), channel_id=1, source_target_pairs={{0,16},{16,0},{1,17},{17,1},{2,18},{18,2},{3,19},{19,3},{4,20},{20... | collective-permute-start | bytes 56 | tf_op jit(solution)/shard_map/ppermute | solution.py:21
  63.9 1.1 collective-permute-start.18
  65.0 3.5 %collective-permute-start.19 = (f32[4]{0:T(128)S(1)}, f32[4]{0:T(128)S(1)}, u32[]{:S(2)}, u32[]{:S(2)}) collective-permute-start(f32[4]{0:T(128)S(1)} %add.355), channel_id=1, source_target_pairs={{0,2},{1,3},{2,0},{3,1},{4,6},{5,7},{6,4},{7,5},{8,10},{9,11},{10,... | collective-permute-start | bytes 56 | tf_op jit(solution)/shard_map/ppermute | solution.py:21
  68.5 3.5 %collective-permute-start.20 = (f32[4]{0:T(128)S(1)}, f32[4]{0:T(128)S(1)}, u32[]{:S(2)}, u32[]{:S(2)}) collective-permute-start(f32[4]{0:T(128)S(1)} %add.356), channel_id=1, source_target_pairs={{0,4},{1,5},{2,6},{3,7},{4,0},{5,1},{6,2},{7,3},{8,12},{9,13},{10,... | collective-permute-start | bytes 56 | tf_op jit(solution)/shard_map/ppermute | solution.py:21
  72.1 4.4 %collective-permute-start.21 = (f32[4]{0:T(128)S(1)}, f32[4]{0:T(128)S(1)}, u32[]{:S(2)}, u32[]{:S(2)}) collective-permute-start(f32[4]{0:T(128)S(1)} %add.357), channel_id=1, source_target_pairs={{0,8},{1,9},{2,10},{3,11},{4,12},{5,13},{6,14},{7,15},{8,0},{9,1},... | collective-permute-start | bytes 56 | tf_op jit(solution)/shard_map/ppermute | solution.py:21
  76.8 1.2 collective-permute-start.24
  78.1 5.2 %collective-permute-start.25 = (f32[2,2,4,64]{3,2,1,0:T(4,128)S(1)}, f32[2,2,4,64]{3,2,1,0:T(4,128)S(1)}, u32[]{:S(2)}, u32[]{:S(2)}) collective-permute-start(f32[2,2,4,64]{3,2,1,0:T(4,128)S(1)} %maximum_select_fusion.9), channel_id=1, source_target_pairs={{0,2},{1,3},{2,0},{3,1},{4,6},{5,7},{6,4},{7,5},{8,10},{9,11},{10,... | collective-permute-start | bytes 12296 | tf_op jit(solution)/shard_map/ppermute | solution.py:34
  78.1 10.1 %collective-permute-start.22 = (bf16[2,4,1,512]{3,1,0,2:T(4,128)(2,1)S(1)}, bf16[2,4,1,512]{3,1,0,2:T(4,128)(2,1)S(1)}, u32[]{:S(2)}, u32[]{:S(2)}) collective-permute-start(bf16[2,4,1,512]{3,1,0,2:T(4,128)(2,1)S(1)} %get-tuple-element.22), channel_id=1, source_target_pairs={{0,1},{1,2},{2,3},{3,4},{4,5},{5,6},{6,7},{7,8},{8,9},{9,10},{10,1... | collective-permute-start | bytes 24584 | tf_op jit(solution)/shard_map/ppermute | solution.py:49
  80.1 8.0 %collective-permute-start.23 = (bf16[2,4,1,512]{3,1,0,2:T(4,128)(2,1)S(1)}, bf16[2,4,1,512]{3,1,0,2:T(4,128)(2,1)S(1)}, u32[]{:S(2)}, u32[]{:S(2)}) collective-permute-start(bf16[2,4,1,512]{3,1,0,2:T(4,128)(2,1)S(1)} %get-tuple-element.22), channel_id=1, source_target_pairs={{1,0},{2,1},{3,2},{4,3},{5,4},{6,5},{7,6},{8,7},{9,8},{10,9},{11,1... | collective-permute-start | bytes 24584 | tf_op jit(solution)/shard_map/ppermute | solution.py:51
  81.4 11.8 %collective-permute-start.28 = (f32[1,2,4,512]{3,2,1,0:T(4,128)S(1)}, f32[1,2,4,512]{3,2,1,0:T(4,128)S(1)}, u32[]{:S(2)}, u32[]{:S(2)}) collective-permute-start(f32[1,2,4,512]{3,2,1,0:T(4,128)S(1)} %bitcast.252), channel_id=1, source_target_pairs={{0,16},{16,0},{1,17},{17,1},{2,18},{18,2},{3,19},{19,3},{4,20},{20... | collective-permute-start | bytes 49160 | tf_op jit(solution)/shard_map/ppermute | solution.py:34
  83.3 6.5 %collective-permute-start.26 = (f32[4,2,4,64]{3,2,1,0:T(4,128)S(1)}, f32[4,2,4,64]{3,2,1,0:T(4,128)S(1)}, u32[]{:S(2)}, u32[]{:S(2)}) collective-permute-start(f32[4,2,4,64]{3,2,1,0:T(4,128)S(1)} %maximum_select_fusion.7), channel_id=1, source_target_pairs={{0,4},{1,5},{2,6},{3,7},{4,0},{5,1},{6,2},{7,3},{8,12},{9,13},{10,... | collective-permute-start | bytes 24584 | tf_op jit(solution)/shard_map/ppermute | solution.py:34
  89.8 5.2 %collective-permute-start.27 = (f32[8,2,4,64]{3,2,1,0:T(4,128)S(1)}, f32[8,2,4,64]{3,2,1,0:T(4,128)S(1)}, u32[]{:S(2)}, u32[]{:S(2)}) collective-permute-start(f32[8,2,4,64]{3,2,1,0:T(4,128)S(1)} %maximum_select_fusion.4), channel_id=1, source_target_pairs={{0,8},{1,9},{2,10},{3,11},{4,12},{5,13},{6,14},{7,15},{8,0},{9,1},... | collective-permute-start | bytes 49160 | tf_op jit(solution)/shard_map/ppermute | solution.py:34
  98.1 3.7 %collective-permute-start.29 = (f32[2,2,4]{2,1,0:T(2,128)S(1)}, f32[2,2,4]{2,1,0:T(2,128)S(1)}, u32[]{:S(2)}, u32[]{:S(2)}) collective-permute-start(f32[2,2,4]{2,1,0:T(2,128)S(1)} %pad_maximum_fusion.2), channel_id=1, source_target_pairs={{0,16},{16,0},{1,17},{17,1},{2,18},{18,2},{3,19},{19,3},{4,20},{20... | collective-permute-start | bytes 200 | tf_op jit(solution)/shard_map/ppermute | solution.py:21
  101.7 1.2 collective-permute-start.30
  102.9 3.6 %collective-permute-start.31 = (f32[2,2,4]{2,1,0:T(2,128)S(1)}, f32[2,2,4]{2,1,0:T(2,128)S(1)}, u32[]{:S(2)}, u32[]{:S(2)}) collective-permute-start(f32[2,2,4]{2,1,0:T(2,128)S(1)} %fusion.67), channel_id=1, source_target_pairs={{0,2},{1,3},{2,0},{3,1},{4,6},{5,7},{6,4},{7,5},{8,10},{9,11},{10,... | collective-permute-start | bytes 200 | tf_op jit(solution)/shard_map/ppermute | solution.py:21
  106.5 3.6 %collective-permute-start.32 = (f32[2,2,4]{2,1,0:T(2,128)S(1)}, f32[2,2,4]{2,1,0:T(2,128)S(1)}, u32[]{:S(2)}, u32[]{:S(2)}) collective-permute-start(f32[2,2,4]{2,1,0:T(2,128)S(1)} %add.374), channel_id=1, source_target_pairs={{0,4},{1,5},{2,6},{3,7},{4,0},{5,1},{6,2},{7,3},{8,12},{9,13},{10,... | collective-permute-start | bytes 200 | tf_op jit(solution)/shard_map/ppermute | solution.py:21
  110.1 4.5 %collective-permute-start.33 = (f32[2,2,4]{2,1,0:T(2,128)S(1)}, f32[2,2,4]{2,1,0:T(2,128)S(1)}, u32[]{:S(2)}, u32[]{:S(2)}) collective-permute-start(f32[2,2,4]{2,1,0:T(2,128)S(1)} %add.375), channel_id=1, source_target_pairs={{0,8},{1,9},{2,10},{3,11},{4,12},{5,13},{6,14},{7,15},{8,0},{9,1},... | collective-permute-start | bytes 200 | tf_op jit(solution)/shard_map/ppermute | solution.py:21
  114.9 3.6 %collective-permute-start.34 = (f32[4]{0:T(128)S(1)}, f32[4]{0:T(128)S(1)}, u32[]{:S(2)}, u32[]{:S(2)}) collective-permute-start(f32[4]{0:T(128)S(1)} %fusion.32), channel_id=1, source_target_pairs={{0,16},{16,0},{1,17},{17,1},{2,18},{18,2},{3,19},{19,3},{4,20},{20... | collective-permute-start | bytes 56 | tf_op jit(solution)/shard_map/ppermute | solution.py:21
  118.5 1.1 collective-permute-start.35
  119.6 3.5 %collective-permute-start.36 = (f32[4]{0:T(128)S(1)}, f32[4]{0:T(128)S(1)}, u32[]{:S(2)}, u32[]{:S(2)}) collective-permute-start(f32[4]{0:T(128)S(1)} %add.381), channel_id=1, source_target_pairs={{0,2},{1,3},{2,0},{3,1},{4,6},{5,7},{6,4},{7,5},{8,10},{9,11},{10,... | collective-permute-start | bytes 56 | tf_op jit(solution)/shard_map/ppermute | solution.py:21
  123.2 3.5 %collective-permute-start.37 = (f32[4]{0:T(128)S(1)}, f32[4]{0:T(128)S(1)}, u32[]{:S(2)}, u32[]{:S(2)}) collective-permute-start(f32[4]{0:T(128)S(1)} %add.382), channel_id=1, source_target_pairs={{0,4},{1,5},{2,6},{3,7},{4,0},{5,1},{6,2},{7,3},{8,12},{9,13},{10,... | collective-permute-start | bytes 56 | tf_op jit(solution)/shard_map/ppermute | solution.py:21
  126.7 4.4 %collective-permute-start.38 = (f32[4]{0:T(128)S(1)}, f32[4]{0:T(128)S(1)}, u32[]{:S(2)}, u32[]{:S(2)}) collective-permute-start(f32[4]{0:T(128)S(1)} %add.383), channel_id=1, source_target_pairs={{0,8},{1,9},{2,10},{3,11},{4,12},{5,13},{6,14},{7,15},{8,0},{9,1},... | collective-permute-start | bytes 56 | tf_op jit(solution)/shard_map/ppermute | solution.py:21

commit v2 on v1

--- a/solution.py
+++ b/solution.py
@@ -142,22 +142,50 @@
     first_vec = right_side / beta[None, :, None, None]
     image_one = operator(first_vec)
 
-    def projections(vectors, image):
-        return tree_sum(local_products(vectors, image), everyone) / total
-
-    def lengths(field):
-        return tree_sum(local_squares(field), everyone) / total
-
-    h_one_one = projections([first_vec], image_one)[0]
+    def reduced(parts):
+        return tree_sum(jnp.concatenate(parts), everyone) / total
+
+    def self_products(field):
+        return local_squares(field)[None]
+
+    one = reduced(
+        [
+            local_products([first_vec], image_one)[0],
+            self_products(image_one),
+            self_products(first_vec),
+        ]
+    )
+    h_one_one = one[0:2]
+    sq_w1 = one[2]
+    sq_v1 = one[3]
+    norm_h11 = h_one_one[0] * h_one_one[0] + h_one_one[1] * h_one_one[1]
+    sq_u1 = jnp.maximum(sq_w1 - norm_h11 * (2.0 - sq_v1), 0.0)
     rest_one = image_one - scaled(h_one_one, first_vec)
-    h_two_one = jnp.sqrt(lengths(rest_one) + EPSILON)
+    h_two_one = jnp.sqrt(sq_u1 + EPSILON)
     second_basis = rest_one / h_two_one[None, :, None, None]
     image_two = operator(second_basis)
-    both = projections([first_vec, second_basis], image_two)
-    h_one_two = both[0]
-    h_two_two = both[1]
+    two = reduced(
+        [
+            local_products([first_vec, second_basis], image_two).reshape(4, -1),
+            local_products([first_vec], second_basis)[0],
+            self_products(image_two),
+            self_products(second_basis),
+        ]
+    )
+    h_one_two = two[0:2]
+    h_two_two = two[2:4]
+    cross = two[4:6]
+    sq_w2 = two[6]
+    sq_v2 = two[7]
+    norm_a = h_one_two[0] * h_one_two[0] + h_one_two[1] * h_one_two[1]
+    norm_b = h_two_two[0] * h_two_two[0] + h_two_two[1] * h_two_two[1]
+    ab_re = h_one_two[0] * h_two_two[0] + h_one_two[1] * h_two_two[1]
+    ab_im = h_one_two[0] * h_two_two[1] - h_one_two[1] * h_two_two[0]
+    mixed = ab_re * cross[0] - ab_im * cross[1]
+    sq_u2 = sq_w2 - norm_a * (2.0 - sq_v1) - norm_b * (2.0 - sq_v2) + 2.0 * mixed
+    sq_u2 = jnp.maximum(sq_u2, 0.0)
     rest_two = image_two - scaled(h_one_two, first_vec) - scaled(h_two_two, second_basis)
-    h_three_two = jnp.sqrt(lengths(rest_two) + EPSILON)
+    h_three_two = jnp.sqrt(sq_u2 + EPSILON)
     third_basis = rest_two / h_three_two[None, :, None, None]
     hessenberg = jnp.stack(
         [

time: 133 us -> 101 us (0.76)
  waiting for transfers between devices: 49.9 us -> 31.2 us
  starting transfers between devices: 61.8 us -> 48.6 us
    ppermute x25 -> x15, waiting for transfers between devices: 44.8 us -> 26.1 us  [tree_sum(): x = x + lax.ppermute(x, axis, [(i, i ^ k) for i in range(n)])]
    ppermute x25 -> x15, starting transfers between devices: 35 us -> 21.9 us  [tree_sum(): x = x + lax.ppermute(x, axis, [(i, i ^ k) for i in range(n)])]
  transfers between devices with their start and end apart: 39 -> 29, of which waited for: 30 -> 20; matrix products, arithmetic and copies ran while one was open for 7% -> 8% of each run, Pallas kernels for 0% -> 0%
where the time goes in v2:
time: 101 us
  starting transfers between devices  48.6 us (48%)
  waiting for transfers between devices  31.2 us (31%)
  matrix products  8.04 us (8%)
  local copies, waits for them, and re-layouts  6.11 us (6%)
  other arithmetic  5.56 us (6%)
  between operations  1.1 us (1%)
    ppermute x15, waiting for transfers between devices, tree_sum(): x = x + lax.ppermute(x, axis, [(i, i ^ k) for i in range(n)])  26.1 us
    ppermute x15, starting transfers between devices, tree_sum(): x = x + lax.ppermute(x, axis, [(i, i ^ k) for i in range(n)])  21.9 us
    ppermute x10, starting transfers between devices, tree_gather(): other = lax.ppermute(buf, axis, [(i, i ^ k) for i in range(n)])  20.3 us
    dot_general x2, matrix products, apply_operator(): jnp.einsum('sakl,spql->apqk', weights, tree_gather(coeffs, 'blk'), precis...  5.23 us
    ppermute x10, waiting for transfers between devices, tree_gather(): other = lax.ppermute(buf, axis, [(i, i ^ k) for i in range(n)])  5.08 us
    ppermute x2, starting transfers between devices, extended(): lax.ppermute(tail, axis, [(i, (i + 1) % count) for i in range(ends)])  3.85 us
    ppermute x2, starting transfers between devices, extended(): lax.ppermute(head, axis, [((i + 1) % count, i) for i in range(ends)])  2.58 us
  transfers between devices with their start and end apart: 29, of which 20 were waited for; matrix products, arithmetic and copies ran while one was open for 8% of the time, Pallas kernels for 0%

profile of v2, /device:TPU:0, one launch (start us, length us, event | category | flops | bytes accessed | tf_op | source)
XLA Modules:
  0.0 100.6 jit_solution(17932889044627908649)
XLA Ops:
  0.6 1.0 add_reduce_fusion.8
  1.6 3.0 %collective-permute-start = (f32[4]{0:T(128)S(1)}, f32[4]{0:T(128)S(1)}, u32[]{:S(2)}, u32[]{:S(2)}) collective-permute-start(f32[4]{0:T(128)S(1)} %add_reduce_fusion.8), channel_id=1, source_target_pairs={{0,16},{16,0},{1,17},{17,1},{2,18},{18,2},{3,19},{19,3},{4,20},{20... | collective-permute-start | bytes 56 | tf_op jit(solution)/shard_map/ppermute | solution.py:21
  4.6 0.7 compare_select_fusion
  5.3 0.7 compare_and_fusion
  6.0 0.8 reshape_squeeze.4
  6.7 0.7 iota_compare_fusion
  7.5 0.2 and_convert_fusion
  7.8 1.1 %collective-permute-done.1 = f32[4]{0:T(128)S(1)} collective-permute-done((f32[4]{0:T(128)S(1)}, f32[4]{0:T(128)S(1)}, u32[]{:S(2)}, u32[]{:S(2)}) %collective-permute-start.1) | collective-permute-done | bytes 48 | tf_op jit(solution)/shard_map/ppermute | solution.py:21
  8.9 1.5 %collective-permute-start.2 = (f32[4]{0:T(128)S(1)}, f32[4]{0:T(128)S(1)}, u32[]{:S(2)}, u32[]{:S(2)}) collective-permute-start(f32[4]{0:T(128)S(1)} %add.438), channel_id=1, source_target_pairs={{0,2},{1,3},{2,0},{3,1},{4,6},{5,7},{6,4},{7,5},{8,10},{9,11},{10,... | collective-permute-start | bytes 56 | tf_op jit(solution)/shard_map/ppermute | solution.py:21
  10.4 2.0 %collective-permute-done.2 = f32[4]{0:T(128)S(1)} collective-permute-done((f32[4]{0:T(128)S(1)}, f32[4]{0:T(128)S(1)}, u32[]{:S(2)}, u32[]{:S(2)}) %collective-permute-start.2) | collective-permute-done | bytes 48 | tf_op jit(solution)/shard_map/ppermute | solution.py:21
  12.4 1.6 %collective-permute-start.3 = (f32[4]{0:T(128)S(1)}, f32[4]{0:T(128)S(1)}, u32[]{:S(2)}, u32[]{:S(2)}) collective-permute-start(f32[4]{0:T(128)S(1)} %add.439), channel_id=1, source_target_pairs={{0,4},{1,5},{2,6},{3,7},{4,0},{5,1},{6,2},{7,3},{8,12},{9,13},{10,... | collective-permute-start | bytes 56 | tf_op jit(solution)/shard_map/ppermute | solution.py:21
  14.0 2.0 %collective-permute-done.3 = f32[4]{0:T(128)S(1)} collective-permute-done((f32[4]{0:T(128)S(1)}, f32[4]{0:T(128)S(1)}, u32[]{:S(2)}, u32[]{:S(2)}) %collective-permute-start.3) | collective-permute-done | bytes 48 | tf_op jit(solution)/shard_map/ppermute | solution.py:21
  16.0 2.6 %collective-permute-start.4 = (f32[4]{0:T(128)S(1)}, f32[4]{0:T(128)S(1)}, u32[]{:S(2)}, u32[]{:S(2)}) collective-permute-start(f32[4]{0:T(128)S(1)} %add.440), channel_id=1, source_target_pairs={{0,8},{1,9},{2,10},{3,11},{4,12},{5,13},{6,14},{7,15},{8,0},{9,1},... | collective-permute-start | bytes 56 | tf_op jit(solution)/shard_map/ppermute | solution.py:21
  18.6 1.9 %collective-permute-done.4 = f32[4]{0:T(128)S(1)} collective-permute-done((f32[4]{0:T(128)S(1)}, f32[4]{0:T(128)S(1)}, u32[]{:S(2)}, u32[]{:S(2)}) %collective-permute-start.4) | collective-permute-done | bytes 48 | tf_op jit(solution)/shard_map/ppermute | solution.py:21
  20.4 0.8 fusion.76
  21.2 1.1 %convolution_bitcast_fusion.5 = f32[2,2,4,64]{3,2,0,1:T(4,128)S(1)} fusion(bf16[1,2,64,512]{3,2,1,0:T(8,128)(2,1)} %param.16, bf16[2,4,1,512]{3,1,0,2:T(4,128)(2,1)S(1)} %get-tuple-element.30), kind=kOutput, calls=%fused_computation.15 | convolution fusion | flops 1048576 | bytes 143360 | tf_op jit(solution)/shard_map/akr,pqr->apqk/dot_general | solution.py:81
  22.4 1.1 %collective-permute-done.7 = f32[1,2,4,64]{3,2,1,0:T(4,128)S(1)} collective-permute-done((f32[1,2,4,64]{3,2,1,0:T(4,128)S(1)}, f32[1,2,4,64]{3,2,1,0:T(4,128)S(1)}, u32[]{:S(2)}, u32[]{:S(2)}) %collective-permute-start.7) | collective-permute-done | bytes 2080 | tf_op jit(solution)/shard_map/ppermute | solution.py:34
  23.6 1.5 %collective-permute-start.8 = (f32[2,2,4,64]{3,2,1,0:T(4,128)S(1)}, f32[2,2,4,64]{3,2,1,0:T(4,128)S(1)}, u32[]{:S(2)}, u32[]{:S(2)}) collective-permute-start(f32[2,2,4,64]{3,2,1,0:T(4,128)S(1)} %maximum_select_fusion.8), channel_id=1, source_target_pairs={{0,2},{1,3},{2,0},{3,1},{4,6},{5,7},{6,4},{7,5},{8,10},{9,11},{10,... | collective-permute-start | bytes 12296 | tf_op jit(solution)/shard_map/ppermute | solution.py:34
  25.1 1.8 %collective-permute-start.5 = (bf16[2,4,1,512]{3,1,0,2:T(4,128)(2,1)S(1)}, bf16[2,4,1,512]{3,1,0,2:T(4,128)(2,1)S(1)}, u32[]{:S(2)}, u32[]{:S(2)}) collective-permute-start(bf16[2,4,1,512]{3,1,0,2:T(4,128)(2,1)S(1)} %get-tuple-element.30), channel_id=1, source_target_pairs={{0,1},{1,2},{2,3},{3,4},{4,5},{5,6},{6,7},{7,8},{8,9},{9,10},{10,1... | collective-permute-start | bytes 24584 | tf_op jit(solution)/shard_map/ppermute | solution.py:49
  26.9 1.3 %collective-permute-start.6 = (bf16[2,4,1,512]{3,1,0,2:T(4,128)(2,1)S(1)}, bf16[2,4,1,512]{3,1,0,2:T(4,128)(2,1)S(1)}, u32[]{:S(2)}, u32[]{:S(2)}) collective-permute-start(bf16[2,4,1,512]{3,1,0,2:T(4,128)(2,1)S(1)} %get-tuple-element.30), channel_id=1, source_target_pairs={{1,0},{2,1},{3,2},{4,3},{5,4},{6,5},{7,6},{8,7},{9,8},{10,9},{11,1... | collective-permute-start | bytes 24584 | tf_op jit(solution)/shard_map/ppermute | solution.py:51
  28.1 0.6 collective-permute-start.11
  28.7 5.0 %collective-permute-start.9 = (f32[4,2,4,64]{3,2,1,0:T(4,128)S(1)}, f32[4,2,4,64]{3,2,1,0:T(4,128)S(1)}, u32[]{:S(2)}, u32[]{:S(2)}) collective-permute-start(f32[4,2,4,64]{3,2,1,0:T(4,128)S(1)} %maximum_select_fusion.6), channel_id=1, source_target_pairs={{0,4},{1,5},{2,6},{3,7},{4,0},{5,1},{6,2},{7,3},{8,12},{9,13},{10,... | collective-permute-start | bytes 24584 | tf_op jit(solution)/shard_map/ppermute | solution.py:34
  33.8 0.6 gather_fusion
  34.5 0.7 fusion.4
  35.2 0.3 collective-permute-done.9
  35.5 3.1 %collective-permute-start.10 = (f32[8,2,4,64]{3,2,1,0:T(4,128)S(1)}, f32[8,2,4,64]{3,2,1,0:T(4,128)S(1)}, u32[]{:S(2)}, u32[]{:S(2)}) collective-permute-start(f32[8,2,4,64]{3,2,1,0:T(4,128)S(1)} %maximum_select_fusion.2), channel_id=1, source_target_pairs={{0,8},{1,9},{2,10},{3,11},{4,12},{5,13},{6,14},{7,15},{8,0},{9,1},... | collective-permute-start | bytes 49160 | tf_op jit(solution)/shard_map/ppermute | solution.py:34
  38.7 0.6 gather_fusion.1
  39.4 1.1 %collective-permute-done.10 = f32[8,2,4,64]{3,2,1,0:T(4,128)S(1)} collective-permute-done((f32[8,2,4,64]{3,2,1,0:T(4,128)S(1)}, f32[8,2,4,64]{3,2,1,0:T(4,128)S(1)}, u32[]{:S(2)}, u32[]{:S(2)}) %collective-permute-start.10) | collective-permute-done | bytes 16416 | tf_op jit(solution)/shard_map/ppermute | solution.py:34
  40.5 2.6 %convolution_bitcast_fusion.4 = f32[2,2,4,64]{3,2,0,1:T(4,128)S(1)} fusion(f32[1,1,16,2,64,64]{5,4,3,2,1,0:T(8,128)} %param.18, f32[16,64,64]{2,1,0:T(8,128)S(1)} %and_convert_fusion, f32[8,2,4,64]{3,2,1,0:T(4,128)S(1)} %collective-permute-done.10, f32[8,2,4,64]{3,2,1,0:T(4,128)S(1)} %maximum_select_fusion.2, pred[]{:T(512)S(6)} %eq.31), kind=kOutput, calls=%fused_computation.14 | convolution fusion | flops 12738560 | bytes 823297 | tf_op jit(solution)/shard_map/sakl,spql->apqk/dot_general | solution.py:91
  43.3 0.2 add_reduce_fusion.7
  43.5 1.8 %collective-permute-start.12 = (f32[4,4]{1,0:T(4,128)S(1)}, f32[4,4]{1,0:T(4,128)S(1)}, u32[]{:S(2)}, u32[]{:S(2)}) collective-permute-start(f32[4,4]{1,0:T(4,128)S(1)} %pad_maximum_fusion.2), channel_id=1, source_target_pairs={{0,16},{16,0},{1,17},{17,1},{2,18},{18,2},{3,19},{19,3},{4,20},{20... | collective-permute-start | bytes 200 | tf_op jit(solution)/shard_map/ppermute | solution.py:21
  45.2 1.9 %collective-permute-done.12 = f32[4,4]{1,0:T(4,128)S(1)} collective-permute-done((f32[4,4]{1,0:T(4,128)S(1)}, f32[4,4]{1,0:T(4,128)S(1)}, u32[]{:S(2)}, u32[]{:S(2)}) %collective-permute-start.12) | collective-permute-done | bytes 96 | tf_op jit(solution)/shard_map/ppermute | solution.py:21
  47.2 1.1 %collective-permute-done.13 = f32[4,4]{1,0:T(4,128)S(1)} collective-permute-done((f32[4,4]{1,0:T(4,128)S(1)}, f32[4,4]{1,0:T(4,128)S(1)}, u32[]{:S(2)}, u32[]{:S(2)}) %collective-permute-start.13) | collective-permute-done | bytes 96 | tf_op jit(solution)/shard_map/ppermute | solution.py:21
  48.5 3.6 %collective-permute-done.14 = f32[4,4]{1,0:T(4,128)S(1)} collective-permute-done((f32[4,4]{1,0:T(4,128)S(1)}, f32[4,4]{1,0:T(4,128)S(1)}, u32[]{:S(2)}, u32[]{:S(2)}) %collective-permute-start.14) | collective-permute-done | bytes 96 | tf_op jit(solution)/shard_map/ppermute | solution.py:21
  52.0 1.9 %collective-permute-start.15 = (f32[4,4]{1,0:T(4,128)S(1)}, f32[4,4]{1,0:T(4,128)S(1)}, u32[]{:S(2)}, u32[]{:S(2)}) collective-permute-start(f32[4,4]{1,0:T(4,128)S(1)} %add.463), channel_id=1, source_target_pairs={{0,4},{1,5},{2,6},{3,7},{4,0},{5,1},{6,2},{7,3},{8,12},{9,13},{10,... | collective-permute-start | bytes 200 | tf_op jit(solution)/shard_map/ppermute | solution.py:21
  54.0 1.7 %collective-permute-done.15 = f32[4,4]{1,0:T(4,128)S(1)} collective-permute-done((f32[4,4]{1,0:T(4,128)S(1)}, f32[4,4]{1,0:T(4,128)S(1)}, u32[]{:S(2)}, u32[]{:S(2)}) %collective-permute-start.15) | collective-permute-done | bytes 96 | tf_op jit(solution)/shard_map/ppermute | solution.py:21
  55.6 2.9 %collective-permute-start.16 = (f32[4,4]{1,0:T(4,128)S(1)}, f32[4,4]{1,0:T(4,128)S(1)}, u32[]{:S(2)}, u32[]{:S(2)}) collective-permute-start(f32[4,4]{1,0:T(4,128)S(1)} %add.464), channel_id=1, source_target_pairs={{0,8},{1,9},{2,10},{3,11},{4,12},{5,13},{6,14},{7,15},{8,0},{9,1},... | collective-permute-start | bytes 200 | tf_op jit(solution)/shard_map/ppermute | solution.py:21
  58.6 1.6 %collective-permute-done.16 = f32[4,4]{1,0:T(4,128)S(1)} collective-permute-done((f32[4,4]{1,0:T(4,128)S(1)}, f32[4,4]{1,0:T(4,128)S(1)}, u32[]{:S(2)}, u32[]{:S(2)}) %collective-permute-start.16) | collective-permute-done | bytes 96 | tf_op jit(solution)/shard_map/ppermute | solution.py:21
  60.3 0.1 convolution_bitcast_fusion.3
  60.6 1.2 %collective-permute-done.19 = f32[1,2,4,64]{3,2,1,0:T(4,128)S(1)} collective-permute-done((f32[1,2,4,64]{3,2,1,0:T(4,128)S(1)}, f32[1,2,4,64]{3,2,1,0:T(4,128)S(1)}, u32[]{:S(2)}, u32[]{:S(2)}) %collective-permute-start.19) | collective-permute-done | bytes 2080 | tf_op jit(solution)/shard_map/ppermute | solution.py:34
  61.8 2.1 %collective-permute-start.17 = (bf16[2,4,1,512]{3,1,0,2:T(4,128)(2,1)S(1)}, bf16[2,4,1,512]{3,1,0,2:T(4,128)(2,1)S(1)}, u32[]{:S(2)}, u32[]{:S(2)}) collective-permute-start(bf16[2,4,1,512]{3,1,0,2:T(4,128)(2,1)S(1)} %get-tuple-element.28), channel_id=1, source_target_pairs={{0,1},{1,2},{2,3},{3,4},{4,5},{5,6},{6,7},{7,8},{8,9},{9,10},{10,1... | collective-permute-start | bytes 24584 | tf_op jit(solution)/shard_map/ppermute | solution.py:49
  63.8 1.3 %collective-permute-start.18 = (bf16[2,4,1,512]{3,1,0,2:T(4,128)(2,1)S(1)}, bf16[2,4,1,512]{3,1,0,2:T(4,128)(2,1)S(1)}, u32[]{:S(2)}, u32[]{:S(2)}) collective-permute-start(bf16[2,4,1,512]{3,1,0,2:T(4,128)(2,1)S(1)} %get-tuple-element.28), channel_id=1, source_target_pairs={{1,0},{2,1},{3,2},{4,3},{5,4},{6,5},{7,6},{8,7},{9,8},{10,9},{11,1... | collective-permute-start | bytes 24584 | tf_op jit(solution)/shard_map/ppermute | solution.py:51
  65.1 1.8 %collective-permute-start.23 = (f32[1,2,4,512]{3,2,1,0:T(4,128)S(1)}, f32[1,2,4,512]{3,2,1,0:T(4,128)S(1)}, u32[]{:S(2)}, u32[]{:S(2)}) collective-permute-start(f32[1,2,4,512]{3,2,1,0:T(4,128)S(1)} %bitcast.369), channel_id=1, source_target_pairs={{0,16},{16,0},{1,17},{17,1},{2,18},{18,2},{3,19},{19,3},{4,20},{20... | collective-permute-start | bytes 49160 | tf_op jit(solution)/shard_map/ppermute | solution.py:34
  67.0 4.8 %collective-permute-start.21 = (f32[4,2,4,64]{3,2,1,0:T(4,128)S(1)}, f32[4,2,4,64]{3,2,1,0:T(4,128)S(1)}, u32[]{:S(2)}, u32[]{:S(2)}) collective-permute-start(f32[4,2,4,64]{3,2,1,0:T(4,128)S(1)} %maximum_select_fusion.7), channel_id=1, source_target_pairs={{0,4},{1,5},{2,6},{3,7},{4,0},{5,1},{6,2},{7,3},{8,12},{9,13},{10,... | collective-permute-start | bytes 24584 | tf_op jit(solution)/shard_map/ppermute | solution.py:34
  71.8 0.6 gather_fusion.2
  72.5 0.7 fusion.7
  73.2 0.3 collective-permute-done.21
  73.6 3.4 %collective-permute-start.22 = (f32[8,2,4,64]{3,2,1,0:T(4,128)S(1)}, f32[8,2,4,64]{3,2,1,0:T(4,128)S(1)}, u32[]{:S(2)}, u32[]{:S(2)}) collective-permute-start(f32[8,2,4,64]{3,2,1,0:T(4,128)S(1)} %maximum_select_fusion.4), channel_id=1, source_target_pairs={{0,8},{1,9},{2,10},{3,11},{4,12},{5,13},{6,14},{7,15},{8,0},{9,1},... | collective-permute-start | bytes 49160 | tf_op jit(solution)/shard_map/ppermute | solution.py:34
  77.0 0.6 gather_fusion.3
  77.7 1.1 %collective-permute-done.22 = f32[8,2,4,64]{3,2,1,0:T(4,128)S(1)} collective-permute-done((f32[8,2,4,64]{3,2,1,0:T(4,128)S(1)}, f32[8,2,4,64]{3,2,1,0:T(4,128)S(1)}, u32[]{:S(2)}, u32[]{:S(2)}) %collective-permute-start.22) | collective-permute-done | bytes 16416 | tf_op jit(solution)/shard_map/ppermute | solution.py:34
  78.8 2.6 %convolution_bitcast_fusion.2 = f32[2,2,4,64]{3,2,0,1:T(4,128)S(1)} fusion(f32[1,1,16,2,64,64]{5,4,3,2,1,0:T(8,128)} %param.18, f32[16,64,64]{2,1,0:T(8,128)S(1)} %and_convert_fusion, f32[8,2,4,64]{3,2,1,0:T(4,128)S(1)} %collective-permute-done.22, f32[8,2,4,64]{3,2,1,0:T(4,128)S(1)} %maximum_select_fusion.4, pred[]{:T(512)S(6)} %eq.31), kind=kOutput, calls=%fused_computation.12 | convolution fusion | flops 12738560 | bytes 823297 | tf_op jit(solution)/shard_map/sakl,spql->apqk/dot_general | solution.py:91
  81.6 0.2 subtract_reduce_fusion
  81.9 0.7 collective-permute-start.24
  82.6 3.0 %collective-permute-done.24 = f32[8,4]{1,0:T(8,128)S(1)} collective-permute-done((f32[8,4]{1,0:T(8,128)S(1)}, f32[8,4]{1,0:T(8,128)S(1)}, u32[]{:S(2)}, u32[]{:S(2)}) %collective-permute-start.24) | collective-permute-done | bytes 160 | tf_op jit(solution)/shard_map/ppermute | solution.py:21
  85.6 1.2 %collective-permute-done.25 = f32[8,4]{1,0:T(8,128)S(1)} collective-permute-done((f32[8,4]{1,0:T(8,128)S(1)}, f32[8,4]{1,0:T(8,128)S(1)}, u32[]{:S(2)}, u32[]{:S(2)}) %collective-permute-start.25) | collective-permute-done | bytes 160 | tf_op jit(solution)/shard_map/ppermute | solution.py:21
  86.7 1.1 %collective-permute-start.26 = (f32[8,4]{1,0:T(8,128)S(1)}, f32[8,4]{1,0:T(8,128)S(1)}, u32[]{:S(2)}, u32[]{:S(2)}) collective-permute-start(f32[8,4]{1,0:T(8,128)S(1)} %add.485), channel_id=1, source_target_pairs={{0,2},{1,3},{2,0},{3,1},{4,6},{5,7},{6,4},{7,5},{8,10},{9,11},{10,... | collective-permute-start | bytes 392 | tf_op jit(solution)/shard_map/ppermute | solution.py:21
  87.9 0.6 copy.101
  88.6 1.8 %collective-permute-done.26 = f32[8,4]{1,0:T(8,128)S(1)} collective-permute-done((f32[8,4]{1,0:T(8,128)S(1)}, f32[8,4]{1,0:T(8,128)S(1)}, u32[]{:S(2)}, u32[]{:S(2)}) %collective-permute-start.26) | collective-permute-done | bytes 160 | tf_op jit(solution)/shard_map/ppermute | solution.py:21
  90.4 1.7 %collective-permute-start.27 = (f32[8,4]{1,0:T(8,128)S(1)}, f32[8,4]{1,0:T(8,128)S(1)}, u32[]{:S(2)}, u32[]{:S(2)}) collective-permute-start(f32[8,4]{1,0:T(8,128)S(1)} %add.486), channel_id=1, source_target_pairs={{0,4},{1,5},{2,6},{3,7},{4,0},{5,1},{6,2},{7,3},{8,12},{9,13},{10,... | collective-permute-start | bytes 392 | tf_op jit(solution)/shard_map/ppermute | solution.py:21
  92.1 1.9 %collective-permute-done.27 = f32[8,4]{1,0:T(8,128)S(1)} collective-permute-done((f32[8,4]{1,0:T(8,128)S(1)}, f32[8,4]{1,0:T(8,128)S(1)}, u32[]{:S(2)}, u32[]{:S(2)}) %collective-permute-start.27) | collective-permute-done | bytes 160 | tf_op jit(solution)/shard_map/ppermute | solution.py:21
  94.0 2.9 %collective-permute-start.28 = (f32[8,4]{1,0:T(8,128)S(1)}, f32[8,4]{1,0:T(8,128)S(1)}, u32[]{:S(2)}, u32[]{:S(2)}) collective-permute-start(f32[8,4]{1,0:T(8,128)S(1)} %add.487), channel_id=1, source_target_pairs={{0,8},{1,9},{2,10},{3,11},{4,12},{5,13},{6,14},{7,15},{8,0},{9,1},... | collective-permute-start | bytes 392 | tf_op jit(solution)/shard_map/ppermute | solution.py:21
  97.0 1.5 %collective-permute-done.28 = f32[8,4]{1,0:T(8,128)S(1)} collective-permute-done((f32[8,4]{1,0:T(8,128)S(1)}, f32[8,4]{1,0:T(8,128)S(1)}, u32[]{:S(2)}, u32[]{:S(2)}) %collective-permute-start.28) | collective-permute-done | bytes 160 | tf_op jit(solution)/shard_map/ppermute | solution.py:21
  99.3 0.6 copy.102
  100.0 0.7 stack.129
  (106 shorter events, 2.9 us)
Async XLA Ops:
  0.6 33.8 %copy-start = (bf16[1,2,4,2,256,256]{5,4,3,2,1,0:T(8,128)(2,1)S(1)}, bf16[1,2,4,2,256,256]{5,4,3,2,1,0:T(8,128)(2,1)}, u32[]{:S(2)}) copy-start(bf16[1,2,4,2,256,256]{5,4,3,2,1,0:T(8,128)(2,1)} %param.13) | copy-start | bytes 6291460
  1.6 6.1 %collective-permute-start = (f32[4]{0:T(128)S(1)}, f32[4]{0:T(128)S(1)}, u32[]{:S(2)}, u32[]{:S(2)}) collective-permute-start(f32[4]{0:T(128)S(1)} %add_reduce_fusion.8), channel_id=1, source_target_pairs={{0,16},{16,0},{1,17},{17,1},{2,18},{18,2},{3,19},{19,3},{4,20},{20... | collective-permute-start | bytes 56 | tf_op jit(solution)/shard_map/ppermute | solution.py:21
  7.7 1.2 %collective-permute-start.1 = (f32[4]{0:T(128)S(1)}, f32[4]{0:T(128)S(1)}, u32[]{:S(2)}, u32[]{:S(2)}) collective-permute-start(f32[4]{0:T(128)S(1)} %add.437), channel_id=1, source_target_pairs={{0,1},{1,0},{2,3},{3,2},{4,5},{5,4},{6,7},{7,6},{8,9},{9,8},{10,11... | collective-permute-start | bytes 56 | tf_op jit(solution)/shard_map/ppermute | solution.py:21
  8.9 3.5 %collective-permute-start.2 = (f32[4]{0:T(128)S(1)}, f32[4]{0:T(128)S(1)}, u32[]{:S(2)}, u32[]{:S(2)}) collective-permute-start(f32[4]{0:T(128)S(1)} %add.438), channel_id=1, source_target_pairs={{0,2},{1,3},{2,0},{3,1},{4,6},{5,7},{6,4},{7,5},{8,10},{9,11},{10,... | collective-permute-start | bytes 56 | tf_op jit(solution)/shard_map/ppermute | solution.py:21
  12.4 3.5 %collective-permute-start.3 = (f32[4]{0:T(128)S(1)}, f32[4]{0:T(128)S(1)}, u32[]{:S(2)}, u32[]{:S(2)}) collective-permute-start(f32[4]{0:T(128)S(1)} %add.439), channel_id=1, source_target_pairs={{0,4},{1,5},{2,6},{3,7},{4,0},{5,1},{6,2},{7,3},{8,12},{9,13},{10,... | collective-permute-start | bytes 56 | tf_op jit(solution)/shard_map/ppermute | solution.py:21
  16.0 4.4 %collective-permute-start.4 = (f32[4]{0:T(128)S(1)}, f32[4]{0:T(128)S(1)}, u32[]{:S(2)}, u32[]{:S(2)}) collective-permute-start(f32[4]{0:T(128)S(1)} %add.440), channel_id=1, source_target_pairs={{0,8},{1,9},{2,10},{3,11},{4,12},{5,13},{6,14},{7,15},{8,0},{9,1},... | collective-permute-start | bytes 56 | tf_op jit(solution)/shard_map/ppermute | solution.py:21
  22.3 1.2 %collective-permute-start.7 = (f32[1,2,4,64]{3,2,1,0:T(4,128)S(1)}, f32[1,2,4,64]{3,2,1,0:T(4,128)S(1)}, u32[]{:S(2)}, u32[]{:S(2)}) collective-permute-start(f32[1,2,4,64]{3,2,1,0:T(4,128)S(1)} %maximum_bitcast_fusion.2), channel_id=1, source_target_pairs={{0,1},{1,0},{2,3},{3,2},{4,5},{5,4},{6,7},{7,6},{8,9},{9,8},{10,11... | collective-permute-start | bytes 6152 | tf_op jit(solution)/shard_map/ppermute | solution.py:34
  23.6 5.2 %collective-permute-start.8 = (f32[2,2,4,64]{3,2,1,0:T(4,128)S(1)}, f32[2,2,4,64]{3,2,1,0:T(4,128)S(1)}, u32[]{:S(2)}, u32[]{:S(2)}) collective-permute-start(f32[2,2,4,64]{3,2,1,0:T(4,128)S(1)} %maximum_select_fusion.8), channel_id=1, source_target_pairs={{0,2},{1,3},{2,0},{3,1},{4,6},{5,7},{6,4},{7,5},{8,10},{9,11},{10,... | collective-permute-start | bytes 12296 | tf_op jit(solution)/shard_map/ppermute | solution.py:34
  25.1 8.7 %collective-permute-start.5 = (bf16[2,4,1,512]{3,1,0,2:T(4,128)(2,1)S(1)}, bf16[2,4,1,512]{3,1,0,2:T(4,128)(2,1)S(1)}, u32[]{:S(2)}, u32[]{:S(2)}) collective-permute-start(bf16[2,4,1,512]{3,1,0,2:T(4,128)(2,1)S(1)} %get-tuple-element.30), channel_id=1, source_target_pairs={{0,1},{1,2},{2,3},{3,4},{4,5},{5,6},{6,7},{7,8},{8,9},{9,10},{10,1... | collective-permute-start | bytes 24584 | tf_op jit(solution)/shard_map/ppermute | solution.py:49
  26.9 6.9 %collective-permute-start.6 = (bf16[2,4,1,512]{3,1,0,2:T(4,128)(2,1)S(1)}, bf16[2,4,1,512]{3,1,0,2:T(4,128)(2,1)S(1)}, u32[]{:S(2)}, u32[]{:S(2)}) collective-permute-start(bf16[2,4,1,512]{3,1,0,2:T(4,128)(2,1)S(1)} %get-tuple-element.30), channel_id=1, source_target_pairs={{1,0},{2,1},{3,2},{4,3},{5,4},{6,5},{7,6},{8,7},{9,8},{10,9},{11,1... | collective-permute-start | bytes 24584 | tf_op jit(solution)/shard_map/ppermute | solution.py:51
  28.1 10.4 %collective-permute-start.11 = (f32[1,2,4,512]{3,2,1,0:T(4,128)S(1)}, f32[1,2,4,512]{3,2,1,0:T(4,128)S(1)}, u32[]{:S(2)}, u32[]{:S(2)}) collective-permute-start(f32[1,2,4,512]{3,2,1,0:T(4,128)S(1)} %bitcast.367), channel_id=1, source_target_pairs={{0,16},{16,0},{1,17},{17,1},{2,18},{18,2},{3,19},{19,3},{4,20},{20... | collective-permute-start | bytes 49160 | tf_op jit(solution)/shard_map/ppermute | solution.py:34
  28.7 6.7 %collective-permute-start.9 = (f32[4,2,4,64]{3,2,1,0:T(4,128)S(1)}, f32[4,2,4,64]{3,2,1,0:T(4,128)S(1)}, u32[]{:S(2)}, u32[]{:S(2)}) collective-permute-start(f32[4,2,4,64]{3,2,1,0:T(4,128)S(1)} %maximum_select_fusion.6), channel_id=1, source_target_pairs={{0,4},{1,5},{2,6},{3,7},{4,0},{5,1},{6,2},{7,3},{8,12},{9,13},{10,... | collective-permute-start | bytes 24584 | tf_op jit(solution)/shard_map/ppermute | solution.py:34
  34.5 8.7 %copy-start.2 = (bf16[1,2,64,512]{3,2,1,0:T(8,128)(2,1)S(1)}, bf16[1,2,64,512]{3,2,1,0:T(8,128)(2,1)}, u32[]{:S(2)}) copy-start(bf16[1,2,64,512]{3,2,1,0:T(8,128)(2,1)} %param.17) | copy-start | bytes 393220
  34.5 25.8 %copy-start.1 = (bf16[1,2,64,512]{3,2,1,0:T(8,128)(2,1)S(1)}, bf16[1,2,64,512]{3,2,1,0:T(8,128)(2,1)}, u32[]{:S(2)}) copy-start(bf16[1,2,64,512]{3,2,1,0:T(8,128)(2,1)} %param.16) | copy-start | bytes 393220
  35.5 5.0 %collective-permute-start.10 = (f32[8,2,4,64]{3,2,1,0:T(4,128)S(1)}, f32[8,2,4,64]{3,2,1,0:T(4,128)S(1)}, u32[]{:S(2)}, u32[]{:S(2)}) collective-permute-start(f32[8,2,4,64]{3,2,1,0:T(4,128)S(1)} %maximum_select_fusion.2), channel_id=1, source_target_pairs={{0,8},{1,9},{2,10},{3,11},{4,12},{5,13},{6,14},{7,15},{8,0},{9,1},... | collective-permute-start | bytes 49160 | tf_op jit(solution)/shard_map/ppermute | solution.py:34
  43.5 3.7 %collective-permute-start.12 = (f32[4,4]{1,0:T(4,128)S(1)}, f32[4,4]{1,0:T(4,128)S(1)}, u32[]{:S(2)}, u32[]{:S(2)}) collective-permute-start(f32[4,4]{1,0:T(4,128)S(1)} %pad_maximum_fusion.2), channel_id=1, source_target_pairs={{0,16},{16,0},{1,17},{17,1},{2,18},{18,2},{3,19},{19,3},{4,20},{20... | collective-permute-start | bytes 200 | tf_op jit(solution)/shard_map/ppermute | solution.py:21
  47.2 1.2 %collective-permute-start.13 = (f32[4,4]{1,0:T(4,128)S(1)}, f32[4,4]{1,0:T(4,128)S(1)}, u32[]{:S(2)}, u32[]{:S(2)}) collective-permute-start(f32[4,4]{1,0:T(4,128)S(1)} %fusion.73), channel_id=1, source_target_pairs={{0,1},{1,0},{2,3},{3,2},{4,5},{5,4},{6,7},{7,6},{8,9},{9,8},{10,11... | collective-permute-start | bytes 200 | tf_op jit(solution)/shard_map/ppermute | solution.py:21
  48.4 3.7 %collective-permute-start.14 = (f32[4,4]{1,0:T(4,128)S(1)}, f32[4,4]{1,0:T(4,128)S(1)}, u32[]{:S(2)}, u32[]{:S(2)}) collective-permute-start(f32[4,4]{1,0:T(4,128)S(1)} %fusion.77), channel_id=1, source_target_pairs={{0,2},{1,3},{2,0},{3,1},{4,6},{5,7},{6,4},{7,5},{8,10},{9,11},{10,... | collective-permute-start | bytes 200 | tf_op jit(solution)/shard_map/ppermute | solution.py:21
  52.0 3.6 %collective-permute-start.15 = (f32[4,4]{1,0:T(4,128)S(1)}, f32[4,4]{1,0:T(4,128)S(1)}, u32[]{:S(2)}, u32[]{:S(2)}) collective-permute-start(f32[4,4]{1,0:T(4,128)S(1)} %add.463), channel_id=1, source_target_pairs={{0,4},{1,5},{2,6},{3,7},{4,0},{5,1},{6,2},{7,3},{8,12},{9,13},{10,... | collective-permute-start | bytes 200 | tf_op jit(solution)/shard_map/ppermute | solution.py:21
  55.6 4.5 %collective-permute-start.16 = (f32[4,4]{1,0:T(4,128)S(1)}, f32[4,4]{1,0:T(4,128)S(1)}, u32[]{:S(2)}, u32[]{:S(2)}) collective-permute-start(f32[4,4]{1,0:T(4,128)S(1)} %add.464), channel_id=1, source_target_pairs={{0,8},{1,9},{2,10},{3,11},{4,12},{5,13},{6,14},{7,15},{8,0},{9,1},... | collective-permute-start | bytes 200 | tf_op jit(solution)/shard_map/ppermute | solution.py:21
  60.5 1.2 %collective-permute-start.19 = (f32[1,2,4,64]{3,2,1,0:T(4,128)S(1)}, f32[1,2,4,64]{3,2,1,0:T(4,128)S(1)}, u32[]{:S(2)}, u32[]{:S(2)}) collective-permute-start(f32[1,2,4,64]{3,2,1,0:T(4,128)S(1)} %maximum_bitcast_fusion.3), channel_id=1, source_target_pairs={{0,1},{1,0},{2,3},{3,2},{4,5},{5,4},{6,7},{7,6},{8,9},{9,8},{10,11... | collective-permute-start | bytes 6152 | tf_op jit(solution)/shard_map/ppermute | solution.py:34
  61.8 5.2 %collective-permute-start.20 = (f32[2,2,4,64]{3,2,1,0:T(4,128)S(1)}, f32[2,2,4,64]{3,2,1,0:T(4,128)S(1)}, u32[]{:S(2)}, u32[]{:S(2)}) collective-permute-start(f32[2,2,4,64]{3,2,1,0:T(4,128)S(1)} %maximum_select_fusion.9), channel_id=1, source_target_pairs={{0,2},{1,3},{2,0},{3,1},{4,6},{5,7},{6,4},{7,5},{8,10},{9,11},{10,... | collective-permute-start | bytes 12296 | tf_op jit(solution)/shard_map/ppermute | solution.py:34
  61.8 10.1 %collective-permute-start.17 = (bf16[2,4,1,512]{3,1,0,2:T(4,128)(2,1)S(1)}, bf16[2,4,1,512]{3,1,0,2:T(4,128)(2,1)S(1)}, u32[]{:S(2)}, u32[]{:S(2)}) collective-permute-start(bf16[2,4,1,512]{3,1,0,2:T(4,128)(2,1)S(1)} %get-tuple-element.28), channel_id=1, source_target_pairs={{0,1},{1,2},{2,3},{3,4},{4,5},{5,6},{6,7},{7,8},{8,9},{9,10},{10,1... | collective-permute-start | bytes 24584 | tf_op jit(solution)/shard_map/ppermute | solution.py:49
  63.8 8.0 %collective-permute-start.18 = (bf16[2,4,1,512]{3,1,0,2:T(4,128)(2,1)S(1)}, bf16[2,4,1,512]{3,1,0,2:T(4,128)(2,1)S(1)}, u32[]{:S(2)}, u32[]{:S(2)}) collective-permute-start(bf16[2,4,1,512]{3,1,0,2:T(4,128)(2,1)S(1)} %get-tuple-element.28), channel_id=1, source_target_pairs={{1,0},{2,1},{3,2},{4,3},{5,4},{6,5},{7,6},{8,7},{9,8},{10,9},{11,1... | collective-permute-start | bytes 24584 | tf_op jit(solution)/shard_map/ppermute | solution.py:51
  65.1 11.8 %collective-permute-start.23 = (f32[1,2,4,512]{3,2,1,0:T(4,128)S(1)}, f32[1,2,4,512]{3,2,1,0:T(4,128)S(1)}, u32[]{:S(2)}, u32[]{:S(2)}) collective-permute-start(f32[1,2,4,512]{3,2,1,0:T(4,128)S(1)} %bitcast.369), channel_id=1, source_target_pairs={{0,16},{16,0},{1,17},{17,1},{2,18},{18,2},{3,19},{19,3},{4,20},{20... | collective-permute-start | bytes 49160 | tf_op jit(solution)/shard_map/ppermute | solution.py:34
  67.0 6.5 %collective-permute-start.21 = (f32[4,2,4,64]{3,2,1,0:T(4,128)S(1)}, f32[4,2,4,64]{3,2,1,0:T(4,128)S(1)}, u32[]{:S(2)}, u32[]{:S(2)}) collective-permute-start(f32[4,2,4,64]{3,2,1,0:T(4,128)S(1)} %maximum_select_fusion.7), channel_id=1, source_target_pairs={{0,4},{1,5},{2,6},{3,7},{4,0},{5,1},{6,2},{7,3},{8,12},{9,13},{10,... | collective-permute-start | bytes 24584 | tf_op jit(solution)/shard_map/ppermute | solution.py:34
  73.6 5.2 %collective-permute-start.22 = (f32[8,2,4,64]{3,2,1,0:T(4,128)S(1)}, f32[8,2,4,64]{3,2,1,0:T(4,128)S(1)}, u32[]{:S(2)}, u32[]{:S(2)}) collective-permute-start(f32[8,2,4,64]{3,2,1,0:T(4,128)S(1)} %maximum_select_fusion.4), channel_id=1, source_target_pairs={{0,8},{1,9},{2,10},{3,11},{4,12},{5,13},{6,14},{7,15},{8,0},{9,1},... | collective-permute-start | bytes 49160 | tf_op jit(solution)/shard_map/ppermute | solution.py:34
  81.9 3.7 %collective-permute-start.24 = (f32[8,4]{1,0:T(8,128)S(1)}, f32[8,4]{1,0:T(8,128)S(1)}, u32[]{:S(2)}, u32[]{:S(2)}) collective-permute-start(f32[8,4]{1,0:T(8,128)S(1)} %concatenate.97), channel_id=1, source_target_pairs={{0,16},{16,0},{1,17},{17,1},{2,18},{18,2},{3,19},{19,3},{4,20},{20... | collective-permute-start | bytes 392 | tf_op jit(solution)/shard_map/ppermute | solution.py:21
  85.6 1.2 %collective-permute-start.25 = (f32[8,4]{1,0:T(8,128)S(1)}, f32[8,4]{1,0:T(8,128)S(1)}, u32[]{:S(2)}, u32[]{:S(2)}) collective-permute-start(f32[8,4]{1,0:T(8,128)S(1)} %add.484), channel_id=1, source_target_pairs={{0,1},{1,0},{2,3},{3,2},{4,5},{5,4},{6,7},{7,6},{8,9},{9,8},{10,11... | collective-permute-start | bytes 392 | tf_op jit(solution)/shard_map/ppermute | solution.py:21
  86.7 3.6 %collective-permute-start.26 = (f32[8,4]{1,0:T(8,128)S(1)}, f32[8,4]{1,0:T(8,128)S(1)}, u32[]{:S(2)}, u32[]{:S(2)}) collective-permute-start(f32[8,4]{1,0:T(8,128)S(1)} %add.485), channel_id=1, source_target_pairs={{0,2},{1,3},{2,0},{3,1},{4,6},{5,7},{6,4},{7,5},{8,10},{9,11},{10,... | collective-permute-start | bytes 392 | tf_op jit(solution)/shard_map/ppermute | solution.py:21
  90.4 3.6 %collective-permute-start.27 = (f32[8,4]{1,0:T(8,128)S(1)}, f32[8,4]{1,0:T(8,128)S(1)}, u32[]{:S(2)}, u32[]{:S(2)}) collective-permute-start(f32[8,4]{1,0:T(8,128)S(1)} %add.486), channel_id=1, source_target_pairs={{0,4},{1,5},{2,6},{3,7},{4,0},{5,1},{6,2},{7,3},{8,12},{9,13},{10,... | collective-permute-start | bytes 392 | tf_op jit(solution)/shard_map/ppermute | solution.py:21
  94.0 4.5 %collective-permute-start.28 = (f32[8,4]{1,0:T(8,128)S(1)}, f32[8,4]{1,0:T(8,128)S(1)}, u32[]{:S(2)}, u32[]{:S(2)}) collective-permute-start(f32[8,4]{1,0:T(8,128)S(1)} %add.487), channel_id=1, source_target_pairs={{0,8},{1,9},{2,10},{3,11},{4,12},{5,13},{6,14},{7,15},{8,0},{9,1},... | collective-permute-start | bytes 392 | tf_op jit(solution)/shard_map/ppermute | solution.py:21

commit v3 on v2

v3 whole, which is shorter than its diff:
```python
import jax
import jax.numpy as jnp
from jax import lax
from jax.sharding import PartitionSpec as P

EPSILON = 1e-06


def _pow2(n):
    return n > 0 and (n & (n - 1)) == 0


def tree_sum(x, axes):
    for axis in axes:
        n = lax.axis_size(axis)
        if not _pow2(n):
            x = lax.psum(x, axis)
            continue
        k = 1
        while k < n:
            x = x + lax.ppermute(x, axis, [(i, i ^ k) for i in range(n)])
            k *= 2
    return x


def tree_collect(red, gat_blk, gat_dom):
    for axis, gat in (("blk", gat_blk), ("dom", gat_dom)):
        n = lax.axis_size(axis)
        if not _pow2(n):
            red = lax.psum(red, axis)
            buf = lax.all_gather(gat, axis, axis=0)
        else:
            idx = lax.axis_index(axis)
            buf = gat[None]
            k = 1
            while k < n:
                packed = jnp.concatenate([red.reshape(-1), buf.reshape(-1)])
                got = lax.ppermute(packed, axis, [(i, i ^ k) for i in range(n)])
                red = red + got[: red.size].reshape(red.shape)
                other = got[red.size :].reshape(buf.shape)
                low = (idx // k) % 2 == 0
                buf = jnp.where(low, jnp.concatenate([buf, other]), jnp.concatenate([other, buf]))
                k *= 2
        if axis == "blk":
            gat_blk = buf
        else:
            gat_dom = buf
    return red, gat_blk, gat_dom


def neighbours(field):
    count = lax.axis_size("blk")
    ends = count - 1
    left = lax.ppermute(field, "blk", [(i, i + 1) for i in range(ends)])
    right = lax.ppermute(field, "blk", [(i + 1, i) for i in range(ends)])
    return jnp.concatenate([left, field, right], axis=3)


def complex_mix(products):
    return jnp.stack([products[0, 0] - products[1, 1], products[0, 1] + products[1, 0]])


def coefficients(field, source_basis):
    rounded = field.astype(jnp.bfloat16)
    coef_prod = jnp.einsum(
        "akr,pqr->apqk", source_basis[0], rounded[:, :, 0], preferred_element_type=jnp.float32
    )
    return jnp.stack([coef_prod[0, 0] + coef_prod[1, 1], coef_prod[0, 1] - coef_prod[1, 0]])


def near_field(window, near_blocks, near_cols):
    nrhs = window.shape[1]
    blocks_dev = near_blocks.shape[1]
    slots = near_blocks.shape[2]
    width = near_blocks.shape[4]
    rounded = window.astype(jnp.bfloat16).reshape(2, nrhs, 3 * blocks_dev, width)
    chosen = jnp.take(rounded, near_cols[0].reshape(-1), axis=2).reshape(
        2, nrhs, blocks_dev, slots, width
    )
    near_prod = jnp.einsum(
        "ikarc,pqikc->apqir", near_blocks[0], chosen, preferred_element_type=jnp.float32
    )
    return complex_mix(near_prod).reshape(2, nrhs, 1, blocks_dev * width)


def far_weights(coupling, far_ranks, rank_cap):
    row_coupling = coupling[0, 0]
    row_ranks = far_ranks[0, 0]
    levels = jnp.arange(rank_cap, dtype=jnp.int32)
    limit = row_ranks[:, None, None]
    keep = (levels[None, :, None] < limit) & (levels[None, None, :] < limit)
    return row_coupling * keep[:, None].astype(jnp.float32)


def far_field(gathered, weights, target_basis):
    nrhs = gathered.shape[2]
    rows = target_basis.shape[3]
    inner = jnp.einsum("sakl,spql->apqk", weights, gathered, precision=lax.Precision.HIGHEST)
    rounded_coef = complex_mix(inner).astype(jnp.bfloat16)
    outward = jnp.einsum(
        "akr,pqk->apqr", target_basis[0], rounded_coef, preferred_element_type=jnp.float32
    )
    return complex_mix(outward).reshape(2, nrhs, 1, rows)


def swapped(every, partner, width):
    nrhs = every.shape[1]
    rows = every.shape[3]
    tiles = every.reshape(2, nrhs, -1, width)
    return jnp.take(tiles, partner[0], axis=2).reshape(2, nrhs, 1, rows)


def local_products(vectors, image):
    stacked = []
    for basis in vectors:
        real_part = jnp.sum(basis[0] * image[0] + basis[1] * image[1], axis=(1, 2))
        imag_part = jnp.sum(basis[0] * image[1] - basis[1] * image[0], axis=(1, 2))
        stacked.append(jnp.stack([real_part, imag_part]))
    return jnp.stack(stacked)


def local_squares(field):
    return jnp.sum(field[0] * field[0] + field[1] * field[1], axis=(1, 2))


def scaled(factor, field):
    real_f = factor[0][:, None, None]
    imag_f = factor[1][:, None, None]
    return jnp.stack([real_f * field[0] - imag_f * field[1], real_f * field[1] + imag_f * field[0]])


def coef_scaled(factor, coef):
    real_f = factor[0][None, :, None]
    imag_f = factor[1][None, :, None]
    return jnp.stack(
        [real_f * coef[:, 0] - imag_f * coef[:, 1], real_f * coef[:, 1] + imag_f * coef[:, 0]],
        axis=1,
    )


def shards(
    right_side, near_blocks, near_cols, partner, source_basis, target_basis, coupling, far_ranks
):
    rows = right_side.shape[3]
    width = near_blocks.shape[4]
    total = float(rows * lax.axis_size("dom") * lax.axis_size("blk"))
    everyone = ("dom", "blk")
    weights = far_weights(coupling, far_ranks, source_basis.shape[2])

    def spread(every):
        return jnp.moveaxis(every, 0, 2)

    window_rhs = neighbours(right_side)
    start_sum, coef_rhs, every_rhs = tree_collect(
        local_squares(right_side), coefficients(right_side, source_basis), right_side[:, :, 0]
    )
    beta = jnp.sqrt(start_sum / total + EPSILON)
    inv_scale = beta[None, :, None, None]
    first_vec = right_side / inv_scale
    window_one = window_rhs / inv_scale
    every_one = spread(every_rhs) / inv_scale
    coef_one = coef_rhs / beta[None, None, :, None]
    image_one = (
        first_vec
        + near_field(window_one, near_blocks, near_cols)
        + far_field(coef_one, weights, target_basis)
        - swapped(every_one, partner, width)
    )

    window_img = neighbours(image_one)
    parts = jnp.concatenate(
        [
            local_products([first_vec], image_one)[0],
            local_squares(image_one)[None],
            local_squares(first_vec)[None],
        ]
    )
    one, coef_img, every_img = tree_collect(
        parts, coefficients(image_one, source_basis), image_one[:, :, 0]
    )
    one = one / total
    h_one_one = one[0:2]
    sq_w1 = one[2]
    sq_v1 = one[3]
    norm_h11 = h_one_one[0] * h_one_one[0] + h_one_one[1] * h_one_one[1]
    sq_u1 = jnp.maximum(sq_w1 - norm_h11 * (2.0 - sq_v1), 0.0)
    h_two_one = jnp.sqrt(sq_u1 + EPSILON)
    inv_two = h_two_one[None, :, None, None]
    second_basis = (image_one - scaled(h_one_one, first_vec)) / inv_two
    window_two = (window_img - scaled(h_one_one, window_one)) / inv_two
    every_two = (spread(every_img) - scaled(h_one_one, every_one)) / inv_two
    coef_two = (coef_img - coef_scaled(h_one_one, coef_one)) / h_two_one[None, None, :, None]
    image_two = (
        second_basis
        + near_field(window_two, near_blocks, near_cols)
        + far_field(coef_two, weights, target_basis)
        - swapped(every_two, partner, width)
    )

    two = (
        tree_sum(
            jnp.concatenate(
                [
                    local_products([first_vec, second_basis], image_two).reshape(4, -1),
                    local_products([first_vec], second_basis)[0],
                    local_squares(image_two)[None],
                    local_squares(second_basis)[None],
                ]
            ),
            everyone,
        )
        / total
    )
    h_one_two = two[0:2]
    h_two_two = two[2:4]
    cross = two[4:6]
    sq_w2 = two[6]
    sq_v2 = two[7]
    norm_a = h_one_two[0] * h_one_two[0] + h_one_two[1] * h_one_two[1]
    norm_b = h_two_two[0] * h_two_two[0] + h_two_two[1] * h_two_two[1]
    ab_re = h_one_two[0] * h_two_two[0] + h_one_two[1] * h_two_two[1]
    ab_im = h_one_two[0] * h_two_two[1] - h_one_two[1] * h_two_two[0]
    mixed = ab_re * cross[0] - ab_im * cross[1]
    sq_u2 = sq_w2 - norm_a * (2.0 - sq_v1) - norm_b * (2.0 - sq_v2) + 2.0 * mixed
    sq_u2 = jnp.maximum(sq_u2, 0.0)
    rest_two = image_two - scaled(h_one_two, first_vec) - scaled(h_two_two, second_basis)
    h_three_two = jnp.sqrt(sq_u2 + EPSILON)
    third_basis = rest_two / h_three_two[None, :, None, None]
    hessenberg = jnp.stack(
        [
            beta,
            h_one_one[0],
            h_one_one[1],
            h_two_one,
            h_one_two[0],
            h_one_two[1],
            h_two_two[0],
            h_two_two[1],
            h_three_two,
        ],
        axis=1,
    )
    return (second_basis, third_basis, hessenberg)


def solution(mesh):
    return jax.shard_map(
        shards,
        mesh=mesh,
        in_specs=(
            P(None, None, "dom", "blk"),
            P("dom", "blk", None, None, None, None),
            P("dom", "blk", None),
            P("dom", "blk"),
            P("dom", None, None, "blk"),
            P("dom", None, None, "blk"),
            P("dom", "blk", None, None, None, None),
            P("dom", "blk", None),
        ),
        out_specs=(P(None, None, "dom", "blk"), P(None, None, "dom", "blk"), P()),
        check_vma=False,
    )
```

time: 101 us -> 85.9 us (0.85)
  starting transfers between devices: 48.6 us -> 32.3 us
  waiting for transfers between devices: 31.2 us -> 26.4 us
  local copies, waits for them, and re-layouts: 6.11 us -> 9.41 us
  other arithmetic: 5.56 us -> 7.89 us
    ppermute x15 -> x5, starting transfers between devices: 21.9 us -> 4.19 us  [tree_sum(): x = x + lax.ppermute(x, axis, [(i, i ^ k) for i in range(n)])]
    ppermute x15 -> x5, waiting for transfers between devices: 26.1 us -> 11.5 us  [tree_sum(): x = x + lax.ppermute(x, axis, [(i, i ^ k) for i in range(n)])]
    ppermute x14, waiting for transfers between devices: 5.09 us -> 15 us  [the longest x10 15 us: tree_collect(): got = lax.ppermute(packed, axis, [(i, i ^ k) for i in range(n)])]
    concatenate x3 -> x12, other arithmetic: 0.04 us -> 1.5 us  [the longest x10 1.47 us: tree_collect(): packed = jnp.concatenate([red.reshape(-1), buf.reshape(-1)])]
    ppermute x14, starting transfers between devices: 26.8 us -> 28.1 us  [the longest x10 20 us: tree_collect(): got = lax.ppermute(packed, axis, [(i, i ^ k) for i in range(n)])]
    reshape x6 -> x22, local copies, waits for them, and re-layouts: 0.13 us -> 1.31 us  [the longest x10 0.68 us: tree_collect(): other = got[red.size:].reshape(buf.shape)]
  transfers between devices with their start and end apart: 29 -> 19, of which waited for: 20 -> 14; matrix products, arithmetic and copies ran while one was open for 8% -> 12% of each run, Pallas kernels for 0% -> 0%
where the time goes in v3:
time: 85.9 us; the launch traced here: 85.1 us
  starting transfers between devices  32.3 us (38%)
  waiting for transfers between devices  26.4 us (31%)
  local copies, waits for them, and re-layouts  9.41 us (11%)
  matrix products  8.06 us (9%)
  other arithmetic  7.89 us (9%)
  between operations  1.08 us (1%)
    ppermute x10, starting transfers between devices, tree_collect(): got = lax.ppermute(packed, axis, [(i, i ^ k) for i in range(n)])  20 us
    ppermute x10, waiting for transfers between devices, tree_collect(): got = lax.ppermute(packed, axis, [(i, i ^ k) for i in range(n)])  15 us
    ppermute x5, waiting for transfers between devices, tree_sum(): x = x + lax.ppermute(x, axis, [(i, i ^ k) for i in range(n)])  11.5 us
    ppermute x2, starting transfers between devices, neighbours(): left = lax.ppermute(field, 'blk', [(i, i + 1) for i in range(ends)])  5.52 us
    dot_general x2, matrix products, far_field(): jnp.einsum('sakl,spql->apqk', weights, gathered, precision=lax.Precision....  5.26 us
    ppermute x5, starting transfers between devices, tree_sum(): x = x + lax.ppermute(x, axis, [(i, i ^ k) for i in range(n)])  4.19 us
    ppermute x2, starting transfers between devices, neighbours(): right = lax.ppermute(field, 'blk', [(i + 1, i) for i in range(ends)])  2.57 us
    unnamed x13, local copies, waits for them, and re-layouts  2.01 us
  transfers between devices with their start and end apart: 19, of which 14 were waited for; matrix products, arithmetic and copies ran while one was open for 12% of the time, Pallas kernels for 0%

profile of v3, /device:TPU:0, one launch (start us, length us, event | category | flops | bytes accessed | tf_op | source)
XLA Modules:
  0.0 85.1 jit_solution(14968815097036814727)
XLA Ops:
  0.7 2.5 %collective-permute-start.5 = (f32[2,4,1,512]{3,2,1,0:T(1,128)}, f32[2,4,1,512]{3,2,1,0:T(1,128)S(1)}, u32[]{:S(2)}, u32[]{:S(2)}) collective-permute-start(f32[2,4,1,512]{3,2,1,0:T(1,128)} %param.12), channel_id=1, source_target_pairs={{0,1},{1,2},{2,3},{3,4},{4,5},{5,6},{6,7},{7,8},{8,9},{9,10},{10,1... | collective-permute-start | bytes 49160 | tf_op jit(solution)/shard_map/ppermute | solution.py:54
  3.2 1.3 %collective-permute-start.6 = (f32[2,4,1,512]{3,2,1,0:T(1,128)}, f32[2,4,1,512]{3,2,1,0:T(1,128)S(1)}, u32[]{:S(2)}, u32[]{:S(2)}) collective-permute-start(f32[2,4,1,512]{3,2,1,0:T(1,128)} %param.12), channel_id=1, source_target_pairs={{1,0},{2,1},{3,2},{4,3},{5,4},{6,5},{7,6},{8,7},{9,8},{10,9},{11,1... | collective-permute-start | bytes 49160 | tf_op jit(solution)/shard_map/ppermute | solution.py:55
  4.5 0.7 compare_select_fusion
  5.1 0.7 compare_and_fusion
  5.8 0.7 iota_compare_fusion
  6.5 0.2 and_convert_fusion
  6.7 0.8 add_reduce_fusion.9
  7.5 0.8 reshape_squeeze.4
  8.3 0.8 constant_dynamic-update-slice_fusion.1
  9.1 1.1 %convolution_bitcast_fusion.5 = f32[2,2,4,64]{3,2,0,1:T(4,128)S(1)} fusion(bf16[1,2,64,512]{3,2,1,0:T(8,128)(2,1)} %param.16, bf16[2,4,1,512]{3,2,1,0:T(2,128)(2,1)S(1)} %get-tuple-element.58), kind=kOutput, calls=%fused_computation.15 | convolution fusion | flops 1048576 | bytes 143360 | tf_op jit(solution)/shard_map/akr,pqr->apqk/dot_general | solution.py:65
  10.4 3.2 %collective-permute-start = (f32[516]{0:T(1024)S(1)}, f32[516]{0:T(1024)S(1)}, u32[]{:S(2)}, u32[]{:S(2)}) collective-permute-start(f32[516]{0:T(1024)S(1)} %pad_maximum_fusion.10), channel_id=1, source_target_pairs={{0,1},{1,0},{2,3},{3,2},{4,5},{5,4},{6,7},{7,6},{8,9},{9,8},{10,11... | collective-permute-start | bytes 6200 | tf_op jit(solution)/shard_map/ppermute | solution.py:38
  13.6 0.8 collective-permute-done
  14.8 2.0 %collective-permute-start.1 = (f32[1028]{0:T(1024)S(1)}, f32[1028]{0:T(1024)S(1)}, u32[]{:S(2)}, u32[]{:S(2)}) collective-permute-start(f32[1028]{0:T(1024)S(1)} %pad_maximum_fusion.7), channel_id=1, source_target_pairs={{0,2},{1,3},{2,0},{3,1},{4,6},{5,7},{6,4},{7,5},{8,10},{9,11},{10,... | collective-permute-start | bytes 12344 | tf_op jit(solution)/shard_map/ppermute | solution.py:38
  16.7 1.7 %collective-permute-done.1 = f32[1028]{0:T(1024)S(1)} collective-permute-done((f32[1028]{0:T(1024)S(1)}, f32[1028]{0:T(1024)S(1)}, u32[]{:S(2)}, u32[]{:S(2)}) %collective-permute-start.1) | collective-permute-done | bytes 4144 | tf_op jit(solution)/shard_map/ppermute | solution.py:38
  18.7 2.9 %collective-permute-start.2 = (f32[2052]{0:T(1024)S(1)}, f32[2052]{0:T(1024)S(1)}, u32[]{:S(2)}, u32[]{:S(2)}) collective-permute-start(f32[2052]{0:T(1024)S(1)} %pad_maximum_fusion.5), channel_id=1, source_target_pairs={{0,4},{1,5},{2,6},{3,7},{4,0},{5,1},{6,2},{7,3},{8,12},{9,13},{10,... | collective-permute-start | bytes 24632 | tf_op jit(solution)/shard_map/ppermute | solution.py:38
  21.7 1.7 %collective-permute-done.2 = f32[2052]{0:T(1024)S(1)} collective-permute-done((f32[2052]{0:T(1024)S(1)}, f32[2052]{0:T(1024)S(1)}, u32[]{:S(2)}, u32[]{:S(2)}) %collective-permute-start.2) | collective-permute-done | bytes 8240 | tf_op jit(solution)/shard_map/ppermute | solution.py:38
  23.7 3.0 %collective-permute-start.3 = (f32[4100]{0:T(1024)S(1)}, f32[4100]{0:T(1024)S(1)}, u32[]{:S(2)}, u32[]{:S(2)}) collective-permute-start(f32[4100]{0:T(1024)S(1)} %pad_maximum_fusion.1), channel_id=1, source_target_pairs={{0,8},{1,9},{2,10},{3,11},{4,12},{5,13},{6,14},{7,15},{8,0},{9,1},... | collective-permute-start | bytes 49208 | tf_op jit(solution)/shard_map/ppermute | solution.py:38
  26.7 0.7 copy.181
  27.5 1.0 %collective-permute-done.3 = f32[4100]{0:T(1024)S(1)} collective-permute-done((f32[4100]{0:T(1024)S(1)}, f32[4100]{0:T(1024)S(1)}, u32[]{:S(2)}, u32[]{:S(2)}) %collective-permute-start.3) | collective-permute-done | bytes 16432 | tf_op jit(solution)/shard_map/ppermute | solution.py:38
  28.5 0.8 pad_maximum_fusion.2
  29.3 1.5 %collective-permute-start.4 = (f32[4100]{0:T(1024)S(1)}, f32[4100]{0:T(1024)S(1)}, u32[]{:S(2)}, u32[]{:S(2)}) collective-permute-start(f32[4100]{0:T(1024)S(1)} %pad_maximum_fusion.2), channel_id=1, source_target_pairs={{0,16},{16,0},{1,17},{17,1},{2,18},{18,2},{3,19},{19,3},{4,20},{20... | collective-permute-start | bytes 49208 | tf_op jit(solution)/shard_map/ppermute | solution.py:38
  31.0 2.1 %collective-permute-done.4 = f32[4100]{0:T(1024)S(1)} collective-permute-done((f32[4100]{0:T(1024)S(1)}, f32[4100]{0:T(1024)S(1)}, u32[]{:S(2)}, u32[]{:S(2)}) %collective-permute-start.4) | collective-permute-done | bytes 16432 | tf_op jit(solution)/shard_map/ppermute | solution.py:38
  33.2 2.6 %convolution_bitcast_fusion.4 = f32[2,2,4,64]{3,2,0,1:T(4,128)S(1)} fusion(f32[1,1,16,2,64,64]{5,4,3,2,1,0:T(8,128)} %param.18, f32[16,64,64]{2,1,0:T(8,128)S(1)} %and_convert_fusion, f32[16,2,4,64]{3,2,1,0:T(4,128)S(1)} %fusion.18), kind=kOutput, calls=%fused_computation.14 | convolution fusion | flops 12713984 | bytes 823296 | tf_op jit(solution)/shard_map/sakl,spql->apqk/dot_general | solution.py:98
  35.9 0.1 convolution_bitcast_fusion.1
  36.3 0.6 gather_fusion.1
  37.0 0.2 broadcast_divide_fusion
  37.2 0.6 gather_fusion
  37.9 0.7 fusion.4
  38.7 0.1 convolution_bitcast_fusion.3
  39.0 0.2 add_reduce_fusion.8
  39.3 1.2 %collective-permute-done.7 = f32[528]{0:T(1024)S(1)} collective-permute-done((f32[528]{0:T(1024)S(1)}, f32[528]{0:T(1024)S(1)}, u32[]{:S(2)}, u32[]{:S(2)}) %collective-permute-start.7) | collective-permute-done | bytes 2144 | tf_op jit(solution)/shard_map/ppermute | solution.py:38
  40.8 0.9 %collective-permute-start.8 = (f32[1040]{0:T(1024)S(1)}, f32[1040]{0:T(1024)S(1)}, u32[]{:S(2)}, u32[]{:S(2)}) collective-permute-start(f32[1040]{0:T(1024)S(1)} %pad_maximum_fusion.8), channel_id=1, source_target_pairs={{0,2},{1,3},{2,0},{3,1},{4,6},{5,7},{6,4},{7,5},{8,10},{9,11},{10,... | collective-permute-start | bytes 12488 | tf_op jit(solution)/shard_map/ppermute | solution.py:38
  41.7 2.7 %collective-permute-done.8 = f32[1040]{0:T(1024)S(1)} collective-permute-done((f32[1040]{0:T(1024)S(1)}, f32[1040]{0:T(1024)S(1)}, u32[]{:S(2)}, u32[]{:S(2)}) %collective-permute-start.8) | collective-permute-done | bytes 4192 | tf_op jit(solution)/shard_map/ppermute | solution.py:38
  44.8 1.9 %collective-permute-start.9 = (f32[2064]{0:T(1024)S(1)}, f32[2064]{0:T(1024)S(1)}, u32[]{:S(2)}, u32[]{:S(2)}) collective-permute-start(f32[2064]{0:T(1024)S(1)} %pad_maximum_fusion.6), channel_id=1, source_target_pairs={{0,4},{1,5},{2,6},{3,7},{4,0},{5,1},{6,2},{7,3},{8,12},{9,13},{10,... | collective-permute-start | bytes 24776 | tf_op jit(solution)/shard_map/ppermute | solution.py:38
  46.7 1.8 %collective-permute-done.9 = f32[2064]{0:T(1024)S(1)} collective-permute-done((f32[2064]{0:T(1024)S(1)}, f32[2064]{0:T(1024)S(1)}, u32[]{:S(2)}, u32[]{:S(2)}) %collective-permute-start.9) | collective-permute-done | bytes 8288 | tf_op jit(solution)/shard_map/ppermute | solution.py:38
  48.8 2.9 %collective-permute-start.10 = (f32[4112]{0:T(1024)S(1)}, f32[4112]{0:T(1024)S(1)}, u32[]{:S(2)}, u32[]{:S(2)}) collective-permute-start(f32[4112]{0:T(1024)S(1)} %pad_maximum_fusion.3), channel_id=1, source_target_pairs={{0,8},{1,9},{2,10},{3,11},{4,12},{5,13},{6,14},{7,15},{8,0},{9,1},... | collective-permute-start | bytes 49352 | tf_op jit(solution)/shard_map/ppermute | solution.py:38
  51.8 1.3 %collective-permute-start.13 = (f32[2,4,1,512]{3,1,0,2:T(4,128)S(1)}, f32[2,4,1,512]{3,1,0,2:T(4,128)S(1)}, u32[]{:S(2)}, u32[]{:S(2)}) collective-permute-start(f32[2,4,1,512]{3,1,0,2:T(4,128)S(1)} %get-tuple-element.32), channel_id=1, source_target_pairs={{1,0},{2,1},{3,2},{4,3},{5,4},{6,5},{7,6},{8,7},{9,8},{10,9},{11,1... | collective-permute-start | bytes 49160 | tf_op jit(solution)/shard_map/ppermute | solution.py:55
  53.0 3.0 %collective-permute-start.12 = (f32[2,4,1,512]{3,1,0,2:T(4,128)S(1)}, f32[2,4,1,512]{3,1,0,2:T(4,128)S(1)}, u32[]{:S(2)}, u32[]{:S(2)}) collective-permute-start(f32[2,4,1,512]{3,1,0,2:T(4,128)S(1)} %get-tuple-element.32), channel_id=1, source_target_pairs={{0,1},{1,2},{2,3},{3,4},{4,5},{5,6},{6,7},{7,8},{8,9},{9,10},{10,1... | collective-permute-start | bytes 49160 | tf_op jit(solution)/shard_map/ppermute | solution.py:54
  56.4 1.5 %collective-permute-start.11 = (f32[4112]{0:T(1024)S(1)}, f32[4112]{0:T(1024)S(1)}, u32[]{:S(2)}, u32[]{:S(2)}) collective-permute-start(f32[4112]{0:T(1024)S(1)} %pad_maximum_fusion.4), channel_id=1, source_target_pairs={{0,16},{16,0},{1,17},{17,1},{2,18},{18,2},{3,19},{19,3},{4,20},{20... | collective-permute-start | bytes 49352 | tf_op jit(solution)/shard_map/ppermute | solution.py:38
  58.2 2.0 %collective-permute-done.11 = f32[4112]{0:T(1024)S(1)} collective-permute-done((f32[4112]{0:T(1024)S(1)}, f32[4112]{0:T(1024)S(1)}, u32[]{:S(2)}, u32[]{:S(2)}) %collective-permute-start.11) | collective-permute-done | bytes 16480 | tf_op jit(solution)/shard_map/ppermute | solution.py:38
  60.5 2.6 %convolution_bitcast_fusion.2 = f32[2,2,4,64]{3,2,0,1:T(4,128)S(1)} fusion(f32[1,1,16,2,64,64]{5,4,3,2,1,0:T(8,128)} %param.18, f32[16,64,64]{2,1,0:T(8,128)S(1)} %and_convert_fusion, f32[16,1,4,64]{3,2,1,0:T(4,128)S(1)} %get-tuple-element.35, f32[16,1,4,64]{3,2,1,0:T(4,128)S(1)} %get-tuple-element.34, f32[8,2,4,64]{3,2,1,0:T(4,128)S(1)} %maximum_select_fusion.4, ...), kind=kOutput, calls=%fused_computation.12 | convolution fusion | flops 12763136 | bytes 856081 | tf_op jit(solution)/shard_map/sakl,spql->apqk/dot_general | solution.py:98
  63.5 0.6 gather_fusion.3
  64.2 0.2 subtract_reduce_fusion
  64.5 0.6 gather_fusion.2
  65.2 0.7 fusion.7
  65.9 0.1 convolution_bitcast_fusion
  66.1 0.2 subtract_reduce_fusion.1
  66.4 1.6 %collective-permute-start.14 = (f32[8,4]{1,0:T(8,128)S(1)}, f32[8,4]{1,0:T(8,128)S(1)}, u32[]{:S(2)}, u32[]{:S(2)}) collective-permute-start(f32[8,4]{1,0:T(8,128)S(1)} %concatenate.157), channel_id=1, source_target_pairs={{0,16},{16,0},{1,17},{17,1},{2,18},{18,2},{3,19},{19,3},{4,20},{20... | collective-permute-start | bytes 392 | tf_op jit(solution)/shard_map/ppermute | solution.py:21
  68.0 2.1 %collective-permute-done.14 = f32[8,4]{1,0:T(8,128)S(1)} collective-permute-done((f32[8,4]{1,0:T(8,128)S(1)}, f32[8,4]{1,0:T(8,128)S(1)}, u32[]{:S(2)}, u32[]{:S(2)}) %collective-permute-start.14) | collective-permute-done | bytes 160 | tf_op jit(solution)/shard_map/ppermute | solution.py:21
  70.1 1.2 %collective-permute-done.15 = f32[8,4]{1,0:T(8,128)S(1)} collective-permute-done((f32[8,4]{1,0:T(8,128)S(1)}, f32[8,4]{1,0:T(8,128)S(1)}, u32[]{:S(2)}, u32[]{:S(2)}) %collective-permute-start.15) | collective-permute-done | bytes 160 | tf_op jit(solution)/shard_map/ppermute | solution.py:21
  71.3 0.6 collective-permute-start.16
  71.9 0.1 copy.96
  72.0 0.6 copy.105
  72.6 2.3 %collective-permute-done.16 = f32[8,4]{1,0:T(8,128)S(1)} collective-permute-done((f32[8,4]{1,0:T(8,128)S(1)}, f32[8,4]{1,0:T(8,128)S(1)}, u32[]{:S(2)}, u32[]{:S(2)}) %collective-permute-start.16) | collective-permute-done | bytes 160 | tf_op jit(solution)/shard_map/ppermute | solution.py:21
  74.9 1.7 %collective-permute-start.17 = (f32[8,4]{1,0:T(8,128)S(1)}, f32[8,4]{1,0:T(8,128)S(1)}, u32[]{:S(2)}, u32[]{:S(2)}) collective-permute-start(f32[8,4]{1,0:T(8,128)S(1)} %add.533), channel_id=1, source_target_pairs={{0,4},{1,5},{2,6},{3,7},{4,0},{5,1},{6,2},{7,3},{8,12},{9,13},{10,... | collective-permute-start | bytes 392 | tf_op jit(solution)/shard_map/ppermute | solution.py:21
  76.6 0.1 copy.97
  76.7 1.8 %collective-permute-done.17 = f32[8,4]{1,0:T(8,128)S(1)} collective-permute-done((f32[8,4]{1,0:T(8,128)S(1)}, f32[8,4]{1,0:T(8,128)S(1)}, u32[]{:S(2)}, u32[]{:S(2)}) %collective-permute-start.17) | collective-permute-done | bytes 160 | tf_op jit(solution)/shard_map/ppermute | solution.py:21
  78.5 0.3 collective-permute-start.18
  78.8 0.1 copy.98
  78.9 4.1 %collective-permute-done.18 = f32[8,4]{1,0:T(8,128)S(1)} collective-permute-done((f32[8,4]{1,0:T(8,128)S(1)}, f32[8,4]{1,0:T(8,128)S(1)}, u32[]{:S(2)}, u32[]{:S(2)}) %collective-permute-start.18) | collective-permute-done | bytes 160 | tf_op jit(solution)/shard_map/ppermute | solution.py:21
  83.3 0.6 copy.106
  83.9 0.1 copy.99
  84.3 0.1 copy.103
  84.5 0.7 stack.153
  (142 shorter events, 5.7 us)
Async XLA Ops:
  0.6 37.3 %copy-start = (bf16[1,2,4,2,256,256]{5,4,3,2,1,0:T(8,128)(2,1)S(1)}, bf16[1,2,4,2,256,256]{5,4,3,2,1,0:T(8,128)(2,1)}, u32[]{:S(2)}) copy-start(bf16[1,2,4,2,256,256]{5,4,3,2,1,0:T(8,128)(2,1)} %param.13) | copy-start | bytes 6291460
  0.6 35.2 %copy-start.2 = (bf16[1,2,64,512]{3,2,1,0:T(8,128)(2,1)S(1)}, bf16[1,2,64,512]{3,2,1,0:T(8,128)(2,1)}, u32[]{:S(2)}) copy-start(bf16[1,2,64,512]{3,2,1,0:T(8,128)(2,1)} %param.17) | copy-start | bytes 393220
  0.7 7.7 %collective-permute-start.5 = (f32[2,4,1,512]{3,2,1,0:T(1,128)}, f32[2,4,1,512]{3,2,1,0:T(1,128)S(1)}, u32[]{:S(2)}, u32[]{:S(2)}) collective-permute-start(f32[2,4,1,512]{3,2,1,0:T(1,128)} %param.12), channel_id=1, source_target_pairs={{0,1},{1,2},{2,3},{3,4},{4,5},{5,6},{6,7},{7,8},{8,9},{9,10},{10,1... | collective-permute-start | bytes 49160 | tf_op jit(solution)/shard_map/ppermute | solution.py:54
  3.2 27.7 %collective-permute-start.6 = (f32[2,4,1,512]{3,2,1,0:T(1,128)}, f32[2,4,1,512]{3,2,1,0:T(1,128)S(1)}, u32[]{:S(2)}, u32[]{:S(2)}) collective-permute-start(f32[2,4,1,512]{3,2,1,0:T(1,128)} %param.12), channel_id=1, source_target_pairs={{1,0},{2,1},{3,2},{4,3},{5,4},{6,5},{7,6},{8,7},{9,8},{10,9},{11,1... | collective-permute-start | bytes 49160 | tf_op jit(solution)/shard_map/ppermute | solution.py:55
  10.4 4.1 %collective-permute-start = (f32[516]{0:T(1024)S(1)}, f32[516]{0:T(1024)S(1)}, u32[]{:S(2)}, u32[]{:S(2)}) collective-permute-start(f32[516]{0:T(1024)S(1)} %pad_maximum_fusion.10), channel_id=1, source_target_pairs={{0,1},{1,0},{2,3},{3,2},{4,5},{5,4},{6,7},{7,6},{8,9},{9,8},{10,11... | collective-permute-start | bytes 6200 | tf_op jit(solution)/shard_map/ppermute | solution.py:38
  14.8 3.7 %collective-permute-start.1 = (f32[1028]{0:T(1024)S(1)}, f32[1028]{0:T(1024)S(1)}, u32[]{:S(2)}, u32[]{:S(2)}) collective-permute-start(f32[1028]{0:T(1024)S(1)} %pad_maximum_fusion.7), channel_id=1, source_target_pairs={{0,2},{1,3},{2,0},{3,1},{4,6},{5,7},{6,4},{7,5},{8,10},{9,11},{10,... | collective-permute-start | bytes 12344 | tf_op jit(solution)/shard_map/ppermute | solution.py:38
  18.7 4.6 %collective-permute-start.2 = (f32[2052]{0:T(1024)S(1)}, f32[2052]{0:T(1024)S(1)}, u32[]{:S(2)}, u32[]{:S(2)}) collective-permute-start(f32[2052]{0:T(1024)S(1)} %pad_maximum_fusion.5), channel_id=1, source_target_pairs={{0,4},{1,5},{2,6},{3,7},{4,0},{5,1},{6,2},{7,3},{8,12},{9,13},{10,... | collective-permute-start | bytes 24632 | tf_op jit(solution)/shard_map/ppermute | solution.py:38
  23.7 4.8 %collective-permute-start.3 = (f32[4100]{0:T(1024)S(1)}, f32[4100]{0:T(1024)S(1)}, u32[]{:S(2)}, u32[]{:S(2)}) collective-permute-start(f32[4100]{0:T(1024)S(1)} %pad_maximum_fusion.1), channel_id=1, source_target_pairs={{0,8},{1,9},{2,10},{3,11},{4,12},{5,13},{6,14},{7,15},{8,0},{9,1},... | collective-permute-start | bytes 49208 | tf_op jit(solution)/shard_map/ppermute | solution.py:38
  29.3 3.8 %collective-permute-start.4 = (f32[4100]{0:T(1024)S(1)}, f32[4100]{0:T(1024)S(1)}, u32[]{:S(2)}, u32[]{:S(2)}) collective-permute-start(f32[4100]{0:T(1024)S(1)} %pad_maximum_fusion.2), channel_id=1, source_target_pairs={{0,16},{16,0},{1,17},{17,1},{2,18},{18,2},{3,19},{19,3},{4,20},{20... | collective-permute-start | bytes 49208 | tf_op jit(solution)/shard_map/ppermute | solution.py:38
  33.2 5.4 %copy-start.3 = (f32[2,4,1,512]{3,2,1,0:T(1,128)S(1)}, f32[2,4,1,512]{3,2,1,0:T(1,128)}, u32[]{:S(2)}) copy-start(f32[2,4,1,512]{3,2,1,0:T(1,128)} %param.12) | copy-start | bytes 49156
  35.8 2.9 %copy-start.1 = (bf16[1,2,64,512]{3,2,1,0:T(8,128)(2,1)S(1)}, bf16[1,2,64,512]{3,2,1,0:T(8,128)(2,1)}, u32[]{:S(2)}) copy-start(bf16[1,2,64,512]{3,2,1,0:T(8,128)(2,1)} %param.16) | copy-start | bytes 393220
  39.3 1.2 %collective-permute-start.7 = (f32[528]{0:T(1024)S(1)}, f32[528]{0:T(1024)S(1)}, u32[]{:S(2)}, u32[]{:S(2)}) collective-permute-start(f32[528]{0:T(1024)S(1)} %pad_maximum_fusion.12), channel_id=1, source_target_pairs={{0,1},{1,0},{2,3},{3,2},{4,5},{5,4},{6,7},{7,6},{8,9},{9,8},{10,11... | collective-permute-start | bytes 6344 | tf_op jit(solution)/shard_map/ppermute | solution.py:38
  40.8 3.7 %collective-permute-start.8 = (f32[1040]{0:T(1024)S(1)}, f32[1040]{0:T(1024)S(1)}, u32[]{:S(2)}, u32[]{:S(2)}) collective-permute-start(f32[1040]{0:T(1024)S(1)} %pad_maximum_fusion.8), channel_id=1, source_target_pairs={{0,2},{1,3},{2,0},{3,1},{4,6},{5,7},{6,4},{7,5},{8,10},{9,11},{10,... | collective-permute-start | bytes 12488 | tf_op jit(solution)/shard_map/ppermute | solution.py:38
  44.8 3.7 %collective-permute-start.9 = (f32[2064]{0:T(1024)S(1)}, f32[2064]{0:T(1024)S(1)}, u32[]{:S(2)}, u32[]{:S(2)}) collective-permute-start(f32[2064]{0:T(1024)S(1)} %pad_maximum_fusion.6), channel_id=1, source_target_pairs={{0,4},{1,5},{2,6},{3,7},{4,0},{5,1},{6,2},{7,3},{8,12},{9,13},{10,... | collective-permute-start | bytes 24776 | tf_op jit(solution)/shard_map/ppermute | solution.py:38
  48.8 7.5 %collective-permute-start.10 = (f32[4112]{0:T(1024)S(1)}, f32[4112]{0:T(1024)S(1)}, u32[]{:S(2)}, u32[]{:S(2)}) collective-permute-start(f32[4112]{0:T(1024)S(1)} %pad_maximum_fusion.3), channel_id=1, source_target_pairs={{0,8},{1,9},{2,10},{3,11},{4,12},{5,13},{6,14},{7,15},{8,0},{9,1},... | collective-permute-start | bytes 49352 | tf_op jit(solution)/shard_map/ppermute | solution.py:38
  51.8 6.2 %collective-permute-start.13 = (f32[2,4,1,512]{3,1,0,2:T(4,128)S(1)}, f32[2,4,1,512]{3,1,0,2:T(4,128)S(1)}, u32[]{:S(2)}, u32[]{:S(2)}) collective-permute-start(f32[2,4,1,512]{3,1,0,2:T(4,128)S(1)} %get-tuple-element.32), channel_id=1, source_target_pairs={{1,0},{2,1},{3,2},{4,3},{5,4},{6,5},{7,6},{8,7},{9,8},{10,9},{11,1... | collective-permute-start | bytes 49160 | tf_op jit(solution)/shard_map/ppermute | solution.py:55
  53.0 4.9 %collective-permute-start.12 = (f32[2,4,1,512]{3,1,0,2:T(4,128)S(1)}, f32[2,4,1,512]{3,1,0,2:T(4,128)S(1)}, u32[]{:S(2)}, u32[]{:S(2)}) collective-permute-start(f32[2,4,1,512]{3,1,0,2:T(4,128)S(1)} %get-tuple-element.32), channel_id=1, source_target_pairs={{0,1},{1,2},{2,3},{3,4},{4,5},{5,6},{6,7},{7,8},{8,9},{9,10},{10,1... | collective-permute-start | bytes 49160 | tf_op jit(solution)/shard_map/ppermute | solution.py:54
  56.4 3.8 %collective-permute-start.11 = (f32[4112]{0:T(1024)S(1)}, f32[4112]{0:T(1024)S(1)}, u32[]{:S(2)}, u32[]{:S(2)}) collective-permute-start(f32[4112]{0:T(1024)S(1)} %pad_maximum_fusion.4), channel_id=1, source_target_pairs={{0,16},{16,0},{1,17},{17,1},{2,18},{18,2},{3,19},{19,3},{4,20},{20... | collective-permute-start | bytes 49352 | tf_op jit(solution)/shard_map/ppermute | solution.py:38
  66.4 3.7 %collective-permute-start.14 = (f32[8,4]{1,0:T(8,128)S(1)}, f32[8,4]{1,0:T(8,128)S(1)}, u32[]{:S(2)}, u32[]{:S(2)}) collective-permute-start(f32[8,4]{1,0:T(8,128)S(1)} %concatenate.157), channel_id=1, source_target_pairs={{0,16},{16,0},{1,17},{17,1},{2,18},{18,2},{3,19},{19,3},{4,20},{20... | collective-permute-start | bytes 392 | tf_op jit(solution)/shard_map/ppermute | solution.py:21
  70.1 1.2 %collective-permute-start.15 = (f32[8,4]{1,0:T(8,128)S(1)}, f32[8,4]{1,0:T(8,128)S(1)}, u32[]{:S(2)}, u32[]{:S(2)}) collective-permute-start(f32[8,4]{1,0:T(8,128)S(1)} %add.531), channel_id=1, source_target_pairs={{0,1},{1,0},{2,3},{3,2},{4,5},{5,4},{6,7},{7,6},{8,9},{9,8},{10,11... | collective-permute-start | bytes 392 | tf_op jit(solution)/shard_map/ppermute | solution.py:21
  71.3 3.6 %collective-permute-start.16 = (f32[8,4]{1,0:T(8,128)S(1)}, f32[8,4]{1,0:T(8,128)S(1)}, u32[]{:S(2)}, u32[]{:S(2)}) collective-permute-start(f32[8,4]{1,0:T(8,128)S(1)} %add.532), channel_id=1, source_target_pairs={{0,2},{1,3},{2,0},{3,1},{4,6},{5,7},{6,4},{7,5},{8,10},{9,11},{10,... | collective-permute-start | bytes 392 | tf_op jit(solution)/shard_map/ppermute | solution.py:21
  74.9 3.6 %collective-permute-start.17 = (f32[8,4]{1,0:T(8,128)S(1)}, f32[8,4]{1,0:T(8,128)S(1)}, u32[]{:S(2)}, u32[]{:S(2)}) collective-permute-start(f32[8,4]{1,0:T(8,128)S(1)} %add.533), channel_id=1, source_target_pairs={{0,4},{1,5},{2,6},{3,7},{4,0},{5,1},{6,2},{7,3},{8,12},{9,13},{10,... | collective-permute-start | bytes 392 | tf_op jit(solution)/shard_map/ppermute | solution.py:21
  78.5 4.5 %collective-permute-start.18 = (f32[8,4]{1,0:T(8,128)S(1)}, f32[8,4]{1,0:T(8,128)S(1)}, u32[]{:S(2)}, u32[]{:S(2)}) collective-permute-start(f32[8,4]{1,0:T(8,128)S(1)} %add.534), channel_id=1, source_target_pairs={{0,8},{1,9},{2,10},{3,11},{4,12},{5,13},{6,14},{7,15},{8,0},{9,1},... | collective-permute-start | bytes 392 | tf_op jit(solution)/shard_map/ppermute | solution.py:21

commit v4 on v3

--- a/solution.py
+++ b/solution.py
@@ -24,7 +24,7 @@
 
 
 def tree_collect(red, gat_blk, gat_dom):
-    for axis, gat in (("blk", gat_blk), ("dom", gat_dom)):
+    for axis, gat in (("dom", gat_dom), ("blk", gat_blk)):
         n = lax.axis_size(axis)
         if not _pow2(n):
             red = lax.psum(red, axis)
@@ -83,19 +83,17 @@
     return complex_mix(near_prod).reshape(2, nrhs, 1, blocks_dev * width)
 
 
-def far_weights(coupling, far_ranks, rank_cap):
-    row_coupling = coupling[0, 0]
-    row_ranks = far_ranks[0, 0]
-    levels = jnp.arange(rank_cap, dtype=jnp.int32)
-    limit = row_ranks[:, None, None]
-    keep = (levels[None, :, None] < limit) & (levels[None, None, :] < limit)
-    return row_coupling * keep[:, None].astype(jnp.float32)
-
-
-def far_field(gathered, weights, target_basis):
+def far_field(gathered, coupling, far_ranks, target_basis):
     nrhs = gathered.shape[2]
     rows = target_basis.shape[3]
-    inner = jnp.einsum("sakl,spql->apqk", weights, gathered, precision=lax.Precision.HIGHEST)
+    rank_cap = gathered.shape[3]
+    levels = jnp.arange(rank_cap, dtype=jnp.int32)
+    keep = (levels[None, :] < far_ranks[0, 0][:, None]).astype(jnp.float32)
+    masked = gathered * keep[:, None, None, :]
+    inner = jnp.einsum(
+        "sakl,spql->apqsk", coupling[0, 0], masked, precision=lax.Precision.HIGHEST
+    )
+    inner = jnp.sum(inner * keep[None, None, None], axis=3)
     rounded_coef = complex_mix(inner).astype(jnp.bfloat16)
     outward = jnp.einsum(
         "akr,pqk->apqr", target_basis[0], rounded_coef, preferred_element_type=jnp.float32
@@ -145,7 +143,6 @@
     width = near_blocks.shape[4]
     total = float(rows * lax.axis_size("dom") * lax.axis_size("blk"))
     everyone = ("dom", "blk")
-    weights = far_weights(coupling, far_ranks, source_basis.shape[2])
 
     def spread(every):
         return jnp.moveaxis(every, 0, 2)
@@ -163,7 +160,7 @@
     image_one = (
         first_vec
         + near_field(window_one, near_blocks, near_cols)
-        + far_field(coef_one, weights, target_basis)
+        + far_field(coef_one, coupling, far_ranks, target_basis)
         - swapped(every_one, partner, width)
     )
 
@@ -193,7 +190,7 @@
     image_two = (
         second_basis
         + near_field(window_two, near_blocks, near_cols)
-        + far_field(coef_two, weights, target_basis)
+        + far_field(coef_two, coupling, far_ranks, target_basis)
         - swapped(every_two, partner, width)
     )
 

time: 85.9 us -> 98.9 us (1.15)
  other arithmetic: 7.89 us -> 15.9 us
  local copies, waits for them, and re-layouts: 9.41 us -> 16.6 us
  waiting for transfers between devices: 26.4 us -> 23.4 us
  matrix products: 8.06 us -> 9.84 us
  starting transfers between devices: 32.3 us -> 30.6 us
    ppermute x10, waiting for transfers between devices: 15 us -> 11.4 us  [tree_collect(): got = lax.ppermute(packed, axis, [(i, i ^ k) for i in range(n)])]
    reshape x5, local copies, waits for them, and re-layouts: 0.41 us -> 2.37 us  [tree_collect(): red = red + got[:red.size].reshape(red.shape)]
    ppermute x10, starting transfers between devices: 20 us -> 18.3 us  [tree_collect(): got = lax.ppermute(packed, axis, [(i, i ^ k) for i in range(n)])]
    slice x4, other arithmetic: 0.01 us -> 1.64 us  [tree_collect(): red = red + got[:red.size].reshape(red.shape)]
    slice x10, local copies, waits for them, and re-layouts: 0.72 us -> 2.18 us  [tree_collect(): other = got[red.size:].reshape(buf.shape)]
    sub x5, other arithmetic: 0.53 us -> 1.88 us  [scaled(): real_f * field[0] - imag_f * field[1]]
    dot_general x2, matrix products: 5.26 us -> 6.42 us  [far_field(): jnp.einsum('sakl,spql->apqsk', coupling[0, 0], masked, precision=lax.Prec...]
    unnamed x13 -> x57, local copies, waits for them, and re-layouts: 2.01 us -> 3.1 us
  transfers between devices with their start and end apart: 19 -> 19, of which waited for: 14 -> 12; matrix products, arithmetic and copies ran while one was open for 12% -> 16% of each run, Pallas kernels for 0% -> 0%
where the time goes in v4:
time: 98.9 us; the launch traced here: 97.7 us
  starting transfers between devices  30.6 us (31%)
  waiting for transfers between devices  23.4 us (24%)
  local copies, waits for them, and re-layouts  16.6 us (17%)
  other arithmetic  15.9 us (16%)
  matrix products  9.84 us (10%)
  between operations  1.29 us (1%)
    ppermute x10, starting transfers between devices, tree_collect(): got = lax.ppermute(packed, axis, [(i, i ^ k) for i in range(n)])  18.3 us
    ppermute x5, waiting for transfers between devices, tree_sum(): x = x + lax.ppermute(x, axis, [(i, i ^ k) for i in range(n)])  12 us
    ppermute x10, waiting for transfers between devices, tree_collect(): got = lax.ppermute(packed, axis, [(i, i ^ k) for i in range(n)])  11.4 us
    dot_general x2, matrix products, far_field(): jnp.einsum('sakl,spql->apqsk', coupling[0, 0], masked, precision=lax.Prec...  6.42 us
    ppermute x2, starting transfers between devices, neighbours(): left = lax.ppermute(field, 'blk', [(i, i + 1) for i in range(ends)])  6.12 us
    ppermute x5, starting transfers between devices, tree_sum(): x = x + lax.ppermute(x, axis, [(i, i ^ k) for i in range(n)])  3.65 us
    unnamed x57, local copies, waits for them, and re-layouts  3.1 us
    ppermute x2, starting transfers between devices, neighbours(): right = lax.ppermute(field, 'blk', [(i + 1, i) for i in range(ends)])  2.57 us
  transfers between devices with their start and end apart: 19, of which 12 were waited for; matrix products, arithmetic and copies ran while one was open for 16% of the time, Pallas kernels for 0%

profile of v4, /device:TPU:0, one launch (start us, length us, event | category | flops | bytes accessed | tf_op | source)
XLA Modules:
  0.0 97.7 jit_solution(9601937761956663699)
XLA Ops:
  0.7 2.5 %collective-permute-start.5 = (f32[2,4,1,512]{3,2,1,0:T(1,128)}, f32[2,4,1,512]{3,2,1,0:T(1,128)S(1)}, u32[]{:S(2)}, u32[]{:S(2)}) collective-permute-start(f32[2,4,1,512]{3,2,1,0:T(1,128)} %param.12), channel_id=1, source_target_pairs={{0,1},{1,2},{2,3},{3,4},{4,5},{5,6},{6,7},{7,8},{8,9},{9,10},{10,1... | collective-permute-start | bytes 49160 | tf_op jit(solution)/shard_map/ppermute | solution.py:54
  3.2 1.3 %collective-permute-start.6 = (f32[2,4,1,512]{3,2,1,0:T(1,128)}, f32[2,4,1,512]{3,2,1,0:T(1,128)S(1)}, u32[]{:S(2)}, u32[]{:S(2)}) collective-permute-start(f32[2,4,1,512]{3,2,1,0:T(1,128)} %param.12), channel_id=1, source_target_pairs={{1,0},{2,1},{3,2},{4,3},{5,4},{6,5},{7,6},{8,7},{9,8},{10,9},{11,1... | collective-permute-start | bytes 49160 | tf_op jit(solution)/shard_map/ppermute | solution.py:55
  4.5 0.8 add_reduce_fusion.9
  5.3 0.8 pad_maximum_fusion.1
  6.1 2.4 %collective-permute-start = (f32[4100]{0:T(1024)S(1)}, f32[4100]{0:T(1024)S(1)}, u32[]{:S(2)}, u32[]{:S(2)}) collective-permute-start(f32[4100]{0:T(1024)S(1)} %pad_maximum_fusion.1), channel_id=1, source_target_pairs={{0,16},{16,0},{1,17},{17,1},{2,18},{18,2},{3,19},{19,3},{4,20},{20... | collective-permute-start | bytes 49208 | tf_op jit(solution)/shard_map/ppermute | solution.py:38
  8.4 0.7 compare_select_fusion
  9.1 0.7 compare_and_fusion
  9.8 0.8 reshape_squeeze.4
  10.5 0.7 fusion.55
  11.3 0.8 constant_dynamic-update-slice_fusion.1
  12.1 1.1 %convolution_bitcast_fusion.3 = f32[2,2,4,64]{3,2,0,1:T(4,128)S(1)} fusion(bf16[1,2,64,512]{3,2,1,0:T(8,128)(2,1)} %param.16, bf16[2,4,1,512]{3,2,1,0:T(2,128)(2,1)S(1)} %get-tuple-element.58), kind=kOutput, calls=%fused_computation.17 | convolution fusion | flops 1048576 | bytes 143360 | tf_op jit(solution)/shard_map/akr,pqr->apqk/dot_general | solution.py:65
  13.3 2.1 %collective-permute-start.1 = (f32[516]{0:T(1024)S(1)}, f32[516]{0:T(1024)S(1)}, u32[]{:S(2)}, u32[]{:S(2)}) collective-permute-start(f32[516]{0:T(1024)S(1)} %pad_maximum_fusion.10), channel_id=1, source_target_pairs={{0,1},{1,0},{2,3},{3,2},{4,5},{5,4},{6,7},{7,6},{8,9},{9,8},{10,11... | collective-permute-start | bytes 6200 | tf_op jit(solution)/shard_map/ppermute | solution.py:38
  15.5 0.8 collective-permute-done.1
  16.6 2.3 %collective-permute-start.2 = (f32[1028]{0:T(1024)S(1)}, f32[1028]{0:T(1024)S(1)}, u32[]{:S(2)}, u32[]{:S(2)}) collective-permute-start(f32[1028]{0:T(1024)S(1)} %pad_maximum_fusion.7), channel_id=1, source_target_pairs={{0,2},{1,3},{2,0},{3,1},{4,6},{5,7},{6,4},{7,5},{8,10},{9,11},{10,... | collective-permute-start | bytes 12344 | tf_op jit(solution)/shard_map/ppermute | solution.py:38
  18.9 1.6 %collective-permute-done.2 = f32[1028]{0:T(1024)S(1)} collective-permute-done((f32[1028]{0:T(1024)S(1)}, f32[1028]{0:T(1024)S(1)}, u32[]{:S(2)}, u32[]{:S(2)}) %collective-permute-start.2) | collective-permute-done | bytes 4144 | tf_op jit(solution)/shard_map/ppermute | solution.py:38
  20.9 3.0 %collective-permute-start.3 = (f32[2052]{0:T(1024)S(1)}, f32[2052]{0:T(1024)S(1)}, u32[]{:S(2)}, u32[]{:S(2)}) collective-permute-start(f32[2052]{0:T(1024)S(1)} %pad_maximum_fusion.5), channel_id=1, source_target_pairs={{0,4},{1,5},{2,6},{3,7},{4,0},{5,1},{6,2},{7,3},{8,12},{9,13},{10,... | collective-permute-start | bytes 24632 | tf_op jit(solution)/shard_map/ppermute | solution.py:38
  23.9 0.7 copy.140
  24.6 0.9 collective-permute-done.3
  25.9 3.0 %collective-permute-start.4 = (f32[4100]{0:T(1024)S(1)}, f32[4100]{0:T(1024)S(1)}, u32[]{:S(2)}, u32[]{:S(2)}) collective-permute-start(f32[4100]{0:T(1024)S(1)} %pad_maximum_fusion.2), channel_id=1, source_target_pairs={{0,8},{1,9},{2,10},{3,11},{4,12},{5,13},{6,14},{7,15},{8,0},{9,1},... | collective-permute-start | bytes 49208 | tf_op jit(solution)/shard_map/ppermute | solution.py:38
  29.0 1.7 %collective-permute-done.4 = f32[4100]{0:T(1024)S(1)} collective-permute-done((f32[4100]{0:T(1024)S(1)}, f32[4100]{0:T(1024)S(1)}, u32[]{:S(2)}, u32[]{:S(2)}) %collective-permute-start.4) | collective-permute-done | bytes 16432 | tf_op jit(solution)/shard_map/ppermute | solution.py:38
  31.0 3.8 %fusion.4 = f32[2,4,2,64]{3,1,2,0:T(4,128)S(1)} fusion(f32[1,1,16,2,64,64]{5,4,3,2,1,0:T(8,128)} %param.18, f32[16,64]{1,0:T(8,128)S(1)} %fusion.55, f32[16,2,4,64]{3,2,1,0:T(4,128)S(1)} %fusion.18), kind=kOutput, calls=%fused_computation.10 | convolution fusion | flops 12622848 | bytes 565248 | tf_op jit(solution)/shard_map/sakl,spql->apqsk/dot_general | solution.py:93
  35.9 0.7 broadcast_divide_fusion
  37.4 0.7 fusion.6
  38.2 0.8 convolution_bitcast_fusion.2
  40.3 0.7 fusion.59
  41.1 2.5 %collective-permute-done.7 = f32[4112]{0:T(1024)S(1)} collective-permute-done((f32[4112]{0:T(1024)S(1)}, f32[4112]{0:T(1024)S(1)}, u32[]{:S(2)}, u32[]{:S(2)}) %collective-permute-start.7) | collective-permute-done | bytes 16480 | tf_op jit(solution)/shard_map/ppermute | solution.py:38
  43.6 1.2 %collective-permute-done.8 = f32[528]{0:T(1024)S(1)} collective-permute-done((f32[528]{0:T(1024)S(1)}, f32[528]{0:T(1024)S(1)}, u32[]{:S(2)}, u32[]{:S(2)}) %collective-permute-start.8) | collective-permute-done | bytes 2144 | tf_op jit(solution)/shard_map/ppermute | solution.py:38
  45.6 0.9 collective-permute-start.9
  46.5 2.7 %collective-permute-done.9 = f32[1040]{0:T(1024)S(1)} collective-permute-done((f32[1040]{0:T(1024)S(1)}, f32[1040]{0:T(1024)S(1)}, u32[]{:S(2)}, u32[]{:S(2)}) %collective-permute-start.9) | collective-permute-done | bytes 4192 | tf_op jit(solution)/shard_map/ppermute | solution.py:38
  50.2 1.9 %collective-permute-start.10 = (f32[2064]{0:T(1024)S(1)}, f32[2064]{0:T(1024)S(1)}, u32[]{:S(2)}, u32[]{:S(2)}) collective-permute-start(f32[2064]{0:T(1024)S(1)} %pad_maximum_fusion.6), channel_id=1, source_target_pairs={{0,4},{1,5},{2,6},{3,7},{4,0},{5,1},{6,2},{7,3},{8,12},{9,13},{10,... | collective-permute-start | bytes 24776 | tf_op jit(solution)/shard_map/ppermute | solution.py:38
  52.1 1.3 %collective-permute-start.13 = (f32[2,4,1,512]{3,1,0,2:T(4,128)S(1)}, f32[2,4,1,512]{3,1,0,2:T(4,128)S(1)}, u32[]{:S(2)}, u32[]{:S(2)}) collective-permute-start(f32[2,4,1,512]{3,1,0,2:T(4,128)S(1)} %get-tuple-element.32), channel_id=1, source_target_pairs={{1,0},{2,1},{3,2},{4,3},{5,4},{6,5},{7,6},{8,7},{9,8},{10,9},{11,1... | collective-permute-start | bytes 49160 | tf_op jit(solution)/shard_map/ppermute | solution.py:55
  53.4 3.6 %collective-permute-start.12 = (f32[2,4,1,512]{3,1,0,2:T(4,128)S(1)}, f32[2,4,1,512]{3,1,0,2:T(4,128)}, u32[]{:S(2)}, u32[]{:S(2)}) collective-permute-start(f32[2,4,1,512]{3,1,0,2:T(4,128)S(1)} %get-tuple-element.32), channel_id=1, source_target_pairs={{0,1},{1,2},{2,3},{3,4},{4,5},{5,6},{6,7},{7,8},{8,9},{9,10},{10,1... | collective-permute-start | bytes 49160 | tf_op jit(solution)/shard_map/ppermute | solution.py:54
  57.9 2.1 %collective-permute-start.11 = (f32[4112]{0:T(1024)S(1)}, f32[4112]{0:T(1024)}, u32[]{:S(2)}, u32[]{:S(2)}) collective-permute-start(f32[4112]{0:T(1024)S(1)} %pad_maximum_fusion.4), channel_id=1, source_target_pairs={{0,8},{1,9},{2,10},{3,11},{4,12},{5,13},{6,14},{7,15},{8,0},{9,1},... | collective-permute-start | bytes 49352 | tf_op jit(solution)/shard_map/ppermute | solution.py:38
  60.0 0.6 copy-done.13
  60.6 0.7 pad_maximum_fusion
  61.4 0.8 slice.527
  62.2 0.6 reshape.1738
  62.9 0.7 reshape.1728
  63.6 0.8 reshape.1730
  64.4 0.7 reshape.1732
  65.1 0.7 slice.509
  65.8 0.6 add_multiply_fusion.1
  66.5 0.6 slice_bitcast_fusion.12
  67.3 0.7 multiply_subtract_fusion.4
  67.9 0.9 fusion.32
  68.9 0.7 gather_fusion.3
  69.6 0.8 select_bitcast_fusion
  70.4 0.6 reshape.1740
  71.0 1.0 %subtract_reduce_fusion = (f32[4,1536]{1,0:T(4,128)S(1)}, f32[4,1536]{1,0:T(4,128)S(1)}) fusion(f32[2,4,1,1536]{3,2,1,0:T(1,128)} %get-tuple-element.36, f32[4]{0:T(128)} %copy-done.17, f32[4]{0:T(128)} %copy-done.18), kind=kLoop, calls=%fused_computation.59 | loop fusion | flops 36864 | bytes 98336 | tf_op jit(solution)/shard_map/sub | solution.py:127
  72.0 0.7 fusion.27
  72.7 0.7 gather_fusion.2
  73.4 0.7 broadcast_select_fusion
  74.2 0.7 fusion.9
  74.9 0.8 slice.516
  75.8 2.6 %fusion.5 = f32[2,4,2,64]{3,1,2,0:T(4,128)S(1)} fusion(f32[1,1,16,2,64,64]{5,4,3,2,1,0:T(8,128)S(1)} %copy-done.1, f32[16,64]{1,0:T(8,128)S(1)} %copy-done.6, f32[8,2,4,64]{3,2,1,0:T(4,128)S(1)} %reshape.1736, f32[8,2,4,64]{3,2,1,0:T(4,128)S(1)} %maximum_select_fusion.4, f32[16,1,4,64]{3,2,1,0:T(4,128)S(1)} %get-tuple-element.35, ...), kind=kOutput, calls=%fused_computation.11 | convolution fusion | flops 12672000 | bytes 598033 | tf_op jit(solution)/shard_map/sakl,spql->apqsk/dot_general | solution.py:93
  79.5 3.1 %collective-permute-done.14 = f32[8,4]{1,0:T(8,128)S(1)} collective-permute-done((f32[8,4]{1,0:T(8,128)S(1)}, f32[8,4]{1,0:T(8,128)S(1)}, u32[]{:S(2)}, u32[]{:S(2)}) %collective-permute-start.14) | collective-permute-done | bytes 160 | tf_op jit(solution)/shard_map/ppermute | solution.py:21
  82.6 1.2 %collective-permute-done.15 = f32[8,4]{1,0:T(8,128)S(1)} collective-permute-done((f32[8,4]{1,0:T(8,128)S(1)}, f32[8,4]{1,0:T(8,128)S(1)}, u32[]{:S(2)}, u32[]{:S(2)}) %collective-permute-start.15) | collective-permute-done | bytes 160 | tf_op jit(solution)/shard_map/ppermute | solution.py:21
  84.5 0.6 copy.83
  85.1 2.3 %collective-permute-done.16 = f32[8,4]{1,0:T(8,128)S(1)} collective-permute-done((f32[8,4]{1,0:T(8,128)S(1)}, f32[8,4]{1,0:T(8,128)S(1)}, u32[]{:S(2)}, u32[]{:S(2)}) %collective-permute-start.16) | collective-permute-done | bytes 160 | tf_op jit(solution)/shard_map/ppermute | solution.py:21
  87.8 3.2 %collective-permute-done.17 = f32[8,4]{1,0:T(8,128)S(1)} collective-permute-done((f32[8,4]{1,0:T(8,128)S(1)}, f32[8,4]{1,0:T(8,128)S(1)}, u32[]{:S(2)}, u32[]{:S(2)}) %collective-permute-start.17) | collective-permute-done | bytes 160 | tf_op jit(solution)/shard_map/ppermute | solution.py:21
  91.0 2.1 %collective-permute-start.18 = (f32[8,4]{1,0:T(8,128)S(1)}, f32[8,4]{1,0:T(8,128)S(1)}, u32[]{:S(2)}, u32[]{:S(2)}) collective-permute-start(f32[8,4]{1,0:T(8,128)S(1)} %add.534), channel_id=1, source_target_pairs={{0,8},{1,9},{2,10},{3,11},{4,12},{5,13},{6,14},{7,15},{8,0},{9,1},... | collective-permute-start | bytes 392 | tf_op jit(solution)/shard_map/ppermute | solution.py:21
  93.2 2.3 %collective-permute-done.18 = f32[8,4]{1,0:T(8,128)S(1)} collective-permute-done((f32[8,4]{1,0:T(8,128)S(1)}, f32[8,4]{1,0:T(8,128)S(1)}, u32[]{:S(2)}, u32[]{:S(2)}) %collective-permute-start.18) | collective-permute-done | bytes 160 | tf_op jit(solution)/shard_map/ppermute | solution.py:21
  95.8 0.6 copy.84
  97.0 0.7 stack.153
  (185 shorter events, 11.1 us)
Async XLA Ops:
  0.6 36.7 %copy-start = (bf16[1,2,4,2,256,256]{5,4,3,2,1,0:T(8,128)(2,1)S(1)}, bf16[1,2,4,2,256,256]{5,4,3,2,1,0:T(8,128)(2,1)}, u32[]{:S(2)}) copy-start(bf16[1,2,4,2,256,256]{5,4,3,2,1,0:T(8,128)(2,1)} %param.13) | copy-start | bytes 6291460
  0.6 34.2 %copy-start.3 = (bf16[1,2,64,512]{3,2,1,0:T(8,128)(2,1)S(1)}, bf16[1,2,64,512]{3,2,1,0:T(8,128)(2,1)}, u32[]{:S(2)}) copy-start(bf16[1,2,64,512]{3,2,1,0:T(8,128)(2,1)} %param.17) | copy-start | bytes 393220
  0.7 10.6 %collective-permute-start.5 = (f32[2,4,1,512]{3,2,1,0:T(1,128)}, f32[2,4,1,512]{3,2,1,0:T(1,128)S(1)}, u32[]{:S(2)}, u32[]{:S(2)}) collective-permute-start(f32[2,4,1,512]{3,2,1,0:T(1,128)} %param.12), channel_id=1, source_target_pairs={{0,1},{1,2},{2,3},{3,4},{4,5},{5,6},{6,7},{7,8},{8,9},{9,10},{10,1... | collective-permute-start | bytes 49160 | tf_op jit(solution)/shard_map/ppermute | solution.py:54
  3.2 25.8 %collective-permute-start.6 = (f32[2,4,1,512]{3,2,1,0:T(1,128)}, f32[2,4,1,512]{3,2,1,0:T(1,128)S(1)}, u32[]{:S(2)}, u32[]{:S(2)}) collective-permute-start(f32[2,4,1,512]{3,2,1,0:T(1,128)} %param.12), channel_id=1, source_target_pairs={{1,0},{2,1},{3,2},{4,3},{5,4},{6,5},{7,6},{8,7},{9,8},{10,9},{11,1... | collective-permute-start | bytes 49160 | tf_op jit(solution)/shard_map/ppermute | solution.py:55
  6.1 7.2 %collective-permute-start = (f32[4100]{0:T(1024)S(1)}, f32[4100]{0:T(1024)S(1)}, u32[]{:S(2)}, u32[]{:S(2)}) collective-permute-start(f32[4100]{0:T(1024)S(1)} %pad_maximum_fusion.1), channel_id=1, source_target_pairs={{0,16},{16,0},{1,17},{17,1},{2,18},{18,2},{3,19},{19,3},{4,20},{20... | collective-permute-start | bytes 49208 | tf_op jit(solution)/shard_map/ppermute | solution.py:38
  9.7 28.3 %copy-start.22 = (pred[2]{0:T(512)(128)(4,1)}, pred[2]{0:T(512)(128)(4,1)S(1)}, u32[]{:S(2)}) copy-start(pred[2]{0:T(512)(128)(4,1)S(1)} %compare_and_fusion) | copy-start | bytes 10
  11.2 23.7 %copy-start.5 = (f32[16,64]{1,0:T(8,128)}, f32[16,64]{1,0:T(8,128)S(1)}, u32[]{:S(2)}) copy-start(f32[16,64]{1,0:T(8,128)S(1)} %fusion.55) | copy-start | bytes 12292
  13.3 3.0 %collective-permute-start.1 = (f32[516]{0:T(1024)S(1)}, f32[516]{0:T(1024)S(1)}, u32[]{:S(2)}, u32[]{:S(2)}) collective-permute-start(f32[516]{0:T(1024)S(1)} %pad_maximum_fusion.10), channel_id=1, source_target_pairs={{0,1},{1,0},{2,3},{3,2},{4,5},{5,4},{6,7},{7,6},{8,9},{9,8},{10,11... | collective-permute-start | bytes 6200 | tf_op jit(solution)/shard_map/ppermute | solution.py:38
  15.5 22.6 %copy-start.23 = (pred[8]{0:T(512)(128)(4,1)}, pred[8]{0:T(512)(128)(4,1)S(1)}, u32[]{:S(2)}) copy-start(pred[8]{0:T(512)(128)(4,1)S(1)} %compare_and_fusion.1) | copy-start | bytes 28
  16.6 3.9 %collective-permute-start.2 = (f32[1028]{0:T(1024)S(1)}, f32[1028]{0:T(1024)S(1)}, u32[]{:S(2)}, u32[]{:S(2)}) collective-permute-start(f32[1028]{0:T(1024)S(1)} %pad_maximum_fusion.7), channel_id=1, source_target_pairs={{0,2},{1,3},{2,0},{3,1},{4,6},{5,7},{6,4},{7,5},{8,10},{9,11},{10,... | collective-permute-start | bytes 12344 | tf_op jit(solution)/shard_map/ppermute | solution.py:38
  18.9 19.2 %copy-start.19 = (s32[1024]{0:T(1024)}, s32[1024]{0:T(1024)S(1)}, u32[]{:S(2)}) copy-start(s32[1024]{0:T(1024)S(1)} %pad_clamp_fusion) | copy-start | bytes 12292
  20.9 4.7 %collective-permute-start.3 = (f32[2052]{0:T(1024)S(1)}, f32[2052]{0:T(1024)S(1)}, u32[]{:S(2)}, u32[]{:S(2)}) collective-permute-start(f32[2052]{0:T(1024)S(1)} %pad_maximum_fusion.5), channel_id=1, source_target_pairs={{0,4},{1,5},{2,6},{3,7},{4,0},{5,1},{6,2},{7,3},{8,12},{9,13},{10,... | collective-permute-start | bytes 24632 | tf_op jit(solution)/shard_map/ppermute | solution.py:38
  23.9 14.2 %copy-start.20 = (s32[1024]{0:T(1024)}, s32[1024]{0:T(1024)S(1)}, u32[]{:S(2)}) copy-start(s32[1024]{0:T(1024)S(1)} %pad_clamp_fusion.1) | copy-start | bytes 12292
  25.9 4.8 %collective-permute-start.4 = (f32[4100]{0:T(1024)S(1)}, f32[4100]{0:T(1024)S(1)}, u32[]{:S(2)}, u32[]{:S(2)}) collective-permute-start(f32[4100]{0:T(1024)S(1)} %pad_maximum_fusion.2), channel_id=1, source_target_pairs={{0,8},{1,9},{2,10},{3,11},{4,12},{5,13},{6,14},{7,15},{8,0},{9,1},... | collective-permute-start | bytes 49208 | tf_op jit(solution)/shard_map/ppermute | solution.py:38
  30.8 7.3 %copy-start.11 = (f32[4]{0:T(128)}, f32[4]{0:T(128)S(1)}, u32[]{:S(2)}) copy-start(f32[4]{0:T(128)S(1)} %add_sqrt_fusion.4) | copy-start | bytes 52
  30.9 7.2 %copy-start.4 = (f32[2,4,1,512]{3,2,1,0:T(1,128)S(1)}, f32[2,4,1,512]{3,2,1,0:T(1,128)}, u32[]{:S(2)}) copy-start(f32[2,4,1,512]{3,2,1,0:T(1,128)} %param.12) | copy-start | bytes 49156
  31.0 7.3 %copy-start.2 = (bf16[1,2,64,512]{3,2,1,0:T(8,128)(2,1)S(1)}, bf16[1,2,64,512]{3,2,1,0:T(8,128)(2,1)}, u32[]{:S(2)}) copy-start(bf16[1,2,64,512]{3,2,1,0:T(8,128)(2,1)} %param.16) | copy-start | bytes 393220
  38.2 37.5 %copy-start.1 = (f32[1,1,16,2,64,64]{5,4,3,2,1,0:T(8,128)S(1)}, f32[1,1,16,2,64,64]{5,4,3,2,1,0:T(8,128)}, u32[]{:S(2)}) copy-start(f32[1,1,16,2,64,64]{5,4,3,2,1,0:T(8,128)} %param.18) | copy-start | bytes 1572868
  39.0 36.8 %copy-start.6 = (f32[16,64]{1,0:T(8,128)S(1)}, f32[16,64]{1,0:T(8,128)}, u32[]{:S(2)}) copy-start(f32[16,64]{1,0:T(8,128)} %copy-done.5) | copy-start | bytes 12292
  39.2 0.5 copy-start.21
  39.7 3.8 %collective-permute-start.7 = (f32[4112]{0:T(1024)S(1)}, f32[4112]{0:T(1024)S(1)}, u32[]{:S(2)}, u32[]{:S(2)}) collective-permute-start(f32[4112]{0:T(1024)S(1)} %pad_maximum_fusion.3), channel_id=1, source_target_pairs={{0,16},{16,0},{1,17},{17,1},{2,18},{18,2},{3,19},{19,3},{4,20},{20... | collective-permute-start | bytes 49352 | tf_op jit(solution)/shard_map/ppermute | solution.py:38
  43.5 13.5 %copy-start.14 = (f32[4112]{0:T(1024)}, f32[4112]{0:T(1024)S(1)}, u32[]{:S(2)}) copy-start(f32[4112]{0:T(1024)S(1)} %collective-permute-done.7) | copy-start | bytes 49348
  43.6 1.2 %collective-permute-start.8 = (f32[528]{0:T(1024)S(1)}, f32[528]{0:T(1024)S(1)}, u32[]{:S(2)}, u32[]{:S(2)}) collective-permute-start(f32[528]{0:T(1024)S(1)} %pad_maximum_fusion.12), channel_id=1, source_target_pairs={{0,1},{1,0},{2,3},{3,2},{4,5},{5,4},{6,7},{7,6},{8,9},{9,8},{10,11... | collective-permute-start | bytes 6344 | tf_op jit(solution)/shard_map/ppermute | solution.py:38
  45.6 3.7 %collective-permute-start.9 = (f32[1040]{0:T(1024)S(1)}, f32[1040]{0:T(1024)S(1)}, u32[]{:S(2)}, u32[]{:S(2)}) collective-permute-start(f32[1040]{0:T(1024)S(1)} %pad_maximum_fusion.8), channel_id=1, source_target_pairs={{0,2},{1,3},{2,0},{3,1},{4,6},{5,7},{6,4},{7,5},{8,10},{9,11},{10,... | collective-permute-start | bytes 12488 | tf_op jit(solution)/shard_map/ppermute | solution.py:38
  50.2 6.8 %collective-permute-start.10 = (f32[2064]{0:T(1024)S(1)}, f32[2064]{0:T(1024)S(1)}, u32[]{:S(2)}, u32[]{:S(2)}) collective-permute-start(f32[2064]{0:T(1024)S(1)} %pad_maximum_fusion.6), channel_id=1, source_target_pairs={{0,4},{1,5},{2,6},{3,7},{4,0},{5,1},{6,2},{7,3},{8,12},{9,13},{10,... | collective-permute-start | bytes 24776 | tf_op jit(solution)/shard_map/ppermute | solution.py:38
  52.1 7.9 %collective-permute-start.13 = (f32[2,4,1,512]{3,1,0,2:T(4,128)S(1)}, f32[2,4,1,512]{3,1,0,2:T(4,128)S(1)}, u32[]{:S(2)}, u32[]{:S(2)}) collective-permute-start(f32[2,4,1,512]{3,1,0,2:T(4,128)S(1)} %get-tuple-element.32), channel_id=1, source_target_pairs={{1,0},{2,1},{3,2},{4,3},{5,4},{6,5},{7,6},{8,7},{9,8},{10,9},{11,1... | collective-permute-start | bytes 49160 | tf_op jit(solution)/shard_map/ppermute | solution.py:55
  53.4 7.2 %collective-permute-start.12 = (f32[2,4,1,512]{3,1,0,2:T(4,128)S(1)}, f32[2,4,1,512]{3,1,0,2:T(4,128)}, u32[]{:S(2)}, u32[]{:S(2)}) collective-permute-start(f32[2,4,1,512]{3,1,0,2:T(4,128)S(1)} %get-tuple-element.32), channel_id=1, source_target_pairs={{0,1},{1,2},{2,3},{3,4},{4,5},{5,6},{6,7},{7,8},{8,9},{9,10},{10,1... | collective-permute-start | bytes 49160 | tf_op jit(solution)/shard_map/ppermute | solution.py:54
  57.9 7.2 %collective-permute-start.11 = (f32[4112]{0:T(1024)S(1)}, f32[4112]{0:T(1024)}, u32[]{:S(2)}, u32[]{:S(2)}) collective-permute-start(f32[4112]{0:T(1024)S(1)} %pad_maximum_fusion.4), channel_id=1, source_target_pairs={{0,8},{1,9},{2,10},{3,11},{4,12},{5,13},{6,14},{7,15},{8,0},{9,1},... | collective-permute-start | bytes 49352 | tf_op jit(solution)/shard_map/ppermute | solution.py:38
  60.0 0.6 copy-start.13
  66.5 1.5 %copy-start.9 = (f32[4,4]{1,0:T(4,128)}, f32[4,4]{1,0:T(4,128)S(1)}, u32[]{:S(2)}) copy-start(f32[4,4]{1,0:T(4,128)S(1)} %add_multiply_fusion.1) | copy-start | bytes 196
  67.1 0.9 copy-start.17
  67.1 0.9 copy-start.18
  67.1 1.7 %copy-start.15 = (f32[4]{0:T(128)}, f32[4]{0:T(128)S(1)}, u32[]{:S(2)}) copy-start(f32[4]{0:T(128)S(1)} %add_sqrt_fusion.3) | copy-start | bytes 52
  70.4 8.2 %copy-start.8 = (f32[1,4,1,512]{3,1,0,2:T(4,128)S(1)}, f32[1,4,1,512]{3,1,0,2:T(4,128)}, u32[]{:S(2)}) copy-start(f32[1,4,1,512]{3,1,0,2:T(4,128)} %get-tuple-element.56) | copy-start | bytes 24580
  72.7 3.1 %copy-start.16 = (f32[4]{0:T(128)S(1)}, f32[4]{0:T(128)}, u32[]{:S(2)}) copy-start(f32[4]{0:T(128)} %copy-done.15) | copy-start | bytes 52
  72.7 5.9 %copy-start.7 = (f32[2,4,1,512]{3,1,0,2:T(4,128)S(1)}, f32[2,4,1,512]{3,1,0,2:T(4,128)}, u32[]{:S(2)}) copy-start(f32[2,4,1,512]{3,1,0,2:T(4,128)} %reshape.1740) | copy-start | bytes 49156
  72.7 11.7 %copy-start.12 = (f32[4]{0:T(128)S(1)}, f32[4]{0:T(128)}, u32[]{:S(2)}) copy-start(f32[4]{0:T(128)} %copy-done.11) | copy-start | bytes 52
  72.7 20.5 %copy-start.24 = (f32[4,1]{0,1:T(1,128)S(1)}, f32[4,1]{0,1:T(1,128)}, u32[]{:S(2)}) copy-start(f32[4,1]{0,1:T(1,128)} %get-tuple-element.85) | copy-start | bytes 52
  73.4 14.3 %copy-start.25 = (f32[4,1]{0,1:T(1,128)S(1)}, f32[4,1]{0,1:T(1,128)}, u32[]{:S(2)}) copy-start(f32[4,1]{0,1:T(1,128)} %get-tuple-element.86) | copy-start | bytes 52
  73.4 22.1 %copy-start.10 = (f32[4,4]{1,0:T(4,128)S(1)}, f32[4,4]{1,0:T(4,128)}, u32[]{:S(2)}) copy-start(f32[4,4]{1,0:T(4,128)} %copy-done.9) | copy-start | bytes 196
  78.9 3.7 %collective-permute-start.14 = (f32[8,4]{1,0:T(8,128)S(1)}, f32[8,4]{1,0:T(8,128)S(1)}, u32[]{:S(2)}, u32[]{:S(2)}) collective-permute-start(f32[8,4]{1,0:T(8,128)S(1)} %concatenate.157), channel_id=1, source_target_pairs={{0,16},{16,0},{1,17},{17,1},{2,18},{18,2},{3,19},{19,3},{4,20},{20... | collective-permute-start | bytes 392 | tf_op jit(solution)/shard_map/ppermute | solution.py:21
  82.6 1.2 %collective-permute-start.15 = (f32[8,4]{1,0:T(8,128)S(1)}, f32[8,4]{1,0:T(8,128)S(1)}, u32[]{:S(2)}, u32[]{:S(2)}) collective-permute-start(f32[8,4]{1,0:T(8,128)S(1)} %add.531), channel_id=1, source_target_pairs={{0,1},{1,0},{2,3},{3,2},{4,5},{5,4},{6,7},{7,6},{8,9},{9,8},{10,11... | collective-permute-start | bytes 392 | tf_op jit(solution)/shard_map/ppermute | solution.py:21
  83.8 3.6 %collective-permute-start.16 = (f32[8,4]{1,0:T(8,128)S(1)}, f32[8,4]{1,0:T(8,128)S(1)}, u32[]{:S(2)}, u32[]{:S(2)}) collective-permute-start(f32[8,4]{1,0:T(8,128)S(1)} %add.532), channel_id=1, source_target_pairs={{0,2},{1,3},{2,0},{3,1},{4,6},{5,7},{6,4},{7,5},{8,10},{9,11},{10,... | collective-permute-start | bytes 392 | tf_op jit(solution)/shard_map/ppermute | solution.py:21
  87.4 3.6 %collective-permute-start.17 = (f32[8,4]{1,0:T(8,128)S(1)}, f32[8,4]{1,0:T(8,128)S(1)}, u32[]{:S(2)}, u32[]{:S(2)}) collective-permute-start(f32[8,4]{1,0:T(8,128)S(1)} %add.533), channel_id=1, source_target_pairs={{0,4},{1,5},{2,6},{3,7},{4,0},{5,1},{6,2},{7,3},{8,12},{9,13},{10,... | collective-permute-start | bytes 392 | tf_op jit(solution)/shard_map/ppermute | solution.py:21
  91.0 4.5 %collective-permute-start.18 = (f32[8,4]{1,0:T(8,128)S(1)}, f32[8,4]{1,0:T(8,128)S(1)}, u32[]{:S(2)}, u32[]{:S(2)}) collective-permute-start(f32[8,4]{1,0:T(8,128)S(1)} %add.534), channel_id=1, source_target_pairs={{0,8},{1,9},{2,10},{3,11},{4,12},{5,13},{6,14},{7,15},{8,0},{9,1},... | collective-permute-start | bytes 392 | tf_op jit(solution)/shard_map/ppermute | solution.py:21

commit v5 on v3

--- a/solution.py
+++ b/solution.py
@@ -95,7 +95,9 @@
 def far_field(gathered, weights, target_basis):
     nrhs = gathered.shape[2]
     rows = target_basis.shape[3]
-    inner = jnp.einsum("sakl,spql->apqk", weights, gathered, precision=lax.Precision.HIGHEST)
+    inner = jnp.sum(
+        weights[:, :, None, None, :, :] * gathered[:, None, :, :, None, :], axis=(0, 5)
+    )
     rounded_coef = complex_mix(inner).astype(jnp.bfloat16)
     outward = jnp.einsum(
         "akr,pqk->apqr", target_basis[0], rounded_coef, preferred_element_type=jnp.float32

time: 85.9 us -> 112 us (1.30); the launches traced: 85.1 us -> 110 us
  other arithmetic: 7.89 us -> 26.2 us
  local copies, waits for them, and re-layouts: 9.41 us -> 27 us
  waiting for transfers between devices: 26.4 us -> 18.7 us
  matrix products: 8.06 us -> 1.88 us
  starting transfers between devices: 32.3 us -> 35.2 us
    ppermute x10, waiting for transfers between devices: 15 us -> 8.35 us  [tree_collect(): got = lax.ppermute(packed, axis, [(i, i ^ k) for i in range(n)])]
    dot_general x2 -> x0, matrix products: 5.26 us -> none  [far_field(): jnp.einsum('sakl,spql->apqk', weights, gathered, precision=lax.Precision....]
    ppermute x5, starting transfers between devices: 4.19 us -> 8.86 us  [tree_sum(): x = x + lax.ppermute(x, axis, [(i, i ^ k) for i in range(n)])]
    reshape x5, local copies, waits for them, and re-layouts: 0.41 us -> 4.04 us  [tree_collect(): red = red + got[:red.size].reshape(red.shape)]
    slice x10, local copies, waits for them, and re-layouts: 0.72 us -> 3.64 us  [tree_collect(): other = got[red.size:].reshape(buf.shape)]
    reshape x4, local copies, waits for them, and re-layouts: 0.09 us -> 2.81 us  [swapped(): tiles = every.reshape(2, nrhs, -1, width)]
    unnamed x13 -> x51, local copies, waits for them, and re-layouts: 2.01 us -> 4.13 us
    reduce_sum x0 -> x2, other arithmetic: none -> 1.96 us  [far_field(): jnp.sum(weights[:, :, None, None, :, :] * gathered[:, None, :, :, None, :...]
  transfers between devices with their start and end apart: 19 -> 19, of which waited for: 14 -> 12; matrix products, arithmetic and copies ran while one was open for 12% -> 19% of each run, Pallas kernels for 0% -> 0%
where the time goes in v5:
time: 112 us; the launch traced here: 110 us
  starting transfers between devices  35.2 us (31%)
  local copies, waits for them, and re-layouts  27 us (24%)
  other arithmetic  26.2 us (23%)
  waiting for transfers between devices  18.7 us (17%)
  matrix products  1.88 us (2%)
  between operations  1.15 us (1%)
    ppermute x10, starting transfers between devices, tree_collect(): got = lax.ppermute(packed, axis, [(i, i ^ k) for i in range(n)])  20 us
    ppermute x5, waiting for transfers between devices, tree_sum(): x = x + lax.ppermute(x, axis, [(i, i ^ k) for i in range(n)])  10.3 us
    ppermute x5, starting transfers between devices, tree_sum(): x = x + lax.ppermute(x, axis, [(i, i ^ k) for i in range(n)])  8.86 us
    ppermute x10, waiting for transfers between devices, tree_collect(): got = lax.ppermute(packed, axis, [(i, i ^ k) for i in range(n)])  8.35 us
    unnamed x51, local copies, waits for them, and re-layouts  4.13 us
    reshape x5, local copies, waits for them, and re-layouts, tree_collect(): red = red + got[:red.size].reshape(red.shape)  4.04 us
    ppermute x2, starting transfers between devices, neighbours(): left = lax.ppermute(field, 'blk', [(i, i + 1) for i in range(ends)])  3.77 us
    slice x10, local copies, waits for them, and re-layouts, tree_collect(): other = got[red.size:].reshape(buf.shape)  3.64 us
  transfers between devices with their start and end apart: 19, of which 12 were waited for; matrix products, arithmetic and copies ran while one was open for 19% of the time, Pallas kernels for 0%

profile of v5, /device:TPU:0, one launch (start us, length us, event | category | flops | bytes accessed | tf_op | source)
XLA Modules:
  0.0 110.1 jit_solution(17623281052304149130)
XLA Ops:
  0.7 2.5 %collective-permute-start.5 = (f32[2,4,1,512]{3,2,1,0:T(1,128)}, f32[2,4,1,512]{3,2,1,0:T(1,128)S(1)}, u32[]{:S(2)}, u32[]{:S(2)}) collective-permute-start(f32[2,4,1,512]{3,2,1,0:T(1,128)} %param.12), channel_id=1, source_target_pairs={{0,1},{1,2},{2,3},{3,4},{4,5},{5,6},{6,7},{7,8},{8,9},{9,10},{10,1... | collective-permute-start | bytes 49160 | tf_op jit(solution)/shard_map/ppermute | solution.py:54
  3.2 1.3 %collective-permute-start.6 = (f32[2,4,1,512]{3,2,1,0:T(1,128)}, f32[2,4,1,512]{3,2,1,0:T(1,128)}, u32[]{:S(2)}, u32[]{:S(2)}) collective-permute-start(f32[2,4,1,512]{3,2,1,0:T(1,128)} %param.12), channel_id=1, source_target_pairs={{1,0},{2,1},{3,2},{4,3},{5,4},{6,5},{7,6},{8,7},{9,8},{10,9},{11,1... | collective-permute-start | bytes 49160 | tf_op jit(solution)/shard_map/ppermute | solution.py:55
  4.5 0.8 reshape_squeeze.4
  5.8 0.7 iota_compare_fusion
  6.8 1.4 %bitcast_multiply_fusion = f32[16,2,64,64]{3,2,1,0:T(8,128)S(1)} fusion(f32[1,1,16,2,64,64]{5,4,3,2,1,0:T(8,128)} %param.18, f32[16,64,64]{2,1,0:T(8,128)S(1)} %and_convert_fusion), kind=kLoop, calls=%fused_computation.16 | loop fusion | flops 131072 | bytes 1310720 | tf_op jit(solution)/shard_map/mul | solution.py:92
  8.7 3.2 %collective-permute-start = (f32[516]{0:T(1024)S(1)}, f32[516]{0:T(1024)S(1)}, u32[]{:S(2)}, u32[]{:S(2)}) collective-permute-start(f32[516]{0:T(1024)S(1)} %pad_maximum_fusion.10), channel_id=1, source_target_pairs={{0,1},{1,0},{2,3},{3,2},{4,5},{5,4},{6,7},{7,6},{8,9},{9,8},{10,11... | collective-permute-start | bytes 6200 | tf_op jit(solution)/shard_map/ppermute | solution.py:38
  13.1 2.0 %collective-permute-start.1 = (f32[1028]{0:T(1024)S(1)}, f32[1028]{0:T(1024)S(1)}, u32[]{:S(2)}, u32[]{:S(2)}) collective-permute-start(f32[1028]{0:T(1024)S(1)} %pad_maximum_fusion.7), channel_id=1, source_target_pairs={{0,2},{1,3},{2,0},{3,1},{4,6},{5,7},{6,4},{7,5},{8,10},{9,11},{10,... | collective-permute-start | bytes 12344 | tf_op jit(solution)/shard_map/ppermute | solution.py:38
  15.6 1.1 %collective-permute-done.1 = f32[1028]{0:T(1024)S(1)} collective-permute-done((f32[1028]{0:T(1024)S(1)}, f32[1028]{0:T(1024)S(1)}, u32[]{:S(2)}, u32[]{:S(2)}) %collective-permute-start.1) | collective-permute-done | bytes 4144 | tf_op jit(solution)/shard_map/ppermute | solution.py:38
  17.6 2.9 %collective-permute-start.2 = (f32[2052]{0:T(1024)S(1)}, f32[2052]{0:T(1024)S(1)}, u32[]{:S(2)}, u32[]{:S(2)}) collective-permute-start(f32[2052]{0:T(1024)S(1)} %pad_maximum_fusion.5), channel_id=1, source_target_pairs={{0,4},{1,5},{2,6},{3,7},{4,0},{5,1},{6,2},{7,3},{8,12},{9,13},{10,... | collective-permute-start | bytes 24632 | tf_op jit(solution)/shard_map/ppermute | solution.py:38
  21.1 1.1 collective-permute-done.2
  23.0 0.7 slice_add_fusion.9
  23.7 3.0 %collective-permute-start.3 = (f32[4100]{0:T(1024)S(1)}, f32[4100]{0:T(1024)}, u32[]{:S(2)}, u32[]{:S(2)}) collective-permute-start(f32[4100]{0:T(1024)S(1)} %pad_maximum_fusion.1), channel_id=1, source_target_pairs={{0,8},{1,9},{2,10},{3,11},{4,12},{5,13},{6,14},{7,15},{8,0},{9,1},... | collective-permute-start | bytes 49208 | tf_op jit(solution)/shard_map/ppermute | solution.py:38
  26.8 1.2 %pad_clamp_fusion = s32[1024]{0:T(1024)} fusion(s32[2]{0:T(128)} %compare_select_fusion), kind=kLoop, calls=%fused_computation.122 | loop fusion | flops 1024 | bytes 4104 | tf_op gather
  28.6 0.7 slice_add_fusion.8
  29.4 1.5 %collective-permute-start.4 = (f32[4100]{0:T(1024)S(1)}, f32[4100]{0:T(1024)}, u32[]{:S(2)}, u32[]{:S(2)}) collective-permute-start(f32[4100]{0:T(1024)S(1)} %pad_maximum_fusion.2), channel_id=1, source_target_pairs={{0,16},{16,0},{1,17},{17,1},{2,18},{18,2},{3,19},{19,3},{4,20},{20... | collective-permute-start | bytes 49208 | tf_op jit(solution)/shard_map/ppermute | solution.py:38
  30.9 0.7 constant_dynamic-update-slice_fusion
  31.7 0.8 slice.486
  32.5 0.7 concatenate.171
  33.3 0.7 add_sqrt_fusion.4
  34.0 0.9 fusion.14
  34.9 1.0 multiply_reduce_fusion.1
  37.2 1.5 %broadcast_divide_fusion = (f32[2,4,1,1536]{3,2,1,0:T(1,128)}, f32[2,4,1536]{2,1,0:T(4,128)S(1)}) fusion(f32[2,4,1,1536]{3,2,1,0:T(1,128)} %copy-done.5, f32[4]{0:T(128)S(1)} %add_sqrt_fusion.4), kind=kLoop, calls=%fused_computation.47 | loop fusion | flops 12288 | bytes 147472 | tf_op jit(solution)/shard_map/div | solution.py:162
  38.9 1.3 %gather_fusion = bf16[8,2,4,256]{3,2,1,0:T(4,128)(2,1)} fusion(bf16[2,4,6,256]{3,1,2,0:T(4,128)(2,1)S(1)} %divide_convert_fusion, s32[1024]{0:T(1024)} %pad_clamp_fusion.1), kind=kCustom, calls=%fused_computation.clone | custom fusion | bytes 65568 | tf_op jit(solution)/shard_map/jit(_take)/gather | solution.py:77
  40.2 0.8 broadcast_select_fusion.1
  42.3 0.8 slice.495
  43.1 0.9 fusion.20
  44.6 1.4 %reshape.1852 = f32[2,4,4,256]{3,2,1,0:T(4,128)} reshape(f32[2,4,2,512]{3,2,1,0:T(2,128)} %copy.92) | data formatting | bytes 65536 | tf_op jit(solution)/shard_map/reshape | solution.py:111
  46.0 1.4 %copy.93 = f32[2,4,4,256]{3,1,2,0:T(4,128)} copy(f32[2,4,4,256]{3,2,1,0:T(4,128)} %reshape.1852) | data formatting | bytes 65536 | tf_op jit(solution)/shard_map/reshape | solution.py:111
  47.4 1.4 %gather_fusion.1 = f32[2,2,4,256]{3,2,1,0:T(4,128)S(1)} fusion(f32[2,4,4,256]{3,1,2,0:T(4,128)} %copy.93, s32[1024]{0:T(1024)} %pad_clamp_fusion), kind=kCustom, calls=%fused_computation.1.clone | custom fusion | bytes 32776 | tf_op jit(solution)/shard_map/jit(_take)/gather | solution.py:112
  48.9 0.7 select_bitcast_fusion.1
  50.2 0.8 fusion.27
  52.2 1.2 %collective-permute-done.7 = f32[528]{0:T(1024)S(1)} collective-permute-done((f32[528]{0:T(1024)S(1)}, f32[528]{0:T(1024)S(1)}, u32[]{:S(2)}, u32[]{:S(2)}) %collective-permute-start.7) | collective-permute-done | bytes 2144 | tf_op jit(solution)/shard_map/ppermute | solution.py:38
  53.7 0.9 collective-permute-start.8
  54.6 2.7 %collective-permute-done.8 = f32[1040]{0:T(1024)S(1)} collective-permute-done((f32[1040]{0:T(1024)S(1)}, f32[1040]{0:T(1024)S(1)}, u32[]{:S(2)}, u32[]{:S(2)}) %collective-permute-start.8) | collective-permute-done | bytes 4192 | tf_op jit(solution)/shard_map/ppermute | solution.py:38
  57.7 1.9 %collective-permute-start.9 = (f32[2064]{0:T(1024)S(1)}, f32[2064]{0:T(1024)S(1)}, u32[]{:S(2)}, u32[]{:S(2)}) collective-permute-start(f32[2064]{0:T(1024)S(1)} %pad_maximum_fusion.6), channel_id=1, source_target_pairs={{0,4},{1,5},{2,6},{3,7},{4,0},{5,1},{6,2},{7,3},{8,12},{9,13},{10,... | collective-permute-start | bytes 24776 | tf_op jit(solution)/shard_map/ppermute | solution.py:38
  59.6 1.8 %collective-permute-done.9 = f32[2064]{0:T(1024)S(1)} collective-permute-done((f32[2064]{0:T(1024)S(1)}, f32[2064]{0:T(1024)S(1)}, u32[]{:S(2)}, u32[]{:S(2)}) %collective-permute-start.9) | collective-permute-done | bytes 8288 | tf_op jit(solution)/shard_map/ppermute | solution.py:38
  62.2 2.9 %collective-permute-start.10 = (f32[4112]{0:T(1024)S(1)}, f32[4112]{0:T(1024)}, u32[]{:S(2)}, u32[]{:S(2)}) collective-permute-start(f32[4112]{0:T(1024)S(1)} %pad_maximum_fusion.3), channel_id=1, source_target_pairs={{0,8},{1,9},{2,10},{3,11},{4,12},{5,13},{6,14},{7,15},{8,0},{9,1},... | collective-permute-start | bytes 49352 | tf_op jit(solution)/shard_map/ppermute | solution.py:38
  65.2 1.3 %collective-permute-start.12 = (f32[2,4,1,512]{3,1,0,2:T(4,128)S(1)}, f32[2,4,1,512]{3,1,0,2:T(4,128)S(1)}, u32[]{:S(2)}, u32[]{:S(2)}) collective-permute-start(f32[2,4,1,512]{3,1,0,2:T(4,128)S(1)} %get-tuple-element.35), channel_id=1, source_target_pairs={{0,1},{1,2},{2,3},{3,4},{4,5},{5,6},{6,7},{7,8},{8,9},{9,10},{10,1... | collective-permute-start | bytes 49160 | tf_op jit(solution)/shard_map/ppermute | solution.py:54
  66.5 1.3 %collective-permute-start.13 = (f32[2,4,1,512]{3,1,0,2:T(4,128)S(1)}, f32[2,4,1,512]{3,1,0,2:T(4,128)}, u32[]{:S(2)}, u32[]{:S(2)}) collective-permute-start(f32[2,4,1,512]{3,1,0,2:T(4,128)S(1)} %get-tuple-element.35), channel_id=1, source_target_pairs={{1,0},{2,1},{3,2},{4,3},{5,4},{6,5},{7,6},{8,7},{9,8},{10,9},{11,1... | collective-permute-start | bytes 49160 | tf_op jit(solution)/shard_map/ppermute | solution.py:55
  69.1 1.3 %reshape.1859 = f32[4,4]{1,0:T(4,128)} reshape(f32[16]{0:T(128)} %get-tuple-element.62) | data formatting | bytes 128 | tf_op jit(solution)/shard_map/reshape | solution.py:39
  70.4 1.3 %fusion.77 = (f32[16]{0:T(128)}, f32[16]{0:T(128)S(1)}) fusion(f32[4112]{0:T(1024)} %collective-permute-done.10, f32[16]{0:T(128)S(1)} %get-tuple-element.63), kind=kLoop, calls=%fused_computation.223 | loop fusion | flops 16 | bytes 256 | tf_op jit(solution)/shard_map/slice | solution.py:39
  71.7 0.7 pad_maximum_fusion.4
  72.3 1.5 %collective-permute-start.11 = (f32[4112]{0:T(1024)}, f32[4112]{0:T(1024)}, u32[]{:S(2)}, u32[]{:S(2)}) collective-permute-start(f32[4112]{0:T(1024)} %pad_maximum_fusion.4), channel_id=1, source_target_pairs={{0,16},{16,0},{1,17},{17,1},{2,18},{18,2},{3,19},{19,3},{4,20},{20... | collective-permute-start | bytes 49352 | tf_op jit(solution)/shard_map/ppermute | solution.py:38
  74.5 0.7 pad_maximum_fusion
  75.2 1.3 %reshape.1861 = f32[4,4]{1,0:T(4,128)} reshape(f32[16]{0:T(128)} %get-tuple-element.52) | data formatting | bytes 128 | tf_op jit(solution)/shard_map/reshape | solution.py:39
  76.5 0.8 slice.516
  77.3 0.7 concatenate.190
  78.0 0.7 slice.509
  78.8 0.7 add_multiply_fusion.1
  80.1 0.7 multiply_subtract_fusion.4
  81.0 0.9 fusion.16
  82.0 1.0 multiply_reduce_fusion
  83.5 0.7 gather_fusion.2
  84.2 0.8 broadcast_select_fusion
  85.6 0.8 slice.527
  86.6 0.7 gather_fusion.3
  88.4 3.1 %collective-permute-done.14 = f32[8,4]{1,0:T(8,128)S(1)} collective-permute-done((f32[8,4]{1,0:T(8,128)S(1)}, f32[8,4]{1,0:T(8,128)S(1)}, u32[]{:S(2)}, u32[]{:S(2)}) %collective-permute-start.14) | collective-permute-done | bytes 160 | tf_op jit(solution)/shard_map/ppermute | solution.py:21
  92.0 0.8 collective-permute-done.15
  92.9 3.4 %collective-permute-start.16 = (f32[8,4]{1,0:T(8,128)S(1)}, f32[8,4]{1,0:T(8,128)S(1)}, u32[]{:S(2)}, u32[]{:S(2)}) collective-permute-start(f32[8,4]{1,0:T(8,128)S(1)} %add.532), channel_id=1, source_target_pairs={{0,2},{1,3},{2,0},{3,1},{4,6},{5,7},{6,4},{7,5},{8,10},{9,11},{10,... | collective-permute-start | bytes 392 | tf_op jit(solution)/shard_map/ppermute | solution.py:21
  97.0 0.9 collective-permute-done.16
  97.8 4.0 %collective-permute-start.17 = (f32[8,4]{1,0:T(8,128)S(1)}, f32[8,4]{1,0:T(8,128)S(1)}, u32[]{:S(2)}, u32[]{:S(2)}) collective-permute-start(f32[8,4]{1,0:T(8,128)S(1)} %add.533), channel_id=1, source_target_pairs={{0,4},{1,5},{2,6},{3,7},{4,0},{5,1},{6,2},{7,3},{8,12},{9,13},{10,... | collective-permute-start | bytes 392 | tf_op jit(solution)/shard_map/ppermute | solution.py:21
  101.9 1.5 %collective-permute-done.17 = f32[8,4]{1,0:T(8,128)S(1)} collective-permute-done((f32[8,4]{1,0:T(8,128)S(1)}, f32[8,4]{1,0:T(8,128)S(1)}, u32[]{:S(2)}, u32[]{:S(2)}) %collective-permute-start.17) | collective-permute-done | bytes 160 | tf_op jit(solution)/shard_map/ppermute | solution.py:21
  103.9 4.0 %collective-permute-done.18 = f32[8,4]{1,0:T(8,128)S(1)} collective-permute-done((f32[8,4]{1,0:T(8,128)S(1)}, f32[8,4]{1,0:T(8,128)S(1)}, u32[]{:S(2)}, u32[]{:S(2)}) %collective-permute-start.18) | collective-permute-done | bytes 160 | tf_op jit(solution)/shard_map/ppermute | solution.py:21
  109.4 0.7 stack.153
  (180 shorter events, 21.1 us)
Async XLA Ops:
  0.6 40.4 %copy-start = (bf16[1,2,4,2,256,256]{5,4,3,2,1,0:T(8,128)(2,1)S(1)}, bf16[1,2,4,2,256,256]{5,4,3,2,1,0:T(8,128)(2,1)}, u32[]{:S(2)}) copy-start(bf16[1,2,4,2,256,256]{5,4,3,2,1,0:T(8,128)(2,1)} %param.13) | copy-start | bytes 6291460
  0.6 7.5 %copy-start.3 = (f32[2,4,1,512]{3,2,1,0:T(1,128)S(1)}, f32[2,4,1,512]{3,2,1,0:T(1,128)}, u32[]{:S(2)}) copy-start(f32[2,4,1,512]{3,2,1,0:T(1,128)} %param.12) | copy-start | bytes 49156
  0.7 7.7 %copy-start.1 = (bf16[1,2,64,512]{3,2,1,0:T(8,128)(2,1)S(1)}, bf16[1,2,64,512]{3,2,1,0:T(8,128)(2,1)}, u32[]{:S(2)}) copy-start(bf16[1,2,64,512]{3,2,1,0:T(8,128)(2,1)} %param.16) | copy-start | bytes 393220
  0.7 11.3 %copy-start.22 = (s32[1,2]{1,0:T(1,128)S(1)}, s32[1,2]{1,0:T(1,128)}, u32[]{:S(2)}) copy-start(s32[1,2]{1,0:T(1,128)} %param.15) | copy-start | bytes 28
  0.7 7.6 %collective-permute-start.5 = (f32[2,4,1,512]{3,2,1,0:T(1,128)}, f32[2,4,1,512]{3,2,1,0:T(1,128)S(1)}, u32[]{:S(2)}, u32[]{:S(2)}) collective-permute-start(f32[2,4,1,512]{3,2,1,0:T(1,128)} %param.12), channel_id=1, source_target_pairs={{0,1},{1,2},{2,3},{3,4},{4,5},{5,6},{6,7},{7,8},{8,9},{9,10},{10,1... | collective-permute-start | bytes 49160 | tf_op jit(solution)/shard_map/ppermute | solution.py:54
  3.2 27.8 %collective-permute-start.6 = (f32[2,4,1,512]{3,2,1,0:T(1,128)}, f32[2,4,1,512]{3,2,1,0:T(1,128)}, u32[]{:S(2)}, u32[]{:S(2)}) collective-permute-start(f32[2,4,1,512]{3,2,1,0:T(1,128)} %param.12), channel_id=1, source_target_pairs={{1,0},{2,1},{3,2},{4,3},{5,4},{6,5},{7,6},{8,7},{9,8},{10,9},{11,1... | collective-permute-start | bytes 49160 | tf_op jit(solution)/shard_map/ppermute | solution.py:55
  6.8 29.1 %copy-start.2 = (bf16[1,2,64,512]{3,2,1,0:T(8,128)(2,1)S(1)}, bf16[1,2,64,512]{3,2,1,0:T(8,128)(2,1)}, u32[]{:S(2)}) copy-start(bf16[1,2,64,512]{3,2,1,0:T(8,128)(2,1)} %param.17) | copy-start | bytes 393220
  8.7 4.1 %collective-permute-start = (f32[516]{0:T(1024)S(1)}, f32[516]{0:T(1024)S(1)}, u32[]{:S(2)}, u32[]{:S(2)}) collective-permute-start(f32[516]{0:T(1024)S(1)} %pad_maximum_fusion.10), channel_id=1, source_target_pairs={{0,1},{1,0},{2,3},{3,2},{4,5},{5,4},{6,7},{7,6},{8,9},{9,8},{10,11... | collective-permute-start | bytes 6200 | tf_op jit(solution)/shard_map/ppermute | solution.py:38
  13.1 3.7 %collective-permute-start.1 = (f32[1028]{0:T(1024)S(1)}, f32[1028]{0:T(1024)S(1)}, u32[]{:S(2)}, u32[]{:S(2)}) collective-permute-start(f32[1028]{0:T(1024)S(1)} %pad_maximum_fusion.7), channel_id=1, source_target_pairs={{0,2},{1,3},{2,0},{3,1},{4,6},{5,7},{6,4},{7,5},{8,10},{9,11},{10,... | collective-permute-start | bytes 12344 | tf_op jit(solution)/shard_map/ppermute | solution.py:38
  17.0 0.5 copy-start.21
  17.6 4.6 %collective-permute-start.2 = (f32[2052]{0:T(1024)S(1)}, f32[2052]{0:T(1024)S(1)}, u32[]{:S(2)}, u32[]{:S(2)}) collective-permute-start(f32[2052]{0:T(1024)S(1)} %pad_maximum_fusion.5), channel_id=1, source_target_pairs={{0,4},{1,5},{2,6},{3,7},{4,0},{5,1},{6,2},{7,3},{8,12},{9,13},{10,... | collective-permute-start | bytes 24632 | tf_op jit(solution)/shard_map/ppermute | solution.py:38
  22.2 0.6 copy-start.13
  23.7 4.9 %collective-permute-start.3 = (f32[4100]{0:T(1024)S(1)}, f32[4100]{0:T(1024)}, u32[]{:S(2)}, u32[]{:S(2)}) collective-permute-start(f32[4100]{0:T(1024)S(1)} %pad_maximum_fusion.1), channel_id=1, source_target_pairs={{0,8},{1,9},{2,10},{3,11},{4,12},{5,13},{6,14},{7,15},{8,0},{9,1},... | collective-permute-start | bytes 49208 | tf_op jit(solution)/shard_map/ppermute | solution.py:38
  29.4 3.9 %collective-permute-start.4 = (f32[4100]{0:T(1024)S(1)}, f32[4100]{0:T(1024)}, u32[]{:S(2)}, u32[]{:S(2)}) collective-permute-start(f32[4100]{0:T(1024)S(1)} %pad_maximum_fusion.2), channel_id=1, source_target_pairs={{0,16},{16,0},{1,17},{17,1},{2,18},{18,2},{3,19},{19,3},{4,20},{20... | collective-permute-start | bytes 49208 | tf_op jit(solution)/shard_map/ppermute | solution.py:38
  31.7 1.6 %copy-start.5 = (f32[2,4,1,1536]{3,2,1,0:T(1,128)}, f32[2,4,1,1536]{3,2,1,0:T(1,128)S(1)}, u32[]{:S(2)}) copy-start(f32[2,4,1,1536]{3,2,1,0:T(1,128)S(1)} %constant_dynamic-update-slice_fusion) | copy-start | bytes 147460
  34.0 7.7 %copy-start.10 = (f32[4]{0:T(128)}, f32[4]{0:T(128)S(1)}, u32[]{:S(2)}) copy-start(f32[4]{0:T(128)S(1)} %add_sqrt_fusion.4) | copy-start | bytes 52
  51.2 31.9 %copy-start.4 = (f32[2,4,1,1536]{3,2,1,0:T(1,128)S(1)}, f32[2,4,1,1536]{3,2,1,0:T(1,128)}, u32[]{:S(2)}) copy-start(f32[2,4,1,1536]{3,2,1,0:T(1,128)} %get-tuple-element.39) | copy-start | bytes 147460
  51.4 0.6 copy-start.14
  51.4 2.2 %copy-start.15 = (f32[4]{0:T(128)}, f32[4]{0:T(128)S(1)}, u32[]{:S(2)}) copy-start(f32[4]{0:T(128)S(1)} %get-tuple-element.26) | copy-start | bytes 52
  51.4 2.1 %copy-start.16 = (f32[4]{0:T(128)}, f32[4]{0:T(128)S(1)}, u32[]{:S(2)}) copy-start(f32[4]{0:T(128)S(1)} %get-tuple-element.31) | copy-start | bytes 52
  51.4 6.0 %copy-start.17 = (f32[4]{0:T(128)}, f32[4]{0:T(128)S(1)}, u32[]{:S(2)}) copy-start(f32[4]{0:T(128)S(1)} %get-tuple-element.32) | copy-start | bytes 52
  52.2 1.2 %collective-permute-start.7 = (f32[528]{0:T(1024)S(1)}, f32[528]{0:T(1024)S(1)}, u32[]{:S(2)}, u32[]{:S(2)}) collective-permute-start(f32[528]{0:T(1024)S(1)} %pad_maximum_fusion.12), channel_id=1, source_target_pairs={{0,1},{1,0},{2,3},{3,2},{4,5},{5,4},{6,7},{7,6},{8,9},{9,8},{10,11... | collective-permute-start | bytes 6344 | tf_op jit(solution)/shard_map/ppermute | solution.py:38
  53.7 3.7 %collective-permute-start.8 = (f32[1040]{0:T(1024)S(1)}, f32[1040]{0:T(1024)S(1)}, u32[]{:S(2)}, u32[]{:S(2)}) collective-permute-start(f32[1040]{0:T(1024)S(1)} %pad_maximum_fusion.8), channel_id=1, source_target_pairs={{0,2},{1,3},{2,0},{3,1},{4,6},{5,7},{6,4},{7,5},{8,10},{9,11},{10,... | collective-permute-start | bytes 12488 | tf_op jit(solution)/shard_map/ppermute | solution.py:38
  57.7 3.7 %collective-permute-start.9 = (f32[2064]{0:T(1024)S(1)}, f32[2064]{0:T(1024)S(1)}, u32[]{:S(2)}, u32[]{:S(2)}) collective-permute-start(f32[2064]{0:T(1024)S(1)} %pad_maximum_fusion.6), channel_id=1, source_target_pairs={{0,4},{1,5},{2,6},{3,7},{4,0},{5,1},{6,2},{7,3},{8,12},{9,13},{10,... | collective-permute-start | bytes 24776 | tf_op jit(solution)/shard_map/ppermute | solution.py:38
  62.2 8.2 %collective-permute-start.10 = (f32[4112]{0:T(1024)S(1)}, f32[4112]{0:T(1024)}, u32[]{:S(2)}, u32[]{:S(2)}) collective-permute-start(f32[4112]{0:T(1024)S(1)} %pad_maximum_fusion.3), channel_id=1, source_target_pairs={{0,8},{1,9},{2,10},{3,11},{4,12},{5,13},{6,14},{7,15},{8,0},{9,1},... | collective-permute-start | bytes 49352 | tf_op jit(solution)/shard_map/ppermute | solution.py:38
  65.2 8.7 %collective-permute-start.12 = (f32[2,4,1,512]{3,1,0,2:T(4,128)S(1)}, f32[2,4,1,512]{3,1,0,2:T(4,128)S(1)}, u32[]{:S(2)}, u32[]{:S(2)}) collective-permute-start(f32[2,4,1,512]{3,1,0,2:T(4,128)S(1)} %get-tuple-element.35), channel_id=1, source_target_pairs={{0,1},{1,2},{2,3},{3,4},{4,5},{5,6},{6,7},{7,8},{8,9},{9,10},{10,1... | collective-permute-start | bytes 49160 | tf_op jit(solution)/shard_map/ppermute | solution.py:54
  66.5 8.0 %collective-permute-start.13 = (f32[2,4,1,512]{3,1,0,2:T(4,128)S(1)}, f32[2,4,1,512]{3,1,0,2:T(4,128)}, u32[]{:S(2)}, u32[]{:S(2)}) collective-permute-start(f32[2,4,1,512]{3,1,0,2:T(4,128)S(1)} %get-tuple-element.35), channel_id=1, source_target_pairs={{1,0},{2,1},{3,2},{4,3},{5,4},{6,5},{7,6},{8,7},{9,8},{10,9},{11,1... | collective-permute-start | bytes 49160 | tf_op jit(solution)/shard_map/ppermute | solution.py:55
  72.3 5.7 %collective-permute-start.11 = (f32[4112]{0:T(1024)}, f32[4112]{0:T(1024)}, u32[]{:S(2)}, u32[]{:S(2)}) collective-permute-start(f32[4112]{0:T(1024)} %pad_maximum_fusion.4), channel_id=1, source_target_pairs={{0,16},{16,0},{1,17},{17,1},{2,18},{18,2},{3,19},{19,3},{4,20},{20... | collective-permute-start | bytes 49352 | tf_op jit(solution)/shard_map/ppermute | solution.py:38
  73.9 0.6 copy-start.12
  79.5 1.4 %copy-start.8 = (f32[4,4]{1,0:T(4,128)}, f32[4,4]{1,0:T(4,128)S(1)}, u32[]{:S(2)}) copy-start(f32[4,4]{1,0:T(4,128)S(1)} %add_multiply_fusion.1) | copy-start | bytes 196
  81.9 5.4 %copy-start.18 = (pred[2]{0:T(512)(128)(4,1)S(1)}, pred[2]{0:T(512)(128)(4,1)}, u32[]{:S(2)}) copy-start(pred[2]{0:T(512)(128)(4,1)} %compare_and_fusion) | copy-start | bytes 10
  81.9 5.5 %copy-start.6 = (f32[1,4,1,512]{3,1,0,2:T(4,128)S(1)}, f32[1,4,1,512]{3,1,0,2:T(4,128)}, u32[]{:S(2)}) copy-start(f32[1,4,1,512]{3,1,0,2:T(4,128)} %get-tuple-element.58) | copy-start | bytes 24580
  81.9 5.5 %copy-start.7 = (f32[1,4,1,512]{3,1,0,2:T(4,128)S(1)}, f32[1,4,1,512]{3,1,0,2:T(4,128)}, u32[]{:S(2)}) copy-start(f32[1,4,1,512]{3,1,0,2:T(4,128)} %get-tuple-element.59) | copy-start | bytes 24580
  82.0 14.3 %copy-start.11 = (f32[4]{0:T(128)S(1)}, f32[4]{0:T(128)}, u32[]{:S(2)}) copy-start(f32[4]{0:T(128)} %copy-done.10) | copy-start | bytes 52
  83.0 18.9 %copy-start.20 = (f32[4,1]{0,1:T(1,128)S(1)}, f32[4,1]{0,1:T(1,128)}, u32[]{:S(2)}) copy-start(f32[4,1]{0,1:T(1,128)} %get-tuple-element.89) | copy-start | bytes 52
  83.0 20.8 %copy-start.19 = (f32[4,1]{0,1:T(1,128)S(1)}, f32[4,1]{0,1:T(1,128)}, u32[]{:S(2)}) copy-start(f32[4,1]{0,1:T(1,128)} %get-tuple-element.88) | copy-start | bytes 52
  83.0 25.0 %copy-start.9 = (f32[4,4]{1,0:T(4,128)S(1)}, f32[4,4]{1,0:T(4,128)}, u32[]{:S(2)}) copy-start(f32[4,4]{1,0:T(4,128)} %copy-done.8) | copy-start | bytes 196
  87.8 3.7 %collective-permute-start.14 = (f32[8,4]{1,0:T(8,128)S(1)}, f32[8,4]{1,0:T(8,128)S(1)}, u32[]{:S(2)}, u32[]{:S(2)}) collective-permute-start(f32[8,4]{1,0:T(8,128)S(1)} %concatenate.195), channel_id=1, source_target_pairs={{0,16},{16,0},{1,17},{17,1},{2,18},{18,2},{3,19},{19,3},{4,20},{20... | collective-permute-start | bytes 392 | tf_op jit(solution)/shard_map/ppermute | solution.py:21
  91.5 1.3 %collective-permute-start.15 = (f32[8,4]{1,0:T(8,128)S(1)}, f32[8,4]{1,0:T(8,128)S(1)}, u32[]{:S(2)}, u32[]{:S(2)}) collective-permute-start(f32[8,4]{1,0:T(8,128)S(1)} %add.531), channel_id=1, source_target_pairs={{0,1},{1,0},{2,3},{3,2},{4,5},{5,4},{6,7},{7,6},{8,9},{9,8},{10,11... | collective-permute-start | bytes 392 | tf_op jit(solution)/shard_map/ppermute | solution.py:21
  92.9 5.0 %collective-permute-start.16 = (f32[8,4]{1,0:T(8,128)S(1)}, f32[8,4]{1,0:T(8,128)S(1)}, u32[]{:S(2)}, u32[]{:S(2)}) collective-permute-start(f32[8,4]{1,0:T(8,128)S(1)} %add.532), channel_id=1, source_target_pairs={{0,2},{1,3},{2,0},{3,1},{4,6},{5,7},{6,4},{7,5},{8,10},{9,11},{10,... | collective-permute-start | bytes 392 | tf_op jit(solution)/shard_map/ppermute | solution.py:21
  97.8 5.6 %collective-permute-start.17 = (f32[8,4]{1,0:T(8,128)S(1)}, f32[8,4]{1,0:T(8,128)S(1)}, u32[]{:S(2)}, u32[]{:S(2)}) collective-permute-start(f32[8,4]{1,0:T(8,128)S(1)} %add.533), channel_id=1, source_target_pairs={{0,4},{1,5},{2,6},{3,7},{4,0},{5,1},{6,2},{7,3},{8,12},{9,13},{10,... | collective-permute-start | bytes 392 | tf_op jit(solution)/shard_map/ppermute | solution.py:21
  103.4 4.5 %collective-permute-start.18 = (f32[8,4]{1,0:T(8,128)S(1)}, f32[8,4]{1,0:T(8,128)S(1)}, u32[]{:S(2)}, u32[]{:S(2)}) collective-permute-start(f32[8,4]{1,0:T(8,128)S(1)} %add.534), channel_id=1, source_target_pairs={{0,8},{1,9},{2,10},{3,11},{4,12},{5,13},{6,14},{7,15},{8,0},{9,1},... | collective-permute-start | bytes 392 | tf_op jit(solution)/shard_map/ppermute | solution.py:21

commit v6 on v3

--- a/solution.py
+++ b/solution.py
@@ -84,12 +84,10 @@
 
 
 def far_weights(coupling, far_ranks, rank_cap):
-    row_coupling = coupling[0, 0]
-    row_ranks = far_ranks[0, 0]
     levels = jnp.arange(rank_cap, dtype=jnp.int32)
-    limit = row_ranks[:, None, None]
-    keep = (levels[None, :, None] < limit) & (levels[None, None, :] < limit)
-    return row_coupling * keep[:, None].astype(jnp.float32)
+    limit = far_ranks[0, 0][:, None, None, None]
+    keep = (levels[None, None, :, None] < limit) & (levels[None, None, None, :] < limit)
+    return jnp.where(keep, coupling[0, 0], 0.0)
 
 
 def far_field(gathered, weights, target_basis):

time: 85.9 us -> 108 us (1.26)
  other arithmetic: 7.89 us -> 22.2 us
  local copies, waits for them, and re-layouts: 9.41 us -> 21 us
  waiting for transfers between devices: 26.4 us -> 22.3 us
    ppermute x10, waiting for transfers between devices: 15 us -> 10.8 us  [tree_collect(): got = lax.ppermute(packed, axis, [(i, i ^ k) for i in range(n)])]
    reshape x4, local copies, waits for them, and re-layouts: 0.09 us -> 2.81 us  [swapped(): tiles = every.reshape(2, nrhs, -1, width)]
    reshape x5, local copies, waits for them, and re-layouts: 0.41 us -> 2.88 us  [tree_collect(): red = red + got[:red.size].reshape(red.shape)]
    convert_element_type x2, other arithmetic: 0.16 us -> 1.96 us  [near_field(): window.astype(jnp.bfloat16).reshape(2, nrhs, 3 * blocks_dev, width)]
    gather x2, local copies, waits for them, and re-layouts: 1.18 us -> 2.75 us  [near_field(): jnp.take(rounded, near_cols[0].reshape(-1), axis=2)]
    select_n x3, other arithmetic: 0.18 us -> 1.6 us  [near_field(): jnp.take(rounded, near_cols[0].reshape(-1), axis=2)]
    sub x5, other arithmetic: 0.53 us -> 1.91 us  [scaled(): real_f * field[0] - imag_f * field[1]]
    div x1, other arithmetic: 0.17 us -> 1.53 us  [shards(): window_one = window_rhs / inv_scale]
  transfers between devices with their start and end apart: 19 -> 19, of which waited for: 14 -> 14; matrix products, arithmetic and copies ran while one was open for 12% -> 15% of each run, Pallas kernels for 0% -> 0%
where the time goes in v6:
time: 108 us; the launch traced here: 107 us
  starting transfers between devices  32.2 us (30%)
  waiting for transfers between devices  22.3 us (21%)
  other arithmetic  22.2 us (21%)
  local copies, waits for them, and re-layouts  21 us (19%)
  matrix products  7.77 us (7%)
  between operations  1.29 us (1%)
    ppermute x10, starting transfers between devices, tree_collect(): got = lax.ppermute(packed, axis, [(i, i ^ k) for i in range(n)])  20 us
    ppermute x5, waiting for transfers between devices, tree_sum(): x = x + lax.ppermute(x, axis, [(i, i ^ k) for i in range(n)])  11.5 us
    ppermute x10, waiting for transfers between devices, tree_collect(): got = lax.ppermute(packed, axis, [(i, i ^ k) for i in range(n)])  10.8 us
    ppermute x2, starting transfers between devices, neighbours(): left = lax.ppermute(field, 'blk', [(i, i + 1) for i in range(ends)])  5.52 us
    dot_general x2, matrix products, far_field(): jnp.einsum('sakl,spql->apqk', weights, gathered, precision=lax.Precision....  4.98 us
    ppermute x5, starting transfers between devices, tree_sum(): x = x + lax.ppermute(x, axis, [(i, i ^ k) for i in range(n)])  4.15 us
    reshape x5, local copies, waits for them, and re-layouts, tree_collect(): red = red + got[:red.size].reshape(red.shape)  2.88 us
    reshape x4, local copies, waits for them, and re-layouts, swapped(): tiles = every.reshape(2, nrhs, -1, width)  2.81 us
  transfers between devices with their start and end apart: 19, of which 14 were waited for; matrix products, arithmetic and copies ran while one was open for 15% of the time, Pallas kernels for 0%

profile of v6, /device:TPU:0, one launch (start us, length us, event | category | flops | bytes accessed | tf_op | source)
XLA Modules:
  0.0 106.8 jit_solution(9580207244680168305)
XLA Ops:
  0.7 2.5 %collective-permute-start.5 = (f32[2,4,1,512]{3,2,1,0:T(1,128)}, f32[2,4,1,512]{3,2,1,0:T(1,128)S(1)}, u32[]{:S(2)}, u32[]{:S(2)}) collective-permute-start(f32[2,4,1,512]{3,2,1,0:T(1,128)} %param.12), channel_id=1, source_target_pairs={{0,1},{1,2},{2,3},{3,4},{4,5},{5,6},{6,7},{7,8},{8,9},{9,10},{10,1... | collective-permute-start | bytes 49160 | tf_op jit(solution)/shard_map/ppermute | solution.py:54
  3.2 1.3 %collective-permute-start.6 = (f32[2,4,1,512]{3,2,1,0:T(1,128)}, f32[2,4,1,512]{3,2,1,0:T(1,128)S(1)}, u32[]{:S(2)}, u32[]{:S(2)}) collective-permute-start(f32[2,4,1,512]{3,2,1,0:T(1,128)} %param.12), channel_id=1, source_target_pairs={{1,0},{2,1},{3,2},{4,3},{5,4},{6,5},{7,6},{8,7},{9,8},{10,9},{11,1... | collective-permute-start | bytes 49160 | tf_op jit(solution)/shard_map/ppermute | solution.py:55
  4.5 0.7 compare_select_fusion
  5.1 1.2 %compare_and_fusion = pred[2]{0:T(512)(128)(4,1)} fusion(s32[1,2]{1,0:T(1,128)} %param.15), kind=kLoop, calls=%fused_computation.169 | loop fusion | flops 12 | bytes 10 | tf_op jit(solution)/shard_map/jit(_take)/and | solution.py:108
  6.3 0.7 iota_compare_fusion
  7.3 0.8 add_reduce_fusion.9
  8.1 0.8 reshape_squeeze.4
  8.9 0.8 constant_dynamic-update-slice_fusion.1
  9.7 1.1 convolution_bitcast_fusion.5
  10.9 3.2 %collective-permute-start = (f32[516]{0:T(1024)S(1)}, f32[516]{0:T(1024)S(1)}, u32[]{:S(2)}, u32[]{:S(2)}) collective-permute-start(f32[516]{0:T(1024)S(1)} %pad_maximum_fusion.10), channel_id=1, source_target_pairs={{0,1},{1,0},{2,3},{3,2},{4,5},{5,4},{6,7},{7,6},{8,9},{9,8},{10,11... | collective-permute-start | bytes 6200 | tf_op jit(solution)/shard_map/ppermute | solution.py:38
  14.2 0.8 collective-permute-done
  15.3 2.0 %collective-permute-start.1 = (f32[1028]{0:T(1024)S(1)}, f32[1028]{0:T(1024)S(1)}, u32[]{:S(2)}, u32[]{:S(2)}) collective-permute-start(f32[1028]{0:T(1024)S(1)} %pad_maximum_fusion.7), channel_id=1, source_target_pairs={{0,2},{1,3},{2,0},{3,1},{4,6},{5,7},{6,4},{7,5},{8,10},{9,11},{10,... | collective-permute-start | bytes 12344 | tf_op jit(solution)/shard_map/ppermute | solution.py:38
  17.8 1.1 %collective-permute-done.1 = f32[1028]{0:T(1024)S(1)} collective-permute-done((f32[1028]{0:T(1024)S(1)}, f32[1028]{0:T(1024)S(1)}, u32[]{:S(2)}, u32[]{:S(2)}) %collective-permute-start.1) | collective-permute-done | bytes 4144 | tf_op jit(solution)/shard_map/ppermute | solution.py:38
  19.3 2.9 %collective-permute-start.2 = (f32[2052]{0:T(1024)S(1)}, f32[2052]{0:T(1024)S(1)}, u32[]{:S(2)}, u32[]{:S(2)}) collective-permute-start(f32[2052]{0:T(1024)S(1)} %pad_maximum_fusion.5), channel_id=1, source_target_pairs={{0,4},{1,5},{2,6},{3,7},{4,0},{5,1},{6,2},{7,3},{8,12},{9,13},{10,... | collective-permute-start | bytes 24632 | tf_op jit(solution)/shard_map/ppermute | solution.py:38
  22.8 1.1 %collective-permute-done.2 = f32[2052]{0:T(1024)S(1)} collective-permute-done((f32[2052]{0:T(1024)S(1)}, f32[2052]{0:T(1024)S(1)}, u32[]{:S(2)}, u32[]{:S(2)}) %collective-permute-start.2) | collective-permute-done | bytes 8240 | tf_op jit(solution)/shard_map/ppermute | solution.py:38
  24.3 3.0 %collective-permute-start.3 = (f32[4100]{0:T(1024)S(1)}, f32[4100]{0:T(1024)S(1)}, u32[]{:S(2)}, u32[]{:S(2)}) collective-permute-start(f32[4100]{0:T(1024)S(1)} %pad_maximum_fusion.1), channel_id=1, source_target_pairs={{0,8},{1,9},{2,10},{3,11},{4,12},{5,13},{6,14},{7,15},{8,0},{9,1},... | collective-permute-start | bytes 49208 | tf_op jit(solution)/shard_map/ppermute | solution.py:38
  27.9 0.7 copy.181
  29.1 0.8 pad_maximum_fusion.2
  29.8 1.5 %collective-permute-start.4 = (f32[4100]{0:T(1024)S(1)}, f32[4100]{0:T(1024)S(1)}, u32[]{:S(2)}, u32[]{:S(2)}) collective-permute-start(f32[4100]{0:T(1024)S(1)} %pad_maximum_fusion.2), channel_id=1, source_target_pairs={{0,16},{16,0},{1,17},{17,1},{2,18},{18,2},{3,19},{19,3},{4,20},{20... | collective-permute-start | bytes 49208 | tf_op jit(solution)/shard_map/ppermute | solution.py:38
  32.2 1.5 %collective-permute-done.4 = f32[4100]{0:T(1024)S(1)} collective-permute-done((f32[4100]{0:T(1024)S(1)}, f32[4100]{0:T(1024)S(1)}, u32[]{:S(2)}, u32[]{:S(2)}) %collective-permute-start.4) | collective-permute-done | bytes 16432 | tf_op jit(solution)/shard_map/ppermute | solution.py:38
  33.8 2.7 %convolution_bitcast_fusion.4 = f32[2,2,4,64]{3,2,0,1:T(4,128)S(1)} fusion(f32[1,1,16,2,64,64]{5,4,3,2,1,0:T(8,128)} %param.18, pred[16,64,64]{2,1,0:T(8,128)(4,1)S(1)} %broadcast_and_fusion, f32[16,2,4,64]{3,2,1,0:T(4,128)S(1)} %fusion.18), kind=kOutput, calls=%fused_computation.14 | convolution fusion | flops 12713984 | bytes 626688 | tf_op jit(solution)/shard_map/sakl,spql->apqk/dot_general | solution.py:96
  37.9 0.8 fusion.27
  39.3 1.4 %reshape.1739 = f32[2,4,4,256]{3,2,1,0:T(4,128)} reshape(f32[2,4,2,512]{3,2,1,0:T(2,128)} %copy.78) | data formatting | bytes 65536 | tf_op jit(solution)/shard_map/reshape | solution.py:107
  40.7 1.4 %copy.79 = f32[2,4,4,256]{3,1,2,0:T(4,128)} copy(f32[2,4,4,256]{3,2,1,0:T(4,128)} %reshape.1739) | data formatting | bytes 65536 | tf_op jit(solution)/shard_map/reshape | solution.py:107
  42.1 1.4 %gather_fusion.1 = f32[2,2,4,256]{3,2,1,0:T(4,128)S(1)} fusion(f32[2,4,4,256]{3,1,2,0:T(4,128)} %copy.79, s32[1024]{0:T(1024)} %pad_clamp_fusion), kind=kCustom, calls=%fused_computation.1.clone | custom fusion | bytes 32776 | tf_op jit(solution)/shard_map/jit(_take)/gather | solution.py:108
  43.5 0.7 select_bitcast_fusion.1
  44.9 1.5 %broadcast_divide_fusion = (f32[2,4,1,1536]{3,2,1,0:T(1,128)}, f32[2,4,1536]{2,1,0:T(4,128)S(1)}) fusion(f32[2,4,1,1536]{3,2,1,0:T(1,128)} %copy-done.8, f32[4]{0:T(128)} %copy-done.16), kind=kLoop, calls=%fused_computation.54 | loop fusion | flops 12288 | bytes 147472 | tf_op jit(solution)/shard_map/div | solution.py:158
  46.4 1.3 %divide_convert_fusion = bf16[2,4,6,256]{3,1,2,0:T(4,128)(2,1)} fusion(f32[2,4,6,256]{3,1,2,0:T(4,128)S(1)} %bitcast.382, f32[4]{0:T(128)} %copy-done.16), kind=kLoop, calls=%fused_computation.37 | loop fusion | flops 24576 | bytes 73744 | tf_op jit(solution)/shard_map/convert_element_type | solution.py:76
  47.7 2.0 %gather_fusion = bf16[8,2,4,256]{3,2,1,0:T(4,128)(2,1)} fusion(bf16[2,4,6,256]{3,1,2,0:T(4,128)(2,1)} %divide_convert_fusion, s32[1024]{0:T(1024)} %pad_clamp_fusion.1), kind=kCustom, calls=%fused_computation.clone | custom fusion | bytes 65568 | tf_op jit(solution)/shard_map/jit(_take)/gather | solution.py:77
  49.8 0.9 broadcast_select_fusion.1
  50.7 0.7 fusion.4
  52.2 1.2 %collective-permute-done.7 = f32[528]{0:T(1024)S(1)} collective-permute-done((f32[528]{0:T(1024)S(1)}, f32[528]{0:T(1024)S(1)}, u32[]{:S(2)}, u32[]{:S(2)}) %collective-permute-start.7) | collective-permute-done | bytes 2144 | tf_op jit(solution)/shard_map/ppermute | solution.py:38
  53.7 0.9 collective-permute-start.8
  54.6 2.7 %collective-permute-done.8 = f32[1040]{0:T(1024)S(1)} collective-permute-done((f32[1040]{0:T(1024)S(1)}, f32[1040]{0:T(1024)S(1)}, u32[]{:S(2)}, u32[]{:S(2)}) %collective-permute-start.8) | collective-permute-done | bytes 4192 | tf_op jit(solution)/shard_map/ppermute | solution.py:38
  58.1 1.9 %collective-permute-start.9 = (f32[2064]{0:T(1024)S(1)}, f32[2064]{0:T(1024)S(1)}, u32[]{:S(2)}, u32[]{:S(2)}) collective-permute-start(f32[2064]{0:T(1024)S(1)} %pad_maximum_fusion.6), channel_id=1, source_target_pairs={{0,4},{1,5},{2,6},{3,7},{4,0},{5,1},{6,2},{7,3},{8,12},{9,13},{10,... | collective-permute-start | bytes 24776 | tf_op jit(solution)/shard_map/ppermute | solution.py:38
  60.0 1.8 %collective-permute-done.9 = f32[2064]{0:T(1024)S(1)} collective-permute-done((f32[2064]{0:T(1024)S(1)}, f32[2064]{0:T(1024)S(1)}, u32[]{:S(2)}, u32[]{:S(2)}) %collective-permute-start.9) | collective-permute-done | bytes 8288 | tf_op jit(solution)/shard_map/ppermute | solution.py:38
  62.2 2.9 %collective-permute-start.10 = (f32[4112]{0:T(1024)S(1)}, f32[4112]{0:T(1024)S(1)}, u32[]{:S(2)}, u32[]{:S(2)}) collective-permute-start(f32[4112]{0:T(1024)S(1)} %pad_maximum_fusion.3), channel_id=1, source_target_pairs={{0,8},{1,9},{2,10},{3,11},{4,12},{5,13},{6,14},{7,15},{8,0},{9,1},... | collective-permute-start | bytes 49352 | tf_op jit(solution)/shard_map/ppermute | solution.py:38
  65.1 1.3 %collective-permute-start.13 = (f32[2,4,1,512]{3,1,0,2:T(4,128)S(1)}, f32[2,4,1,512]{3,1,0,2:T(4,128)S(1)}, u32[]{:S(2)}, u32[]{:S(2)}) collective-permute-start(f32[2,4,1,512]{3,1,0,2:T(4,128)S(1)} %get-tuple-element.32), channel_id=1, source_target_pairs={{1,0},{2,1},{3,2},{4,3},{5,4},{6,5},{7,6},{8,7},{9,8},{10,9},{11,1... | collective-permute-start | bytes 49160 | tf_op jit(solution)/shard_map/ppermute | solution.py:55
  66.4 3.0 %collective-permute-start.12 = (f32[2,4,1,512]{3,1,0,2:T(4,128)S(1)}, f32[2,4,1,512]{3,1,0,2:T(4,128)S(1)}, u32[]{:S(2)}, u32[]{:S(2)}) collective-permute-start(f32[2,4,1,512]{3,1,0,2:T(4,128)S(1)} %get-tuple-element.32), channel_id=1, source_target_pairs={{0,1},{1,2},{2,3},{3,4},{4,5},{5,6},{6,7},{7,8},{8,9},{9,10},{10,1... | collective-permute-start | bytes 49160 | tf_op jit(solution)/shard_map/ppermute | solution.py:54
  69.5 1.3 %reshape.1744 = f32[4,4]{1,0:T(4,128)} reshape(f32[16]{0:T(128)} %get-tuple-element.61) | data formatting | bytes 128 | tf_op jit(solution)/shard_map/reshape | solution.py:39
  70.8 0.7 reshape.1746
  72.1 1.5 %collective-permute-start.11 = (f32[4112]{0:T(1024)S(1)}, f32[4112]{0:T(1024)S(1)}, u32[]{:S(2)}, u32[]{:S(2)}) collective-permute-start(f32[4112]{0:T(1024)S(1)} %pad_maximum_fusion.4), channel_id=1, source_target_pairs={{0,16},{16,0},{1,17},{17,1},{2,18},{18,2},{3,19},{19,3},{4,20},{20... | collective-permute-start | bytes 49352 | tf_op jit(solution)/shard_map/ppermute | solution.py:38
  74.3 0.7 reshape.1748
  75.1 0.7 reshape.1751
  76.0 0.7 add_multiply_fusion.1
  77.3 0.7 multiply_subtract_fusion.1
  78.2 2.3 %convolution_bitcast_fusion.2 = f32[2,2,4,64]{3,2,0,1:T(4,128)S(1)} fusion(f32[1,1,16,2,64,64]{5,4,3,2,1,0:T(8,128)S(1)} %copy-done.1, pred[16,64,64]{2,1,0:T(8,128)(4,1)S(1)} %broadcast_and_fusion, f32[16,1,4,64]{3,2,1,0:T(4,128)S(1)} %get-tuple-element.35, f32[16,1,4,64]{3,2,1,0:T(4,128)S(1)} %get-tuple-element.34, f32[8,2,4,64]{3,2,1,0:T(4,128)} %copy-done.7, ...), kind=kOutput, calls=%fused_computation.12 | convolution fusion | flops 12763136 | bytes 659473 | tf_op jit(solution)/shard_map/sakl,spql->apqk/dot_general | solution.py:96
  80.7 0.8 slice.527
  81.5 0.7 fusion.30
  82.3 0.7 gather_fusion.3
  83.0 0.7 select_bitcast_fusion
  83.7 1.0 subtract_reduce_fusion
  85.4 0.7 gather_fusion.2
  86.1 0.7 broadcast_select_fusion
  86.8 0.7 fusion.7
  88.0 1.6 %collective-permute-start.14 = (f32[8,4]{1,0:T(8,128)S(1)}, f32[8,4]{1,0:T(8,128)S(1)}, u32[]{:S(2)}, u32[]{:S(2)}) collective-permute-start(f32[8,4]{1,0:T(8,128)S(1)} %concatenate.157), channel_id=1, source_target_pairs={{0,16},{16,0},{1,17},{17,1},{2,18},{18,2},{3,19},{19,3},{4,20},{20... | collective-permute-start | bytes 392 | tf_op jit(solution)/shard_map/ppermute | solution.py:21
  89.6 2.1 %collective-permute-done.14 = f32[8,4]{1,0:T(8,128)S(1)} collective-permute-done((f32[8,4]{1,0:T(8,128)S(1)}, f32[8,4]{1,0:T(8,128)S(1)}, u32[]{:S(2)}, u32[]{:S(2)}) %collective-permute-start.14) | collective-permute-done | bytes 160 | tf_op jit(solution)/shard_map/ppermute | solution.py:21
  91.7 1.2 %collective-permute-done.15 = f32[8,4]{1,0:T(8,128)S(1)} collective-permute-done((f32[8,4]{1,0:T(8,128)S(1)}, f32[8,4]{1,0:T(8,128)S(1)}, u32[]{:S(2)}, u32[]{:S(2)}) %collective-permute-start.15) | collective-permute-done | bytes 160 | tf_op jit(solution)/shard_map/ppermute | solution.py:21
  92.9 0.9 collective-permute-start.16
  94.5 2.0 %collective-permute-done.16 = f32[8,4]{1,0:T(8,128)S(1)} collective-permute-done((f32[8,4]{1,0:T(8,128)S(1)}, f32[8,4]{1,0:T(8,128)S(1)}, u32[]{:S(2)}, u32[]{:S(2)}) %collective-permute-start.16) | collective-permute-done | bytes 160 | tf_op jit(solution)/shard_map/ppermute | solution.py:21
  96.5 1.7 %collective-permute-start.17 = (f32[8,4]{1,0:T(8,128)S(1)}, f32[8,4]{1,0:T(8,128)S(1)}, u32[]{:S(2)}, u32[]{:S(2)}) collective-permute-start(f32[8,4]{1,0:T(8,128)S(1)} %add.533), channel_id=1, source_target_pairs={{0,4},{1,5},{2,6},{3,7},{4,0},{5,1},{6,2},{7,3},{8,12},{9,13},{10,... | collective-permute-start | bytes 392 | tf_op jit(solution)/shard_map/ppermute | solution.py:21
  98.3 1.8 %collective-permute-done.17 = f32[8,4]{1,0:T(8,128)S(1)} collective-permute-done((f32[8,4]{1,0:T(8,128)S(1)}, f32[8,4]{1,0:T(8,128)S(1)}, u32[]{:S(2)}, u32[]{:S(2)}) %collective-permute-start.17) | collective-permute-done | bytes 160 | tf_op jit(solution)/shard_map/ppermute | solution.py:21
  100.2 4.4 %collective-permute-done.18 = f32[8,4]{1,0:T(8,128)S(1)} collective-permute-done((f32[8,4]{1,0:T(8,128)S(1)}, f32[8,4]{1,0:T(8,128)S(1)}, u32[]{:S(2)}, u32[]{:S(2)}) %collective-permute-start.18) | collective-permute-done | bytes 160 | tf_op jit(solution)/shard_map/ppermute | solution.py:21
  106.1 0.7 stack.153
  (194 shorter events, 15.5 us)
Async XLA Ops:
  0.6 50.0 %copy-start = (bf16[1,2,4,2,256,256]{5,4,3,2,1,0:T(8,128)(2,1)S(1)}, bf16[1,2,4,2,256,256]{5,4,3,2,1,0:T(8,128)(2,1)}, u32[]{:S(2)}) copy-start(bf16[1,2,4,2,256,256]{5,4,3,2,1,0:T(8,128)(2,1)} %param.13) | copy-start | bytes 6291460
  0.6 35.8 %copy-start.3 = (bf16[1,2,64,512]{3,2,1,0:T(8,128)(2,1)S(1)}, bf16[1,2,64,512]{3,2,1,0:T(8,128)(2,1)}, u32[]{:S(2)}) copy-start(bf16[1,2,64,512]{3,2,1,0:T(8,128)(2,1)} %param.17) | copy-start | bytes 393220
  0.7 8.2 %collective-permute-start.5 = (f32[2,4,1,512]{3,2,1,0:T(1,128)}, f32[2,4,1,512]{3,2,1,0:T(1,128)S(1)}, u32[]{:S(2)}, u32[]{:S(2)}) collective-permute-start(f32[2,4,1,512]{3,2,1,0:T(1,128)} %param.12), channel_id=1, source_target_pairs={{0,1},{1,2},{2,3},{3,4},{4,5},{5,6},{6,7},{7,8},{8,9},{9,10},{10,1... | collective-permute-start | bytes 49160 | tf_op jit(solution)/shard_map/ppermute | solution.py:54
  3.2 28.2 %collective-permute-start.6 = (f32[2,4,1,512]{3,2,1,0:T(1,128)}, f32[2,4,1,512]{3,2,1,0:T(1,128)S(1)}, u32[]{:S(2)}, u32[]{:S(2)}) collective-permute-start(f32[2,4,1,512]{3,2,1,0:T(1,128)} %param.12), channel_id=1, source_target_pairs={{1,0},{2,1},{3,2},{4,3},{5,4},{6,5},{7,6},{8,7},{9,8},{10,9},{11,1... | collective-permute-start | bytes 49160 | tf_op jit(solution)/shard_map/ppermute | solution.py:55
  10.9 4.1 %collective-permute-start = (f32[516]{0:T(1024)S(1)}, f32[516]{0:T(1024)S(1)}, u32[]{:S(2)}, u32[]{:S(2)}) collective-permute-start(f32[516]{0:T(1024)S(1)} %pad_maximum_fusion.10), channel_id=1, source_target_pairs={{0,1},{1,0},{2,3},{3,2},{4,5},{5,4},{6,7},{7,6},{8,9},{9,8},{10,11... | collective-permute-start | bytes 6200 | tf_op jit(solution)/shard_map/ppermute | solution.py:38
  15.3 3.7 %collective-permute-start.1 = (f32[1028]{0:T(1024)S(1)}, f32[1028]{0:T(1024)S(1)}, u32[]{:S(2)}, u32[]{:S(2)}) collective-permute-start(f32[1028]{0:T(1024)S(1)} %pad_maximum_fusion.7), channel_id=1, source_target_pairs={{0,2},{1,3},{2,0},{3,1},{4,6},{5,7},{6,4},{7,5},{8,10},{9,11},{10,... | collective-permute-start | bytes 12344 | tf_op jit(solution)/shard_map/ppermute | solution.py:38
  19.3 4.6 %collective-permute-start.2 = (f32[2052]{0:T(1024)S(1)}, f32[2052]{0:T(1024)S(1)}, u32[]{:S(2)}, u32[]{:S(2)}) collective-permute-start(f32[2052]{0:T(1024)S(1)} %pad_maximum_fusion.5), channel_id=1, source_target_pairs={{0,4},{1,5},{2,6},{3,7},{4,0},{5,1},{6,2},{7,3},{8,12},{9,13},{10,... | collective-permute-start | bytes 24632 | tf_op jit(solution)/shard_map/ppermute | solution.py:38
  24.3 4.8 %collective-permute-start.3 = (f32[4100]{0:T(1024)S(1)}, f32[4100]{0:T(1024)S(1)}, u32[]{:S(2)}, u32[]{:S(2)}) collective-permute-start(f32[4100]{0:T(1024)S(1)} %pad_maximum_fusion.1), channel_id=1, source_target_pairs={{0,8},{1,9},{2,10},{3,11},{4,12},{5,13},{6,14},{7,15},{8,0},{9,1},... | collective-permute-start | bytes 49208 | tf_op jit(solution)/shard_map/ppermute | solution.py:38
  29.8 3.8 %collective-permute-start.4 = (f32[4100]{0:T(1024)S(1)}, f32[4100]{0:T(1024)S(1)}, u32[]{:S(2)}, u32[]{:S(2)}) collective-permute-start(f32[4100]{0:T(1024)S(1)} %pad_maximum_fusion.2), channel_id=1, source_target_pairs={{0,16},{16,0},{1,17},{17,1},{2,18},{18,2},{3,19},{19,3},{4,20},{20... | collective-permute-start | bytes 49208 | tf_op jit(solution)/shard_map/ppermute | solution.py:38
  31.4 0.6 copy-start.8
  33.6 4.2 %copy-start.16 = (f32[4]{0:T(128)}, f32[4]{0:T(128)S(1)}, u32[]{:S(2)}) copy-start(f32[4]{0:T(128)S(1)} %add_sqrt_fusion.4) | copy-start | bytes 52
  33.7 17.6 %copy-start.5 = (f32[2,4,1,512]{3,2,1,0:T(1,128)S(1)}, f32[2,4,1,512]{3,2,1,0:T(1,128)}, u32[]{:S(2)}) copy-start(f32[2,4,1,512]{3,2,1,0:T(1,128)} %param.12) | copy-start | bytes 49156
  33.7 17.7 %copy-start.2 = (bf16[1,2,64,512]{3,2,1,0:T(8,128)(2,1)S(1)}, bf16[1,2,64,512]{3,2,1,0:T(8,128)(2,1)}, u32[]{:S(2)}) copy-start(bf16[1,2,64,512]{3,2,1,0:T(8,128)(2,1)} %param.16) | copy-start | bytes 393220
  37.9 40.3 %copy-start.1 = (f32[1,1,16,2,64,64]{5,4,3,2,1,0:T(8,128)S(1)}, f32[1,1,16,2,64,64]{5,4,3,2,1,0:T(8,128)}, u32[]{:S(2)}) copy-start(f32[1,1,16,2,64,64]{5,4,3,2,1,0:T(8,128)} %param.18) | copy-start | bytes 1572868
  49.8 1.6 %copy-start.11 = (f32[2,4,1,512]{3,1,0,2:T(4,128)S(1)}, f32[2,4,1,512]{3,1,0,2:T(4,128)}, u32[]{:S(2)}) copy-start(f32[2,4,1,512]{3,1,0,2:T(4,128)} %reshape.1740) | copy-start | bytes 49156
  49.8 1.6 %copy-start.12 = (f32[1,4,512]{2,1,0:T(4,128)S(1)}, f32[1,4,512]{2,1,0:T(4,128)}, u32[]{:S(2)}) copy-start(f32[1,4,512]{2,1,0:T(4,128)} %fusion.42) | copy-start | bytes 24580
  49.8 1.6 %copy-start.13 = (f32[1,4,512]{2,1,0:T(4,128)S(1)}, f32[1,4,512]{2,1,0:T(4,128)}, u32[]{:S(2)}) copy-start(f32[1,4,512]{2,1,0:T(4,128)} %fusion.44) | copy-start | bytes 24580
  49.8 1.6 %copy-start.17 = (f32[4]{0:T(128)S(1)}, f32[4]{0:T(128)}, u32[]{:S(2)}) copy-start(f32[4]{0:T(128)} %copy-done.16) | copy-start | bytes 52
  51.9 1.5 %copy-start.25 = (f32[4]{0:T(128)}, f32[4]{0:T(128)S(1)}, u32[]{:S(2)}) copy-start(f32[4]{0:T(128)S(1)} %get-tuple-element.23) | copy-start | bytes 52
  51.9 1.5 %copy-start.26 = (f32[4]{0:T(128)}, f32[4]{0:T(128)S(1)}, u32[]{:S(2)}) copy-start(f32[4]{0:T(128)S(1)} %get-tuple-element.28) | copy-start | bytes 52
  52.0 5.4 %copy-start.27 = (f32[4]{0:T(128)}, f32[4]{0:T(128)S(1)}, u32[]{:S(2)}) copy-start(f32[4]{0:T(128)S(1)} %get-tuple-element.29) | copy-start | bytes 52
  52.0 5.4 %copy-start.24 = (f32[4]{0:T(128)}, f32[4]{0:T(128)S(1)}, u32[]{:S(2)}) copy-start(f32[4]{0:T(128)S(1)} %get-tuple-element.22) | copy-start | bytes 52
  52.2 1.2 %collective-permute-start.7 = (f32[528]{0:T(1024)S(1)}, f32[528]{0:T(1024)S(1)}, u32[]{:S(2)}, u32[]{:S(2)}) collective-permute-start(f32[528]{0:T(1024)S(1)} %pad_maximum_fusion.12), channel_id=1, source_target_pairs={{0,1},{1,0},{2,3},{3,2},{4,5},{5,4},{6,7},{7,6},{8,9},{9,8},{10,11... | collective-permute-start | bytes 6344 | tf_op jit(solution)/shard_map/ppermute | solution.py:38
  53.7 3.7 %collective-permute-start.8 = (f32[1040]{0:T(1024)S(1)}, f32[1040]{0:T(1024)S(1)}, u32[]{:S(2)}, u32[]{:S(2)}) collective-permute-start(f32[1040]{0:T(1024)S(1)} %pad_maximum_fusion.8), channel_id=1, source_target_pairs={{0,2},{1,3},{2,0},{3,1},{4,6},{5,7},{6,4},{7,5},{8,10},{9,11},{10,... | collective-permute-start | bytes 12488 | tf_op jit(solution)/shard_map/ppermute | solution.py:38
  58.1 3.7 %collective-permute-start.9 = (f32[2064]{0:T(1024)S(1)}, f32[2064]{0:T(1024)S(1)}, u32[]{:S(2)}, u32[]{:S(2)}) collective-permute-start(f32[2064]{0:T(1024)S(1)} %pad_maximum_fusion.6), channel_id=1, source_target_pairs={{0,4},{1,5},{2,6},{3,7},{4,0},{5,1},{6,2},{7,3},{8,12},{9,13},{10,... | collective-permute-start | bytes 24776 | tf_op jit(solution)/shard_map/ppermute | solution.py:38
  62.0 16.1 %copy-start.7 = (f32[8,2,4,64]{3,2,1,0:T(4,128)}, f32[8,2,4,64]{3,2,1,0:T(4,128)S(1)}, u32[]{:S(2)}) copy-start(f32[8,2,4,64]{3,2,1,0:T(4,128)S(1)} %maximum_select_fusion.4) | copy-start | bytes 49156
  62.2 9.3 %collective-permute-start.10 = (f32[4112]{0:T(1024)S(1)}, f32[4112]{0:T(1024)S(1)}, u32[]{:S(2)}, u32[]{:S(2)}) collective-permute-start(f32[4112]{0:T(1024)S(1)} %pad_maximum_fusion.3), channel_id=1, source_target_pairs={{0,8},{1,9},{2,10},{3,11},{4,12},{5,13},{6,14},{7,15},{8,0},{9,1},... | collective-permute-start | bytes 49352 | tf_op jit(solution)/shard_map/ppermute | solution.py:38
  65.1 8.5 %collective-permute-start.13 = (f32[2,4,1,512]{3,1,0,2:T(4,128)S(1)}, f32[2,4,1,512]{3,1,0,2:T(4,128)S(1)}, u32[]{:S(2)}, u32[]{:S(2)}) collective-permute-start(f32[2,4,1,512]{3,1,0,2:T(4,128)S(1)} %get-tuple-element.32), channel_id=1, source_target_pairs={{1,0},{2,1},{3,2},{4,3},{5,4},{6,5},{7,6},{8,7},{9,8},{10,9},{11,1... | collective-permute-start | bytes 49160 | tf_op jit(solution)/shard_map/ppermute | solution.py:55
  66.4 7.2 %collective-permute-start.12 = (f32[2,4,1,512]{3,1,0,2:T(4,128)S(1)}, f32[2,4,1,512]{3,1,0,2:T(4,128)S(1)}, u32[]{:S(2)}, u32[]{:S(2)}) collective-permute-start(f32[2,4,1,512]{3,1,0,2:T(4,128)S(1)} %get-tuple-element.32), channel_id=1, source_target_pairs={{0,1},{1,2},{2,3},{3,4},{4,5},{5,6},{6,7},{7,8},{8,9},{9,10},{10,1... | collective-permute-start | bytes 49160 | tf_op jit(solution)/shard_map/ppermute | solution.py:54
  72.1 3.8 %collective-permute-start.11 = (f32[4112]{0:T(1024)S(1)}, f32[4112]{0:T(1024)S(1)}, u32[]{:S(2)}, u32[]{:S(2)}) collective-permute-start(f32[4112]{0:T(1024)S(1)} %pad_maximum_fusion.4), channel_id=1, source_target_pairs={{0,16},{16,0},{1,17},{17,1},{2,18},{18,2},{3,19},{19,3},{4,20},{20... | collective-permute-start | bytes 49352 | tf_op jit(solution)/shard_map/ppermute | solution.py:38
  75.9 2.2 %copy-start.19 = (f32[4112]{0:T(1024)}, f32[4112]{0:T(1024)S(1)}, u32[]{:S(2)}) copy-start(f32[4112]{0:T(1024)S(1)} %collective-permute-done.11) | copy-start | bytes 49348
  76.7 1.4 %copy-start.14 = (f32[4,4]{1,0:T(4,128)}, f32[4,4]{1,0:T(4,128)S(1)}, u32[]{:S(2)}) copy-start(f32[4,4]{1,0:T(4,128)S(1)} %add_multiply_fusion.1) | copy-start | bytes 196
  77.3 3.3 %copy-start.20 = (f32[4]{0:T(128)}, f32[4]{0:T(128)S(1)}, u32[]{:S(2)}) copy-start(f32[4]{0:T(128)S(1)} %get-tuple-element.83) | copy-start | bytes 52
  77.3 3.3 %copy-start.21 = (f32[4]{0:T(128)}, f32[4]{0:T(128)S(1)}, u32[]{:S(2)}) copy-start(f32[4]{0:T(128)S(1)} %get-tuple-element.84) | copy-start | bytes 52
  77.3 3.3 %copy-start.22 = (f32[4]{0:T(128)}, f32[4]{0:T(128)S(1)}, u32[]{:S(2)}) copy-start(f32[4]{0:T(128)S(1)} %add_sqrt_fusion.3) | copy-start | bytes 52
  78.0 3.5 %copy-start.9 = (f32[1,4,2,512]{3,1,0,2:T(4,128)S(1)}, f32[1,4,2,512]{3,1,0,2:T(4,128)}, u32[]{:S(2)}) copy-start(f32[1,4,2,512]{3,1,0,2:T(4,128)} %get-tuple-element.38) | copy-start | bytes 49156
  78.0 3.5 %copy-start.10 = (f32[1,4,2,512]{3,1,0,2:T(4,128)S(1)}, f32[1,4,2,512]{3,1,0,2:T(4,128)}, u32[]{:S(2)}) copy-start(f32[1,4,2,512]{3,1,0,2:T(4,128)} %get-tuple-element.39) | copy-start | bytes 49156
  78.1 6.6 %copy-start.6 = (f32[2,4,1,1536]{3,1,0,2:T(4,128)S(1)}, f32[2,4,1,1536]{3,1,0,2:T(4,128)}, u32[]{:S(2)}) copy-start(f32[2,4,1,1536]{3,1,0,2:T(4,128)} %pad_maximum_fusion) | copy-start | bytes 147460
  78.2 9.3 %copy-start.4 = (bf16[1,2,64,512]{3,2,1,0:T(8,128)(2,1)S(1)}, bf16[1,2,64,512]{3,2,1,0:T(8,128)(2,1)}, u32[]{:S(2)}) copy-start(bf16[1,2,64,512]{3,2,1,0:T(8,128)(2,1)} %param.17) | copy-start | bytes 393220
  80.5 13.2 %copy-start.18 = (f32[4]{0:T(128)S(1)}, f32[4]{0:T(128)}, u32[]{:S(2)}) copy-start(f32[4]{0:T(128)} %copy-done.16) | copy-start | bytes 52
  80.5 17.7 %copy-start.29 = (f32[4,1]{0,1:T(1,128)S(1)}, f32[4,1]{0,1:T(1,128)}, u32[]{:S(2)}) copy-start(f32[4,1]{0,1:T(1,128)} %get-tuple-element.82) | copy-start | bytes 52
  80.5 19.6 %copy-start.28 = (f32[4,1]{0,1:T(1,128)S(1)}, f32[4,1]{0,1:T(1,128)}, u32[]{:S(2)}) copy-start(f32[4,1]{0,1:T(1,128)} %get-tuple-element.81) | copy-start | bytes 52
  80.5 24.1 %copy-start.15 = (f32[4,4]{1,0:T(4,128)S(1)}, f32[4,4]{1,0:T(4,128)}, u32[]{:S(2)}) copy-start(f32[4,4]{1,0:T(4,128)} %copy-done.14) | copy-start | bytes 196
  81.5 6.2 %copy-start.23 = (f32[4]{0:T(128)S(1)}, f32[4]{0:T(128)}, u32[]{:S(2)}) copy-start(f32[4]{0:T(128)} %copy-done.22) | copy-start | bytes 52
  88.0 3.7 %collective-permute-start.14 = (f32[8,4]{1,0:T(8,128)S(1)}, f32[8,4]{1,0:T(8,128)S(1)}, u32[]{:S(2)}, u32[]{:S(2)}) collective-permute-start(f32[8,4]{1,0:T(8,128)S(1)} %concatenate.157), channel_id=1, source_target_pairs={{0,16},{16,0},{1,17},{17,1},{2,18},{18,2},{3,19},{19,3},{4,20},{20... | collective-permute-start | bytes 392 | tf_op jit(solution)/shard_map/ppermute | solution.py:21
  91.7 1.2 %collective-permute-start.15 = (f32[8,4]{1,0:T(8,128)S(1)}, f32[8,4]{1,0:T(8,128)S(1)}, u32[]{:S(2)}, u32[]{:S(2)}) collective-permute-start(f32[8,4]{1,0:T(8,128)S(1)} %add.531), channel_id=1, source_target_pairs={{0,1},{1,0},{2,3},{3,2},{4,5},{5,4},{6,7},{7,6},{8,9},{9,8},{10,11... | collective-permute-start | bytes 392 | tf_op jit(solution)/shard_map/ppermute | solution.py:21
  92.9 3.6 %collective-permute-start.16 = (f32[8,4]{1,0:T(8,128)S(1)}, f32[8,4]{1,0:T(8,128)S(1)}, u32[]{:S(2)}, u32[]{:S(2)}) collective-permute-start(f32[8,4]{1,0:T(8,128)S(1)} %add.532), channel_id=1, source_target_pairs={{0,2},{1,3},{2,0},{3,1},{4,6},{5,7},{6,4},{7,5},{8,10},{9,11},{10,... | collective-permute-start | bytes 392 | tf_op jit(solution)/shard_map/ppermute | solution.py:21
  96.5 3.6 %collective-permute-start.17 = (f32[8,4]{1,0:T(8,128)S(1)}, f32[8,4]{1,0:T(8,128)S(1)}, u32[]{:S(2)}, u32[]{:S(2)}) collective-permute-start(f32[8,4]{1,0:T(8,128)S(1)} %add.533), channel_id=1, source_target_pairs={{0,4},{1,5},{2,6},{3,7},{4,0},{5,1},{6,2},{7,3},{8,12},{9,13},{10,... | collective-permute-start | bytes 392 | tf_op jit(solution)/shard_map/ppermute | solution.py:21
  100.1 4.5 %collective-permute-start.18 = (f32[8,4]{1,0:T(8,128)S(1)}, f32[8,4]{1,0:T(8,128)S(1)}, u32[]{:S(2)}, u32[]{:S(2)}) collective-permute-start(f32[8,4]{1,0:T(8,128)S(1)} %add.534), channel_id=1, source_target_pairs={{0,8},{1,9},{2,10},{3,11},{4,12},{5,13},{6,14},{7,15},{8,0},{9,1},... | collective-permute-start | bytes 392 | tf_op jit(solution)/shard_map/ppermute | solution.py:21

commit v7 on v3

--- a/solution.py
+++ b/solution.py
@@ -95,7 +95,7 @@
 def far_field(gathered, weights, target_basis):
     nrhs = gathered.shape[2]
     rows = target_basis.shape[3]
-    inner = jnp.einsum("sakl,spql->apqk", weights, gathered, precision=lax.Precision.HIGHEST)
+    inner = jnp.einsum("sakl,spql->apqk", weights, gathered, precision=lax.Precision.HIGH)
     rounded_coef = complex_mix(inner).astype(jnp.bfloat16)
     outward = jnp.einsum(
         "akr,pqk->apqr", target_basis[0], rounded_coef, preferred_element_type=jnp.float32

time: 85.9 us -> 84.6 us (0.985)
  matrix products: 8.06 us -> 6.78 us
    dot_general x2, matrix products: 5.26 us -> 3.98 us  [far_field(): jnp.einsum('sakl,spql->apqk', weights, gathered, precision=lax.Precision....]
where the time goes in v7:
time: 84.6 us; the launch traced here: 83.9 us
  starting transfers between devices  32.3 us (38%)
  waiting for transfers between devices  26.4 us (31%)
  local copies, waits for them, and re-layouts  9.41 us (11%)
  other arithmetic  7.89 us (9%)
  matrix products  6.78 us (8%)
  between operations  1.07 us (1%)
    ppermute x10, starting transfers between devices, tree_collect(): got = lax.ppermute(packed, axis, [(i, i ^ k) for i in range(n)])  20 us
    ppermute x10, waiting for transfers between devices, tree_collect(): got = lax.ppermute(packed, axis, [(i, i ^ k) for i in range(n)])  15 us
    ppermute x5, waiting for transfers between devices, tree_sum(): x = x + lax.ppermute(x, axis, [(i, i ^ k) for i in range(n)])  11.5 us
    ppermute x2, starting transfers between devices, neighbours(): left = lax.ppermute(field, 'blk', [(i, i + 1) for i in range(ends)])  5.52 us
    ppermute x5, starting transfers between devices, tree_sum(): x = x + lax.ppermute(x, axis, [(i, i ^ k) for i in range(n)])  4.18 us
    dot_general x2, matrix products, far_field(): jnp.einsum('sakl,spql->apqk', weights, gathered, precision=lax.Precision....  3.98 us
    ppermute x2, starting transfers between devices, neighbours(): right = lax.ppermute(field, 'blk', [(i + 1, i) for i in range(ends)])  2.57 us
    unnamed x13, local copies, waits for them, and re-layouts  2.01 us
  transfers between devices with their start and end apart: 19, of which 14 were waited for; matrix products, arithmetic and copies ran while one was open for 12% of the time, Pallas kernels for 0%

profile of v7, /device:TPU:0, one launch (start us, length us, event | category | flops | bytes accessed | tf_op | source)
XLA Modules:
  0.0 83.9 jit_solution(15176557533798138029)
XLA Ops:
  0.7 2.5 %collective-permute-start.5 = (f32[2,4,1,512]{3,2,1,0:T(1,128)}, f32[2,4,1,512]{3,2,1,0:T(1,128)S(1)}, u32[]{:S(2)}, u32[]{:S(2)}) collective-permute-start(f32[2,4,1,512]{3,2,1,0:T(1,128)} %param.12), channel_id=1, source_target_pairs={{0,1},{1,2},{2,3},{3,4},{4,5},{5,6},{6,7},{7,8},{8,9},{9,10},{10,1... | collective-permute-start | bytes 49160 | tf_op jit(solution)/shard_map/ppermute | solution.py:54
  3.2 1.3 %collective-permute-start.6 = (f32[2,4,1,512]{3,2,1,0:T(1,128)}, f32[2,4,1,512]{3,2,1,0:T(1,128)S(1)}, u32[]{:S(2)}, u32[]{:S(2)}) collective-permute-start(f32[2,4,1,512]{3,2,1,0:T(1,128)} %param.12), channel_id=1, source_target_pairs={{1,0},{2,1},{3,2},{4,3},{5,4},{6,5},{7,6},{8,7},{9,8},{10,9},{11,1... | collective-permute-start | bytes 49160 | tf_op jit(solution)/shard_map/ppermute | solution.py:55
  4.5 0.7 compare_select_fusion
  5.1 0.7 compare_and_fusion
  5.8 0.7 iota_compare_fusion
  6.5 0.2 and_convert_fusion
  6.7 0.8 add_reduce_fusion.9
  7.5 0.8 reshape_squeeze.4
  8.3 0.8 constant_dynamic-update-slice_fusion.1
  9.1 1.1 %convolution_bitcast_fusion.5 = f32[2,2,4,64]{3,2,0,1:T(4,128)S(1)} fusion(bf16[1,2,64,512]{3,2,1,0:T(8,128)(2,1)} %param.16, bf16[2,4,1,512]{3,2,1,0:T(2,128)(2,1)S(1)} %get-tuple-element.58), kind=kOutput, calls=%fused_computation.15 | convolution fusion | flops 1048576 | bytes 143360 | tf_op jit(solution)/shard_map/akr,pqr->apqk/dot_general | solution.py:65
  10.4 3.2 %collective-permute-start = (f32[516]{0:T(1024)S(1)}, f32[516]{0:T(1024)S(1)}, u32[]{:S(2)}, u32[]{:S(2)}) collective-permute-start(f32[516]{0:T(1024)S(1)} %pad_maximum_fusion.10), channel_id=1, source_target_pairs={{0,1},{1,0},{2,3},{3,2},{4,5},{5,4},{6,7},{7,6},{8,9},{9,8},{10,11... | collective-permute-start | bytes 6200 | tf_op jit(solution)/shard_map/ppermute | solution.py:38
  13.6 0.8 collective-permute-done
  14.8 2.0 %collective-permute-start.1 = (f32[1028]{0:T(1024)S(1)}, f32[1028]{0:T(1024)S(1)}, u32[]{:S(2)}, u32[]{:S(2)}) collective-permute-start(f32[1028]{0:T(1024)S(1)} %pad_maximum_fusion.7), channel_id=1, source_target_pairs={{0,2},{1,3},{2,0},{3,1},{4,6},{5,7},{6,4},{7,5},{8,10},{9,11},{10,... | collective-permute-start | bytes 12344 | tf_op jit(solution)/shard_map/ppermute | solution.py:38
  16.7 1.7 %collective-permute-done.1 = f32[1028]{0:T(1024)S(1)} collective-permute-done((f32[1028]{0:T(1024)S(1)}, f32[1028]{0:T(1024)S(1)}, u32[]{:S(2)}, u32[]{:S(2)}) %collective-permute-start.1) | collective-permute-done | bytes 4144 | tf_op jit(solution)/shard_map/ppermute | solution.py:38
  18.7 2.9 %collective-permute-start.2 = (f32[2052]{0:T(1024)S(1)}, f32[2052]{0:T(1024)S(1)}, u32[]{:S(2)}, u32[]{:S(2)}) collective-permute-start(f32[2052]{0:T(1024)S(1)} %pad_maximum_fusion.5), channel_id=1, source_target_pairs={{0,4},{1,5},{2,6},{3,7},{4,0},{5,1},{6,2},{7,3},{8,12},{9,13},{10,... | collective-permute-start | bytes 24632 | tf_op jit(solution)/shard_map/ppermute | solution.py:38
  21.7 1.7 %collective-permute-done.2 = f32[2052]{0:T(1024)S(1)} collective-permute-done((f32[2052]{0:T(1024)S(1)}, f32[2052]{0:T(1024)S(1)}, u32[]{:S(2)}, u32[]{:S(2)}) %collective-permute-start.2) | collective-permute-done | bytes 8240 | tf_op jit(solution)/shard_map/ppermute | solution.py:38
  23.7 3.0 %collective-permute-start.3 = (f32[4100]{0:T(1024)S(1)}, f32[4100]{0:T(1024)S(1)}, u32[]{:S(2)}, u32[]{:S(2)}) collective-permute-start(f32[4100]{0:T(1024)S(1)} %pad_maximum_fusion.1), channel_id=1, source_target_pairs={{0,8},{1,9},{2,10},{3,11},{4,12},{5,13},{6,14},{7,15},{8,0},{9,1},... | collective-permute-start | bytes 49208 | tf_op jit(solution)/shard_map/ppermute | solution.py:38
  26.7 0.7 copy.181
  27.5 1.0 %collective-permute-done.3 = f32[4100]{0:T(1024)S(1)} collective-permute-done((f32[4100]{0:T(1024)S(1)}, f32[4100]{0:T(1024)S(1)}, u32[]{:S(2)}, u32[]{:S(2)}) %collective-permute-start.3) | collective-permute-done | bytes 16432 | tf_op jit(solution)/shard_map/ppermute | solution.py:38
  28.5 0.8 pad_maximum_fusion.2
  29.3 1.5 %collective-permute-start.4 = (f32[4100]{0:T(1024)S(1)}, f32[4100]{0:T(1024)S(1)}, u32[]{:S(2)}, u32[]{:S(2)}) collective-permute-start(f32[4100]{0:T(1024)S(1)} %pad_maximum_fusion.2), channel_id=1, source_target_pairs={{0,16},{16,0},{1,17},{17,1},{2,18},{18,2},{3,19},{19,3},{4,20},{20... | collective-permute-start | bytes 49208 | tf_op jit(solution)/shard_map/ppermute | solution.py:38
  31.0 2.1 %collective-permute-done.4 = f32[4100]{0:T(1024)S(1)} collective-permute-done((f32[4100]{0:T(1024)S(1)}, f32[4100]{0:T(1024)S(1)}, u32[]{:S(2)}, u32[]{:S(2)}) %collective-permute-start.4) | collective-permute-done | bytes 16432 | tf_op jit(solution)/shard_map/ppermute | solution.py:38
  33.2 2.0 %convolution_bitcast_fusion.4 = f32[2,2,4,64]{3,2,0,1:T(4,128)S(1)} fusion(f32[1,1,16,2,64,64]{5,4,3,2,1,0:T(8,128)} %param.18, f32[16,64,64]{2,1,0:T(8,128)S(1)} %and_convert_fusion, f32[16,2,4,64]{3,2,1,0:T(4,128)S(1)} %fusion.18), kind=kOutput, calls=%fused_computation.14 | convolution fusion | flops 6422528 | bytes 823296 | tf_op jit(solution)/shard_map/sakl,spql->apqk/dot_general | solution.py:98
  35.2 0.1 convolution_bitcast_fusion.1
  35.6 0.6 gather_fusion.1
  36.3 0.2 broadcast_divide_fusion
  36.6 0.6 gather_fusion
  37.3 0.7 fusion.4
  38.1 0.1 convolution_bitcast_fusion.3
  38.3 0.2 add_reduce_fusion.8
  38.7 1.2 %collective-permute-done.7 = f32[528]{0:T(1024)S(1)} collective-permute-done((f32[528]{0:T(1024)S(1)}, f32[528]{0:T(1024)S(1)}, u32[]{:S(2)}, u32[]{:S(2)}) %collective-permute-start.7) | collective-permute-done | bytes 2144 | tf_op jit(solution)/shard_map/ppermute | solution.py:38
  40.2 0.9 %collective-permute-start.8 = (f32[1040]{0:T(1024)S(1)}, f32[1040]{0:T(1024)S(1)}, u32[]{:S(2)}, u32[]{:S(2)}) collective-permute-start(f32[1040]{0:T(1024)S(1)} %pad_maximum_fusion.8), channel_id=1, source_target_pairs={{0,2},{1,3},{2,0},{3,1},{4,6},{5,7},{6,4},{7,5},{8,10},{9,11},{10,... | collective-permute-start | bytes 12488 | tf_op jit(solution)/shard_map/ppermute | solution.py:38
  41.1 2.7 %collective-permute-done.8 = f32[1040]{0:T(1024)S(1)} collective-permute-done((f32[1040]{0:T(1024)S(1)}, f32[1040]{0:T(1024)S(1)}, u32[]{:S(2)}, u32[]{:S(2)}) %collective-permute-start.8) | collective-permute-done | bytes 4192 | tf_op jit(solution)/shard_map/ppermute | solution.py:38
  44.2 1.9 %collective-permute-start.9 = (f32[2064]{0:T(1024)S(1)}, f32[2064]{0:T(1024)S(1)}, u32[]{:S(2)}, u32[]{:S(2)}) collective-permute-start(f32[2064]{0:T(1024)S(1)} %pad_maximum_fusion.6), channel_id=1, source_target_pairs={{0,4},{1,5},{2,6},{3,7},{4,0},{5,1},{6,2},{7,3},{8,12},{9,13},{10,... | collective-permute-start | bytes 24776 | tf_op jit(solution)/shard_map/ppermute | solution.py:38
  46.1 1.8 %collective-permute-done.9 = f32[2064]{0:T(1024)S(1)} collective-permute-done((f32[2064]{0:T(1024)S(1)}, f32[2064]{0:T(1024)S(1)}, u32[]{:S(2)}, u32[]{:S(2)}) %collective-permute-start.9) | collective-permute-done | bytes 8288 | tf_op jit(solution)/shard_map/ppermute | solution.py:38
  48.2 2.9 %collective-permute-start.10 = (f32[4112]{0:T(1024)S(1)}, f32[4112]{0:T(1024)S(1)}, u32[]{:S(2)}, u32[]{:S(2)}) collective-permute-start(f32[4112]{0:T(1024)S(1)} %pad_maximum_fusion.3), channel_id=1, source_target_pairs={{0,8},{1,9},{2,10},{3,11},{4,12},{5,13},{6,14},{7,15},{8,0},{9,1},... | collective-permute-start | bytes 49352 | tf_op jit(solution)/shard_map/ppermute | solution.py:38
  51.1 1.3 %collective-permute-start.13 = (f32[2,4,1,512]{3,1,0,2:T(4,128)S(1)}, f32[2,4,1,512]{3,1,0,2:T(4,128)S(1)}, u32[]{:S(2)}, u32[]{:S(2)}) collective-permute-start(f32[2,4,1,512]{3,1,0,2:T(4,128)S(1)} %get-tuple-element.32), channel_id=1, source_target_pairs={{1,0},{2,1},{3,2},{4,3},{5,4},{6,5},{7,6},{8,7},{9,8},{10,9},{11,1... | collective-permute-start | bytes 49160 | tf_op jit(solution)/shard_map/ppermute | solution.py:55
  52.4 3.0 %collective-permute-start.12 = (f32[2,4,1,512]{3,1,0,2:T(4,128)S(1)}, f32[2,4,1,512]{3,1,0,2:T(4,128)S(1)}, u32[]{:S(2)}, u32[]{:S(2)}) collective-permute-start(f32[2,4,1,512]{3,1,0,2:T(4,128)S(1)} %get-tuple-element.32), channel_id=1, source_target_pairs={{0,1},{1,2},{2,3},{3,4},{4,5},{5,6},{6,7},{7,8},{8,9},{9,10},{10,1... | collective-permute-start | bytes 49160 | tf_op jit(solution)/shard_map/ppermute | solution.py:54
  55.8 1.5 %collective-permute-start.11 = (f32[4112]{0:T(1024)S(1)}, f32[4112]{0:T(1024)S(1)}, u32[]{:S(2)}, u32[]{:S(2)}) collective-permute-start(f32[4112]{0:T(1024)S(1)} %pad_maximum_fusion.4), channel_id=1, source_target_pairs={{0,16},{16,0},{1,17},{17,1},{2,18},{18,2},{3,19},{19,3},{4,20},{20... | collective-permute-start | bytes 49352 | tf_op jit(solution)/shard_map/ppermute | solution.py:38
  57.6 2.0 %collective-permute-done.11 = f32[4112]{0:T(1024)S(1)} collective-permute-done((f32[4112]{0:T(1024)S(1)}, f32[4112]{0:T(1024)S(1)}, u32[]{:S(2)}, u32[]{:S(2)}) %collective-permute-start.11) | collective-permute-done | bytes 16480 | tf_op jit(solution)/shard_map/ppermute | solution.py:38
  59.9 2.0 %convolution_bitcast_fusion.2 = f32[2,2,4,64]{3,2,0,1:T(4,128)S(1)} fusion(f32[1,1,16,2,64,64]{5,4,3,2,1,0:T(8,128)} %param.18, f32[16,64,64]{2,1,0:T(8,128)S(1)} %and_convert_fusion, f32[16,1,4,64]{3,2,1,0:T(4,128)S(1)} %get-tuple-element.35, f32[16,1,4,64]{3,2,1,0:T(4,128)S(1)} %get-tuple-element.34, f32[8,2,4,64]{3,2,1,0:T(4,128)S(1)} %maximum_select_fusion.4, ...), kind=kOutput, calls=%fused_computation.12 | convolution fusion | flops 6471680 | bytes 856081 | tf_op jit(solution)/shard_map/sakl,spql->apqk/dot_general | solution.py:98
  62.3 0.6 gather_fusion.3
  62.9 0.2 subtract_reduce_fusion
  63.3 0.6 gather_fusion.2
  63.9 0.7 fusion.7
  64.6 0.1 convolution_bitcast_fusion
  64.9 0.2 subtract_reduce_fusion.1
  65.1 1.6 %collective-permute-start.14 = (f32[8,4]{1,0:T(8,128)S(1)}, f32[8,4]{1,0:T(8,128)S(1)}, u32[]{:S(2)}, u32[]{:S(2)}) collective-permute-start(f32[8,4]{1,0:T(8,128)S(1)} %concatenate.157), channel_id=1, source_target_pairs={{0,16},{16,0},{1,17},{17,1},{2,18},{18,2},{3,19},{19,3},{4,20},{20... | collective-permute-start | bytes 392 | tf_op jit(solution)/shard_map/ppermute | solution.py:21
  66.7 2.1 %collective-permute-done.14 = f32[8,4]{1,0:T(8,128)S(1)} collective-permute-done((f32[8,4]{1,0:T(8,128)S(1)}, f32[8,4]{1,0:T(8,128)S(1)}, u32[]{:S(2)}, u32[]{:S(2)}) %collective-permute-start.14) | collective-permute-done | bytes 160 | tf_op jit(solution)/shard_map/ppermute | solution.py:21
  68.8 1.2 %collective-permute-done.15 = f32[8,4]{1,0:T(8,128)S(1)} collective-permute-done((f32[8,4]{1,0:T(8,128)S(1)}, f32[8,4]{1,0:T(8,128)S(1)}, u32[]{:S(2)}, u32[]{:S(2)}) %collective-permute-start.15) | collective-permute-done | bytes 160 | tf_op jit(solution)/shard_map/ppermute | solution.py:21
  70.0 0.6 collective-permute-start.16
  70.6 0.1 copy.96
  70.7 0.6 copy.105
  71.3 2.3 %collective-permute-done.16 = f32[8,4]{1,0:T(8,128)S(1)} collective-permute-done((f32[8,4]{1,0:T(8,128)S(1)}, f32[8,4]{1,0:T(8,128)S(1)}, u32[]{:S(2)}, u32[]{:S(2)}) %collective-permute-start.16) | collective-permute-done | bytes 160 | tf_op jit(solution)/shard_map/ppermute | solution.py:21
  73.6 1.7 %collective-permute-start.17 = (f32[8,4]{1,0:T(8,128)S(1)}, f32[8,4]{1,0:T(8,128)S(1)}, u32[]{:S(2)}, u32[]{:S(2)}) collective-permute-start(f32[8,4]{1,0:T(8,128)S(1)} %add.533), channel_id=1, source_target_pairs={{0,4},{1,5},{2,6},{3,7},{4,0},{5,1},{6,2},{7,3},{8,12},{9,13},{10,... | collective-permute-start | bytes 392 | tf_op jit(solution)/shard_map/ppermute | solution.py:21
  75.3 0.1 copy.97
  75.4 1.8 %collective-permute-done.17 = f32[8,4]{1,0:T(8,128)S(1)} collective-permute-done((f32[8,4]{1,0:T(8,128)S(1)}, f32[8,4]{1,0:T(8,128)S(1)}, u32[]{:S(2)}, u32[]{:S(2)}) %collective-permute-start.17) | collective-permute-done | bytes 160 | tf_op jit(solution)/shard_map/ppermute | solution.py:21
  77.2 0.3 collective-permute-start.18
  77.5 0.1 copy.98
  77.6 4.1 %collective-permute-done.18 = f32[8,4]{1,0:T(8,128)S(1)} collective-permute-done((f32[8,4]{1,0:T(8,128)S(1)}, f32[8,4]{1,0:T(8,128)S(1)}, u32[]{:S(2)}, u32[]{:S(2)}) %collective-permute-start.18) | collective-permute-done | bytes 160 | tf_op jit(solution)/shard_map/ppermute | solution.py:21
  82.0 0.6 copy.106
  82.7 0.1 copy.100
  82.9 0.1 copy.102
  83.2 0.7 stack.153
  (142 shorter events, 5.7 us)
Async XLA Ops:
  0.6 36.6 %copy-start = (bf16[1,2,4,2,256,256]{5,4,3,2,1,0:T(8,128)(2,1)S(1)}, bf16[1,2,4,2,256,256]{5,4,3,2,1,0:T(8,128)(2,1)}, u32[]{:S(2)}) copy-start(bf16[1,2,4,2,256,256]{5,4,3,2,1,0:T(8,128)(2,1)} %param.13) | copy-start | bytes 6291460
  0.6 34.6 %copy-start.2 = (bf16[1,2,64,512]{3,2,1,0:T(8,128)(2,1)S(1)}, bf16[1,2,64,512]{3,2,1,0:T(8,128)(2,1)}, u32[]{:S(2)}) copy-start(bf16[1,2,64,512]{3,2,1,0:T(8,128)(2,1)} %param.17) | copy-start | bytes 393220
  0.7 7.7 %collective-permute-start.5 = (f32[2,4,1,512]{3,2,1,0:T(1,128)}, f32[2,4,1,512]{3,2,1,0:T(1,128)S(1)}, u32[]{:S(2)}, u32[]{:S(2)}) collective-permute-start(f32[2,4,1,512]{3,2,1,0:T(1,128)} %param.12), channel_id=1, source_target_pairs={{0,1},{1,2},{2,3},{3,4},{4,5},{5,6},{6,7},{7,8},{8,9},{9,10},{10,1... | collective-permute-start | bytes 49160 | tf_op jit(solution)/shard_map/ppermute | solution.py:54
  3.2 27.7 %collective-permute-start.6 = (f32[2,4,1,512]{3,2,1,0:T(1,128)}, f32[2,4,1,512]{3,2,1,0:T(1,128)S(1)}, u32[]{:S(2)}, u32[]{:S(2)}) collective-permute-start(f32[2,4,1,512]{3,2,1,0:T(1,128)} %param.12), channel_id=1, source_target_pairs={{1,0},{2,1},{3,2},{4,3},{5,4},{6,5},{7,6},{8,7},{9,8},{10,9},{11,1... | collective-permute-start | bytes 49160 | tf_op jit(solution)/shard_map/ppermute | solution.py:55
  10.4 4.1 %collective-permute-start = (f32[516]{0:T(1024)S(1)}, f32[516]{0:T(1024)S(1)}, u32[]{:S(2)}, u32[]{:S(2)}) collective-permute-start(f32[516]{0:T(1024)S(1)} %pad_maximum_fusion.10), channel_id=1, source_target_pairs={{0,1},{1,0},{2,3},{3,2},{4,5},{5,4},{6,7},{7,6},{8,9},{9,8},{10,11... | collective-permute-start | bytes 6200 | tf_op jit(solution)/shard_map/ppermute | solution.py:38
  14.8 3.7 %collective-permute-start.1 = (f32[1028]{0:T(1024)S(1)}, f32[1028]{0:T(1024)S(1)}, u32[]{:S(2)}, u32[]{:S(2)}) collective-permute-start(f32[1028]{0:T(1024)S(1)} %pad_maximum_fusion.7), channel_id=1, source_target_pairs={{0,2},{1,3},{2,0},{3,1},{4,6},{5,7},{6,4},{7,5},{8,10},{9,11},{10,... | collective-permute-start | bytes 12344 | tf_op jit(solution)/shard_map/ppermute | solution.py:38
  18.7 4.6 %collective-permute-start.2 = (f32[2052]{0:T(1024)S(1)}, f32[2052]{0:T(1024)S(1)}, u32[]{:S(2)}, u32[]{:S(2)}) collective-permute-start(f32[2052]{0:T(1024)S(1)} %pad_maximum_fusion.5), channel_id=1, source_target_pairs={{0,4},{1,5},{2,6},{3,7},{4,0},{5,1},{6,2},{7,3},{8,12},{9,13},{10,... | collective-permute-start | bytes 24632 | tf_op jit(solution)/shard_map/ppermute | solution.py:38
  23.7 4.8 %collective-permute-start.3 = (f32[4100]{0:T(1024)S(1)}, f32[4100]{0:T(1024)S(1)}, u32[]{:S(2)}, u32[]{:S(2)}) collective-permute-start(f32[4100]{0:T(1024)S(1)} %pad_maximum_fusion.1), channel_id=1, source_target_pairs={{0,8},{1,9},{2,10},{3,11},{4,12},{5,13},{6,14},{7,15},{8,0},{9,1},... | collective-permute-start | bytes 49208 | tf_op jit(solution)/shard_map/ppermute | solution.py:38
  29.3 3.8 %collective-permute-start.4 = (f32[4100]{0:T(1024)S(1)}, f32[4100]{0:T(1024)S(1)}, u32[]{:S(2)}, u32[]{:S(2)}) collective-permute-start(f32[4100]{0:T(1024)S(1)} %pad_maximum_fusion.2), channel_id=1, source_target_pairs={{0,16},{16,0},{1,17},{17,1},{2,18},{18,2},{3,19},{19,3},{4,20},{20... | collective-permute-start | bytes 49208 | tf_op jit(solution)/shard_map/ppermute | solution.py:38
  33.2 4.8 %copy-start.3 = (f32[2,4,1,512]{3,2,1,0:T(1,128)S(1)}, f32[2,4,1,512]{3,2,1,0:T(1,128)}, u32[]{:S(2)}) copy-start(f32[2,4,1,512]{3,2,1,0:T(1,128)} %param.12) | copy-start | bytes 49156
  35.2 2.9 %copy-start.1 = (bf16[1,2,64,512]{3,2,1,0:T(8,128)(2,1)S(1)}, bf16[1,2,64,512]{3,2,1,0:T(8,128)(2,1)}, u32[]{:S(2)}) copy-start(bf16[1,2,64,512]{3,2,1,0:T(8,128)(2,1)} %param.16) | copy-start | bytes 393220
  38.7 1.2 %collective-permute-start.7 = (f32[528]{0:T(1024)S(1)}, f32[528]{0:T(1024)S(1)}, u32[]{:S(2)}, u32[]{:S(2)}) collective-permute-start(f32[528]{0:T(1024)S(1)} %pad_maximum_fusion.12), channel_id=1, source_target_pairs={{0,1},{1,0},{2,3},{3,2},{4,5},{5,4},{6,7},{7,6},{8,9},{9,8},{10,11... | collective-permute-start | bytes 6344 | tf_op jit(solution)/shard_map/ppermute | solution.py:38
  40.2 3.7 %collective-permute-start.8 = (f32[1040]{0:T(1024)S(1)}, f32[1040]{0:T(1024)S(1)}, u32[]{:S(2)}, u32[]{:S(2)}) collective-permute-start(f32[1040]{0:T(1024)S(1)} %pad_maximum_fusion.8), channel_id=1, source_target_pairs={{0,2},{1,3},{2,0},{3,1},{4,6},{5,7},{6,4},{7,5},{8,10},{9,11},{10,... | collective-permute-start | bytes 12488 | tf_op jit(solution)/shard_map/ppermute | solution.py:38
  44.2 3.7 %collective-permute-start.9 = (f32[2064]{0:T(1024)S(1)}, f32[2064]{0:T(1024)S(1)}, u32[]{:S(2)}, u32[]{:S(2)}) collective-permute-start(f32[2064]{0:T(1024)S(1)} %pad_maximum_fusion.6), channel_id=1, source_target_pairs={{0,4},{1,5},{2,6},{3,7},{4,0},{5,1},{6,2},{7,3},{8,12},{9,13},{10,... | collective-permute-start | bytes 24776 | tf_op jit(solution)/shard_map/ppermute | solution.py:38
  48.2 7.5 %collective-permute-start.10 = (f32[4112]{0:T(1024)S(1)}, f32[4112]{0:T(1024)S(1)}, u32[]{:S(2)}, u32[]{:S(2)}) collective-permute-start(f32[4112]{0:T(1024)S(1)} %pad_maximum_fusion.3), channel_id=1, source_target_pairs={{0,8},{1,9},{2,10},{3,11},{4,12},{5,13},{6,14},{7,15},{8,0},{9,1},... | collective-permute-start | bytes 49352 | tf_op jit(solution)/shard_map/ppermute | solution.py:38
  51.1 6.2 %collective-permute-start.13 = (f32[2,4,1,512]{3,1,0,2:T(4,128)S(1)}, f32[2,4,1,512]{3,1,0,2:T(4,128)S(1)}, u32[]{:S(2)}, u32[]{:S(2)}) collective-permute-start(f32[2,4,1,512]{3,1,0,2:T(4,128)S(1)} %get-tuple-element.32), channel_id=1, source_target_pairs={{1,0},{2,1},{3,2},{4,3},{5,4},{6,5},{7,6},{8,7},{9,8},{10,9},{11,1... | collective-permute-start | bytes 49160 | tf_op jit(solution)/shard_map/ppermute | solution.py:55
  52.4 4.9 %collective-permute-start.12 = (f32[2,4,1,512]{3,1,0,2:T(4,128)S(1)}, f32[2,4,1,512]{3,1,0,2:T(4,128)S(1)}, u32[]{:S(2)}, u32[]{:S(2)}) collective-permute-start(f32[2,4,1,512]{3,1,0,2:T(4,128)S(1)} %get-tuple-element.32), channel_id=1, source_target_pairs={{0,1},{1,2},{2,3},{3,4},{4,5},{5,6},{6,7},{7,8},{8,9},{9,10},{10,1... | collective-permute-start | bytes 49160 | tf_op jit(solution)/shard_map/ppermute | solution.py:54
  55.8 3.8 %collective-permute-start.11 = (f32[4112]{0:T(1024)S(1)}, f32[4112]{0:T(1024)S(1)}, u32[]{:S(2)}, u32[]{:S(2)}) collective-permute-start(f32[4112]{0:T(1024)S(1)} %pad_maximum_fusion.4), channel_id=1, source_target_pairs={{0,16},{16,0},{1,17},{17,1},{2,18},{18,2},{3,19},{19,3},{4,20},{20... | collective-permute-start | bytes 49352 | tf_op jit(solution)/shard_map/ppermute | solution.py:38
  65.1 3.7 %collective-permute-start.14 = (f32[8,4]{1,0:T(8,128)S(1)}, f32[8,4]{1,0:T(8,128)S(1)}, u32[]{:S(2)}, u32[]{:S(2)}) collective-permute-start(f32[8,4]{1,0:T(8,128)S(1)} %concatenate.157), channel_id=1, source_target_pairs={{0,16},{16,0},{1,17},{17,1},{2,18},{18,2},{3,19},{19,3},{4,20},{20... | collective-permute-start | bytes 392 | tf_op jit(solution)/shard_map/ppermute | solution.py:21
  68.8 1.2 %collective-permute-start.15 = (f32[8,4]{1,0:T(8,128)S(1)}, f32[8,4]{1,0:T(8,128)S(1)}, u32[]{:S(2)}, u32[]{:S(2)}) collective-permute-start(f32[8,4]{1,0:T(8,128)S(1)} %add.531), channel_id=1, source_target_pairs={{0,1},{1,0},{2,3},{3,2},{4,5},{5,4},{6,7},{7,6},{8,9},{9,8},{10,11... | collective-permute-start | bytes 392 | tf_op jit(solution)/shard_map/ppermute | solution.py:21
  70.0 3.6 %collective-permute-start.16 = (f32[8,4]{1,0:T(8,128)S(1)}, f32[8,4]{1,0:T(8,128)S(1)}, u32[]{:S(2)}, u32[]{:S(2)}) collective-permute-start(f32[8,4]{1,0:T(8,128)S(1)} %add.532), channel_id=1, source_target_pairs={{0,2},{1,3},{2,0},{3,1},{4,6},{5,7},{6,4},{7,5},{8,10},{9,11},{10,... | collective-permute-start | bytes 392 | tf_op jit(solution)/shard_map/ppermute | solution.py:21
  73.6 3.6 %collective-permute-start.17 = (f32[8,4]{1,0:T(8,128)S(1)}, f32[8,4]{1,0:T(8,128)S(1)}, u32[]{:S(2)}, u32[]{:S(2)}) collective-permute-start(f32[8,4]{1,0:T(8,128)S(1)} %add.533), channel_id=1, source_target_pairs={{0,4},{1,5},{2,6},{3,7},{4,0},{5,1},{6,2},{7,3},{8,12},{9,13},{10,... | collective-permute-start | bytes 392 | tf_op jit(solution)/shard_map/ppermute | solution.py:21
  77.2 4.5 %collective-permute-start.18 = (f32[8,4]{1,0:T(8,128)S(1)}, f32[8,4]{1,0:T(8,128)S(1)}, u32[]{:S(2)}, u32[]{:S(2)}) collective-permute-start(f32[8,4]{1,0:T(8,128)S(1)} %add.534), channel_id=1, source_target_pairs={{0,8},{1,9},{2,10},{3,11},{4,12},{5,13},{6,14},{7,15},{8,0},{9,1},... | collective-permute-start | bytes 392 | tf_op jit(solution)/shard_map/ppermute | solution.py:21

commit v8 on v7

--- a/solution.py
+++ b/solution.py
@@ -74,7 +74,7 @@
     slots = near_blocks.shape[2]
     width = near_blocks.shape[4]
     rounded = window.astype(jnp.bfloat16).reshape(2, nrhs, 3 * blocks_dev, width)
-    chosen = jnp.take(rounded, near_cols[0].reshape(-1), axis=2).reshape(
+    chosen = rounded.at[:, :, near_cols[0].reshape(-1)].get(mode="promise_in_bounds").reshape(
         2, nrhs, blocks_dev, slots, width
     )
     near_prod = jnp.einsum(
@@ -107,7 +107,7 @@
     nrhs = every.shape[1]
     rows = every.shape[3]
     tiles = every.reshape(2, nrhs, -1, width)
-    return jnp.take(tiles, partner[0], axis=2).reshape(2, nrhs, 1, rows)
+    return tiles.at[:, :, partner[0]].get(mode="promise_in_bounds").reshape(2, nrhs, 1, rows)
 
 
 def local_products(vectors, image):

time: 84.6 us -> 82.5 us (0.975)
  other arithmetic: 7.89 us -> 6.9 us
    gather x4 -> x6, local copies, waits for them, and re-layouts: 2.32 us -> 2.35 us  [the longest x2 1.18 us: near_field(): rounded.at[:, :, near_cols[0].reshape(-1)].get(mode='promise_in_bounds')]
  transfers between devices with their start and end apart: 19 -> 19, of which waited for: 14 -> 13; matrix products, arithmetic and copies ran while one was open for 12% -> 11% of each run, Pallas kernels for 0% -> 0%
where the time goes in v8:
time: 82.5 us; the launch traced here: 81.8 us
  starting transfers between devices  31.6 us (38%)
  waiting for transfers between devices  26 us (32%)
  local copies, waits for them, and re-layouts  9.41 us (11%)
  other arithmetic  6.9 us (8%)
  matrix products  6.81 us (8%)
  between operations  1.07 us (1%)
    ppermute x10, starting transfers between devices, tree_collect(): got = lax.ppermute(packed, axis, [(i, i ^ k) for i in range(n)])  19.3 us
    ppermute x10, waiting for transfers between devices, tree_collect(): got = lax.ppermute(packed, axis, [(i, i ^ k) for i in range(n)])  14.5 us
    ppermute x5, waiting for transfers between devices, tree_sum(): x = x + lax.ppermute(x, axis, [(i, i ^ k) for i in range(n)])  11.5 us
    ppermute x2, starting transfers between devices, neighbours(): left = lax.ppermute(field, 'blk', [(i, i + 1) for i in range(ends)])  5.52 us
    ppermute x5, starting transfers between devices, tree_sum(): x = x + lax.ppermute(x, axis, [(i, i ^ k) for i in range(n)])  4.19 us
    dot_general x2, matrix products, far_field(): jnp.einsum('sakl,spql->apqk', weights, gathered, precision=lax.Precision....  4.01 us
    ppermute x2, starting transfers between devices, neighbours(): right = lax.ppermute(field, 'blk', [(i + 1, i) for i in range(ends)])  2.57 us
    unnamed x13, local copies, waits for them, and re-layouts  2.01 us
  transfers between devices with their start and end apart: 19, of which 13 were waited for; matrix products, arithmetic and copies ran while one was open for 11% of the time, Pallas kernels for 0%

profile of v8, /device:TPU:0, one launch (start us, length us, event | category | flops | bytes accessed | tf_op | source)
XLA Modules:
  0.0 81.8 jit_solution(8221204973967495982)
XLA Ops:
  0.7 2.5 %collective-permute-start.5 = (f32[2,4,1,512]{3,2,1,0:T(1,128)}, f32[2,4,1,512]{3,2,1,0:T(1,128)S(1)}, u32[]{:S(2)}, u32[]{:S(2)}) collective-permute-start(f32[2,4,1,512]{3,2,1,0:T(1,128)} %param.8), channel_id=1, source_target_pairs={{0,1},{1,2},{2,3},{3,4},{4,5},{5,6},{6,7},{7,8},{8,9},{9,10},{10,1... | collective-permute-start | bytes 49160 | tf_op jit(solution)/shard_map/ppermute | solution.py:54
  3.2 1.3 %collective-permute-start.6 = (f32[2,4,1,512]{3,2,1,0:T(1,128)}, f32[2,4,1,512]{3,2,1,0:T(1,128)S(1)}, u32[]{:S(2)}, u32[]{:S(2)}) collective-permute-start(f32[2,4,1,512]{3,2,1,0:T(1,128)} %param.8), channel_id=1, source_target_pairs={{1,0},{2,1},{3,2},{4,3},{5,4},{6,5},{7,6},{8,7},{9,8},{10,9},{11,1... | collective-permute-start | bytes 49160 | tf_op jit(solution)/shard_map/ppermute | solution.py:55
  4.5 0.7 iota_compare_fusion
  5.2 0.2 and_convert_fusion
  5.4 0.8 %add_reduce_fusion.9 = f32[4]{0:T(128)S(1)} fusion(f32[2,4,1,512]{3,2,1,0:T(1,128)} %param.8), kind=kLoop, calls=%fused_computation.121 | loop fusion | flops 8188 | bytes 16400 | tf_op jit(solution)/shard_map/reduce_sum | solution.py:123
  6.2 0.8 constant_dynamic-update-slice_fusion.1
  7.0 1.1 %convolution_bitcast_fusion.5 = f32[2,2,4,64]{3,2,0,1:T(4,128)S(1)} fusion(bf16[1,2,64,512]{3,2,1,0:T(8,128)(2,1)} %param.12, bf16[2,4,1,512]{3,2,1,0:T(2,128)(2,1)S(1)} %get-tuple-element.56), kind=kOutput, calls=%fused_computation.15 | convolution fusion | flops 1048576 | bytes 143360 | tf_op jit(solution)/shard_map/akr,pqr->apqk/dot_general | solution.py:65
  8.3 3.2 %collective-permute-start = (f32[516]{0:T(1024)S(1)}, f32[516]{0:T(1024)S(1)}, u32[]{:S(2)}, u32[]{:S(2)}) collective-permute-start(f32[516]{0:T(1024)S(1)} %pad_maximum_fusion.10), channel_id=1, source_target_pairs={{0,1},{1,0},{2,3},{3,2},{4,5},{5,4},{6,7},{7,6},{8,9},{9,8},{10,11... | collective-permute-start | bytes 6200 | tf_op jit(solution)/shard_map/ppermute | solution.py:38
  11.5 0.7 fusion.69
  12.2 0.8 reshape_squeeze.4
  13.3 1.6 %collective-permute-start.1 = (f32[1028]{0:T(1024)S(1)}, f32[1028]{0:T(1024)S(1)}, u32[]{:S(2)}, u32[]{:S(2)}) collective-permute-start(f32[1028]{0:T(1024)S(1)} %pad_maximum_fusion.7), channel_id=1, source_target_pairs={{0,2},{1,3},{2,0},{3,1},{4,6},{5,7},{6,4},{7,5},{8,10},{9,11},{10,... | collective-permute-start | bytes 12344 | tf_op jit(solution)/shard_map/ppermute | solution.py:38
  14.9 2.0 %collective-permute-done.1 = f32[1028]{0:T(1024)S(1)} collective-permute-done((f32[1028]{0:T(1024)S(1)}, f32[1028]{0:T(1024)S(1)}, u32[]{:S(2)}, u32[]{:S(2)}) %collective-permute-start.1) | collective-permute-done | bytes 4144 | tf_op jit(solution)/shard_map/ppermute | solution.py:38
  17.3 2.6 %collective-permute-start.2 = (f32[2052]{0:T(1024)S(1)}, f32[2052]{0:T(1024)S(1)}, u32[]{:S(2)}, u32[]{:S(2)}) collective-permute-start(f32[2052]{0:T(1024)S(1)} %pad_maximum_fusion.5), channel_id=1, source_target_pairs={{0,4},{1,5},{2,6},{3,7},{4,0},{5,1},{6,2},{7,3},{8,12},{9,13},{10,... | collective-permute-start | bytes 24632 | tf_op jit(solution)/shard_map/ppermute | solution.py:38
  19.9 1.7 %collective-permute-done.2 = f32[2052]{0:T(1024)S(1)} collective-permute-done((f32[2052]{0:T(1024)S(1)}, f32[2052]{0:T(1024)S(1)}, u32[]{:S(2)}, u32[]{:S(2)}) %collective-permute-start.2) | collective-permute-done | bytes 8240 | tf_op jit(solution)/shard_map/ppermute | solution.py:38
  21.9 3.0 %collective-permute-start.3 = (f32[4100]{0:T(1024)S(1)}, f32[4100]{0:T(1024)S(1)}, u32[]{:S(2)}, u32[]{:S(2)}) collective-permute-start(f32[4100]{0:T(1024)S(1)} %pad_maximum_fusion.1), channel_id=1, source_target_pairs={{0,8},{1,9},{2,10},{3,11},{4,12},{5,13},{6,14},{7,15},{8,0},{9,1},... | collective-permute-start | bytes 49208 | tf_op jit(solution)/shard_map/ppermute | solution.py:38
  24.9 0.7 copy.181
  25.7 1.0 %collective-permute-done.3 = f32[4100]{0:T(1024)S(1)} collective-permute-done((f32[4100]{0:T(1024)S(1)}, f32[4100]{0:T(1024)S(1)}, u32[]{:S(2)}, u32[]{:S(2)}) %collective-permute-start.3) | collective-permute-done | bytes 16432 | tf_op jit(solution)/shard_map/ppermute | solution.py:38
  26.7 0.8 pad_maximum_fusion.2
  27.5 1.5 %collective-permute-start.4 = (f32[4100]{0:T(1024)S(1)}, f32[4100]{0:T(1024)S(1)}, u32[]{:S(2)}, u32[]{:S(2)}) collective-permute-start(f32[4100]{0:T(1024)S(1)} %pad_maximum_fusion.2), channel_id=1, source_target_pairs={{0,16},{16,0},{1,17},{17,1},{2,18},{18,2},{3,19},{19,3},{4,20},{20... | collective-permute-start | bytes 49208 | tf_op jit(solution)/shard_map/ppermute | solution.py:38
  29.2 2.1 %collective-permute-done.4 = f32[4100]{0:T(1024)S(1)} collective-permute-done((f32[4100]{0:T(1024)S(1)}, f32[4100]{0:T(1024)S(1)}, u32[]{:S(2)}, u32[]{:S(2)}) %collective-permute-start.4) | collective-permute-done | bytes 16432 | tf_op jit(solution)/shard_map/ppermute | solution.py:38
  31.4 2.0 %convolution_bitcast_fusion.4 = f32[2,2,4,64]{3,2,0,1:T(4,128)S(1)} fusion(f32[1,1,16,2,64,64]{5,4,3,2,1,0:T(8,128)} %param.14, f32[16,64,64]{2,1,0:T(8,128)S(1)} %and_convert_fusion, f32[16,2,4,64]{3,2,1,0:T(4,128)S(1)} %fusion.18), kind=kOutput, calls=%fused_computation.14 | convolution fusion | flops 6422528 | bytes 823296 | tf_op jit(solution)/shard_map/sakl,spql->apqk/dot_general | solution.py:98
  33.4 0.1 convolution_bitcast_fusion.1
  33.9 0.6 gather_fusion.1
  34.5 0.2 broadcast_divide_fusion
  34.7 0.6 gather_fusion
  35.3 0.7 fusion.4
  36.1 0.1 convolution_bitcast_fusion.3
  36.4 0.2 add_reduce_fusion.8
  36.8 1.2 %collective-permute-done.7 = f32[528]{0:T(1024)S(1)} collective-permute-done((f32[528]{0:T(1024)S(1)}, f32[528]{0:T(1024)S(1)}, u32[]{:S(2)}, u32[]{:S(2)}) %collective-permute-start.7) | collective-permute-done | bytes 2144 | tf_op jit(solution)/shard_map/ppermute | solution.py:38
  38.2 0.9 %collective-permute-start.8 = (f32[1040]{0:T(1024)S(1)}, f32[1040]{0:T(1024)S(1)}, u32[]{:S(2)}, u32[]{:S(2)}) collective-permute-start(f32[1040]{0:T(1024)S(1)} %pad_maximum_fusion.8), channel_id=1, source_target_pairs={{0,2},{1,3},{2,0},{3,1},{4,6},{5,7},{6,4},{7,5},{8,10},{9,11},{10,... | collective-permute-start | bytes 12488 | tf_op jit(solution)/shard_map/ppermute | solution.py:38
  39.2 2.7 %collective-permute-done.8 = f32[1040]{0:T(1024)S(1)} collective-permute-done((f32[1040]{0:T(1024)S(1)}, f32[1040]{0:T(1024)S(1)}, u32[]{:S(2)}, u32[]{:S(2)}) %collective-permute-start.8) | collective-permute-done | bytes 4192 | tf_op jit(solution)/shard_map/ppermute | solution.py:38
  42.2 1.9 %collective-permute-start.9 = (f32[2064]{0:T(1024)S(1)}, f32[2064]{0:T(1024)S(1)}, u32[]{:S(2)}, u32[]{:S(2)}) collective-permute-start(f32[2064]{0:T(1024)S(1)} %pad_maximum_fusion.6), channel_id=1, source_target_pairs={{0,4},{1,5},{2,6},{3,7},{4,0},{5,1},{6,2},{7,3},{8,12},{9,13},{10,... | collective-permute-start | bytes 24776 | tf_op jit(solution)/shard_map/ppermute | solution.py:38
  44.1 1.8 %collective-permute-done.9 = f32[2064]{0:T(1024)S(1)} collective-permute-done((f32[2064]{0:T(1024)S(1)}, f32[2064]{0:T(1024)S(1)}, u32[]{:S(2)}, u32[]{:S(2)}) %collective-permute-start.9) | collective-permute-done | bytes 8288 | tf_op jit(solution)/shard_map/ppermute | solution.py:38
  46.2 2.9 %collective-permute-start.10 = (f32[4112]{0:T(1024)S(1)}, f32[4112]{0:T(1024)S(1)}, u32[]{:S(2)}, u32[]{:S(2)}) collective-permute-start(f32[4112]{0:T(1024)S(1)} %pad_maximum_fusion.3), channel_id=1, source_target_pairs={{0,8},{1,9},{2,10},{3,11},{4,12},{5,13},{6,14},{7,15},{8,0},{9,1},... | collective-permute-start | bytes 49352 | tf_op jit(solution)/shard_map/ppermute | solution.py:38
  49.2 1.3 %collective-permute-start.13 = (f32[2,4,1,512]{3,1,0,2:T(4,128)S(1)}, f32[2,4,1,512]{3,1,0,2:T(4,128)S(1)}, u32[]{:S(2)}, u32[]{:S(2)}) collective-permute-start(f32[2,4,1,512]{3,1,0,2:T(4,128)S(1)} %get-tuple-element.30), channel_id=1, source_target_pairs={{1,0},{2,1},{3,2},{4,3},{5,4},{6,5},{7,6},{8,7},{9,8},{10,9},{11,1... | collective-permute-start | bytes 49160 | tf_op jit(solution)/shard_map/ppermute | solution.py:55
  50.5 3.0 %collective-permute-start.12 = (f32[2,4,1,512]{3,1,0,2:T(4,128)S(1)}, f32[2,4,1,512]{3,1,0,2:T(4,128)S(1)}, u32[]{:S(2)}, u32[]{:S(2)}) collective-permute-start(f32[2,4,1,512]{3,1,0,2:T(4,128)S(1)} %get-tuple-element.30), channel_id=1, source_target_pairs={{0,1},{1,2},{2,3},{3,4},{4,5},{5,6},{6,7},{7,8},{8,9},{9,10},{10,1... | collective-permute-start | bytes 49160 | tf_op jit(solution)/shard_map/ppermute | solution.py:54
  53.8 1.5 %collective-permute-start.11 = (f32[4112]{0:T(1024)S(1)}, f32[4112]{0:T(1024)S(1)}, u32[]{:S(2)}, u32[]{:S(2)}) collective-permute-start(f32[4112]{0:T(1024)S(1)} %pad_maximum_fusion.4), channel_id=1, source_target_pairs={{0,16},{16,0},{1,17},{17,1},{2,18},{18,2},{3,19},{19,3},{4,20},{20... | collective-permute-start | bytes 49352 | tf_op jit(solution)/shard_map/ppermute | solution.py:38
  55.6 2.0 %collective-permute-done.11 = f32[4112]{0:T(1024)S(1)} collective-permute-done((f32[4112]{0:T(1024)S(1)}, f32[4112]{0:T(1024)S(1)}, u32[]{:S(2)}, u32[]{:S(2)}) %collective-permute-start.11) | collective-permute-done | bytes 16480 | tf_op jit(solution)/shard_map/ppermute | solution.py:38
  57.9 2.0 %convolution_bitcast_fusion.2 = f32[2,2,4,64]{3,2,0,1:T(4,128)S(1)} fusion(f32[1,1,16,2,64,64]{5,4,3,2,1,0:T(8,128)} %param.14, f32[16,64,64]{2,1,0:T(8,128)S(1)} %and_convert_fusion, f32[16,1,4,64]{3,2,1,0:T(4,128)S(1)} %get-tuple-element.33, f32[16,1,4,64]{3,2,1,0:T(4,128)S(1)} %get-tuple-element.32, f32[8,2,4,64]{3,2,1,0:T(4,128)S(1)} %maximum_select_fusion.4, ...), kind=kOutput, calls=%fused_computation.12 | convolution fusion | flops 6471680 | bytes 856081 | tf_op jit(solution)/shard_map/sakl,spql->apqk/dot_general | solution.py:98
  60.3 0.6 gather_fusion.3
  60.9 0.2 subtract_reduce_fusion
  61.2 0.6 gather_fusion.2
  61.8 0.7 fusion.7
  62.5 0.1 convolution_bitcast_fusion
  62.7 0.2 subtract_reduce_fusion.1
  63.0 1.6 %collective-permute-start.14 = (f32[8,4]{1,0:T(8,128)S(1)}, f32[8,4]{1,0:T(8,128)S(1)}, u32[]{:S(2)}, u32[]{:S(2)}) collective-permute-start(f32[8,4]{1,0:T(8,128)S(1)} %concatenate.157), channel_id=1, source_target_pairs={{0,16},{16,0},{1,17},{17,1},{2,18},{18,2},{3,19},{19,3},{4,20},{20... | collective-permute-start | bytes 392 | tf_op jit(solution)/shard_map/ppermute | solution.py:21
  64.6 2.1 %collective-permute-done.14 = f32[8,4]{1,0:T(8,128)S(1)} collective-permute-done((f32[8,4]{1,0:T(8,128)S(1)}, f32[8,4]{1,0:T(8,128)S(1)}, u32[]{:S(2)}, u32[]{:S(2)}) %collective-permute-start.14) | collective-permute-done | bytes 160 | tf_op jit(solution)/shard_map/ppermute | solution.py:21
  66.7 1.2 %collective-permute-done.15 = f32[8,4]{1,0:T(8,128)S(1)} collective-permute-done((f32[8,4]{1,0:T(8,128)S(1)}, f32[8,4]{1,0:T(8,128)S(1)}, u32[]{:S(2)}, u32[]{:S(2)}) %collective-permute-start.15) | collective-permute-done | bytes 160 | tf_op jit(solution)/shard_map/ppermute | solution.py:21
  67.9 0.6 collective-permute-start.16
  68.5 0.1 copy.96
  68.6 0.6 copy.105
  69.2 2.3 %collective-permute-done.16 = f32[8,4]{1,0:T(8,128)S(1)} collective-permute-done((f32[8,4]{1,0:T(8,128)S(1)}, f32[8,4]{1,0:T(8,128)S(1)}, u32[]{:S(2)}, u32[]{:S(2)}) %collective-permute-start.16) | collective-permute-done | bytes 160 | tf_op jit(solution)/shard_map/ppermute | solution.py:21
  71.5 1.7 %collective-permute-start.17 = (f32[8,4]{1,0:T(8,128)S(1)}, f32[8,4]{1,0:T(8,128)S(1)}, u32[]{:S(2)}, u32[]{:S(2)}) collective-permute-start(f32[8,4]{1,0:T(8,128)S(1)} %add.551), channel_id=1, source_target_pairs={{0,4},{1,5},{2,6},{3,7},{4,0},{5,1},{6,2},{7,3},{8,12},{9,13},{10,... | collective-permute-start | bytes 392 | tf_op jit(solution)/shard_map/ppermute | solution.py:21
  73.2 0.1 copy.97
  73.3 1.8 %collective-permute-done.17 = f32[8,4]{1,0:T(8,128)S(1)} collective-permute-done((f32[8,4]{1,0:T(8,128)S(1)}, f32[8,4]{1,0:T(8,128)S(1)}, u32[]{:S(2)}, u32[]{:S(2)}) %collective-permute-start.17) | collective-permute-done | bytes 160 | tf_op jit(solution)/shard_map/ppermute | solution.py:21
  75.1 0.3 collective-permute-start.18
  75.4 0.1 copy.98
  75.5 4.1 %collective-permute-done.18 = f32[8,4]{1,0:T(8,128)S(1)} collective-permute-done((f32[8,4]{1,0:T(8,128)S(1)}, f32[8,4]{1,0:T(8,128)S(1)}, u32[]{:S(2)}, u32[]{:S(2)}) %collective-permute-start.18) | collective-permute-done | bytes 160 | tf_op jit(solution)/shard_map/ppermute | solution.py:21
  79.9 0.6 copy.106
  80.5 0.1 copy.99
  80.6 0.1 copy.100
  80.7 0.1 copy.101
  80.8 0.1 copy.102
  81.1 0.7 stack.153
  (136 shorter events, 5.1 us)
Async XLA Ops:
  0.6 34.7 %copy-start = (bf16[1,2,4,2,256,256]{5,4,3,2,1,0:T(8,128)(2,1)S(1)}, bf16[1,2,4,2,256,256]{5,4,3,2,1,0:T(8,128)(2,1)}, u32[]{:S(2)}) copy-start(bf16[1,2,4,2,256,256]{5,4,3,2,1,0:T(8,128)(2,1)} %param.9) | copy-start | bytes 6291460
  0.6 32.8 %copy-start.2 = (bf16[1,2,64,512]{3,2,1,0:T(8,128)(2,1)S(1)}, bf16[1,2,64,512]{3,2,1,0:T(8,128)(2,1)}, u32[]{:S(2)}) copy-start(bf16[1,2,64,512]{3,2,1,0:T(8,128)(2,1)} %param.13) | copy-start | bytes 393220
  0.7 5.6 %collective-permute-start.5 = (f32[2,4,1,512]{3,2,1,0:T(1,128)}, f32[2,4,1,512]{3,2,1,0:T(1,128)S(1)}, u32[]{:S(2)}, u32[]{:S(2)}) collective-permute-start(f32[2,4,1,512]{3,2,1,0:T(1,128)} %param.8), channel_id=1, source_target_pairs={{0,1},{1,2},{2,3},{3,4},{4,5},{5,6},{6,7},{7,8},{8,9},{9,10},{10,1... | collective-permute-start | bytes 49160 | tf_op jit(solution)/shard_map/ppermute | solution.py:54
  3.2 25.9 %collective-permute-start.6 = (f32[2,4,1,512]{3,2,1,0:T(1,128)}, f32[2,4,1,512]{3,2,1,0:T(1,128)S(1)}, u32[]{:S(2)}, u32[]{:S(2)}) collective-permute-start(f32[2,4,1,512]{3,2,1,0:T(1,128)} %param.8), channel_id=1, source_target_pairs={{1,0},{2,1},{3,2},{4,3},{5,4},{6,5},{7,6},{8,7},{9,8},{10,9},{11,1... | collective-permute-start | bytes 49160 | tf_op jit(solution)/shard_map/ppermute | solution.py:55
  8.3 4.7 %collective-permute-start = (f32[516]{0:T(1024)S(1)}, f32[516]{0:T(1024)S(1)}, u32[]{:S(2)}, u32[]{:S(2)}) collective-permute-start(f32[516]{0:T(1024)S(1)} %pad_maximum_fusion.10), channel_id=1, source_target_pairs={{0,1},{1,0},{2,3},{3,2},{4,5},{5,4},{6,7},{7,6},{8,9},{9,8},{10,11... | collective-permute-start | bytes 6200 | tf_op jit(solution)/shard_map/ppermute | solution.py:38
  13.3 3.7 %collective-permute-start.1 = (f32[1028]{0:T(1024)S(1)}, f32[1028]{0:T(1024)S(1)}, u32[]{:S(2)}, u32[]{:S(2)}) collective-permute-start(f32[1028]{0:T(1024)S(1)} %pad_maximum_fusion.7), channel_id=1, source_target_pairs={{0,2},{1,3},{2,0},{3,1},{4,6},{5,7},{6,4},{7,5},{8,10},{9,11},{10,... | collective-permute-start | bytes 12344 | tf_op jit(solution)/shard_map/ppermute | solution.py:38
  17.3 4.3 %collective-permute-start.2 = (f32[2052]{0:T(1024)S(1)}, f32[2052]{0:T(1024)S(1)}, u32[]{:S(2)}, u32[]{:S(2)}) collective-permute-start(f32[2052]{0:T(1024)S(1)} %pad_maximum_fusion.5), channel_id=1, source_target_pairs={{0,4},{1,5},{2,6},{3,7},{4,0},{5,1},{6,2},{7,3},{8,12},{9,13},{10,... | collective-permute-start | bytes 24632 | tf_op jit(solution)/shard_map/ppermute | solution.py:38
  21.9 4.8 %collective-permute-start.3 = (f32[4100]{0:T(1024)S(1)}, f32[4100]{0:T(1024)S(1)}, u32[]{:S(2)}, u32[]{:S(2)}) collective-permute-start(f32[4100]{0:T(1024)S(1)} %pad_maximum_fusion.1), channel_id=1, source_target_pairs={{0,8},{1,9},{2,10},{3,11},{4,12},{5,13},{6,14},{7,15},{8,0},{9,1},... | collective-permute-start | bytes 49208 | tf_op jit(solution)/shard_map/ppermute | solution.py:38
  27.5 3.8 %collective-permute-start.4 = (f32[4100]{0:T(1024)S(1)}, f32[4100]{0:T(1024)S(1)}, u32[]{:S(2)}, u32[]{:S(2)}) collective-permute-start(f32[4100]{0:T(1024)S(1)} %pad_maximum_fusion.2), channel_id=1, source_target_pairs={{0,16},{16,0},{1,17},{17,1},{2,18},{18,2},{3,19},{19,3},{4,20},{20... | collective-permute-start | bytes 49208 | tf_op jit(solution)/shard_map/ppermute | solution.py:38
  31.4 4.7 %copy-start.3 = (f32[2,4,1,512]{3,2,1,0:T(1,128)S(1)}, f32[2,4,1,512]{3,2,1,0:T(1,128)}, u32[]{:S(2)}) copy-start(f32[2,4,1,512]{3,2,1,0:T(1,128)} %param.8) | copy-start | bytes 49156
  31.4 4.7 %copy-start.1 = (bf16[1,2,64,512]{3,2,1,0:T(8,128)(2,1)S(1)}, bf16[1,2,64,512]{3,2,1,0:T(8,128)(2,1)}, u32[]{:S(2)}) copy-start(bf16[1,2,64,512]{3,2,1,0:T(8,128)(2,1)} %param.12) | copy-start | bytes 393220
  36.7 1.2 %collective-permute-start.7 = (f32[528]{0:T(1024)S(1)}, f32[528]{0:T(1024)S(1)}, u32[]{:S(2)}, u32[]{:S(2)}) collective-permute-start(f32[528]{0:T(1024)S(1)} %pad_maximum_fusion.12), channel_id=1, source_target_pairs={{0,1},{1,0},{2,3},{3,2},{4,5},{5,4},{6,7},{7,6},{8,9},{9,8},{10,11... | collective-permute-start | bytes 6344 | tf_op jit(solution)/shard_map/ppermute | solution.py:38
  38.2 3.7 %collective-permute-start.8 = (f32[1040]{0:T(1024)S(1)}, f32[1040]{0:T(1024)S(1)}, u32[]{:S(2)}, u32[]{:S(2)}) collective-permute-start(f32[1040]{0:T(1024)S(1)} %pad_maximum_fusion.8), channel_id=1, source_target_pairs={{0,2},{1,3},{2,0},{3,1},{4,6},{5,7},{6,4},{7,5},{8,10},{9,11},{10,... | collective-permute-start | bytes 12488 | tf_op jit(solution)/shard_map/ppermute | solution.py:38
  42.2 3.7 %collective-permute-start.9 = (f32[2064]{0:T(1024)S(1)}, f32[2064]{0:T(1024)S(1)}, u32[]{:S(2)}, u32[]{:S(2)}) collective-permute-start(f32[2064]{0:T(1024)S(1)} %pad_maximum_fusion.6), channel_id=1, source_target_pairs={{0,4},{1,5},{2,6},{3,7},{4,0},{5,1},{6,2},{7,3},{8,12},{9,13},{10,... | collective-permute-start | bytes 24776 | tf_op jit(solution)/shard_map/ppermute | solution.py:38
  46.2 7.5 %collective-permute-start.10 = (f32[4112]{0:T(1024)S(1)}, f32[4112]{0:T(1024)S(1)}, u32[]{:S(2)}, u32[]{:S(2)}) collective-permute-start(f32[4112]{0:T(1024)S(1)} %pad_maximum_fusion.3), channel_id=1, source_target_pairs={{0,8},{1,9},{2,10},{3,11},{4,12},{5,13},{6,14},{7,15},{8,0},{9,1},... | collective-permute-start | bytes 49352 | tf_op jit(solution)/shard_map/ppermute | solution.py:38
  49.2 6.2 %collective-permute-start.13 = (f32[2,4,1,512]{3,1,0,2:T(4,128)S(1)}, f32[2,4,1,512]{3,1,0,2:T(4,128)S(1)}, u32[]{:S(2)}, u32[]{:S(2)}) collective-permute-start(f32[2,4,1,512]{3,1,0,2:T(4,128)S(1)} %get-tuple-element.30), channel_id=1, source_target_pairs={{1,0},{2,1},{3,2},{4,3},{5,4},{6,5},{7,6},{8,7},{9,8},{10,9},{11,1... | collective-permute-start | bytes 49160 | tf_op jit(solution)/shard_map/ppermute | solution.py:55
  50.5 4.9 %collective-permute-start.12 = (f32[2,4,1,512]{3,1,0,2:T(4,128)S(1)}, f32[2,4,1,512]{3,1,0,2:T(4,128)S(1)}, u32[]{:S(2)}, u32[]{:S(2)}) collective-permute-start(f32[2,4,1,512]{3,1,0,2:T(4,128)S(1)} %get-tuple-element.30), channel_id=1, source_target_pairs={{0,1},{1,2},{2,3},{3,4},{4,5},{5,6},{6,7},{7,8},{8,9},{9,10},{10,1... | collective-permute-start | bytes 49160 | tf_op jit(solution)/shard_map/ppermute | solution.py:54
  53.8 3.8 %collective-permute-start.11 = (f32[4112]{0:T(1024)S(1)}, f32[4112]{0:T(1024)S(1)}, u32[]{:S(2)}, u32[]{:S(2)}) collective-permute-start(f32[4112]{0:T(1024)S(1)} %pad_maximum_fusion.4), channel_id=1, source_target_pairs={{0,16},{16,0},{1,17},{17,1},{2,18},{18,2},{3,19},{19,3},{4,20},{20... | collective-permute-start | bytes 49352 | tf_op jit(solution)/shard_map/ppermute | solution.py:38
  63.0 3.7 %collective-permute-start.14 = (f32[8,4]{1,0:T(8,128)S(1)}, f32[8,4]{1,0:T(8,128)S(1)}, u32[]{:S(2)}, u32[]{:S(2)}) collective-permute-start(f32[8,4]{1,0:T(8,128)S(1)} %concatenate.157), channel_id=1, source_target_pairs={{0,16},{16,0},{1,17},{17,1},{2,18},{18,2},{3,19},{19,3},{4,20},{20... | collective-permute-start | bytes 392 | tf_op jit(solution)/shard_map/ppermute | solution.py:21
  66.7 1.2 %collective-permute-start.15 = (f32[8,4]{1,0:T(8,128)S(1)}, f32[8,4]{1,0:T(8,128)S(1)}, u32[]{:S(2)}, u32[]{:S(2)}) collective-permute-start(f32[8,4]{1,0:T(8,128)S(1)} %add.549), channel_id=1, source_target_pairs={{0,1},{1,0},{2,3},{3,2},{4,5},{5,4},{6,7},{7,6},{8,9},{9,8},{10,11... | collective-permute-start | bytes 392 | tf_op jit(solution)/shard_map/ppermute | solution.py:21
  67.9 3.6 %collective-permute-start.16 = (f32[8,4]{1,0:T(8,128)S(1)}, f32[8,4]{1,0:T(8,128)S(1)}, u32[]{:S(2)}, u32[]{:S(2)}) collective-permute-start(f32[8,4]{1,0:T(8,128)S(1)} %add.550), channel_id=1, source_target_pairs={{0,2},{1,3},{2,0},{3,1},{4,6},{5,7},{6,4},{7,5},{8,10},{9,11},{10,... | collective-permute-start | bytes 392 | tf_op jit(solution)/shard_map/ppermute | solution.py:21
  71.5 3.6 %collective-permute-start.17 = (f32[8,4]{1,0:T(8,128)S(1)}, f32[8,4]{1,0:T(8,128)S(1)}, u32[]{:S(2)}, u32[]{:S(2)}) collective-permute-start(f32[8,4]{1,0:T(8,128)S(1)} %add.551), channel_id=1, source_target_pairs={{0,4},{1,5},{2,6},{3,7},{4,0},{5,1},{6,2},{7,3},{8,12},{9,13},{10,... | collective-permute-start | bytes 392 | tf_op jit(solution)/shard_map/ppermute | solution.py:21
  75.1 4.5 %collective-permute-start.18 = (f32[8,4]{1,0:T(8,128)S(1)}, f32[8,4]{1,0:T(8,128)S(1)}, u32[]{:S(2)}, u32[]{:S(2)}) collective-permute-start(f32[8,4]{1,0:T(8,128)S(1)} %add.552), channel_id=1, source_target_pairs={{0,8},{1,9},{2,10},{3,11},{4,12},{5,13},{6,14},{7,15},{8,0},{9,1},... | collective-permute-start | bytes 392 | tf_op jit(solution)/shard_map/ppermute | solution.py:21

commit v9 on v8

--- a/solution.py
+++ b/solution.py
@@ -23,8 +23,11 @@
     return x
 
 
-def tree_collect(red, gat_blk, gat_dom):
-    for axis, gat in (("blk", gat_blk), ("dom", gat_dom)):
+def tree_collect(red, gat_blk, gat_dom, dom_first=False):
+    rounds = (("blk", gat_blk), ("dom", gat_dom))
+    if dom_first:
+        rounds = rounds[::-1]
+    for axis, gat in rounds:
         n = lax.axis_size(axis)
         if not _pow2(n):
             red = lax.psum(red, axis)
@@ -152,7 +155,10 @@
 
     window_rhs = neighbours(right_side)
     start_sum, coef_rhs, every_rhs = tree_collect(
-        local_squares(right_side), coefficients(right_side, source_basis), right_side[:, :, 0]
+        local_squares(right_side),
+        coefficients(right_side, source_basis),
+        right_side[:, :, 0],
+        dom_first=True,
     )
     beta = jnp.sqrt(start_sum / total + EPSILON)
     inv_scale = beta[None, :, None, None]

time: 82.5 us -> 81.5 us (0.988)
  starting transfers between devices: 31.6 us -> 30.3 us
    ppermute x5, waiting for transfers between devices: 11.5 us -> 12.5 us  [tree_sum(): x = x + lax.ppermute(x, axis, [(i, i ^ k) for i in range(n)])]
    ppermute x5, starting transfers between devices: 4.19 us -> 3.17 us  [tree_sum(): x = x + lax.ppermute(x, axis, [(i, i ^ k) for i in range(n)])]
  transfers between devices with their start and end apart: 19 -> 19, of which waited for: 13 -> 13; matrix products, arithmetic and copies ran while one was open for 11% -> 12% of each run, Pallas kernels for 0% -> 0%
where the time goes in v9:
time: 81.5 us; the launch traced here: 80.8 us
  starting transfers between devices  30.3 us (37%)
  waiting for transfers between devices  26.2 us (32%)
  local copies, waits for them, and re-layouts  9.41 us (12%)
  other arithmetic  6.89 us (8%)
  matrix products  6.81 us (8%)
  between operations  1.08 us (1%)
    ppermute x10, starting transfers between devices, tree_collect(): got = lax.ppermute(packed, axis, [(i, i ^ k) for i in range(n)])  19.1 us
    ppermute x10, waiting for transfers between devices, tree_collect(): got = lax.ppermute(packed, axis, [(i, i ^ k) for i in range(n)])  13.7 us
    ppermute x5, waiting for transfers between devices, tree_sum(): x = x + lax.ppermute(x, axis, [(i, i ^ k) for i in range(n)])  12.5 us
    ppermute x2, starting transfers between devices, neighbours(): left = lax.ppermute(field, 'blk', [(i, i + 1) for i in range(ends)])  5.52 us
    dot_general x2, matrix products, far_field(): jnp.einsum('sakl,spql->apqk', weights, gathered, precision=lax.Precision....  4.01 us
    ppermute x5, starting transfers between devices, tree_sum(): x = x + lax.ppermute(x, axis, [(i, i ^ k) for i in range(n)])  3.17 us
    ppermute x2, starting transfers between devices, neighbours(): right = lax.ppermute(field, 'blk', [(i + 1, i) for i in range(ends)])  2.57 us
    unnamed x13, local copies, waits for them, and re-layouts  2.01 us
  transfers between devices with their start and end apart: 19, of which 13 were waited for; matrix products, arithmetic and copies ran while one was open for 12% of the time, Pallas kernels for 0%

profile of v9, /device:TPU:0, one launch (start us, length us, event | category | flops | bytes accessed | tf_op | source)
XLA Modules:
  0.0 80.8 jit_solution(9060469826148460690)
XLA Ops:
  0.7 2.5 %collective-permute-start.5 = (f32[2,4,1,512]{3,2,1,0:T(1,128)}, f32[2,4,1,512]{3,2,1,0:T(1,128)S(1)}, u32[]{:S(2)}, u32[]{:S(2)}) collective-permute-start(f32[2,4,1,512]{3,2,1,0:T(1,128)} %param.8), channel_id=1, source_target_pairs={{0,1},{1,2},{2,3},{3,4},{4,5},{5,6},{6,7},{7,8},{8,9},{9,10},{10,1... | collective-permute-start | bytes 49160 | tf_op jit(solution)/shard_map/ppermute | solution.py:57
  3.2 1.3 %collective-permute-start.6 = (f32[2,4,1,512]{3,2,1,0:T(1,128)}, f32[2,4,1,512]{3,2,1,0:T(1,128)S(1)}, u32[]{:S(2)}, u32[]{:S(2)}) collective-permute-start(f32[2,4,1,512]{3,2,1,0:T(1,128)} %param.8), channel_id=1, source_target_pairs={{1,0},{2,1},{3,2},{4,3},{5,4},{6,5},{7,6},{8,7},{9,8},{10,9},{11,1... | collective-permute-start | bytes 49160 | tf_op jit(solution)/shard_map/ppermute | solution.py:58
  4.5 0.8 %add_reduce_fusion.9 = f32[4]{0:T(128)S(1)} fusion(f32[2,4,1,512]{3,2,1,0:T(1,128)} %param.8), kind=kLoop, calls=%fused_computation.121 | loop fusion | flops 8188 | bytes 16400 | tf_op jit(solution)/shard_map/reduce_sum | solution.py:126
  5.3 0.8 pad_maximum_fusion.1
  6.1 2.4 %collective-permute-start = (f32[4100]{0:T(1024)S(1)}, f32[4100]{0:T(1024)S(1)}, u32[]{:S(2)}, u32[]{:S(2)}) collective-permute-start(f32[4100]{0:T(1024)S(1)} %pad_maximum_fusion.1), channel_id=1, source_target_pairs={{0,16},{16,0},{1,17},{17,1},{2,18},{18,2},{3,19},{19,3},{4,20},{20... | collective-permute-start | bytes 49208 | tf_op jit(solution)/shard_map/ppermute | solution.py:41
  8.4 0.7 iota_compare_fusion
  9.2 0.2 and_convert_fusion
  9.4 0.7 fusion.69
  10.0 0.8 reshape_squeeze.4
  10.8 0.8 %constant_dynamic-update-slice_fusion.1 = (f32[2,4,1,1536]{3,2,1,0:T(1,128)S(1)}, bf16[2,4,1,512]{3,2,1,0:T(2,128)(2,1)S(1)}) fusion(f32[2,4,1,1536]{3,2,1,0:T(1,128)S(1)} %constant_dynamic-update-slice_fusion.2, f32[2,4,1,512]{3,2,1,0:T(1,128)} %param.8), kind=kLoop, calls=%fused_computation.123 | loop fusion | flops 4096 | bytes 49152
  11.6 1.1 %convolution_bitcast_fusion.5 = f32[2,2,4,64]{3,2,0,1:T(4,128)S(1)} fusion(bf16[1,2,64,512]{3,2,1,0:T(8,128)(2,1)} %param.12, bf16[2,4,1,512]{3,2,1,0:T(2,128)(2,1)S(1)} %get-tuple-element.56), kind=kOutput, calls=%fused_computation.15 | convolution fusion | flops 1048576 | bytes 143360 | tf_op jit(solution)/shard_map/akr,pqr->apqk/dot_general | solution.py:68
  12.9 2.1 %collective-permute-start.1 = (f32[516]{0:T(1024)S(1)}, f32[516]{0:T(1024)S(1)}, u32[]{:S(2)}, u32[]{:S(2)}) collective-permute-start(f32[516]{0:T(1024)S(1)} %pad_maximum_fusion.10), channel_id=1, source_target_pairs={{0,1},{1,0},{2,3},{3,2},{4,5},{5,4},{6,7},{7,6},{8,9},{9,8},{10,11... | collective-permute-start | bytes 6200 | tf_op jit(solution)/shard_map/ppermute | solution.py:41
  15.0 0.8 %collective-permute-done.1 = f32[516]{0:T(1024)S(1)} collective-permute-done((f32[516]{0:T(1024)S(1)}, f32[516]{0:T(1024)S(1)}, u32[]{:S(2)}, u32[]{:S(2)}) %collective-permute-start.1) | collective-permute-done | bytes 2096 | tf_op jit(solution)/shard_map/ppermute | solution.py:41
  16.1 2.3 %collective-permute-start.2 = (f32[1028]{0:T(1024)S(1)}, f32[1028]{0:T(1024)S(1)}, u32[]{:S(2)}, u32[]{:S(2)}) collective-permute-start(f32[1028]{0:T(1024)S(1)} %pad_maximum_fusion.7), channel_id=1, source_target_pairs={{0,2},{1,3},{2,0},{3,1},{4,6},{5,7},{6,4},{7,5},{8,10},{9,11},{10,... | collective-permute-start | bytes 12344 | tf_op jit(solution)/shard_map/ppermute | solution.py:41
  18.4 1.6 %collective-permute-done.2 = f32[1028]{0:T(1024)S(1)} collective-permute-done((f32[1028]{0:T(1024)S(1)}, f32[1028]{0:T(1024)S(1)}, u32[]{:S(2)}, u32[]{:S(2)}) %collective-permute-start.2) | collective-permute-done | bytes 4144 | tf_op jit(solution)/shard_map/ppermute | solution.py:41
  20.4 3.0 %collective-permute-start.3 = (f32[2052]{0:T(1024)S(1)}, f32[2052]{0:T(1024)S(1)}, u32[]{:S(2)}, u32[]{:S(2)}) collective-permute-start(f32[2052]{0:T(1024)S(1)} %pad_maximum_fusion.5), channel_id=1, source_target_pairs={{0,4},{1,5},{2,6},{3,7},{4,0},{5,1},{6,2},{7,3},{8,12},{9,13},{10,... | collective-permute-start | bytes 24632 | tf_op jit(solution)/shard_map/ppermute | solution.py:41
  23.4 0.7 copy.181
  24.1 0.9 %collective-permute-done.3 = f32[2052]{0:T(1024)S(1)} collective-permute-done((f32[2052]{0:T(1024)S(1)}, f32[2052]{0:T(1024)S(1)}, u32[]{:S(2)}, u32[]{:S(2)}) %collective-permute-start.3) | collective-permute-done | bytes 8240 | tf_op jit(solution)/shard_map/ppermute | solution.py:41
  25.4 3.0 %collective-permute-start.4 = (f32[4100]{0:T(1024)S(1)}, f32[4100]{0:T(1024)S(1)}, u32[]{:S(2)}, u32[]{:S(2)}) collective-permute-start(f32[4100]{0:T(1024)S(1)} %pad_maximum_fusion.2), channel_id=1, source_target_pairs={{0,8},{1,9},{2,10},{3,11},{4,12},{5,13},{6,14},{7,15},{8,0},{9,1},... | collective-permute-start | bytes 49208 | tf_op jit(solution)/shard_map/ppermute | solution.py:41
  28.5 1.7 %collective-permute-done.4 = f32[4100]{0:T(1024)S(1)} collective-permute-done((f32[4100]{0:T(1024)S(1)}, f32[4100]{0:T(1024)S(1)}, u32[]{:S(2)}, u32[]{:S(2)}) %collective-permute-start.4) | collective-permute-done | bytes 16432 | tf_op jit(solution)/shard_map/ppermute | solution.py:41
  30.5 2.0 %convolution_bitcast_fusion.4 = f32[2,2,4,64]{3,2,0,1:T(4,128)S(1)} fusion(f32[1,1,16,2,64,64]{5,4,3,2,1,0:T(8,128)} %param.14, f32[16,64,64]{2,1,0:T(8,128)S(1)} %and_convert_fusion, f32[16,2,4,64]{3,2,1,0:T(4,128)S(1)} %fusion.18), kind=kOutput, calls=%fused_computation.14 | convolution fusion | flops 6422528 | bytes 823296 | tf_op jit(solution)/shard_map/sakl,spql->apqk/dot_general | solution.py:101
  32.5 0.1 convolution_bitcast_fusion.1
  32.9 0.6 gather_fusion.1
  33.5 0.2 broadcast_divide_fusion
  33.7 0.6 gather_fusion
  34.3 0.7 fusion.4
  35.1 0.1 convolution_bitcast_fusion.3
  35.4 0.2 add_reduce_fusion.8
  35.7 1.2 %collective-permute-done.7 = f32[528]{0:T(1024)S(1)} collective-permute-done((f32[528]{0:T(1024)S(1)}, f32[528]{0:T(1024)S(1)}, u32[]{:S(2)}, u32[]{:S(2)}) %collective-permute-start.7) | collective-permute-done | bytes 2144 | tf_op jit(solution)/shard_map/ppermute | solution.py:41
  37.2 0.9 %collective-permute-start.8 = (f32[1040]{0:T(1024)S(1)}, f32[1040]{0:T(1024)S(1)}, u32[]{:S(2)}, u32[]{:S(2)}) collective-permute-start(f32[1040]{0:T(1024)S(1)} %pad_maximum_fusion.8), channel_id=1, source_target_pairs={{0,2},{1,3},{2,0},{3,1},{4,6},{5,7},{6,4},{7,5},{8,10},{9,11},{10,... | collective-permute-start | bytes 12488 | tf_op jit(solution)/shard_map/ppermute | solution.py:41
  38.2 2.7 %collective-permute-done.8 = f32[1040]{0:T(1024)S(1)} collective-permute-done((f32[1040]{0:T(1024)S(1)}, f32[1040]{0:T(1024)S(1)}, u32[]{:S(2)}, u32[]{:S(2)}) %collective-permute-start.8) | collective-permute-done | bytes 4192 | tf_op jit(solution)/shard_map/ppermute | solution.py:41
  41.2 1.9 %collective-permute-start.9 = (f32[2064]{0:T(1024)S(1)}, f32[2064]{0:T(1024)S(1)}, u32[]{:S(2)}, u32[]{:S(2)}) collective-permute-start(f32[2064]{0:T(1024)S(1)} %pad_maximum_fusion.6), channel_id=1, source_target_pairs={{0,4},{1,5},{2,6},{3,7},{4,0},{5,1},{6,2},{7,3},{8,12},{9,13},{10,... | collective-permute-start | bytes 24776 | tf_op jit(solution)/shard_map/ppermute | solution.py:41
  43.1 1.8 %collective-permute-done.9 = f32[2064]{0:T(1024)S(1)} collective-permute-done((f32[2064]{0:T(1024)S(1)}, f32[2064]{0:T(1024)S(1)}, u32[]{:S(2)}, u32[]{:S(2)}) %collective-permute-start.9) | collective-permute-done | bytes 8288 | tf_op jit(solution)/shard_map/ppermute | solution.py:41
  45.2 2.9 %collective-permute-start.10 = (f32[4112]{0:T(1024)S(1)}, f32[4112]{0:T(1024)S(1)}, u32[]{:S(2)}, u32[]{:S(2)}) collective-permute-start(f32[4112]{0:T(1024)S(1)} %pad_maximum_fusion.3), channel_id=1, source_target_pairs={{0,8},{1,9},{2,10},{3,11},{4,12},{5,13},{6,14},{7,15},{8,0},{9,1},... | collective-permute-start | bytes 49352 | tf_op jit(solution)/shard_map/ppermute | solution.py:41
  48.2 1.3 %collective-permute-start.13 = (f32[2,4,1,512]{3,1,0,2:T(4,128)S(1)}, f32[2,4,1,512]{3,1,0,2:T(4,128)S(1)}, u32[]{:S(2)}, u32[]{:S(2)}) collective-permute-start(f32[2,4,1,512]{3,1,0,2:T(4,128)S(1)} %get-tuple-element.30), channel_id=1, source_target_pairs={{1,0},{2,1},{3,2},{4,3},{5,4},{6,5},{7,6},{8,7},{9,8},{10,9},{11,1... | collective-permute-start | bytes 49160 | tf_op jit(solution)/shard_map/ppermute | solution.py:58
  49.5 3.0 %collective-permute-start.12 = (f32[2,4,1,512]{3,1,0,2:T(4,128)S(1)}, f32[2,4,1,512]{3,1,0,2:T(4,128)S(1)}, u32[]{:S(2)}, u32[]{:S(2)}) collective-permute-start(f32[2,4,1,512]{3,1,0,2:T(4,128)S(1)} %get-tuple-element.30), channel_id=1, source_target_pairs={{0,1},{1,2},{2,3},{3,4},{4,5},{5,6},{6,7},{7,8},{8,9},{9,10},{10,1... | collective-permute-start | bytes 49160 | tf_op jit(solution)/shard_map/ppermute | solution.py:57
  52.8 0.5 collective-permute-start.11
  53.6 3.0 %collective-permute-done.11 = f32[4112]{0:T(1024)S(1)} collective-permute-done((f32[4112]{0:T(1024)S(1)}, f32[4112]{0:T(1024)S(1)}, u32[]{:S(2)}, u32[]{:S(2)}) %collective-permute-start.11) | collective-permute-done | bytes 16480 | tf_op jit(solution)/shard_map/ppermute | solution.py:41
  56.9 2.0 %convolution_bitcast_fusion.2 = f32[2,2,4,64]{3,2,0,1:T(4,128)S(1)} fusion(f32[1,1,16,2,64,64]{5,4,3,2,1,0:T(8,128)} %param.14, f32[16,64,64]{2,1,0:T(8,128)S(1)} %and_convert_fusion, f32[16,1,4,64]{3,2,1,0:T(4,128)S(1)} %get-tuple-element.33, f32[16,1,4,64]{3,2,1,0:T(4,128)S(1)} %get-tuple-element.32, f32[8,2,4,64]{3,2,1,0:T(4,128)S(1)} %maximum_select_fusion.4, ...), kind=kOutput, calls=%fused_computation.12 | convolution fusion | flops 6471680 | bytes 856081 | tf_op jit(solution)/shard_map/sakl,spql->apqk/dot_general | solution.py:101
  59.3 0.6 gather_fusion.3
  59.9 0.2 subtract_reduce_fusion
  60.2 0.6 gather_fusion.2
  60.8 0.7 fusion.7
  61.5 0.1 convolution_bitcast_fusion
  61.7 0.2 subtract_reduce_fusion.1
  62.0 0.6 collective-permute-start.14
  62.6 3.1 %collective-permute-done.14 = f32[8,4]{1,0:T(8,128)S(1)} collective-permute-done((f32[8,4]{1,0:T(8,128)S(1)}, f32[8,4]{1,0:T(8,128)S(1)}, u32[]{:S(2)}, u32[]{:S(2)}) %collective-permute-start.14) | collective-permute-done | bytes 160 | tf_op jit(solution)/shard_map/ppermute | solution.py:21
  65.7 1.2 %collective-permute-done.15 = f32[8,4]{1,0:T(8,128)S(1)} collective-permute-done((f32[8,4]{1,0:T(8,128)S(1)}, f32[8,4]{1,0:T(8,128)S(1)}, u32[]{:S(2)}, u32[]{:S(2)}) %collective-permute-start.15) | collective-permute-done | bytes 160 | tf_op jit(solution)/shard_map/ppermute | solution.py:21
  66.9 0.6 collective-permute-start.16
  67.5 0.1 copy.96
  67.6 0.6 copy.105
  68.2 2.3 %collective-permute-done.16 = f32[8,4]{1,0:T(8,128)S(1)} collective-permute-done((f32[8,4]{1,0:T(8,128)S(1)}, f32[8,4]{1,0:T(8,128)S(1)}, u32[]{:S(2)}, u32[]{:S(2)}) %collective-permute-start.16) | collective-permute-done | bytes 160 | tf_op jit(solution)/shard_map/ppermute | solution.py:21
  70.5 1.7 %collective-permute-start.17 = (f32[8,4]{1,0:T(8,128)S(1)}, f32[8,4]{1,0:T(8,128)S(1)}, u32[]{:S(2)}, u32[]{:S(2)}) collective-permute-start(f32[8,4]{1,0:T(8,128)S(1)} %add.551), channel_id=1, source_target_pairs={{0,4},{1,5},{2,6},{3,7},{4,0},{5,1},{6,2},{7,3},{8,12},{9,13},{10,... | collective-permute-start | bytes 392 | tf_op jit(solution)/shard_map/ppermute | solution.py:21
  72.2 0.1 copy.97
  72.3 1.8 %collective-permute-done.17 = f32[8,4]{1,0:T(8,128)S(1)} collective-permute-done((f32[8,4]{1,0:T(8,128)S(1)}, f32[8,4]{1,0:T(8,128)S(1)}, u32[]{:S(2)}, u32[]{:S(2)}) %collective-permute-start.17) | collective-permute-done | bytes 160 | tf_op jit(solution)/shard_map/ppermute | solution.py:21
  74.1 0.3 collective-permute-start.18
  74.4 0.1 copy.98
  74.5 4.1 %collective-permute-done.18 = f32[8,4]{1,0:T(8,128)S(1)} collective-permute-done((f32[8,4]{1,0:T(8,128)S(1)}, f32[8,4]{1,0:T(8,128)S(1)}, u32[]{:S(2)}, u32[]{:S(2)}) %collective-permute-start.18) | collective-permute-done | bytes 160 | tf_op jit(solution)/shard_map/ppermute | solution.py:21
  78.9 0.6 copy.106
  79.5 0.1 copy.99
  79.6 0.1 copy.100
  79.7 0.1 copy.101
  79.8 0.1 copy.102
  80.1 0.7 stack.153
  (136 shorter events, 5.1 us)
Async XLA Ops:
  0.6 33.7 %copy-start = (bf16[1,2,4,2,256,256]{5,4,3,2,1,0:T(8,128)(2,1)S(1)}, bf16[1,2,4,2,256,256]{5,4,3,2,1,0:T(8,128)(2,1)}, u32[]{:S(2)}) copy-start(bf16[1,2,4,2,256,256]{5,4,3,2,1,0:T(8,128)(2,1)} %param.9) | copy-start | bytes 6291460
  0.6 31.9 %copy-start.2 = (bf16[1,2,64,512]{3,2,1,0:T(8,128)(2,1)S(1)}, bf16[1,2,64,512]{3,2,1,0:T(8,128)(2,1)}, u32[]{:S(2)}) copy-start(bf16[1,2,64,512]{3,2,1,0:T(8,128)(2,1)} %param.13) | copy-start | bytes 393220
  0.7 10.1 %collective-permute-start.5 = (f32[2,4,1,512]{3,2,1,0:T(1,128)}, f32[2,4,1,512]{3,2,1,0:T(1,128)S(1)}, u32[]{:S(2)}, u32[]{:S(2)}) collective-permute-start(f32[2,4,1,512]{3,2,1,0:T(1,128)} %param.8), channel_id=1, source_target_pairs={{0,1},{1,2},{2,3},{3,4},{4,5},{5,6},{6,7},{7,8},{8,9},{9,10},{10,1... | collective-permute-start | bytes 49160 | tf_op jit(solution)/shard_map/ppermute | solution.py:57
  3.2 25.3 %collective-permute-start.6 = (f32[2,4,1,512]{3,2,1,0:T(1,128)}, f32[2,4,1,512]{3,2,1,0:T(1,128)S(1)}, u32[]{:S(2)}, u32[]{:S(2)}) collective-permute-start(f32[2,4,1,512]{3,2,1,0:T(1,128)} %param.8), channel_id=1, source_target_pairs={{1,0},{2,1},{3,2},{4,3},{5,4},{6,5},{7,6},{8,7},{9,8},{10,9},{11,1... | collective-permute-start | bytes 49160 | tf_op jit(solution)/shard_map/ppermute | solution.py:58
  6.1 6.7 %collective-permute-start = (f32[4100]{0:T(1024)S(1)}, f32[4100]{0:T(1024)S(1)}, u32[]{:S(2)}, u32[]{:S(2)}) collective-permute-start(f32[4100]{0:T(1024)S(1)} %pad_maximum_fusion.1), channel_id=1, source_target_pairs={{0,16},{16,0},{1,17},{17,1},{2,18},{18,2},{3,19},{19,3},{4,20},{20... | collective-permute-start | bytes 49208 | tf_op jit(solution)/shard_map/ppermute | solution.py:41
  12.9 3.0 %collective-permute-start.1 = (f32[516]{0:T(1024)S(1)}, f32[516]{0:T(1024)S(1)}, u32[]{:S(2)}, u32[]{:S(2)}) collective-permute-start(f32[516]{0:T(1024)S(1)} %pad_maximum_fusion.10), channel_id=1, source_target_pairs={{0,1},{1,0},{2,3},{3,2},{4,5},{5,4},{6,7},{7,6},{8,9},{9,8},{10,11... | collective-permute-start | bytes 6200 | tf_op jit(solution)/shard_map/ppermute | solution.py:41
  16.1 3.9 %collective-permute-start.2 = (f32[1028]{0:T(1024)S(1)}, f32[1028]{0:T(1024)S(1)}, u32[]{:S(2)}, u32[]{:S(2)}) collective-permute-start(f32[1028]{0:T(1024)S(1)} %pad_maximum_fusion.7), channel_id=1, source_target_pairs={{0,2},{1,3},{2,0},{3,1},{4,6},{5,7},{6,4},{7,5},{8,10},{9,11},{10,... | collective-permute-start | bytes 12344 | tf_op jit(solution)/shard_map/ppermute | solution.py:41
  20.4 4.7 %collective-permute-start.3 = (f32[2052]{0:T(1024)S(1)}, f32[2052]{0:T(1024)S(1)}, u32[]{:S(2)}, u32[]{:S(2)}) collective-permute-start(f32[2052]{0:T(1024)S(1)} %pad_maximum_fusion.5), channel_id=1, source_target_pairs={{0,4},{1,5},{2,6},{3,7},{4,0},{5,1},{6,2},{7,3},{8,12},{9,13},{10,... | collective-permute-start | bytes 24632 | tf_op jit(solution)/shard_map/ppermute | solution.py:41
  25.4 4.8 %collective-permute-start.4 = (f32[4100]{0:T(1024)S(1)}, f32[4100]{0:T(1024)S(1)}, u32[]{:S(2)}, u32[]{:S(2)}) collective-permute-start(f32[4100]{0:T(1024)S(1)} %pad_maximum_fusion.2), channel_id=1, source_target_pairs={{0,8},{1,9},{2,10},{3,11},{4,12},{5,13},{6,14},{7,15},{8,0},{9,1},... | collective-permute-start | bytes 49208 | tf_op jit(solution)/shard_map/ppermute | solution.py:41
  30.5 4.6 %copy-start.3 = (f32[2,4,1,512]{3,2,1,0:T(1,128)S(1)}, f32[2,4,1,512]{3,2,1,0:T(1,128)}, u32[]{:S(2)}) copy-start(f32[2,4,1,512]{3,2,1,0:T(1,128)} %param.8) | copy-start | bytes 49156
  30.5 4.6 %copy-start.1 = (bf16[1,2,64,512]{3,2,1,0:T(8,128)(2,1)S(1)}, bf16[1,2,64,512]{3,2,1,0:T(8,128)(2,1)}, u32[]{:S(2)}) copy-start(bf16[1,2,64,512]{3,2,1,0:T(8,128)(2,1)} %param.12) | copy-start | bytes 393220
  35.7 1.2 %collective-permute-start.7 = (f32[528]{0:T(1024)S(1)}, f32[528]{0:T(1024)S(1)}, u32[]{:S(2)}, u32[]{:S(2)}) collective-permute-start(f32[528]{0:T(1024)S(1)} %pad_maximum_fusion.12), channel_id=1, source_target_pairs={{0,1},{1,0},{2,3},{3,2},{4,5},{5,4},{6,7},{7,6},{8,9},{9,8},{10,11... | collective-permute-start | bytes 6344 | tf_op jit(solution)/shard_map/ppermute | solution.py:41
  37.2 3.7 %collective-permute-start.8 = (f32[1040]{0:T(1024)S(1)}, f32[1040]{0:T(1024)S(1)}, u32[]{:S(2)}, u32[]{:S(2)}) collective-permute-start(f32[1040]{0:T(1024)S(1)} %pad_maximum_fusion.8), channel_id=1, source_target_pairs={{0,2},{1,3},{2,0},{3,1},{4,6},{5,7},{6,4},{7,5},{8,10},{9,11},{10,... | collective-permute-start | bytes 12488 | tf_op jit(solution)/shard_map/ppermute | solution.py:41
  41.2 3.7 %collective-permute-start.9 = (f32[2064]{0:T(1024)S(1)}, f32[2064]{0:T(1024)S(1)}, u32[]{:S(2)}, u32[]{:S(2)}) collective-permute-start(f32[2064]{0:T(1024)S(1)} %pad_maximum_fusion.6), channel_id=1, source_target_pairs={{0,4},{1,5},{2,6},{3,7},{4,0},{5,1},{6,2},{7,3},{8,12},{9,13},{10,... | collective-permute-start | bytes 24776 | tf_op jit(solution)/shard_map/ppermute | solution.py:41
  45.2 7.5 %collective-permute-start.10 = (f32[4112]{0:T(1024)S(1)}, f32[4112]{0:T(1024)S(1)}, u32[]{:S(2)}, u32[]{:S(2)}) collective-permute-start(f32[4112]{0:T(1024)S(1)} %pad_maximum_fusion.3), channel_id=1, source_target_pairs={{0,8},{1,9},{2,10},{3,11},{4,12},{5,13},{6,14},{7,15},{8,0},{9,1},... | collective-permute-start | bytes 49352 | tf_op jit(solution)/shard_map/ppermute | solution.py:41
  48.2 5.2 %collective-permute-start.13 = (f32[2,4,1,512]{3,1,0,2:T(4,128)S(1)}, f32[2,4,1,512]{3,1,0,2:T(4,128)S(1)}, u32[]{:S(2)}, u32[]{:S(2)}) collective-permute-start(f32[2,4,1,512]{3,1,0,2:T(4,128)S(1)} %get-tuple-element.30), channel_id=1, source_target_pairs={{1,0},{2,1},{3,2},{4,3},{5,4},{6,5},{7,6},{8,7},{9,8},{10,9},{11,1... | collective-permute-start | bytes 49160 | tf_op jit(solution)/shard_map/ppermute | solution.py:58
  49.5 3.9 %collective-permute-start.12 = (f32[2,4,1,512]{3,1,0,2:T(4,128)S(1)}, f32[2,4,1,512]{3,1,0,2:T(4,128)S(1)}, u32[]{:S(2)}, u32[]{:S(2)}) collective-permute-start(f32[2,4,1,512]{3,1,0,2:T(4,128)S(1)} %get-tuple-element.30), channel_id=1, source_target_pairs={{0,1},{1,2},{2,3},{3,4},{4,5},{5,6},{6,7},{7,8},{8,9},{9,10},{10,1... | collective-permute-start | bytes 49160 | tf_op jit(solution)/shard_map/ppermute | solution.py:57
  52.8 3.8 %collective-permute-start.11 = (f32[4112]{0:T(1024)S(1)}, f32[4112]{0:T(1024)S(1)}, u32[]{:S(2)}, u32[]{:S(2)}) collective-permute-start(f32[4112]{0:T(1024)S(1)} %pad_maximum_fusion.4), channel_id=1, source_target_pairs={{0,16},{16,0},{1,17},{17,1},{2,18},{18,2},{3,19},{19,3},{4,20},{20... | collective-permute-start | bytes 49352 | tf_op jit(solution)/shard_map/ppermute | solution.py:41
  62.0 3.7 %collective-permute-start.14 = (f32[8,4]{1,0:T(8,128)S(1)}, f32[8,4]{1,0:T(8,128)S(1)}, u32[]{:S(2)}, u32[]{:S(2)}) collective-permute-start(f32[8,4]{1,0:T(8,128)S(1)} %concatenate.157), channel_id=1, source_target_pairs={{0,16},{16,0},{1,17},{17,1},{2,18},{18,2},{3,19},{19,3},{4,20},{20... | collective-permute-start | bytes 392 | tf_op jit(solution)/shard_map/ppermute | solution.py:21
  65.7 1.2 %collective-permute-start.15 = (f32[8,4]{1,0:T(8,128)S(1)}, f32[8,4]{1,0:T(8,128)S(1)}, u32[]{:S(2)}, u32[]{:S(2)}) collective-permute-start(f32[8,4]{1,0:T(8,128)S(1)} %add.549), channel_id=1, source_target_pairs={{0,1},{1,0},{2,3},{3,2},{4,5},{5,4},{6,7},{7,6},{8,9},{9,8},{10,11... | collective-permute-start | bytes 392 | tf_op jit(solution)/shard_map/ppermute | solution.py:21
  66.9 3.6 %collective-permute-start.16 = (f32[8,4]{1,0:T(8,128)S(1)}, f32[8,4]{1,0:T(8,128)S(1)}, u32[]{:S(2)}, u32[]{:S(2)}) collective-permute-start(f32[8,4]{1,0:T(8,128)S(1)} %add.550), channel_id=1, source_target_pairs={{0,2},{1,3},{2,0},{3,1},{4,6},{5,7},{6,4},{7,5},{8,10},{9,11},{10,... | collective-permute-start | bytes 392 | tf_op jit(solution)/shard_map/ppermute | solution.py:21
  70.5 3.6 %collective-permute-start.17 = (f32[8,4]{1,0:T(8,128)S(1)}, f32[8,4]{1,0:T(8,128)S(1)}, u32[]{:S(2)}, u32[]{:S(2)}) collective-permute-start(f32[8,4]{1,0:T(8,128)S(1)} %add.551), channel_id=1, source_target_pairs={{0,4},{1,5},{2,6},{3,7},{4,0},{5,1},{6,2},{7,3},{8,12},{9,13},{10,... | collective-permute-start | bytes 392 | tf_op jit(solution)/shard_map/ppermute | solution.py:21
  74.1 4.5 %collective-permute-start.18 = (f32[8,4]{1,0:T(8,128)S(1)}, f32[8,4]{1,0:T(8,128)S(1)}, u32[]{:S(2)}, u32[]{:S(2)}) collective-permute-start(f32[8,4]{1,0:T(8,128)S(1)} %add.552), channel_id=1, source_target_pairs={{0,8},{1,9},{2,10},{3,11},{4,12},{5,13},{6,14},{7,15},{8,0},{9,1},... | collective-permute-start | bytes 392 | tf_op jit(solution)/shard_map/ppermute | solution.py:21

commit v10 on v9

--- a/solution.py
+++ b/solution.py
@@ -23,7 +23,7 @@
     return x
 
 
-def tree_collect(red, gat_blk, gat_dom, dom_first=False):
+def tree_collect(red, gat_blk, gat_dom, dom_first=False, halo=None):
     rounds = (("blk", gat_blk), ("dom", gat_dom))
     if dom_first:
         rounds = rounds[::-1]
@@ -38,6 +38,9 @@
             k = 1
             while k < n:
                 packed = jnp.concatenate([red.reshape(-1), buf.reshape(-1)])
+                if halo is not None and axis == "blk" and k == 2:
+                    packed, halo = lax.optimization_barrier((packed, halo))
+                    halo = neighbours(halo)
                 got = lax.ppermute(packed, axis, [(i, i ^ k) for i in range(n)])
                 red = red + got[: red.size].reshape(red.shape)
                 other = got[red.size :].reshape(buf.shape)
@@ -48,6 +51,8 @@
             gat_blk = buf
         else:
             gat_dom = buf
+    if halo is not None:
+        return red, gat_blk, gat_dom, halo
     return red, gat_blk, gat_dom
 
 
@@ -153,12 +158,12 @@
     def spread(every):
         return jnp.moveaxis(every, 0, 2)
 
-    window_rhs = neighbours(right_side)
-    start_sum, coef_rhs, every_rhs = tree_collect(
+    start_sum, coef_rhs, every_rhs, window_rhs = tree_collect(
         local_squares(right_side),
         coefficients(right_side, source_basis),
         right_side[:, :, 0],
         dom_first=True,
+        halo=right_side,
     )
     beta = jnp.sqrt(start_sum / total + EPSILON)
     inv_scale = beta[None, :, None, None]

time: 81.5 us -> 80.1 us (0.983)
  starting transfers between devices: 30.3 us -> 26.8 us
  waiting for transfers between devices: 26.2 us -> 27.6 us
    ppermute x5, starting transfers between devices: 3.17 us -> 1.93 us  [tree_sum(): x = x + lax.ppermute(x, axis, [(i, i ^ k) for i in range(n)])]
    ppermute x5, waiting for transfers between devices: 12.5 us -> 13.7 us  [tree_sum(): x = x + lax.ppermute(x, axis, [(i, i ^ k) for i in range(n)])]
    ppermute x2, starting transfers between devices: 5.52 us -> 4.32 us  [neighbours(): left = lax.ppermute(field, 'blk', [(i, i + 1) for i in range(ends)])]
    ppermute x10, starting transfers between devices: 19.1 us -> 17.9 us  [tree_collect(): got = lax.ppermute(packed, axis, [(i, i ^ k) for i in range(n)])]
    unnamed x13 -> x14, local copies, waits for them, and re-layouts: 2.01 us -> 2.74 us
  transfers between devices with their start and end apart: 19 -> 19, of which waited for: 13 -> 12; matrix products, arithmetic and copies ran while one was open for 12% -> 10% of each run, Pallas kernels for 0% -> 0%
where the time goes in v10:
time: 80.1 us; the launch traced here: 79.4 us
  waiting for transfers between devices  27.6 us (34%)
  starting transfers between devices  26.8 us (33%)
  local copies, waits for them, and re-layouts  10.1 us (13%)
  other arithmetic  6.98 us (9%)
  matrix products  6.81 us (9%)
  between operations  1.12 us (1%)
    ppermute x10, starting transfers between devices, tree_collect(): got = lax.ppermute(packed, axis, [(i, i ^ k) for i in range(n)])  17.9 us
    ppermute x10, waiting for transfers between devices, tree_collect(): got = lax.ppermute(packed, axis, [(i, i ^ k) for i in range(n)])  13.8 us
    ppermute x5, waiting for transfers between devices, tree_sum(): x = x + lax.ppermute(x, axis, [(i, i ^ k) for i in range(n)])  13.7 us
    ppermute x2, starting transfers between devices, neighbours(): left = lax.ppermute(field, 'blk', [(i, i + 1) for i in range(ends)])  4.32 us
    dot_general x2, matrix products, far_field(): jnp.einsum('sakl,spql->apqk', weights, gathered, precision=lax.Precision....  4.01 us
    unnamed x14, local copies, waits for them, and re-layouts  2.74 us
    ppermute x2, starting transfers between devices, neighbours(): right = lax.ppermute(field, 'blk', [(i + 1, i) for i in range(ends)])  2.57 us
    ppermute x5, starting transfers between devices, tree_sum(): x = x + lax.ppermute(x, axis, [(i, i ^ k) for i in range(n)])  1.93 us
  transfers between devices with their start and end apart: 19, of which 12 were waited for; matrix products, arithmetic and copies ran while one was open for 10% of the time, Pallas kernels for 0%

profile of v10, /device:TPU:0, one launch (start us, length us, event | category | flops | bytes accessed | tf_op | source)
XLA Modules:
  0.0 79.4 jit_solution(7433403946724252961)
XLA Ops:
  0.7 1.0 %add_reduce_fusion.9 = f32[4]{0:T(128)S(1)} fusion(f32[2,4,1,512]{3,2,1,0:T(1,128)} %param.8), kind=kLoop, calls=%fused_computation.121 | loop fusion | flops 8188 | bytes 16400 | tf_op jit(solution)/shard_map/reduce_sum | solution.py:131
  1.7 0.8 pad_maximum_fusion.1
  2.4 3.0 %collective-permute-start = (f32[4100]{0:T(1024)S(1)}, f32[4100]{0:T(1024)S(1)}, u32[]{:S(2)}, u32[]{:S(2)}) collective-permute-start(f32[4100]{0:T(1024)S(1)} %pad_maximum_fusion.1), channel_id=1, source_target_pairs={{0,16},{16,0},{1,17},{17,1},{2,18},{18,2},{3,19},{19,3},{4,20},{20... | collective-permute-start | bytes 49208 | tf_op jit(solution)/shard_map/ppermute | solution.py:44
  5.4 0.7 convert_element_type.28
  6.1 1.1 %convolution_bitcast_fusion.5 = f32[2,2,4,64]{3,2,0,1:T(4,128)S(1)} fusion(bf16[1,2,64,512]{3,2,1,0:T(8,128)(2,1)} %param.12, bf16[2,4,1,512]{3,2,1,0:T(2,128)(2,1)S(1)} %convert_element_type.28), kind=kOutput, calls=%fused_computation.15 | convolution fusion | flops 1048576 | bytes 143360 | tf_op jit(solution)/shard_map/akr,pqr->apqk/dot_general | solution.py:73
  7.2 0.7 fusion.69
  7.9 0.7 iota_compare_fusion
  8.6 0.2 and_convert_fusion
  8.9 0.8 reshape_squeeze.4
  9.8 1.1 %collective-permute-done.1 = f32[516]{0:T(1024)S(1)} collective-permute-done((f32[516]{0:T(1024)S(1)}, f32[516]{0:T(1024)S(1)}, u32[]{:S(2)}, u32[]{:S(2)}) %collective-permute-start.1) | collective-permute-done | bytes 2096 | tf_op jit(solution)/shard_map/ppermute | solution.py:44
  11.3 1.5 %collective-permute-start.2 = (f32[1028]{0:T(1024)S(1)}, f32[1028]{0:T(1024)S(1)}, u32[]{:S(2)}, u32[]{:S(2)}) collective-permute-start(f32[1028]{0:T(1024)S(1)} %pad_maximum_fusion.7), channel_id=1, source_target_pairs={{0,2},{1,3},{2,0},{3,1},{4,6},{5,7},{6,4},{7,5},{8,10},{9,11},{10,... | collective-permute-start | bytes 12344 | tf_op jit(solution)/shard_map/ppermute | solution.py:44
  12.8 2.2 %collective-permute-done.2 = f32[1028]{0:T(1024)S(1)} collective-permute-done((f32[1028]{0:T(1024)S(1)}, f32[1028]{0:T(1024)S(1)}, u32[]{:S(2)}, u32[]{:S(2)}) %collective-permute-start.2) | collective-permute-done | bytes 4144 | tf_op jit(solution)/shard_map/ppermute | solution.py:44
  15.2 1.6 %collective-permute-start.3 = (f32[2052]{0:T(1024)S(1)}, f32[2052]{0:T(1024)S(1)}, u32[]{:S(2)}, u32[]{:S(2)}) collective-permute-start(f32[2052]{0:T(1024)S(1)} %pad_maximum_fusion.5), channel_id=1, source_target_pairs={{0,4},{1,5},{2,6},{3,7},{4,0},{5,1},{6,2},{7,3},{8,12},{9,13},{10,... | collective-permute-start | bytes 24632 | tf_op jit(solution)/shard_map/ppermute | solution.py:44
  16.8 0.7 copy.181
  17.6 1.3 %collective-permute-start.5 = (f32[2,4,1,512]{3,2,1,0:T(1,128)}, f32[2,4,1,512]{3,2,1,0:T(1,128)S(1)}, u32[]{:S(2)}, u32[]{:S(2)}) collective-permute-start(f32[2,4,1,512]{3,2,1,0:T(1,128)} %param.8), channel_id=1, source_target_pairs={{0,1},{1,2},{2,3},{3,4},{4,5},{5,6},{6,7},{7,8},{8,9},{9,10},{10,1... | collective-permute-start | bytes 49160 | tf_op jit(solution)/shard_map/ppermute | solution.py:62
  18.9 1.3 %collective-permute-start.6 = (f32[2,4,1,512]{3,2,1,0:T(1,128)}, f32[2,4,1,512]{3,2,1,0:T(1,128)S(1)}, u32[]{:S(2)}, u32[]{:S(2)}) collective-permute-start(f32[2,4,1,512]{3,2,1,0:T(1,128)} %param.8), channel_id=1, source_target_pairs={{1,0},{2,1},{3,2},{4,3},{5,4},{6,5},{7,6},{8,7},{9,8},{10,9},{11,1... | collective-permute-start | bytes 49160 | tf_op jit(solution)/shard_map/ppermute | solution.py:63
  20.6 6.5 %collective-permute-start.4 = (f32[4100]{0:T(1024)S(1)}, f32[4100]{0:T(1024)S(1)}, u32[]{:S(2)}, u32[]{:S(2)}) collective-permute-start(f32[4100]{0:T(1024)S(1)} %pad_maximum_fusion.2), channel_id=1, source_target_pairs={{0,8},{1,9},{2,10},{3,11},{4,12},{5,13},{6,14},{7,15},{8,0},{9,1},... | collective-permute-start | bytes 49208 | tf_op jit(solution)/shard_map/ppermute | solution.py:44
  27.1 0.7 constant_dynamic-update-slice_fusion.1
  27.8 1.0 %collective-permute-done.4 = f32[4100]{0:T(1024)S(1)} collective-permute-done((f32[4100]{0:T(1024)S(1)}, f32[4100]{0:T(1024)S(1)}, u32[]{:S(2)}, u32[]{:S(2)}) %collective-permute-start.4) | collective-permute-done | bytes 16432 | tf_op jit(solution)/shard_map/ppermute | solution.py:44
  29.1 2.0 %convolution_bitcast_fusion.4 = f32[2,2,4,64]{3,2,0,1:T(4,128)S(1)} fusion(f32[1,1,16,2,64,64]{5,4,3,2,1,0:T(8,128)} %param.14, f32[16,64,64]{2,1,0:T(8,128)S(1)} %and_convert_fusion, f32[16,2,4,64]{3,2,1,0:T(4,128)S(1)} %fusion.18), kind=kOutput, calls=%fused_computation.14 | convolution fusion | flops 6422528 | bytes 823296 | tf_op jit(solution)/shard_map/sakl,spql->apqk/dot_general | solution.py:106
  31.2 0.1 convolution_bitcast_fusion.1
  31.5 0.6 gather_fusion.1
  32.1 0.2 broadcast_divide_fusion
  32.4 0.6 gather_fusion
  33.0 0.7 fusion.4
  33.8 0.1 convolution_bitcast_fusion.3
  34.0 0.2 add_reduce_fusion.8
  34.4 1.2 %collective-permute-done.7 = f32[528]{0:T(1024)S(1)} collective-permute-done((f32[528]{0:T(1024)S(1)}, f32[528]{0:T(1024)S(1)}, u32[]{:S(2)}, u32[]{:S(2)}) %collective-permute-start.7) | collective-permute-done | bytes 2144 | tf_op jit(solution)/shard_map/ppermute | solution.py:44
  35.9 1.2 %collective-permute-start.8 = (f32[1040]{0:T(1024)S(1)}, f32[1040]{0:T(1024)S(1)}, u32[]{:S(2)}, u32[]{:S(2)}) collective-permute-start(f32[1040]{0:T(1024)S(1)} %pad_maximum_fusion.8), channel_id=1, source_target_pairs={{0,2},{1,3},{2,0},{3,1},{4,6},{5,7},{6,4},{7,5},{8,10},{9,11},{10,... | collective-permute-start | bytes 12488 | tf_op jit(solution)/shard_map/ppermute | solution.py:44
  37.1 2.4 %collective-permute-done.8 = f32[1040]{0:T(1024)S(1)} collective-permute-done((f32[1040]{0:T(1024)S(1)}, f32[1040]{0:T(1024)S(1)}, u32[]{:S(2)}, u32[]{:S(2)}) %collective-permute-start.8) | collective-permute-done | bytes 4192 | tf_op jit(solution)/shard_map/ppermute | solution.py:44
  39.8 0.8 collective-permute-start.9
  40.6 2.9 %collective-permute-done.9 = f32[2064]{0:T(1024)S(1)} collective-permute-done((f32[2064]{0:T(1024)S(1)}, f32[2064]{0:T(1024)S(1)}, u32[]{:S(2)}, u32[]{:S(2)}) %collective-permute-start.9) | collective-permute-done | bytes 8288 | tf_op jit(solution)/shard_map/ppermute | solution.py:44
  43.9 2.9 %collective-permute-start.10 = (f32[4112]{0:T(1024)S(1)}, f32[4112]{0:T(1024)S(1)}, u32[]{:S(2)}, u32[]{:S(2)}) collective-permute-start(f32[4112]{0:T(1024)S(1)} %pad_maximum_fusion.3), channel_id=1, source_target_pairs={{0,8},{1,9},{2,10},{3,11},{4,12},{5,13},{6,14},{7,15},{8,0},{9,1},... | collective-permute-start | bytes 49352 | tf_op jit(solution)/shard_map/ppermute | solution.py:44
  46.8 1.3 %collective-permute-start.13 = (f32[2,4,1,512]{3,1,0,2:T(4,128)S(1)}, f32[2,4,1,512]{3,1,0,2:T(4,128)S(1)}, u32[]{:S(2)}, u32[]{:S(2)}) collective-permute-start(f32[2,4,1,512]{3,1,0,2:T(4,128)S(1)} %get-tuple-element.34), channel_id=1, source_target_pairs={{1,0},{2,1},{3,2},{4,3},{5,4},{6,5},{7,6},{8,7},{9,8},{10,9},{11,1... | collective-permute-start | bytes 49160 | tf_op jit(solution)/shard_map/ppermute | solution.py:63
  48.1 3.0 %collective-permute-start.12 = (f32[2,4,1,512]{3,1,0,2:T(4,128)S(1)}, f32[2,4,1,512]{3,1,0,2:T(4,128)S(1)}, u32[]{:S(2)}, u32[]{:S(2)}) collective-permute-start(f32[2,4,1,512]{3,1,0,2:T(4,128)S(1)} %get-tuple-element.34), channel_id=1, source_target_pairs={{0,1},{1,2},{2,3},{3,4},{4,5},{5,6},{6,7},{7,8},{8,9},{9,10},{10,1... | collective-permute-start | bytes 49160 | tf_op jit(solution)/shard_map/ppermute | solution.py:62
  51.5 0.5 collective-permute-start.11
  52.2 3.0 %collective-permute-done.11 = f32[4112]{0:T(1024)S(1)} collective-permute-done((f32[4112]{0:T(1024)S(1)}, f32[4112]{0:T(1024)S(1)}, u32[]{:S(2)}, u32[]{:S(2)}) %collective-permute-start.11) | collective-permute-done | bytes 16480 | tf_op jit(solution)/shard_map/ppermute | solution.py:44
  55.5 2.0 %convolution_bitcast_fusion.2 = f32[2,2,4,64]{3,2,0,1:T(4,128)S(1)} fusion(f32[1,1,16,2,64,64]{5,4,3,2,1,0:T(8,128)} %param.14, f32[16,64,64]{2,1,0:T(8,128)S(1)} %and_convert_fusion, f32[16,1,4,64]{3,2,1,0:T(4,128)S(1)} %get-tuple-element.37, f32[16,1,4,64]{3,2,1,0:T(4,128)S(1)} %get-tuple-element.36, f32[8,2,4,64]{3,2,1,0:T(4,128)S(1)} %maximum_select_fusion.4, ...), kind=kOutput, calls=%fused_computation.12 | convolution fusion | flops 6471680 | bytes 856081 | tf_op jit(solution)/shard_map/sakl,spql->apqk/dot_general | solution.py:106
  57.9 0.6 gather_fusion.3
  58.5 0.2 subtract_reduce_fusion
  58.9 0.6 gather_fusion.2
  59.4 0.7 fusion.7
  60.1 0.1 convolution_bitcast_fusion
  60.4 0.2 subtract_reduce_fusion.1
  60.7 0.6 collective-permute-start.14
  61.2 3.1 %collective-permute-done.14 = f32[8,4]{1,0:T(8,128)S(1)} collective-permute-done((f32[8,4]{1,0:T(8,128)S(1)}, f32[8,4]{1,0:T(8,128)S(1)}, u32[]{:S(2)}, u32[]{:S(2)}) %collective-permute-start.14) | collective-permute-done | bytes 160 | tf_op jit(solution)/shard_map/ppermute | solution.py:21
  64.3 1.2 %collective-permute-done.15 = f32[8,4]{1,0:T(8,128)S(1)} collective-permute-done((f32[8,4]{1,0:T(8,128)S(1)}, f32[8,4]{1,0:T(8,128)S(1)}, u32[]{:S(2)}, u32[]{:S(2)}) %collective-permute-start.15) | collective-permute-done | bytes 160 | tf_op jit(solution)/shard_map/ppermute | solution.py:21
  65.5 0.8 collective-permute-start.16
  66.3 0.1 copy.96
  66.4 0.6 copy.105
  67.0 2.1 %collective-permute-done.16 = f32[8,4]{1,0:T(8,128)S(1)} collective-permute-done((f32[8,4]{1,0:T(8,128)S(1)}, f32[8,4]{1,0:T(8,128)S(1)}, u32[]{:S(2)}, u32[]{:S(2)}) %collective-permute-start.16) | collective-permute-done | bytes 160 | tf_op jit(solution)/shard_map/ppermute | solution.py:21
  69.1 0.5 collective-permute-start.17
  69.6 0.1 copy.97
  69.7 3.1 %collective-permute-done.17 = f32[8,4]{1,0:T(8,128)S(1)} collective-permute-done((f32[8,4]{1,0:T(8,128)S(1)}, f32[8,4]{1,0:T(8,128)S(1)}, u32[]{:S(2)}, u32[]{:S(2)}) %collective-permute-start.17) | collective-permute-done | bytes 160 | tf_op jit(solution)/shard_map/ppermute | solution.py:21
  72.7 0.1 collective-permute-start.18
  72.8 0.1 copy.98
  72.9 4.3 %collective-permute-done.18 = f32[8,4]{1,0:T(8,128)S(1)} collective-permute-done((f32[8,4]{1,0:T(8,128)S(1)}, f32[8,4]{1,0:T(8,128)S(1)}, u32[]{:S(2)}, u32[]{:S(2)}) %collective-permute-start.18) | collective-permute-done | bytes 160 | tf_op jit(solution)/shard_map/ppermute | solution.py:21
  77.5 0.6 copy.106
  78.1 0.1 copy.99
  78.2 0.1 copy.100
  78.3 0.1 copy.101
  78.4 0.1 copy.102
  78.5 0.1 copy.103
  78.7 0.7 stack.153
  (137 shorter events, 5.1 us)
Async XLA Ops:
  0.6 32.3 %copy-start = (bf16[1,2,4,2,256,256]{5,4,3,2,1,0:T(8,128)(2,1)S(1)}, bf16[1,2,4,2,256,256]{5,4,3,2,1,0:T(8,128)(2,1)}, u32[]{:S(2)}) copy-start(bf16[1,2,4,2,256,256]{5,4,3,2,1,0:T(8,128)(2,1)} %param.9) | copy-start | bytes 6291460
  0.6 30.5 %copy-start.3 = (bf16[1,2,64,512]{3,2,1,0:T(8,128)(2,1)S(1)}, bf16[1,2,64,512]{3,2,1,0:T(8,128)(2,1)}, u32[]{:S(2)}) copy-start(bf16[1,2,64,512]{3,2,1,0:T(8,128)(2,1)} %param.13) | copy-start | bytes 393220
  2.4 7.2 %collective-permute-start = (f32[4100]{0:T(1024)S(1)}, f32[4100]{0:T(1024)S(1)}, u32[]{:S(2)}, u32[]{:S(2)}) collective-permute-start(f32[4100]{0:T(1024)S(1)} %pad_maximum_fusion.1), channel_id=1, source_target_pairs={{0,16},{16,0},{1,17},{17,1},{2,18},{18,2},{3,19},{19,3},{4,20},{20... | collective-permute-start | bytes 49208 | tf_op jit(solution)/shard_map/ppermute | solution.py:44
  9.8 1.2 %collective-permute-start.1 = (f32[516]{0:T(1024)S(1)}, f32[516]{0:T(1024)S(1)}, u32[]{:S(2)}, u32[]{:S(2)}) collective-permute-start(f32[516]{0:T(1024)S(1)} %pad_maximum_fusion.10), channel_id=1, source_target_pairs={{0,1},{1,0},{2,3},{3,2},{4,5},{5,4},{6,7},{7,6},{8,9},{9,8},{10,11... | collective-permute-start | bytes 6200 | tf_op jit(solution)/shard_map/ppermute | solution.py:44
  11.3 3.7 %collective-permute-start.2 = (f32[1028]{0:T(1024)S(1)}, f32[1028]{0:T(1024)S(1)}, u32[]{:S(2)}, u32[]{:S(2)}) collective-permute-start(f32[1028]{0:T(1024)S(1)} %pad_maximum_fusion.7), channel_id=1, source_target_pairs={{0,2},{1,3},{2,0},{3,1},{4,6},{5,7},{6,4},{7,5},{8,10},{9,11},{10,... | collective-permute-start | bytes 12344 | tf_op jit(solution)/shard_map/ppermute | solution.py:44
  15.2 5.0 %collective-permute-start.3 = (f32[2052]{0:T(1024)S(1)}, f32[2052]{0:T(1024)S(1)}, u32[]{:S(2)}, u32[]{:S(2)}) collective-permute-start(f32[2052]{0:T(1024)S(1)} %pad_maximum_fusion.5), channel_id=1, source_target_pairs={{0,4},{1,5},{2,6},{3,7},{4,0},{5,1},{6,2},{7,3},{8,12},{9,13},{10,... | collective-permute-start | bytes 24632 | tf_op jit(solution)/shard_map/ppermute | solution.py:44
  17.6 9.4 %collective-permute-start.5 = (f32[2,4,1,512]{3,2,1,0:T(1,128)}, f32[2,4,1,512]{3,2,1,0:T(1,128)S(1)}, u32[]{:S(2)}, u32[]{:S(2)}) collective-permute-start(f32[2,4,1,512]{3,2,1,0:T(1,128)} %param.8), channel_id=1, source_target_pairs={{0,1},{1,2},{2,3},{3,4},{4,5},{5,6},{6,7},{7,8},{8,9},{9,10},{10,1... | collective-permute-start | bytes 49160 | tf_op jit(solution)/shard_map/ppermute | solution.py:62
  18.9 8.9 %collective-permute-start.6 = (f32[2,4,1,512]{3,2,1,0:T(1,128)}, f32[2,4,1,512]{3,2,1,0:T(1,128)S(1)}, u32[]{:S(2)}, u32[]{:S(2)}) collective-permute-start(f32[2,4,1,512]{3,2,1,0:T(1,128)} %param.8), channel_id=1, source_target_pairs={{1,0},{2,1},{3,2},{4,3},{5,4},{6,5},{7,6},{8,7},{9,8},{10,9},{11,1... | collective-permute-start | bytes 49160 | tf_op jit(solution)/shard_map/ppermute | solution.py:63
  20.6 8.3 %collective-permute-start.4 = (f32[4100]{0:T(1024)S(1)}, f32[4100]{0:T(1024)S(1)}, u32[]{:S(2)}, u32[]{:S(2)}) collective-permute-start(f32[4100]{0:T(1024)S(1)} %pad_maximum_fusion.2), channel_id=1, source_target_pairs={{0,8},{1,9},{2,10},{3,11},{4,12},{5,13},{6,14},{7,15},{8,0},{9,1},... | collective-permute-start | bytes 49208 | tf_op jit(solution)/shard_map/ppermute | solution.py:44
  29.1 4.6 %copy-start.1 = (f32[2,4,1,512]{3,2,1,0:T(1,128)S(1)}, f32[2,4,1,512]{3,2,1,0:T(1,128)}, u32[]{:S(2)}) copy-start(f32[2,4,1,512]{3,2,1,0:T(1,128)} %param.8) | copy-start | bytes 49156
  29.1 4.6 %copy-start.2 = (bf16[1,2,64,512]{3,2,1,0:T(8,128)(2,1)S(1)}, bf16[1,2,64,512]{3,2,1,0:T(8,128)(2,1)}, u32[]{:S(2)}) copy-start(bf16[1,2,64,512]{3,2,1,0:T(8,128)(2,1)} %param.12) | copy-start | bytes 393220
  34.4 1.2 %collective-permute-start.7 = (f32[528]{0:T(1024)S(1)}, f32[528]{0:T(1024)S(1)}, u32[]{:S(2)}, u32[]{:S(2)}) collective-permute-start(f32[528]{0:T(1024)S(1)} %pad_maximum_fusion.12), channel_id=1, source_target_pairs={{0,1},{1,0},{2,3},{3,2},{4,5},{5,4},{6,7},{7,6},{8,9},{9,8},{10,11... | collective-permute-start | bytes 6344 | tf_op jit(solution)/shard_map/ppermute | solution.py:44
  35.9 3.7 %collective-permute-start.8 = (f32[1040]{0:T(1024)S(1)}, f32[1040]{0:T(1024)S(1)}, u32[]{:S(2)}, u32[]{:S(2)}) collective-permute-start(f32[1040]{0:T(1024)S(1)} %pad_maximum_fusion.8), channel_id=1, source_target_pairs={{0,2},{1,3},{2,0},{3,1},{4,6},{5,7},{6,4},{7,5},{8,10},{9,11},{10,... | collective-permute-start | bytes 12488 | tf_op jit(solution)/shard_map/ppermute | solution.py:44
  39.8 3.7 %collective-permute-start.9 = (f32[2064]{0:T(1024)S(1)}, f32[2064]{0:T(1024)S(1)}, u32[]{:S(2)}, u32[]{:S(2)}) collective-permute-start(f32[2064]{0:T(1024)S(1)} %pad_maximum_fusion.6), channel_id=1, source_target_pairs={{0,4},{1,5},{2,6},{3,7},{4,0},{5,1},{6,2},{7,3},{8,12},{9,13},{10,... | collective-permute-start | bytes 24776 | tf_op jit(solution)/shard_map/ppermute | solution.py:44
  43.9 7.5 %collective-permute-start.10 = (f32[4112]{0:T(1024)S(1)}, f32[4112]{0:T(1024)S(1)}, u32[]{:S(2)}, u32[]{:S(2)}) collective-permute-start(f32[4112]{0:T(1024)S(1)} %pad_maximum_fusion.3), channel_id=1, source_target_pairs={{0,8},{1,9},{2,10},{3,11},{4,12},{5,13},{6,14},{7,15},{8,0},{9,1},... | collective-permute-start | bytes 49352 | tf_op jit(solution)/shard_map/ppermute | solution.py:44
  46.8 5.2 %collective-permute-start.13 = (f32[2,4,1,512]{3,1,0,2:T(4,128)S(1)}, f32[2,4,1,512]{3,1,0,2:T(4,128)S(1)}, u32[]{:S(2)}, u32[]{:S(2)}) collective-permute-start(f32[2,4,1,512]{3,1,0,2:T(4,128)S(1)} %get-tuple-element.34), channel_id=1, source_target_pairs={{1,0},{2,1},{3,2},{4,3},{5,4},{6,5},{7,6},{8,7},{9,8},{10,9},{11,1... | collective-permute-start | bytes 49160 | tf_op jit(solution)/shard_map/ppermute | solution.py:63
  48.1 3.9 %collective-permute-start.12 = (f32[2,4,1,512]{3,1,0,2:T(4,128)S(1)}, f32[2,4,1,512]{3,1,0,2:T(4,128)S(1)}, u32[]{:S(2)}, u32[]{:S(2)}) collective-permute-start(f32[2,4,1,512]{3,1,0,2:T(4,128)S(1)} %get-tuple-element.34), channel_id=1, source_target_pairs={{0,1},{1,2},{2,3},{3,4},{4,5},{5,6},{6,7},{7,8},{8,9},{9,10},{10,1... | collective-permute-start | bytes 49160 | tf_op jit(solution)/shard_map/ppermute | solution.py:62
  51.5 3.8 %collective-permute-start.11 = (f32[4112]{0:T(1024)S(1)}, f32[4112]{0:T(1024)S(1)}, u32[]{:S(2)}, u32[]{:S(2)}) collective-permute-start(f32[4112]{0:T(1024)S(1)} %pad_maximum_fusion.4), channel_id=1, source_target_pairs={{0,16},{16,0},{1,17},{17,1},{2,18},{18,2},{3,19},{19,3},{4,20},{20... | collective-permute-start | bytes 49352 | tf_op jit(solution)/shard_map/ppermute | solution.py:44
  60.7 3.7 %collective-permute-start.14 = (f32[8,4]{1,0:T(8,128)S(1)}, f32[8,4]{1,0:T(8,128)S(1)}, u32[]{:S(2)}, u32[]{:S(2)}) collective-permute-start(f32[8,4]{1,0:T(8,128)S(1)} %concatenate.157), channel_id=1, source_target_pairs={{0,16},{16,0},{1,17},{17,1},{2,18},{18,2},{3,19},{19,3},{4,20},{20... | collective-permute-start | bytes 392 | tf_op jit(solution)/shard_map/ppermute | solution.py:21
  64.3 1.2 %collective-permute-start.15 = (f32[8,4]{1,0:T(8,128)S(1)}, f32[8,4]{1,0:T(8,128)S(1)}, u32[]{:S(2)}, u32[]{:S(2)}) collective-permute-start(f32[8,4]{1,0:T(8,128)S(1)} %add.549), channel_id=1, source_target_pairs={{0,1},{1,0},{2,3},{3,2},{4,5},{5,4},{6,7},{7,6},{8,9},{9,8},{10,11... | collective-permute-start | bytes 392 | tf_op jit(solution)/shard_map/ppermute | solution.py:21
  65.5 3.6 %collective-permute-start.16 = (f32[8,4]{1,0:T(8,128)S(1)}, f32[8,4]{1,0:T(8,128)S(1)}, u32[]{:S(2)}, u32[]{:S(2)}) collective-permute-start(f32[8,4]{1,0:T(8,128)S(1)} %add.550), channel_id=1, source_target_pairs={{0,2},{1,3},{2,0},{3,1},{4,6},{5,7},{6,4},{7,5},{8,10},{9,11},{10,... | collective-permute-start | bytes 392 | tf_op jit(solution)/shard_map/ppermute | solution.py:21
  69.1 3.6 %collective-permute-start.17 = (f32[8,4]{1,0:T(8,128)S(1)}, f32[8,4]{1,0:T(8,128)S(1)}, u32[]{:S(2)}, u32[]{:S(2)}) collective-permute-start(f32[8,4]{1,0:T(8,128)S(1)} %add.551), channel_id=1, source_target_pairs={{0,4},{1,5},{2,6},{3,7},{4,0},{5,1},{6,2},{7,3},{8,12},{9,13},{10,... | collective-permute-start | bytes 392 | tf_op jit(solution)/shard_map/ppermute | solution.py:21
  72.7 4.5 %collective-permute-start.18 = (f32[8,4]{1,0:T(8,128)S(1)}, f32[8,4]{1,0:T(8,128)S(1)}, u32[]{:S(2)}, u32[]{:S(2)}) collective-permute-start(f32[8,4]{1,0:T(8,128)S(1)} %add.552), channel_id=1, source_target_pairs={{0,8},{1,9},{2,10},{3,11},{4,12},{5,13},{6,14},{7,15},{8,0},{9,1},... | collective-permute-start | bytes 392 | tf_op jit(solution)/shard_map/ppermute | solution.py:21

commit v11 on v10

--- a/solution.py
+++ b/solution.py
@@ -24,6 +24,8 @@
 
 
 def tree_collect(red, gat_blk, gat_dom, dom_first=False, halo=None):
+    left = None
+    right = None
     rounds = (("blk", gat_blk), ("dom", gat_dom))
     if dom_first:
         rounds = rounds[::-1]
@@ -38,9 +40,17 @@
             k = 1
             while k < n:
                 packed = jnp.concatenate([red.reshape(-1), buf.reshape(-1)])
-                if halo is not None and axis == "blk" and k == 2:
-                    packed, halo = lax.optimization_barrier((packed, halo))
-                    halo = neighbours(halo)
+                if halo is not None and axis == "blk":
+                    if left is not None and k == min(4, n // 2) and k > 2:
+                        packed, left = lax.optimization_barrier((packed, left))
+                    if right is not None and k == min(8, n // 2) and k > 4:
+                        packed, right = lax.optimization_barrier((packed, right))
+                    if k == min(2, n // 2) and left is None:
+                        packed, tied = lax.optimization_barrier((packed, halo))
+                        left = lax.ppermute(tied, "blk", [(i, i + 1) for i in range(n - 1)])
+                    if k == min(4, n // 2) and right is None:
+                        packed, tied = lax.optimization_barrier((packed, halo))
+                        right = lax.ppermute(tied, "blk", [(i + 1, i) for i in range(n - 1)])
                 got = lax.ppermute(packed, axis, [(i, i ^ k) for i in range(n)])
                 red = red + got[: red.size].reshape(red.shape)
                 other = got[red.size :].reshape(buf.shape)
@@ -52,7 +62,9 @@
         else:
             gat_dom = buf
     if halo is not None:
-        return red, gat_blk, gat_dom, halo
+        if left is None or right is None:
+            return red, gat_blk, gat_dom, neighbours(halo)
+        return red, gat_blk, gat_dom, jnp.concatenate([left, halo, right], axis=3)
     return red, gat_blk, gat_dom
 
 
@@ -178,7 +190,6 @@
         - swapped(every_one, partner, width)
     )
 
-    window_img = neighbours(image_one)
     parts = jnp.concatenate(
         [
             local_products([first_vec], image_one)[0],
@@ -186,8 +197,8 @@
             local_squares(first_vec)[None],
         ]
     )
-    one, coef_img, every_img = tree_collect(
-        parts, coefficients(image_one, source_basis), image_one[:, :, 0]
+    one, coef_img, every_img, window_img = tree_collect(
+        parts, coefficients(image_one, source_basis), image_one[:, :, 0], halo=image_one
     )
     one = one / total
     h_one_one = one[0:2]

time: 80.1 us -> 81.7 us (1.020)
  starting transfers between devices: 26.8 us -> 29.1 us
    ppermute x10, waiting for transfers between devices: 13.8 us -> 11.2 us  [tree_collect(): got = lax.ppermute(packed, axis, [(i, i ^ k) for i in range(n)])]
    ppermute x10, starting transfers between devices: 17.9 us -> 20.4 us  [tree_collect(): got = lax.ppermute(packed, axis, [(i, i ^ k) for i in range(n)])]
    ppermute x4, waiting for transfers between devices: 0.01 us -> 2.4 us  [the longest x2 1.97 us: tree_collect(): right = lax.ppermute(tied, 'blk', [(i + 1, i) for i in range(n - 1)])]
  transfers between devices with their start and end apart: 19 -> 19, of which waited for: 12 -> 16; matrix products, arithmetic and copies ran while one was open for 10% -> 11% of each run, Pallas kernels for 0% -> 0%
where the time goes in v11:
time: 81.7 us; the launch traced here: 81 us
  starting transfers between devices  29.1 us (36%)
  waiting for transfers between devices  26.8 us (33%)
  local copies, waits for them, and re-layouts  10.1 us (12%)
  other arithmetic  6.99 us (9%)
  matrix products  6.81 us (8%)
  between operations  1.09 us (1%)
    ppermute x10, starting transfers between devices, tree_collect(): got = lax.ppermute(packed, axis, [(i, i ^ k) for i in range(n)])  20.4 us
    ppermute x5, waiting for transfers between devices, tree_sum(): x = x + lax.ppermute(x, axis, [(i, i ^ k) for i in range(n)])  13.2 us
    ppermute x10, waiting for transfers between devices, tree_collect(): got = lax.ppermute(packed, axis, [(i, i ^ k) for i in range(n)])  11.2 us
    dot_general x2, matrix products, far_field(): jnp.einsum('sakl,spql->apqk', weights, gathered, precision=lax.Precision....  4.01 us
    ppermute x2, starting transfers between devices, tree_collect(): left = lax.ppermute(tied, 'blk', [(i, i + 1) for i in range(n - 1)])  3.75 us
    unnamed x14, local copies, waits for them, and re-layouts  2.74 us
    ppermute x2, starting transfers between devices, tree_collect(): right = lax.ppermute(tied, 'blk', [(i + 1, i) for i in range(n - 1)])  2.56 us
    ppermute x5, starting transfers between devices, tree_sum(): x = x + lax.ppermute(x, axis, [(i, i ^ k) for i in range(n)])  2.45 us
  transfers between devices with their start and end apart: 19, of which 16 were waited for; matrix products, arithmetic and copies ran while one was open for 11% of the time, Pallas kernels for 0%

profile of v11, /device:TPU:0, one launch (start us, length us, event | category | flops | bytes accessed | tf_op | source)
XLA Modules:
  0.0 81.0 jit_solution(70538591286873384)
XLA Ops:
  0.7 1.0 %add_reduce_fusion.9 = f32[4]{0:T(128)S(1)} fusion(f32[2,4,1,512]{3,2,1,0:T(1,128)} %param.8), kind=kLoop, calls=%fused_computation.121 | loop fusion | flops 8188 | bytes 16400 | tf_op jit(solution)/shard_map/reduce_sum | solution.py:143
  1.7 0.8 pad_maximum_fusion.1
  2.4 3.0 %collective-permute-start = (f32[4100]{0:T(1024)S(1)}, f32[4100]{0:T(1024)S(1)}, u32[]{:S(2)}, u32[]{:S(2)}) collective-permute-start(f32[4100]{0:T(1024)S(1)} %pad_maximum_fusion.1), channel_id=1, source_target_pairs={{0,16},{16,0},{1,17},{17,1},{2,18},{18,2},{3,19},{19,3},{4,20},{20... | collective-permute-start | bytes 49208 | tf_op jit(solution)/shard_map/ppermute | solution.py:54
  5.4 0.7 convert_element_type.28
  6.1 1.1 %convolution_bitcast_fusion.5 = f32[2,2,4,64]{3,2,0,1:T(4,128)S(1)} fusion(bf16[1,2,64,512]{3,2,1,0:T(8,128)(2,1)} %param.12, bf16[2,4,1,512]{3,2,1,0:T(2,128)(2,1)S(1)} %convert_element_type.28), kind=kOutput, calls=%fused_computation.15 | convolution fusion | flops 1048576 | bytes 143360 | tf_op jit(solution)/shard_map/akr,pqr->apqk/dot_general | solution.py:85
  7.2 0.7 fusion.69
  7.9 0.8 reshape_squeeze.4
  8.7 0.7 iota_compare_fusion
  9.4 0.2 and_convert_fusion
  9.8 0.7 copy.181
  10.5 0.4 collective-permute-done.1
  11.3 1.5 %collective-permute-start.2 = (f32[1028]{0:T(1024)S(1)}, f32[1028]{0:T(1024)S(1)}, u32[]{:S(2)}, u32[]{:S(2)}) collective-permute-start(f32[1028]{0:T(1024)S(1)} %pad_maximum_fusion.7), channel_id=1, source_target_pairs={{0,2},{1,3},{2,0},{3,1},{4,6},{5,7},{6,4},{7,5},{8,10},{9,11},{10,... | collective-permute-start | bytes 12344 | tf_op jit(solution)/shard_map/ppermute | solution.py:54
  12.9 1.8 %collective-permute-start.3 = (f32[2,4,1,512]{3,2,1,0:T(1,128)}, f32[2,4,1,512]{3,2,1,0:T(1,128)S(1)}, u32[]{:S(2)}, u32[]{:S(2)}) collective-permute-start(f32[2,4,1,512]{3,2,1,0:T(1,128)} %param.8), channel_id=1, source_target_pairs={{0,1},{1,2},{2,3},{3,4},{4,5},{5,6},{6,7},{7,8},{8,9},{9,10},{10,1... | collective-permute-start | bytes 49160 | tf_op jit(solution)/shard_map/ppermute | solution.py:50
  14.7 0.3 collective-permute-done.2
  15.3 0.4 collective-permute-done.3
  15.7 4.9 %collective-permute-start.4 = (f32[2052]{0:T(1024)S(1)}, f32[2052]{0:T(1024)S(1)}, u32[]{:S(2)}, u32[]{:S(2)}) collective-permute-start(f32[2052]{0:T(1024)S(1)} %pad_maximum_fusion.5), channel_id=1, source_target_pairs={{0,4},{1,5},{2,6},{3,7},{4,0},{5,1},{6,2},{7,3},{8,12},{9,13},{10,... | collective-permute-start | bytes 24632 | tf_op jit(solution)/shard_map/ppermute | solution.py:54
  20.6 1.3 %collective-permute-start.5 = (f32[2,4,1,512]{3,2,1,0:T(1,128)}, f32[2,4,1,512]{3,2,1,0:T(1,128)S(1)}, u32[]{:S(2)}, u32[]{:S(2)}) collective-permute-start(f32[2,4,1,512]{3,2,1,0:T(1,128)} %param.8), channel_id=1, source_target_pairs={{1,0},{2,1},{3,2},{4,3},{5,4},{6,5},{7,6},{8,7},{9,8},{10,9},{11,1... | collective-permute-start | bytes 49160 | tf_op jit(solution)/shard_map/ppermute | solution.py:53
  21.9 0.7 constant_dynamic-update-slice_fusion.1
  23.0 0.9 %collective-permute-done.5 = f32[2,4,1,512]{3,2,1,0:T(1,128)S(1)} collective-permute-done((f32[2,4,1,512]{3,2,1,0:T(1,128)}, f32[2,4,1,512]{3,2,1,0:T(1,128)S(1)}, u32[]{:S(2)}, u32[]{:S(2)}) %collective-permute-start.5) | collective-permute-done | bytes 16416 | tf_op jit(solution)/shard_map/ppermute | solution.py:53
  23.9 2.9 %collective-permute-start.6 = (f32[4100]{0:T(1024)S(1)}, f32[4100]{0:T(1024)S(1)}, u32[]{:S(2)}, u32[]{:S(2)}) collective-permute-start(f32[4100]{0:T(1024)S(1)} %pad_maximum_fusion.2), channel_id=1, source_target_pairs={{0,8},{1,9},{2,10},{3,11},{4,12},{5,13},{6,14},{7,15},{8,0},{9,1},... | collective-permute-start | bytes 49208 | tf_op jit(solution)/shard_map/ppermute | solution.py:54
  26.8 1.8 %collective-permute-done.6 = f32[4100]{0:T(1024)S(1)} collective-permute-done((f32[4100]{0:T(1024)S(1)}, f32[4100]{0:T(1024)S(1)}, u32[]{:S(2)}, u32[]{:S(2)}) %collective-permute-start.6) | collective-permute-done | bytes 16432 | tf_op jit(solution)/shard_map/ppermute | solution.py:54
  28.9 2.0 %convolution_bitcast_fusion.4 = f32[2,2,4,64]{3,2,0,1:T(4,128)S(1)} fusion(f32[1,1,16,2,64,64]{5,4,3,2,1,0:T(8,128)} %param.14, f32[16,64,64]{2,1,0:T(8,128)S(1)} %and_convert_fusion, f32[16,2,4,64]{3,2,1,0:T(4,128)S(1)} %fusion.18), kind=kOutput, calls=%fused_computation.14 | convolution fusion | flops 6422528 | bytes 823296 | tf_op jit(solution)/shard_map/sakl,spql->apqk/dot_general | solution.py:118
  30.9 0.1 convolution_bitcast_fusion.1
  31.2 0.6 gather_fusion.1
  31.8 0.2 broadcast_divide_fusion
  32.1 0.6 gather_fusion
  32.7 0.7 fusion.4
  33.5 0.1 convolution_bitcast_fusion.3
  33.8 0.2 add_reduce_fusion.8
  34.1 1.2 %collective-permute-done.7 = f32[528]{0:T(1024)S(1)} collective-permute-done((f32[528]{0:T(1024)S(1)}, f32[528]{0:T(1024)S(1)}, u32[]{:S(2)}, u32[]{:S(2)}) %collective-permute-start.7) | collective-permute-done | bytes 2144 | tf_op jit(solution)/shard_map/ppermute | solution.py:54
  35.6 1.1 %collective-permute-start.8 = (f32[1040]{0:T(1024)S(1)}, f32[1040]{0:T(1024)S(1)}, u32[]{:S(2)}, u32[]{:S(2)}) collective-permute-start(f32[1040]{0:T(1024)S(1)} %pad_maximum_fusion.8), channel_id=1, source_target_pairs={{0,2},{1,3},{2,0},{3,1},{4,6},{5,7},{6,4},{7,5},{8,10},{9,11},{10,... | collective-permute-start | bytes 12488 | tf_op jit(solution)/shard_map/ppermute | solution.py:54
  36.7 2.0 %collective-permute-start.9 = (f32[2,4,1,512]{3,1,0,2:T(4,128)S(1)}, f32[2,4,1,512]{3,1,0,2:T(4,128)S(1)}, u32[]{:S(2)}, u32[]{:S(2)}) collective-permute-start(f32[2,4,1,512]{3,1,0,2:T(4,128)S(1)} %get-tuple-element.31), channel_id=1, source_target_pairs={{0,1},{1,2},{2,3},{3,4},{4,5},{5,6},{6,7},{7,8},{8,9},{9,10},{10,1... | collective-permute-start | bytes 49160 | tf_op jit(solution)/shard_map/ppermute | solution.py:50
  38.6 0.6 collective-permute-done.8
  39.6 5.7 %collective-permute-start.10 = (f32[2064]{0:T(1024)S(1)}, f32[2064]{0:T(1024)S(1)}, u32[]{:S(2)}, u32[]{:S(2)}) collective-permute-start(f32[2064]{0:T(1024)S(1)} %pad_maximum_fusion.6), channel_id=1, source_target_pairs={{0,4},{1,5},{2,6},{3,7},{4,0},{5,1},{6,2},{7,3},{8,12},{9,13},{10,... | collective-permute-start | bytes 24776 | tf_op jit(solution)/shard_map/ppermute | solution.py:54
  45.3 1.3 %collective-permute-start.11 = (f32[2,4,1,512]{3,1,0,2:T(4,128)S(1)}, f32[2,4,1,512]{3,1,0,2:T(4,128)S(1)}, u32[]{:S(2)}, u32[]{:S(2)}) collective-permute-start(f32[2,4,1,512]{3,1,0,2:T(4,128)S(1)} %get-tuple-element.31), channel_id=1, source_target_pairs={{1,0},{2,1},{3,2},{4,3},{5,4},{6,5},{7,6},{8,7},{9,8},{10,9},{11,1... | collective-permute-start | bytes 49160 | tf_op jit(solution)/shard_map/ppermute | solution.py:53
  46.5 0.4 collective-permute-done.10
  47.3 1.1 %collective-permute-done.11 = f32[2,4,1,512]{3,1,0,2:T(4,128)S(1)} collective-permute-done((f32[2,4,1,512]{3,1,0,2:T(4,128)S(1)}, f32[2,4,1,512]{3,1,0,2:T(4,128)S(1)}, u32[]{:S(2)}, u32[]{:S(2)}) %collective-permute-start.11) | collective-permute-done | bytes 16416 | tf_op jit(solution)/shard_map/ppermute | solution.py:53
  48.3 0.9 %collective-permute-start.12 = (f32[4112]{0:T(1024)S(1)}, f32[4112]{0:T(1024)S(1)}, u32[]{:S(2)}, u32[]{:S(2)}) collective-permute-start(f32[4112]{0:T(1024)S(1)} %pad_maximum_fusion.3), channel_id=1, source_target_pairs={{0,8},{1,9},{2,10},{3,11},{4,12},{5,13},{6,14},{7,15},{8,0},{9,1},... | collective-permute-start | bytes 49352 | tf_op jit(solution)/shard_map/ppermute | solution.py:54
  49.5 3.5 %collective-permute-done.12 = f32[4112]{0:T(1024)S(1)} collective-permute-done((f32[4112]{0:T(1024)S(1)}, f32[4112]{0:T(1024)S(1)}, u32[]{:S(2)}, u32[]{:S(2)}) %collective-permute-start.12) | collective-permute-done | bytes 16480 | tf_op jit(solution)/shard_map/ppermute | solution.py:54
  53.1 0.5 collective-permute-start.13
  53.9 3.0 %collective-permute-done.13 = f32[4112]{0:T(1024)S(1)} collective-permute-done((f32[4112]{0:T(1024)S(1)}, f32[4112]{0:T(1024)S(1)}, u32[]{:S(2)}, u32[]{:S(2)}) %collective-permute-start.13) | collective-permute-done | bytes 16480 | tf_op jit(solution)/shard_map/ppermute | solution.py:54
  57.2 2.0 %convolution_bitcast_fusion.2 = f32[2,2,4,64]{3,2,0,1:T(4,128)S(1)} fusion(f32[1,1,16,2,64,64]{5,4,3,2,1,0:T(8,128)} %param.14, f32[16,64,64]{2,1,0:T(8,128)S(1)} %and_convert_fusion, f32[16,1,4,64]{3,2,1,0:T(4,128)S(1)} %get-tuple-element.65, f32[16,1,4,64]{3,2,1,0:T(4,128)S(1)} %get-tuple-element.64, f32[8,2,4,64]{3,2,1,0:T(4,128)S(1)} %maximum_select_fusion.4, ...), kind=kOutput, calls=%fused_computation.12 | convolution fusion | flops 6471680 | bytes 856081 | tf_op jit(solution)/shard_map/sakl,spql->apqk/dot_general | solution.py:118
  59.5 0.6 gather_fusion.3
  60.2 0.2 subtract_reduce_fusion
  60.5 0.6 gather_fusion.2
  61.1 0.7 fusion.7
  61.8 0.1 convolution_bitcast_fusion
  62.0 0.2 subtract_reduce_fusion.1
  62.3 0.6 collective-permute-start.14
  62.8 3.1 %collective-permute-done.14 = f32[8,4]{1,0:T(8,128)S(1)} collective-permute-done((f32[8,4]{1,0:T(8,128)S(1)}, f32[8,4]{1,0:T(8,128)S(1)}, u32[]{:S(2)}, u32[]{:S(2)}) %collective-permute-start.14) | collective-permute-done | bytes 160 | tf_op jit(solution)/shard_map/ppermute | solution.py:21
  66.0 1.2 %collective-permute-done.15 = f32[8,4]{1,0:T(8,128)S(1)} collective-permute-done((f32[8,4]{1,0:T(8,128)S(1)}, f32[8,4]{1,0:T(8,128)S(1)}, u32[]{:S(2)}, u32[]{:S(2)}) %collective-permute-start.15) | collective-permute-done | bytes 160 | tf_op jit(solution)/shard_map/ppermute | solution.py:21
  67.1 0.1 copy.96
  67.2 0.6 copy.105
  67.8 2.9 %collective-permute-done.16 = f32[8,4]{1,0:T(8,128)S(1)} collective-permute-done((f32[8,4]{1,0:T(8,128)S(1)}, f32[8,4]{1,0:T(8,128)S(1)}, u32[]{:S(2)}, u32[]{:S(2)}) %collective-permute-start.16) | collective-permute-done | bytes 160 | tf_op jit(solution)/shard_map/ppermute | solution.py:21
  70.7 1.0 %collective-permute-start.17 = (f32[8,4]{1,0:T(8,128)S(1)}, f32[8,4]{1,0:T(8,128)S(1)}, u32[]{:S(2)}, u32[]{:S(2)}) collective-permute-start(f32[8,4]{1,0:T(8,128)S(1)} %add.551), channel_id=1, source_target_pairs={{0,4},{1,5},{2,6},{3,7},{4,0},{5,1},{6,2},{7,3},{8,12},{9,13},{10,... | collective-permute-start | bytes 392 | tf_op jit(solution)/shard_map/ppermute | solution.py:21
  71.7 0.1 copy.97
  71.8 2.5 %collective-permute-done.17 = f32[8,4]{1,0:T(8,128)S(1)} collective-permute-done((f32[8,4]{1,0:T(8,128)S(1)}, f32[8,4]{1,0:T(8,128)S(1)}, u32[]{:S(2)}, u32[]{:S(2)}) %collective-permute-start.17) | collective-permute-done | bytes 160 | tf_op jit(solution)/shard_map/ppermute | solution.py:21
  74.3 0.9 %collective-permute-start.18 = (f32[8,4]{1,0:T(8,128)S(1)}, f32[8,4]{1,0:T(8,128)S(1)}, u32[]{:S(2)}, u32[]{:S(2)}) collective-permute-start(f32[8,4]{1,0:T(8,128)S(1)} %add.552), channel_id=1, source_target_pairs={{0,8},{1,9},{2,10},{3,11},{4,12},{5,13},{6,14},{7,15},{8,0},{9,1},... | collective-permute-start | bytes 392 | tf_op jit(solution)/shard_map/ppermute | solution.py:21
  75.2 0.1 copy.98
  75.3 3.5 %collective-permute-done.18 = f32[8,4]{1,0:T(8,128)S(1)} collective-permute-done((f32[8,4]{1,0:T(8,128)S(1)}, f32[8,4]{1,0:T(8,128)S(1)}, u32[]{:S(2)}, u32[]{:S(2)}) %collective-permute-start.18) | collective-permute-done | bytes 160 | tf_op jit(solution)/shard_map/ppermute | solution.py:21
  79.1 0.6 copy.106
  80.0 0.1 copy.102
  80.2 0.1 copy.104
  80.3 0.7 stack.153
  (137 shorter events, 5.3 us)
Async XLA Ops:
  0.6 32.1 %copy-start = (bf16[1,2,4,2,256,256]{5,4,3,2,1,0:T(8,128)(2,1)S(1)}, bf16[1,2,4,2,256,256]{5,4,3,2,1,0:T(8,128)(2,1)}, u32[]{:S(2)}) copy-start(bf16[1,2,4,2,256,256]{5,4,3,2,1,0:T(8,128)(2,1)} %param.9) | copy-start | bytes 6291460
  0.6 30.3 %copy-start.3 = (bf16[1,2,64,512]{3,2,1,0:T(8,128)(2,1)S(1)}, bf16[1,2,64,512]{3,2,1,0:T(8,128)(2,1)}, u32[]{:S(2)}) copy-start(bf16[1,2,64,512]{3,2,1,0:T(8,128)(2,1)} %param.13) | copy-start | bytes 393220
  2.4 7.3 %collective-permute-start = (f32[4100]{0:T(1024)S(1)}, f32[4100]{0:T(1024)S(1)}, u32[]{:S(2)}, u32[]{:S(2)}) collective-permute-start(f32[4100]{0:T(1024)S(1)} %pad_maximum_fusion.1), channel_id=1, source_target_pairs={{0,16},{16,0},{1,17},{17,1},{2,18},{18,2},{3,19},{19,3},{4,20},{20... | collective-permute-start | bytes 49208 | tf_op jit(solution)/shard_map/ppermute | solution.py:54
  9.8 1.2 %collective-permute-start.1 = (f32[516]{0:T(1024)S(1)}, f32[516]{0:T(1024)S(1)}, u32[]{:S(2)}, u32[]{:S(2)}) collective-permute-start(f32[516]{0:T(1024)S(1)} %pad_maximum_fusion.10), channel_id=1, source_target_pairs={{0,1},{1,0},{2,3},{3,2},{4,5},{5,4},{6,7},{7,6},{8,9},{9,8},{10,11... | collective-permute-start | bytes 6200 | tf_op jit(solution)/shard_map/ppermute | solution.py:54
  11.3 3.7 %collective-permute-start.2 = (f32[1028]{0:T(1024)S(1)}, f32[1028]{0:T(1024)S(1)}, u32[]{:S(2)}, u32[]{:S(2)}) collective-permute-start(f32[1028]{0:T(1024)S(1)} %pad_maximum_fusion.7), channel_id=1, source_target_pairs={{0,2},{1,3},{2,0},{3,1},{4,6},{5,7},{6,4},{7,5},{8,10},{9,11},{10,... | collective-permute-start | bytes 12344 | tf_op jit(solution)/shard_map/ppermute | solution.py:54
  12.9 2.8 %collective-permute-start.3 = (f32[2,4,1,512]{3,2,1,0:T(1,128)}, f32[2,4,1,512]{3,2,1,0:T(1,128)S(1)}, u32[]{:S(2)}, u32[]{:S(2)}) collective-permute-start(f32[2,4,1,512]{3,2,1,0:T(1,128)} %param.8), channel_id=1, source_target_pairs={{0,1},{1,2},{2,3},{3,4},{4,5},{5,6},{6,7},{7,8},{8,9},{9,10},{10,1... | collective-permute-start | bytes 49160 | tf_op jit(solution)/shard_map/ppermute | solution.py:50
  15.7 6.9 %collective-permute-start.4 = (f32[2052]{0:T(1024)S(1)}, f32[2052]{0:T(1024)S(1)}, u32[]{:S(2)}, u32[]{:S(2)}) collective-permute-start(f32[2052]{0:T(1024)S(1)} %pad_maximum_fusion.5), channel_id=1, source_target_pairs={{0,4},{1,5},{2,6},{3,7},{4,0},{5,1},{6,2},{7,3},{8,12},{9,13},{10,... | collective-permute-start | bytes 24632 | tf_op jit(solution)/shard_map/ppermute | solution.py:54
  20.6 3.3 %collective-permute-start.5 = (f32[2,4,1,512]{3,2,1,0:T(1,128)}, f32[2,4,1,512]{3,2,1,0:T(1,128)S(1)}, u32[]{:S(2)}, u32[]{:S(2)}) collective-permute-start(f32[2,4,1,512]{3,2,1,0:T(1,128)} %param.8), channel_id=1, source_target_pairs={{1,0},{2,1},{3,2},{4,3},{5,4},{6,5},{7,6},{8,7},{9,8},{10,9},{11,1... | collective-permute-start | bytes 49160 | tf_op jit(solution)/shard_map/ppermute | solution.py:53
  23.9 4.7 %collective-permute-start.6 = (f32[4100]{0:T(1024)S(1)}, f32[4100]{0:T(1024)S(1)}, u32[]{:S(2)}, u32[]{:S(2)}) collective-permute-start(f32[4100]{0:T(1024)S(1)} %pad_maximum_fusion.2), channel_id=1, source_target_pairs={{0,8},{1,9},{2,10},{3,11},{4,12},{5,13},{6,14},{7,15},{8,0},{9,1},... | collective-permute-start | bytes 49208 | tf_op jit(solution)/shard_map/ppermute | solution.py:54
  28.8 4.6 %copy-start.1 = (f32[2,4,1,512]{3,2,1,0:T(1,128)S(1)}, f32[2,4,1,512]{3,2,1,0:T(1,128)}, u32[]{:S(2)}) copy-start(f32[2,4,1,512]{3,2,1,0:T(1,128)} %param.8) | copy-start | bytes 49156
  28.8 4.6 %copy-start.2 = (bf16[1,2,64,512]{3,2,1,0:T(8,128)(2,1)S(1)}, bf16[1,2,64,512]{3,2,1,0:T(8,128)(2,1)}, u32[]{:S(2)}) copy-start(bf16[1,2,64,512]{3,2,1,0:T(8,128)(2,1)} %param.12) | copy-start | bytes 393220
  34.1 1.2 %collective-permute-start.7 = (f32[528]{0:T(1024)S(1)}, f32[528]{0:T(1024)S(1)}, u32[]{:S(2)}, u32[]{:S(2)}) collective-permute-start(f32[528]{0:T(1024)S(1)} %pad_maximum_fusion.12), channel_id=1, source_target_pairs={{0,1},{1,0},{2,3},{3,2},{4,5},{5,4},{6,7},{7,6},{8,9},{9,8},{10,11... | collective-permute-start | bytes 6344 | tf_op jit(solution)/shard_map/ppermute | solution.py:54
  35.6 3.7 %collective-permute-start.8 = (f32[1040]{0:T(1024)S(1)}, f32[1040]{0:T(1024)S(1)}, u32[]{:S(2)}, u32[]{:S(2)}) collective-permute-start(f32[1040]{0:T(1024)S(1)} %pad_maximum_fusion.8), channel_id=1, source_target_pairs={{0,2},{1,3},{2,0},{3,1},{4,6},{5,7},{6,4},{7,5},{8,10},{9,11},{10,... | collective-permute-start | bytes 12488 | tf_op jit(solution)/shard_map/ppermute | solution.py:54
  36.7 2.9 %collective-permute-start.9 = (f32[2,4,1,512]{3,1,0,2:T(4,128)S(1)}, f32[2,4,1,512]{3,1,0,2:T(4,128)S(1)}, u32[]{:S(2)}, u32[]{:S(2)}) collective-permute-start(f32[2,4,1,512]{3,1,0,2:T(4,128)S(1)} %get-tuple-element.31), channel_id=1, source_target_pairs={{0,1},{1,2},{2,3},{3,4},{4,5},{5,6},{6,7},{7,8},{8,9},{9,10},{10,1... | collective-permute-start | bytes 49160 | tf_op jit(solution)/shard_map/ppermute | solution.py:50
  39.6 7.3 %collective-permute-start.10 = (f32[2064]{0:T(1024)S(1)}, f32[2064]{0:T(1024)S(1)}, u32[]{:S(2)}, u32[]{:S(2)}) collective-permute-start(f32[2064]{0:T(1024)S(1)} %pad_maximum_fusion.6), channel_id=1, source_target_pairs={{0,4},{1,5},{2,6},{3,7},{4,0},{5,1},{6,2},{7,3},{8,12},{9,13},{10,... | collective-permute-start | bytes 24776 | tf_op jit(solution)/shard_map/ppermute | solution.py:54
  45.3 3.1 %collective-permute-start.11 = (f32[2,4,1,512]{3,1,0,2:T(4,128)S(1)}, f32[2,4,1,512]{3,1,0,2:T(4,128)S(1)}, u32[]{:S(2)}, u32[]{:S(2)}) collective-permute-start(f32[2,4,1,512]{3,1,0,2:T(4,128)S(1)} %get-tuple-element.31), channel_id=1, source_target_pairs={{1,0},{2,1},{3,2},{4,3},{5,4},{6,5},{7,6},{8,7},{9,8},{10,9},{11,1... | collective-permute-start | bytes 49160 | tf_op jit(solution)/shard_map/ppermute | solution.py:53
  48.3 4.7 %collective-permute-start.12 = (f32[4112]{0:T(1024)S(1)}, f32[4112]{0:T(1024)S(1)}, u32[]{:S(2)}, u32[]{:S(2)}) collective-permute-start(f32[4112]{0:T(1024)S(1)} %pad_maximum_fusion.3), channel_id=1, source_target_pairs={{0,8},{1,9},{2,10},{3,11},{4,12},{5,13},{6,14},{7,15},{8,0},{9,1},... | collective-permute-start | bytes 49352 | tf_op jit(solution)/shard_map/ppermute | solution.py:54
  53.1 3.8 %collective-permute-start.13 = (f32[4112]{0:T(1024)S(1)}, f32[4112]{0:T(1024)S(1)}, u32[]{:S(2)}, u32[]{:S(2)}) collective-permute-start(f32[4112]{0:T(1024)S(1)} %pad_maximum_fusion.4), channel_id=1, source_target_pairs={{0,16},{16,0},{1,17},{17,1},{2,18},{18,2},{3,19},{19,3},{4,20},{20... | collective-permute-start | bytes 49352 | tf_op jit(solution)/shard_map/ppermute | solution.py:54
  62.3 3.7 %collective-permute-start.14 = (f32[8,4]{1,0:T(8,128)S(1)}, f32[8,4]{1,0:T(8,128)S(1)}, u32[]{:S(2)}, u32[]{:S(2)}) collective-permute-start(f32[8,4]{1,0:T(8,128)S(1)} %concatenate.157), channel_id=1, source_target_pairs={{0,16},{16,0},{1,17},{17,1},{2,18},{18,2},{3,19},{19,3},{4,20},{20... | collective-permute-start | bytes 392 | tf_op jit(solution)/shard_map/ppermute | solution.py:21
  66.0 1.2 %collective-permute-start.15 = (f32[8,4]{1,0:T(8,128)S(1)}, f32[8,4]{1,0:T(8,128)S(1)}, u32[]{:S(2)}, u32[]{:S(2)}) collective-permute-start(f32[8,4]{1,0:T(8,128)S(1)} %add.549), channel_id=1, source_target_pairs={{0,1},{1,0},{2,3},{3,2},{4,5},{5,4},{6,7},{7,6},{8,9},{9,8},{10,11... | collective-permute-start | bytes 392 | tf_op jit(solution)/shard_map/ppermute | solution.py:21
  67.1 3.6 %collective-permute-start.16 = (f32[8,4]{1,0:T(8,128)S(1)}, f32[8,4]{1,0:T(8,128)S(1)}, u32[]{:S(2)}, u32[]{:S(2)}) collective-permute-start(f32[8,4]{1,0:T(8,128)S(1)} %add.550), channel_id=1, source_target_pairs={{0,2},{1,3},{2,0},{3,1},{4,6},{5,7},{6,4},{7,5},{8,10},{9,11},{10,... | collective-permute-start | bytes 392 | tf_op jit(solution)/shard_map/ppermute | solution.py:21
  70.7 3.6 %collective-permute-start.17 = (f32[8,4]{1,0:T(8,128)S(1)}, f32[8,4]{1,0:T(8,128)S(1)}, u32[]{:S(2)}, u32[]{:S(2)}) collective-permute-start(f32[8,4]{1,0:T(8,128)S(1)} %add.551), channel_id=1, source_target_pairs={{0,4},{1,5},{2,6},{3,7},{4,0},{5,1},{6,2},{7,3},{8,12},{9,13},{10,... | collective-permute-start | bytes 392 | tf_op jit(solution)/shard_map/ppermute | solution.py:21
  74.3 4.5 %collective-permute-start.18 = (f32[8,4]{1,0:T(8,128)S(1)}, f32[8,4]{1,0:T(8,128)S(1)}, u32[]{:S(2)}, u32[]{:S(2)}) collective-permute-start(f32[8,4]{1,0:T(8,128)S(1)} %add.552), channel_id=1, source_target_pairs={{0,8},{1,9},{2,10},{3,11},{4,12},{5,13},{6,14},{7,15},{8,0},{9,1},... | collective-permute-start | bytes 392 | tf_op jit(solution)/shard_map/ppermute | solution.py:21

commit v12 on v10

--- a/solution.py
+++ b/solution.py
@@ -201,6 +201,7 @@
     window_two = (window_img - scaled(h_one_one, window_one)) / inv_two
     every_two = (spread(every_img) - scaled(h_one_one, every_one)) / inv_two
     coef_two = (coef_img - coef_scaled(h_one_one, coef_one)) / h_two_one[None, None, :, None]
+    early_columns = jnp.stack([beta, h_one_one[0], h_one_one[1], h_two_one], axis=1)
     image_two = (
         second_basis
         + near_field(window_two, near_blocks, near_cols)
@@ -237,19 +238,8 @@
     rest_two = image_two - scaled(h_one_two, first_vec) - scaled(h_two_two, second_basis)
     h_three_two = jnp.sqrt(sq_u2 + EPSILON)
     third_basis = rest_two / h_three_two[None, :, None, None]
-    hessenberg = jnp.stack(
-        [
-            beta,
-            h_one_one[0],
-            h_one_one[1],
-            h_two_one,
-            h_one_two[0],
-            h_one_two[1],
-            h_two_two[0],
-            h_two_two[1],
-            h_three_two,
-        ],
-        axis=1,
+    hessenberg = jnp.concatenate(
+        [early_columns, two[0:4].T, h_three_two[:, None]], axis=1
     )
     return (second_basis, third_basis, hessenberg)
 

time: 80.1 us -> 79.8 us (level)
    another operation x10 -> x4, local copies, waits for them, and re-layouts: 1.33 us -> 0.28 us  [shards(): jnp.stack([beta, h_one_one[0], h_one_one[1], h_two_one], axis=1)]
where the time goes in v12:
time: 79.8 us; the launch traced here: 79.1 us
  waiting for transfers between devices  27.6 us (35%)
  starting transfers between devices  26.8 us (34%)
  local copies, waits for them, and re-layouts  9.86 us (12%)
  other arithmetic  6.98 us (9%)
  matrix products  6.81 us (9%)
  between operations  1.12 us (1%)
    ppermute x10, starting transfers between devices, tree_collect(): got = lax.ppermute(packed, axis, [(i, i ^ k) for i in range(n)])  17.9 us
    ppermute x10, waiting for transfers between devices, tree_collect(): got = lax.ppermute(packed, axis, [(i, i ^ k) for i in range(n)])  13.8 us
    ppermute x5, waiting for transfers between devices, tree_sum(): x = x + lax.ppermute(x, axis, [(i, i ^ k) for i in range(n)])  13.7 us
    ppermute x2, starting transfers between devices, neighbours(): left = lax.ppermute(field, 'blk', [(i, i + 1) for i in range(ends)])  4.32 us
    dot_general x2, matrix products, far_field(): jnp.einsum('sakl,spql->apqk', weights, gathered, precision=lax.Precision....  4.01 us
    unnamed x14, local copies, waits for them, and re-layouts  2.74 us
    ppermute x2, starting transfers between devices, neighbours(): right = lax.ppermute(field, 'blk', [(i + 1, i) for i in range(ends)])  2.57 us
    ppermute x5, starting transfers between devices, tree_sum(): x = x + lax.ppermute(x, axis, [(i, i ^ k) for i in range(n)])  1.93 us
  transfers between devices with their start and end apart: 19, of which 12 were waited for; matrix products, arithmetic and copies ran while one was open for 10% of the time, Pallas kernels for 0%

profile of v12, /device:TPU:0, one launch (start us, length us, event | category | flops | bytes accessed | tf_op | source)
XLA Modules:
  0.0 79.1 jit_solution(14405831870549578256)
XLA Ops:
  0.7 1.0 %add_reduce_fusion.9 = f32[4]{0:T(128)S(1)} fusion(f32[2,4,1,512]{3,2,1,0:T(1,128)} %param.8), kind=kLoop, calls=%fused_computation.121 | loop fusion | flops 8188 | bytes 16400 | tf_op jit(solution)/shard_map/reduce_sum | solution.py:131
  1.7 0.8 pad_maximum_fusion.1
  2.4 3.0 %collective-permute-start = (f32[4100]{0:T(1024)S(1)}, f32[4100]{0:T(1024)S(1)}, u32[]{:S(2)}, u32[]{:S(2)}) collective-permute-start(f32[4100]{0:T(1024)S(1)} %pad_maximum_fusion.1), channel_id=1, source_target_pairs={{0,16},{16,0},{1,17},{17,1},{2,18},{18,2},{3,19},{19,3},{4,20},{20... | collective-permute-start | bytes 49208 | tf_op jit(solution)/shard_map/ppermute | solution.py:44
  5.4 0.7 convert_element_type.28
  6.1 1.1 %convolution_bitcast_fusion.5 = f32[2,2,4,64]{3,2,0,1:T(4,128)S(1)} fusion(bf16[1,2,64,512]{3,2,1,0:T(8,128)(2,1)} %param.12, bf16[2,4,1,512]{3,2,1,0:T(2,128)(2,1)S(1)} %convert_element_type.28), kind=kOutput, calls=%fused_computation.15 | convolution fusion | flops 1048576 | bytes 143360 | tf_op jit(solution)/shard_map/akr,pqr->apqk/dot_general | solution.py:73
  7.2 0.7 fusion.69
  7.9 0.7 iota_compare_fusion
  8.6 0.2 and_convert_fusion
  8.9 0.8 reshape_squeeze.4
  9.8 1.1 %collective-permute-done.1 = f32[516]{0:T(1024)S(1)} collective-permute-done((f32[516]{0:T(1024)S(1)}, f32[516]{0:T(1024)S(1)}, u32[]{:S(2)}, u32[]{:S(2)}) %collective-permute-start.1) | collective-permute-done | bytes 2096 | tf_op jit(solution)/shard_map/ppermute | solution.py:44
  11.0 0.1 reshape.1792
  11.3 1.5 %collective-permute-start.2 = (f32[1028]{0:T(1024)S(1)}, f32[1028]{0:T(1024)S(1)}, u32[]{:S(2)}, u32[]{:S(2)}) collective-permute-start(f32[1028]{0:T(1024)S(1)} %pad_maximum_fusion.7), channel_id=1, source_target_pairs={{0,2},{1,3},{2,0},{3,1},{4,6},{5,7},{6,4},{7,5},{8,10},{9,11},{10,... | collective-permute-start | bytes 12344 | tf_op jit(solution)/shard_map/ppermute | solution.py:44
  12.8 2.2 %collective-permute-done.2 = f32[1028]{0:T(1024)S(1)} collective-permute-done((f32[1028]{0:T(1024)S(1)}, f32[1028]{0:T(1024)S(1)}, u32[]{:S(2)}, u32[]{:S(2)}) %collective-permute-start.2) | collective-permute-done | bytes 4144 | tf_op jit(solution)/shard_map/ppermute | solution.py:44
  15.2 1.6 %collective-permute-start.3 = (f32[2052]{0:T(1024)S(1)}, f32[2052]{0:T(1024)S(1)}, u32[]{:S(2)}, u32[]{:S(2)}) collective-permute-start(f32[2052]{0:T(1024)S(1)} %pad_maximum_fusion.5), channel_id=1, source_target_pairs={{0,4},{1,5},{2,6},{3,7},{4,0},{5,1},{6,2},{7,3},{8,12},{9,13},{10,... | collective-permute-start | bytes 24632 | tf_op jit(solution)/shard_map/ppermute | solution.py:44
  16.8 0.7 copy.178
  17.6 1.3 %collective-permute-start.5 = (f32[2,4,1,512]{3,2,1,0:T(1,128)}, f32[2,4,1,512]{3,2,1,0:T(1,128)S(1)}, u32[]{:S(2)}, u32[]{:S(2)}) collective-permute-start(f32[2,4,1,512]{3,2,1,0:T(1,128)} %param.8), channel_id=1, source_target_pairs={{0,1},{1,2},{2,3},{3,4},{4,5},{5,6},{6,7},{7,8},{8,9},{9,10},{10,1... | collective-permute-start | bytes 49160 | tf_op jit(solution)/shard_map/ppermute | solution.py:62
  18.9 1.3 %collective-permute-start.6 = (f32[2,4,1,512]{3,2,1,0:T(1,128)}, f32[2,4,1,512]{3,2,1,0:T(1,128)S(1)}, u32[]{:S(2)}, u32[]{:S(2)}) collective-permute-start(f32[2,4,1,512]{3,2,1,0:T(1,128)} %param.8), channel_id=1, source_target_pairs={{1,0},{2,1},{3,2},{4,3},{5,4},{6,5},{7,6},{8,7},{9,8},{10,9},{11,1... | collective-permute-start | bytes 49160 | tf_op jit(solution)/shard_map/ppermute | solution.py:63
  20.6 6.5 %collective-permute-start.4 = (f32[4100]{0:T(1024)S(1)}, f32[4100]{0:T(1024)S(1)}, u32[]{:S(2)}, u32[]{:S(2)}) collective-permute-start(f32[4100]{0:T(1024)S(1)} %pad_maximum_fusion.2), channel_id=1, source_target_pairs={{0,8},{1,9},{2,10},{3,11},{4,12},{5,13},{6,14},{7,15},{8,0},{9,1},... | collective-permute-start | bytes 49208 | tf_op jit(solution)/shard_map/ppermute | solution.py:44
  27.1 0.7 constant_dynamic-update-slice_fusion.1
  27.8 1.0 %collective-permute-done.4 = f32[4100]{0:T(1024)S(1)} collective-permute-done((f32[4100]{0:T(1024)S(1)}, f32[4100]{0:T(1024)S(1)}, u32[]{:S(2)}, u32[]{:S(2)}) %collective-permute-start.4) | collective-permute-done | bytes 16432 | tf_op jit(solution)/shard_map/ppermute | solution.py:44
  29.1 2.0 %convolution_bitcast_fusion.4 = f32[2,2,4,64]{3,2,0,1:T(4,128)S(1)} fusion(f32[1,1,16,2,64,64]{5,4,3,2,1,0:T(8,128)} %param.14, f32[16,64,64]{2,1,0:T(8,128)S(1)} %and_convert_fusion, f32[16,2,4,64]{3,2,1,0:T(4,128)S(1)} %fusion.18), kind=kOutput, calls=%fused_computation.14 | convolution fusion | flops 6422528 | bytes 823296 | tf_op jit(solution)/shard_map/sakl,spql->apqk/dot_general | solution.py:106
  31.2 0.1 convolution_bitcast_fusion.1
  31.5 0.6 gather_fusion.1
  32.1 0.2 broadcast_divide_fusion
  32.4 0.6 gather_fusion
  33.0 0.7 fusion.4
  33.8 0.1 convolution_bitcast_fusion.3
  34.0 0.2 add_reduce_fusion.8
  34.4 1.2 %collective-permute-done.7 = f32[528]{0:T(1024)S(1)} collective-permute-done((f32[528]{0:T(1024)S(1)}, f32[528]{0:T(1024)S(1)}, u32[]{:S(2)}, u32[]{:S(2)}) %collective-permute-start.7) | collective-permute-done | bytes 2144 | tf_op jit(solution)/shard_map/ppermute | solution.py:44
  35.9 1.2 %collective-permute-start.8 = (f32[1040]{0:T(1024)S(1)}, f32[1040]{0:T(1024)S(1)}, u32[]{:S(2)}, u32[]{:S(2)}) collective-permute-start(f32[1040]{0:T(1024)S(1)} %pad_maximum_fusion.8), channel_id=1, source_target_pairs={{0,2},{1,3},{2,0},{3,1},{4,6},{5,7},{6,4},{7,5},{8,10},{9,11},{10,... | collective-permute-start | bytes 12488 | tf_op jit(solution)/shard_map/ppermute | solution.py:44
  37.1 2.4 %collective-permute-done.8 = f32[1040]{0:T(1024)S(1)} collective-permute-done((f32[1040]{0:T(1024)S(1)}, f32[1040]{0:T(1024)S(1)}, u32[]{:S(2)}, u32[]{:S(2)}) %collective-permute-start.8) | collective-permute-done | bytes 4192 | tf_op jit(solution)/shard_map/ppermute | solution.py:44
  39.8 0.8 collective-permute-start.9
  40.6 2.9 %collective-permute-done.9 = f32[2064]{0:T(1024)S(1)} collective-permute-done((f32[2064]{0:T(1024)S(1)}, f32[2064]{0:T(1024)S(1)}, u32[]{:S(2)}, u32[]{:S(2)}) %collective-permute-start.9) | collective-permute-done | bytes 8288 | tf_op jit(solution)/shard_map/ppermute | solution.py:44
  43.9 2.9 %collective-permute-start.10 = (f32[4112]{0:T(1024)S(1)}, f32[4112]{0:T(1024)S(1)}, u32[]{:S(2)}, u32[]{:S(2)}) collective-permute-start(f32[4112]{0:T(1024)S(1)} %pad_maximum_fusion.3), channel_id=1, source_target_pairs={{0,8},{1,9},{2,10},{3,11},{4,12},{5,13},{6,14},{7,15},{8,0},{9,1},... | collective-permute-start | bytes 49352 | tf_op jit(solution)/shard_map/ppermute | solution.py:44
  46.8 1.3 %collective-permute-start.13 = (f32[2,4,1,512]{3,1,0,2:T(4,128)S(1)}, f32[2,4,1,512]{3,1,0,2:T(4,128)S(1)}, u32[]{:S(2)}, u32[]{:S(2)}) collective-permute-start(f32[2,4,1,512]{3,1,0,2:T(4,128)S(1)} %get-tuple-element.34), channel_id=1, source_target_pairs={{1,0},{2,1},{3,2},{4,3},{5,4},{6,5},{7,6},{8,7},{9,8},{10,9},{11,1... | collective-permute-start | bytes 49160 | tf_op jit(solution)/shard_map/ppermute | solution.py:63
  48.1 3.0 %collective-permute-start.12 = (f32[2,4,1,512]{3,1,0,2:T(4,128)S(1)}, f32[2,4,1,512]{3,1,0,2:T(4,128)S(1)}, u32[]{:S(2)}, u32[]{:S(2)}) collective-permute-start(f32[2,4,1,512]{3,1,0,2:T(4,128)S(1)} %get-tuple-element.34), channel_id=1, source_target_pairs={{0,1},{1,2},{2,3},{3,4},{4,5},{5,6},{6,7},{7,8},{8,9},{9,10},{10,1... | collective-permute-start | bytes 49160 | tf_op jit(solution)/shard_map/ppermute | solution.py:62
  51.5 0.5 collective-permute-start.11
  52.2 3.0 %collective-permute-done.11 = f32[4112]{0:T(1024)S(1)} collective-permute-done((f32[4112]{0:T(1024)S(1)}, f32[4112]{0:T(1024)S(1)}, u32[]{:S(2)}, u32[]{:S(2)}) %collective-permute-start.11) | collective-permute-done | bytes 16480 | tf_op jit(solution)/shard_map/ppermute | solution.py:44
  55.2 0.1 reshape.1809
  55.5 2.0 %convolution_bitcast_fusion.2 = f32[2,2,4,64]{3,2,0,1:T(4,128)S(1)} fusion(f32[1,1,16,2,64,64]{5,4,3,2,1,0:T(8,128)} %param.14, f32[16,64,64]{2,1,0:T(8,128)S(1)} %and_convert_fusion, f32[16,1,4,64]{3,2,1,0:T(4,128)S(1)} %get-tuple-element.37, f32[16,1,4,64]{3,2,1,0:T(4,128)S(1)} %get-tuple-element.36, f32[8,2,4,64]{3,2,1,0:T(4,128)S(1)} %maximum_select_fusion.4, ...), kind=kOutput, calls=%fused_computation.12 | convolution fusion | flops 6471680 | bytes 856081 | tf_op jit(solution)/shard_map/sakl,spql->apqk/dot_general | solution.py:106
  57.9 0.6 gather_fusion.3
  58.5 0.2 subtract_reduce_fusion
  58.9 0.6 gather_fusion.2
  59.4 0.7 fusion.7
  60.1 0.1 convolution_bitcast_fusion
  60.4 0.2 subtract_reduce_fusion.1
  60.7 0.6 collective-permute-start.14
  61.2 3.1 %collective-permute-done.14 = f32[8,4]{1,0:T(8,128)S(1)} collective-permute-done((f32[8,4]{1,0:T(8,128)S(1)}, f32[8,4]{1,0:T(8,128)S(1)}, u32[]{:S(2)}, u32[]{:S(2)}) %collective-permute-start.14) | collective-permute-done | bytes 160 | tf_op jit(solution)/shard_map/ppermute | solution.py:21
  64.3 1.2 %collective-permute-done.15 = f32[8,4]{1,0:T(8,128)S(1)} collective-permute-done((f32[8,4]{1,0:T(8,128)S(1)}, f32[8,4]{1,0:T(8,128)S(1)}, u32[]{:S(2)}, u32[]{:S(2)}) %collective-permute-start.15) | collective-permute-done | bytes 160 | tf_op jit(solution)/shard_map/ppermute | solution.py:21
  65.5 0.8 collective-permute-start.16
  66.3 0.1 copy.96
  66.4 0.6 copy.102
  67.0 2.1 %collective-permute-done.16 = f32[8,4]{1,0:T(8,128)S(1)} collective-permute-done((f32[8,4]{1,0:T(8,128)S(1)}, f32[8,4]{1,0:T(8,128)S(1)}, u32[]{:S(2)}, u32[]{:S(2)}) %collective-permute-start.16) | collective-permute-done | bytes 160 | tf_op jit(solution)/shard_map/ppermute | solution.py:21
  69.1 0.5 collective-permute-start.17
  69.6 0.1 copy.97
  69.7 3.1 %collective-permute-done.17 = f32[8,4]{1,0:T(8,128)S(1)} collective-permute-done((f32[8,4]{1,0:T(8,128)S(1)}, f32[8,4]{1,0:T(8,128)S(1)}, u32[]{:S(2)}, u32[]{:S(2)}) %collective-permute-start.17) | collective-permute-done | bytes 160 | tf_op jit(solution)/shard_map/ppermute | solution.py:21
  72.7 0.1 collective-permute-start.18
  72.8 0.1 copy.98
  72.9 4.3 %collective-permute-done.18 = f32[8,4]{1,0:T(8,128)S(1)} collective-permute-done((f32[8,4]{1,0:T(8,128)S(1)}, f32[8,4]{1,0:T(8,128)S(1)}, u32[]{:S(2)}, u32[]{:S(2)}) %collective-permute-start.18) | collective-permute-done | bytes 160 | tf_op jit(solution)/shard_map/ppermute | solution.py:21
  77.5 0.6 copy.103
  78.2 0.1 copy.99
  78.2 0.1 copy.100
  78.3 0.1 copy.101
  78.4 0.7 concatenate.161
  (135 shorter events, 4.8 us)
Async XLA Ops:
  0.6 32.3 %copy-start = (bf16[1,2,4,2,256,256]{5,4,3,2,1,0:T(8,128)(2,1)S(1)}, bf16[1,2,4,2,256,256]{5,4,3,2,1,0:T(8,128)(2,1)}, u32[]{:S(2)}) copy-start(bf16[1,2,4,2,256,256]{5,4,3,2,1,0:T(8,128)(2,1)} %param.9) | copy-start | bytes 6291460
  0.6 30.5 %copy-start.3 = (bf16[1,2,64,512]{3,2,1,0:T(8,128)(2,1)S(1)}, bf16[1,2,64,512]{3,2,1,0:T(8,128)(2,1)}, u32[]{:S(2)}) copy-start(bf16[1,2,64,512]{3,2,1,0:T(8,128)(2,1)} %param.13) | copy-start | bytes 393220
  2.4 7.2 %collective-permute-start = (f32[4100]{0:T(1024)S(1)}, f32[4100]{0:T(1024)S(1)}, u32[]{:S(2)}, u32[]{:S(2)}) collective-permute-start(f32[4100]{0:T(1024)S(1)} %pad_maximum_fusion.1), channel_id=1, source_target_pairs={{0,16},{16,0},{1,17},{17,1},{2,18},{18,2},{3,19},{19,3},{4,20},{20... | collective-permute-start | bytes 49208 | tf_op jit(solution)/shard_map/ppermute | solution.py:44
  9.8 1.2 %collective-permute-start.1 = (f32[516]{0:T(1024)S(1)}, f32[516]{0:T(1024)S(1)}, u32[]{:S(2)}, u32[]{:S(2)}) collective-permute-start(f32[516]{0:T(1024)S(1)} %pad_maximum_fusion.10), channel_id=1, source_target_pairs={{0,1},{1,0},{2,3},{3,2},{4,5},{5,4},{6,7},{7,6},{8,9},{9,8},{10,11... | collective-permute-start | bytes 6200 | tf_op jit(solution)/shard_map/ppermute | solution.py:44
  11.3 3.7 %collective-permute-start.2 = (f32[1028]{0:T(1024)S(1)}, f32[1028]{0:T(1024)S(1)}, u32[]{:S(2)}, u32[]{:S(2)}) collective-permute-start(f32[1028]{0:T(1024)S(1)} %pad_maximum_fusion.7), channel_id=1, source_target_pairs={{0,2},{1,3},{2,0},{3,1},{4,6},{5,7},{6,4},{7,5},{8,10},{9,11},{10,... | collective-permute-start | bytes 12344 | tf_op jit(solution)/shard_map/ppermute | solution.py:44
  15.2 5.0 %collective-permute-start.3 = (f32[2052]{0:T(1024)S(1)}, f32[2052]{0:T(1024)S(1)}, u32[]{:S(2)}, u32[]{:S(2)}) collective-permute-start(f32[2052]{0:T(1024)S(1)} %pad_maximum_fusion.5), channel_id=1, source_target_pairs={{0,4},{1,5},{2,6},{3,7},{4,0},{5,1},{6,2},{7,3},{8,12},{9,13},{10,... | collective-permute-start | bytes 24632 | tf_op jit(solution)/shard_map/ppermute | solution.py:44
  17.6 9.4 %collective-permute-start.5 = (f32[2,4,1,512]{3,2,1,0:T(1,128)}, f32[2,4,1,512]{3,2,1,0:T(1,128)S(1)}, u32[]{:S(2)}, u32[]{:S(2)}) collective-permute-start(f32[2,4,1,512]{3,2,1,0:T(1,128)} %param.8), channel_id=1, source_target_pairs={{0,1},{1,2},{2,3},{3,4},{4,5},{5,6},{6,7},{7,8},{8,9},{9,10},{10,1... | collective-permute-start | bytes 49160 | tf_op jit(solution)/shard_map/ppermute | solution.py:62
  18.9 8.9 %collective-permute-start.6 = (f32[2,4,1,512]{3,2,1,0:T(1,128)}, f32[2,4,1,512]{3,2,1,0:T(1,128)S(1)}, u32[]{:S(2)}, u32[]{:S(2)}) collective-permute-start(f32[2,4,1,512]{3,2,1,0:T(1,128)} %param.8), channel_id=1, source_target_pairs={{1,0},{2,1},{3,2},{4,3},{5,4},{6,5},{7,6},{8,7},{9,8},{10,9},{11,1... | collective-permute-start | bytes 49160 | tf_op jit(solution)/shard_map/ppermute | solution.py:63
  20.6 8.3 %collective-permute-start.4 = (f32[4100]{0:T(1024)S(1)}, f32[4100]{0:T(1024)S(1)}, u32[]{:S(2)}, u32[]{:S(2)}) collective-permute-start(f32[4100]{0:T(1024)S(1)} %pad_maximum_fusion.2), channel_id=1, source_target_pairs={{0,8},{1,9},{2,10},{3,11},{4,12},{5,13},{6,14},{7,15},{8,0},{9,1},... | collective-permute-start | bytes 49208 | tf_op jit(solution)/shard_map/ppermute | solution.py:44
  29.1 4.6 %copy-start.1 = (f32[2,4,1,512]{3,2,1,0:T(1,128)S(1)}, f32[2,4,1,512]{3,2,1,0:T(1,128)}, u32[]{:S(2)}) copy-start(f32[2,4,1,512]{3,2,1,0:T(1,128)} %param.8) | copy-start | bytes 49156
  29.1 4.6 %copy-start.2 = (bf16[1,2,64,512]{3,2,1,0:T(8,128)(2,1)S(1)}, bf16[1,2,64,512]{3,2,1,0:T(8,128)(2,1)}, u32[]{:S(2)}) copy-start(bf16[1,2,64,512]{3,2,1,0:T(8,128)(2,1)} %param.12) | copy-start | bytes 393220
  34.4 1.2 %collective-permute-start.7 = (f32[528]{0:T(1024)S(1)}, f32[528]{0:T(1024)S(1)}, u32[]{:S(2)}, u32[]{:S(2)}) collective-permute-start(f32[528]{0:T(1024)S(1)} %pad_maximum_fusion.12), channel_id=1, source_target_pairs={{0,1},{1,0},{2,3},{3,2},{4,5},{5,4},{6,7},{7,6},{8,9},{9,8},{10,11... | collective-permute-start | bytes 6344 | tf_op jit(solution)/shard_map/ppermute | solution.py:44
  35.9 3.7 %collective-permute-start.8 = (f32[1040]{0:T(1024)S(1)}, f32[1040]{0:T(1024)S(1)}, u32[]{:S(2)}, u32[]{:S(2)}) collective-permute-start(f32[1040]{0:T(1024)S(1)} %pad_maximum_fusion.8), channel_id=1, source_target_pairs={{0,2},{1,3},{2,0},{3,1},{4,6},{5,7},{6,4},{7,5},{8,10},{9,11},{10,... | collective-permute-start | bytes 12488 | tf_op jit(solution)/shard_map/ppermute | solution.py:44
  39.8 3.7 %collective-permute-start.9 = (f32[2064]{0:T(1024)S(1)}, f32[2064]{0:T(1024)S(1)}, u32[]{:S(2)}, u32[]{:S(2)}) collective-permute-start(f32[2064]{0:T(1024)S(1)} %pad_maximum_fusion.6), channel_id=1, source_target_pairs={{0,4},{1,5},{2,6},{3,7},{4,0},{5,1},{6,2},{7,3},{8,12},{9,13},{10,... | collective-permute-start | bytes 24776 | tf_op jit(solution)/shard_map/ppermute | solution.py:44
  43.9 7.5 %collective-permute-start.10 = (f32[4112]{0:T(1024)S(1)}, f32[4112]{0:T(1024)S(1)}, u32[]{:S(2)}, u32[]{:S(2)}) collective-permute-start(f32[4112]{0:T(1024)S(1)} %pad_maximum_fusion.3), channel_id=1, source_target_pairs={{0,8},{1,9},{2,10},{3,11},{4,12},{5,13},{6,14},{7,15},{8,0},{9,1},... | collective-permute-start | bytes 49352 | tf_op jit(solution)/shard_map/ppermute | solution.py:44
  46.8 5.2 %collective-permute-start.13 = (f32[2,4,1,512]{3,1,0,2:T(4,128)S(1)}, f32[2,4,1,512]{3,1,0,2:T(4,128)S(1)}, u32[]{:S(2)}, u32[]{:S(2)}) collective-permute-start(f32[2,4,1,512]{3,1,0,2:T(4,128)S(1)} %get-tuple-element.34), channel_id=1, source_target_pairs={{1,0},{2,1},{3,2},{4,3},{5,4},{6,5},{7,6},{8,7},{9,8},{10,9},{11,1... | collective-permute-start | bytes 49160 | tf_op jit(solution)/shard_map/ppermute | solution.py:63
  48.1 3.9 %collective-permute-start.12 = (f32[2,4,1,512]{3,1,0,2:T(4,128)S(1)}, f32[2,4,1,512]{3,1,0,2:T(4,128)S(1)}, u32[]{:S(2)}, u32[]{:S(2)}) collective-permute-start(f32[2,4,1,512]{3,1,0,2:T(4,128)S(1)} %get-tuple-element.34), channel_id=1, source_target_pairs={{0,1},{1,2},{2,3},{3,4},{4,5},{5,6},{6,7},{7,8},{8,9},{9,10},{10,1... | collective-permute-start | bytes 49160 | tf_op jit(solution)/shard_map/ppermute | solution.py:62
  51.5 3.8 %collective-permute-start.11 = (f32[4112]{0:T(1024)S(1)}, f32[4112]{0:T(1024)S(1)}, u32[]{:S(2)}, u32[]{:S(2)}) collective-permute-start(f32[4112]{0:T(1024)S(1)} %pad_maximum_fusion.4), channel_id=1, source_target_pairs={{0,16},{16,0},{1,17},{17,1},{2,18},{18,2},{3,19},{19,3},{4,20},{20... | collective-permute-start | bytes 49352 | tf_op jit(solution)/shard_map/ppermute | solution.py:44
  60.7 3.7 %collective-permute-start.14 = (f32[8,4]{1,0:T(8,128)S(1)}, f32[8,4]{1,0:T(8,128)S(1)}, u32[]{:S(2)}, u32[]{:S(2)}) collective-permute-start(f32[8,4]{1,0:T(8,128)S(1)} %concatenate.160), channel_id=1, source_target_pairs={{0,16},{16,0},{1,17},{17,1},{2,18},{18,2},{3,19},{19,3},{4,20},{20... | collective-permute-start | bytes 392 | tf_op jit(solution)/shard_map/ppermute | solution.py:21
  64.3 1.2 %collective-permute-start.15 = (f32[8,4]{1,0:T(8,128)S(1)}, f32[8,4]{1,0:T(8,128)S(1)}, u32[]{:S(2)}, u32[]{:S(2)}) collective-permute-start(f32[8,4]{1,0:T(8,128)S(1)} %add.554), channel_id=1, source_target_pairs={{0,1},{1,0},{2,3},{3,2},{4,5},{5,4},{6,7},{7,6},{8,9},{9,8},{10,11... | collective-permute-start | bytes 392 | tf_op jit(solution)/shard_map/ppermute | solution.py:21
  65.5 3.6 %collective-permute-start.16 = (f32[8,4]{1,0:T(8,128)S(1)}, f32[8,4]{1,0:T(8,128)S(1)}, u32[]{:S(2)}, u32[]{:S(2)}) collective-permute-start(f32[8,4]{1,0:T(8,128)S(1)} %add.555), channel_id=1, source_target_pairs={{0,2},{1,3},{2,0},{3,1},{4,6},{5,7},{6,4},{7,5},{8,10},{9,11},{10,... | collective-permute-start | bytes 392 | tf_op jit(solution)/shard_map/ppermute | solution.py:21
  69.1 3.6 %collective-permute-start.17 = (f32[8,4]{1,0:T(8,128)S(1)}, f32[8,4]{1,0:T(8,128)S(1)}, u32[]{:S(2)}, u32[]{:S(2)}) collective-permute-start(f32[8,4]{1,0:T(8,128)S(1)} %add.556), channel_id=1, source_target_pairs={{0,4},{1,5},{2,6},{3,7},{4,0},{5,1},{6,2},{7,3},{8,12},{9,13},{10,... | collective-permute-start | bytes 392 | tf_op jit(solution)/shard_map/ppermute | solution.py:21
  72.7 4.5 %collective-permute-start.18 = (f32[8,4]{1,0:T(8,128)S(1)}, f32[8,4]{1,0:T(8,128)S(1)}, u32[]{:S(2)}, u32[]{:S(2)}) collective-permute-start(f32[8,4]{1,0:T(8,128)S(1)} %add.557), channel_id=1, source_target_pairs={{0,8},{1,9},{2,10},{3,11},{4,12},{5,13},{6,14},{7,15},{8,0},{9,1},... | collective-permute-start | bytes 392 | tf_op jit(solution)/shard_map/ppermute | solution.py:21

commit v13 on v12

--- a/solution.py
+++ b/solution.py
@@ -76,17 +76,22 @@
     return jnp.stack([coef_prod[0, 0] + coef_prod[1, 1], coef_prod[0, 1] - coef_prod[1, 0]])
 
 
-def near_field(window, near_blocks, near_cols):
+def near_tiles(window, near_blocks, near_cols):
     nrhs = window.shape[1]
+    blocks_dev = near_blocks.shape[1]
+    width = near_blocks.shape[4]
+    tiles = window.reshape(2, nrhs, 3 * blocks_dev, width)
+    return tiles.at[:, :, near_cols[0].reshape(-1)].get(mode="promise_in_bounds")
+
+
+def near_field(chosen, near_blocks):
+    nrhs = chosen.shape[1]
     blocks_dev = near_blocks.shape[1]
     slots = near_blocks.shape[2]
     width = near_blocks.shape[4]
-    rounded = window.astype(jnp.bfloat16).reshape(2, nrhs, 3 * blocks_dev, width)
-    chosen = rounded.at[:, :, near_cols[0].reshape(-1)].get(mode="promise_in_bounds").reshape(
-        2, nrhs, blocks_dev, slots, width
-    )
+    rounded = chosen.astype(jnp.bfloat16).reshape(2, nrhs, blocks_dev, slots, width)
     near_prod = jnp.einsum(
-        "ikarc,pqikc->apqir", near_blocks[0], chosen, preferred_element_type=jnp.float32
+        "ikarc,pqikc->apqir", near_blocks[0], rounded, preferred_element_type=jnp.float32
     )
     return complex_mix(near_prod).reshape(2, nrhs, 1, blocks_dev * width)
 
@@ -113,9 +118,8 @@
 
 def swapped(every, partner, width):
     nrhs = every.shape[1]
-    rows = every.shape[3]
     tiles = every.reshape(2, nrhs, -1, width)
-    return tiles.at[:, :, partner[0]].get(mode="promise_in_bounds").reshape(2, nrhs, 1, rows)
+    return tiles.at[:, :, partner[0]].get(mode="promise_in_bounds")
 
 
 def local_products(vectors, image):
@@ -168,14 +172,14 @@
     beta = jnp.sqrt(start_sum / total + EPSILON)
     inv_scale = beta[None, :, None, None]
     first_vec = right_side / inv_scale
-    window_one = window_rhs / inv_scale
-    every_one = spread(every_rhs) / inv_scale
+    chosen_one = near_tiles(window_rhs, near_blocks, near_cols) / inv_scale
+    mates_one = swapped(spread(every_rhs), partner, width) / inv_scale
     coef_one = coef_rhs / beta[None, None, :, None]
     image_one = (
         first_vec
-        + near_field(window_one, near_blocks, near_cols)
+        + near_field(chosen_one, near_blocks)
         + far_field(coef_one, weights, target_basis)
-        - swapped(every_one, partner, width)
+        - mates_one.reshape(first_vec.shape)
     )
 
     window_img = neighbours(image_one)
@@ -198,15 +202,17 @@
     h_two_one = jnp.sqrt(sq_u1 + EPSILON)
     inv_two = h_two_one[None, :, None, None]
     second_basis = (image_one - scaled(h_one_one, first_vec)) / inv_two
-    window_two = (window_img - scaled(h_one_one, window_one)) / inv_two
-    every_two = (spread(every_img) - scaled(h_one_one, every_one)) / inv_two
+    chosen_img = near_tiles(window_img, near_blocks, near_cols)
+    chosen_two = (chosen_img - scaled(h_one_one, chosen_one)) / inv_two
+    mates_img = swapped(spread(every_img), partner, width)
+    mates_two = (mates_img - scaled(h_one_one, mates_one)) / inv_two
     coef_two = (coef_img - coef_scaled(h_one_one, coef_one)) / h_two_one[None, None, :, None]
     early_columns = jnp.stack([beta, h_one_one[0], h_one_one[1], h_two_one], axis=1)
     image_two = (
         second_basis
-        + near_field(window_two, near_blocks, near_cols)
+        + near_field(chosen_two, near_blocks)
         + far_field(coef_two, weights, target_basis)
-        - swapped(every_two, partner, width)
+        - mates_two.reshape(second_basis.shape)
     )
 
     two = (

time: 79.8 us -> 77.3 us (0.969)
  waiting for transfers between devices: 27.6 us -> 20.9 us
  starting transfers between devices: 26.8 us -> 31.2 us
    ppermute x5, starting transfers between devices: 1.93 us -> 9.28 us  [tree_sum(): x = x + lax.ppermute(x, axis, [(i, i ^ k) for i in range(n)])]
    ppermute x5, waiting for transfers between devices: 13.7 us -> 8.67 us  [tree_sum(): x = x + lax.ppermute(x, axis, [(i, i ^ k) for i in range(n)])]
    ppermute x10, waiting for transfers between devices: 13.8 us -> 10.5 us  [tree_collect(): got = lax.ppermute(packed, axis, [(i, i ^ k) for i in range(n)])]
    ppermute x2, starting transfers between devices: 4.32 us -> 2.57 us  [neighbours(): left = lax.ppermute(field, 'blk', [(i, i + 1) for i in range(ends)])]
    ppermute x2, waiting for transfers between devices: 0.01 us -> 1.75 us  [neighbours(): right = lax.ppermute(field, 'blk', [(i + 1, i) for i in range(ends)])]
    ppermute x10, starting transfers between devices: 17.9 us -> 16.7 us  [tree_collect(): got = lax.ppermute(packed, axis, [(i, i ^ k) for i in range(n)])]
    concatenate x1 -> x2, other arithmetic: 0.01 us -> 0.87 us  [neighbours(): return jnp.concatenate([left, field, right], axis=3)]
    unnamed x14 -> x12, local copies, waits for them, and re-layouts: 2.74 us -> 2.01 us
  transfers between devices with their start and end apart: 19 -> 19, of which waited for: 12 -> 12; matrix products, arithmetic and copies ran while one was open for 10% -> 13% of each run, Pallas kernels for 0% -> 0%
where the time goes in v13:
time: 77.3 us; the launch traced here: 76.6 us
  starting transfers between devices  31.2 us (40%)
  waiting for transfers between devices  20.9 us (27%)
  local copies, waits for them, and re-layouts  9.13 us (12%)
  other arithmetic  7.4 us (10%)
  matrix products  6.83 us (9%)
  between operations  1.14 us (1%)
    ppermute x10, starting transfers between devices, tree_collect(): got = lax.ppermute(packed, axis, [(i, i ^ k) for i in range(n)])  16.7 us
    ppermute x10, waiting for transfers between devices, tree_collect(): got = lax.ppermute(packed, axis, [(i, i ^ k) for i in range(n)])  10.5 us
    ppermute x5, starting transfers between devices, tree_sum(): x = x + lax.ppermute(x, axis, [(i, i ^ k) for i in range(n)])  9.28 us
    ppermute x5, waiting for transfers between devices, tree_sum(): x = x + lax.ppermute(x, axis, [(i, i ^ k) for i in range(n)])  8.67 us
    dot_general x2, matrix products, far_field(): jnp.einsum('sakl,spql->apqk', weights, gathered, precision=lax.Precision....  4.01 us
    ppermute x2, starting transfers between devices, neighbours(): right = lax.ppermute(field, 'blk', [(i + 1, i) for i in range(ends)])  2.58 us
    ppermute x2, starting transfers between devices, neighbours(): left = lax.ppermute(field, 'blk', [(i, i + 1) for i in range(ends)])  2.57 us
    unnamed x12, local copies, waits for them, and re-layouts  2.01 us
  transfers between devices with their start and end apart: 19, of which 12 were waited for; matrix products, arithmetic and copies ran while one was open for 13% of the time, Pallas kernels for 0%

profile of v13, /device:TPU:0, one launch (start us, length us, event | category | flops | bytes accessed | tf_op | source)
XLA Modules:
  0.0 76.6 jit_solution(13827785479049995503)
XLA Ops:
  0.7 1.0 %add_reduce_fusion.8 = f32[4]{0:T(128)S(1)} fusion(f32[2,4,1,512]{3,2,1,0:T(1,128)} %param.8), kind=kLoop, calls=%fused_computation.123 | loop fusion | flops 8188 | bytes 16400 | tf_op jit(solution)/shard_map/reduce_sum | solution.py:135
  1.7 0.8 %pad_maximum_fusion.1 = f32[4100]{0:T(1024)S(1)} fusion(f32[4096]{0:T(1024)} %bitcast.363, f32[4]{0:T(128)S(1)} %add_reduce_fusion.8), kind=kLoop, calls=%fused_computation.55 | loop fusion | flops 4100 | bytes 32800 | tf_op jit(solution)/shard_map/concatenate | solution.py:40
  2.4 3.0 %collective-permute-start = (f32[4100]{0:T(1024)S(1)}, f32[4100]{0:T(1024)S(1)}, u32[]{:S(2)}, u32[]{:S(2)}) collective-permute-start(f32[4100]{0:T(1024)S(1)} %pad_maximum_fusion.1), channel_id=1, source_target_pairs={{0,16},{16,0},{1,17},{17,1},{2,18},{18,2},{3,19},{19,3},{4,20},{20... | collective-permute-start | bytes 49208 | tf_op jit(solution)/shard_map/ppermute | solution.py:44
  5.4 0.7 convert_element_type.24
  6.1 1.1 %convolution_bitcast_fusion.5 = f32[2,2,4,64]{3,2,0,1:T(4,128)S(1)} fusion(bf16[1,2,64,512]{3,2,1,0:T(8,128)(2,1)} %param.12, bf16[2,4,1,512]{3,2,1,0:T(2,128)(2,1)S(1)} %convert_element_type.24), kind=kOutput, calls=%fused_computation.15 | convolution fusion | flops 1048576 | bytes 143360 | tf_op jit(solution)/shard_map/akr,pqr->apqk/dot_general | solution.py:73
  7.2 0.7 iota_compare_fusion
  8.0 0.2 and_convert_fusion
  8.2 0.8 reshape_squeeze.4
  9.1 0.7 fusion.66
  9.8 0.5 collective-permute-done.1
  10.6 1.5 %collective-permute-start.2 = (f32[1028]{0:T(1024)S(1)}, f32[1028]{0:T(1024)S(1)}, u32[]{:S(2)}, u32[]{:S(2)}) collective-permute-start(f32[1028]{0:T(1024)S(1)} %pad_maximum_fusion.7), channel_id=1, source_target_pairs={{0,2},{1,3},{2,0},{3,1},{4,6},{5,7},{6,4},{7,5},{8,10},{9,11},{10,... | collective-permute-start | bytes 12344 | tf_op jit(solution)/shard_map/ppermute | solution.py:44
  12.1 2.2 %collective-permute-done.2 = f32[1028]{0:T(1024)S(1)} collective-permute-done((f32[1028]{0:T(1024)S(1)}, f32[1028]{0:T(1024)S(1)}, u32[]{:S(2)}, u32[]{:S(2)}) %collective-permute-start.2) | collective-permute-done | bytes 4144 | tf_op jit(solution)/shard_map/ppermute | solution.py:44
  14.6 1.6 %collective-permute-start.3 = (f32[2052]{0:T(1024)S(1)}, f32[2052]{0:T(1024)S(1)}, u32[]{:S(2)}, u32[]{:S(2)}) collective-permute-start(f32[2052]{0:T(1024)S(1)} %pad_maximum_fusion.5), channel_id=1, source_target_pairs={{0,4},{1,5},{2,6},{3,7},{4,0},{5,1},{6,2},{7,3},{8,12},{9,13},{10,... | collective-permute-start | bytes 24632 | tf_op jit(solution)/shard_map/ppermute | solution.py:44
  16.2 0.7 copy.173
  17.0 1.3 %collective-permute-start.5 = (f32[2,4,1,512]{3,2,1,0:T(1,128)}, f32[2,4,1,512]{3,2,1,0:T(1,128)S(1)}, u32[]{:S(2)}, u32[]{:S(2)}) collective-permute-start(f32[2,4,1,512]{3,2,1,0:T(1,128)} %param.8), channel_id=1, source_target_pairs={{0,1},{1,2},{2,3},{3,4},{4,5},{5,6},{6,7},{7,8},{8,9},{9,10},{10,1... | collective-permute-start | bytes 49160 | tf_op jit(solution)/shard_map/ppermute | solution.py:62
  18.3 1.3 %collective-permute-start.6 = (f32[2,4,1,512]{3,2,1,0:T(1,128)}, f32[2,4,1,512]{3,2,1,0:T(1,128)S(1)}, u32[]{:S(2)}, u32[]{:S(2)}) collective-permute-start(f32[2,4,1,512]{3,2,1,0:T(1,128)} %param.8), channel_id=1, source_target_pairs={{1,0},{2,1},{3,2},{4,3},{5,4},{6,5},{7,6},{8,7},{9,8},{10,9},{11,1... | collective-permute-start | bytes 49160 | tf_op jit(solution)/shard_map/ppermute | solution.py:63
  19.9 6.5 %collective-permute-start.4 = (f32[4100]{0:T(1024)S(1)}, f32[4100]{0:T(1024)S(1)}, u32[]{:S(2)}, u32[]{:S(2)}) collective-permute-start(f32[4100]{0:T(1024)S(1)} %pad_maximum_fusion.2), channel_id=1, source_target_pairs={{0,8},{1,9},{2,10},{3,11},{4,12},{5,13},{6,14},{7,15},{8,0},{9,1},... | collective-permute-start | bytes 49208 | tf_op jit(solution)/shard_map/ppermute | solution.py:44
  26.5 0.6 gather_fusion.1
  27.1 0.9 %maximum_reduce_fusion = f32[2,4,1536]{2,1,0:T(4,128)S(1)} fusion(f32[2,4,1,512]{3,2,1,0:T(1,128)S(1)} %collective-permute-done.6, f32[2,4,1,512]{3,2,1,0:T(1,128)} %param.8, f32[2,4,1,512]{3,2,1,0:T(1,128)S(1)} %collective-permute-done.5), kind=kLoop, calls=%fused_computation.38 | loop fusion | flops 24576 | bytes 98304 | tf_op jit(solution)/shard_map/concatenate | solution.py:64
  28.0 0.6 gather_fusion
  28.9 2.0 %convolution_bitcast_fusion.4 = f32[2,2,4,64]{3,2,0,1:T(4,128)S(1)} fusion(f32[1,1,16,2,64,64]{5,4,3,2,1,0:T(8,128)} %param.14, f32[16,64,64]{2,1,0:T(8,128)S(1)} %and_convert_fusion, f32[16,2,4,64]{3,2,1,0:T(4,128)S(1)} %fusion.18), kind=kOutput, calls=%fused_computation.14 | convolution fusion | flops 6422528 | bytes 823296 | tf_op jit(solution)/shard_map/sakl,spql->apqk/dot_general | solution.py:111
  31.0 0.1 convolution_bitcast_fusion.1
  31.1 0.7 fusion.4
  31.9 0.1 convolution_bitcast_fusion.3
  32.1 0.2 add_reduce_fusion.7
  32.5 1.2 %collective-permute-done.7 = f32[528]{0:T(1024)S(1)} collective-permute-done((f32[528]{0:T(1024)S(1)}, f32[528]{0:T(1024)S(1)}, u32[]{:S(2)}, u32[]{:S(2)}) %collective-permute-start.7) | collective-permute-done | bytes 2144 | tf_op jit(solution)/shard_map/ppermute | solution.py:44
  33.8 0.1 reshape.1721
  34.0 0.8 %collective-permute-start.8 = (f32[1040]{0:T(1024)S(1)}, f32[1040]{0:T(1024)S(1)}, u32[]{:S(2)}, u32[]{:S(2)}) collective-permute-start(f32[1040]{0:T(1024)S(1)} %pad_maximum_fusion.8), channel_id=1, source_target_pairs={{0,2},{1,3},{2,0},{3,1},{4,6},{5,7},{6,4},{7,5},{8,10},{9,11},{10,... | collective-permute-start | bytes 12488 | tf_op jit(solution)/shard_map/ppermute | solution.py:44
  34.8 2.9 %collective-permute-done.8 = f32[1040]{0:T(1024)S(1)} collective-permute-done((f32[1040]{0:T(1024)S(1)}, f32[1040]{0:T(1024)S(1)}, u32[]{:S(2)}, u32[]{:S(2)}) %collective-permute-start.8) | collective-permute-done | bytes 4192 | tf_op jit(solution)/shard_map/ppermute | solution.py:44
  38.0 0.5 collective-permute-start.9
  38.5 3.2 %collective-permute-done.9 = f32[2064]{0:T(1024)S(1)} collective-permute-done((f32[2064]{0:T(1024)S(1)}, f32[2064]{0:T(1024)S(1)}, u32[]{:S(2)}, u32[]{:S(2)}) %collective-permute-start.9) | collective-permute-done | bytes 8288 | tf_op jit(solution)/shard_map/ppermute | solution.py:44
  42.0 2.5 %collective-permute-start.10 = (f32[4112]{0:T(1024)S(1)}, f32[4112]{0:T(1024)S(1)}, u32[]{:S(2)}, u32[]{:S(2)}) collective-permute-start(f32[4112]{0:T(1024)S(1)} %pad_maximum_fusion.3), channel_id=1, source_target_pairs={{0,8},{1,9},{2,10},{3,11},{4,12},{5,13},{6,14},{7,15},{8,0},{9,1},... | collective-permute-start | bytes 49352 | tf_op jit(solution)/shard_map/ppermute | solution.py:44
  44.6 1.3 %collective-permute-start.12 = (f32[2,4,1,512]{3,1,0,2:T(4,128)S(1)}, f32[2,4,1,512]{3,1,0,2:T(4,128)S(1)}, u32[]{:S(2)}, u32[]{:S(2)}) collective-permute-start(f32[2,4,1,512]{3,1,0,2:T(4,128)S(1)} %get-tuple-element.56), channel_id=1, source_target_pairs={{0,1},{1,2},{2,3},{3,4},{4,5},{5,6},{6,7},{7,8},{8,9},{9,10},{10,1... | collective-permute-start | bytes 49160 | tf_op jit(solution)/shard_map/ppermute | solution.py:62
  45.9 1.3 %collective-permute-start.13 = (f32[2,4,1,512]{3,1,0,2:T(4,128)S(1)}, f32[2,4,1,512]{3,1,0,2:T(4,128)S(1)}, u32[]{:S(2)}, u32[]{:S(2)}) collective-permute-start(f32[2,4,1,512]{3,1,0,2:T(4,128)S(1)} %get-tuple-element.56), channel_id=1, source_target_pairs={{1,0},{2,1},{3,2},{4,3},{5,4},{6,5},{7,6},{8,7},{9,8},{10,9},{11,1... | collective-permute-start | bytes 49160 | tf_op jit(solution)/shard_map/ppermute | solution.py:63
  47.5 0.5 collective-permute-start.11
  48.0 1.7 %collective-permute-done.13 = f32[2,4,1,512]{3,1,0,2:T(4,128)S(1)} collective-permute-done((f32[2,4,1,512]{3,1,0,2:T(4,128)S(1)}, f32[2,4,1,512]{3,1,0,2:T(4,128)S(1)}, u32[]{:S(2)}, u32[]{:S(2)}) %collective-permute-start.13) | collective-permute-done | bytes 16416 | tf_op jit(solution)/shard_map/ppermute | solution.py:63
  49.8 0.6 gather_fusion.2
  50.6 0.7 collective-permute-done.11
  51.3 0.1 reshape.1727
  51.6 2.0 %convolution_bitcast_fusion.2 = f32[2,2,4,64]{3,2,0,1:T(4,128)S(1)} fusion(f32[1,1,16,2,64,64]{5,4,3,2,1,0:T(8,128)} %param.14, f32[16,64,64]{2,1,0:T(8,128)S(1)} %and_convert_fusion, f32[16,1,4,64]{3,2,1,0:T(4,128)S(1)} %get-tuple-element.33, f32[16,1,4,64]{3,2,1,0:T(4,128)S(1)} %get-tuple-element.32, f32[8,2,4,64]{3,2,1,0:T(4,128)S(1)} %maximum_select_fusion.4, ...), kind=kOutput, calls=%fused_computation.12 | convolution fusion | flops 6471680 | bytes 856081 | tf_op jit(solution)/shard_map/sakl,spql->apqk/dot_general | solution.py:111
  53.9 0.6 gather_fusion.3
  54.5 0.1 convolution_bitcast_fusion
  54.7 0.1 multiply_subtract_fusion.1
  54.8 0.7 fusion.7
  55.6 0.2 subtract_reduce_fusion
  55.9 0.6 collective-permute-start.14
  56.4 3.1 %collective-permute-done.14 = f32[8,4]{1,0:T(8,128)S(1)} collective-permute-done((f32[8,4]{1,0:T(8,128)S(1)}, f32[8,4]{1,0:T(8,128)S(1)}, u32[]{:S(2)}, u32[]{:S(2)}) %collective-permute-start.14) | collective-permute-done | bytes 160 | tf_op jit(solution)/shard_map/ppermute | solution.py:21
  59.5 0.7 collective-permute-start.15
  60.2 0.8 %collective-permute-done.15 = f32[8,4]{1,0:T(8,128)S(1)} collective-permute-done((f32[8,4]{1,0:T(8,128)S(1)}, f32[8,4]{1,0:T(8,128)S(1)}, u32[]{:S(2)}, u32[]{:S(2)}) %collective-permute-start.15) | collective-permute-done | bytes 160 | tf_op jit(solution)/shard_map/ppermute | solution.py:21
  61.0 3.2 %collective-permute-start.16 = (f32[8,4]{1,0:T(8,128)S(1)}, f32[8,4]{1,0:T(8,128)S(1)}, u32[]{:S(2)}, u32[]{:S(2)}) collective-permute-start(f32[8,4]{1,0:T(8,128)S(1)} %add.551), channel_id=1, source_target_pairs={{0,2},{1,3},{2,0},{3,1},{4,6},{5,7},{6,4},{7,5},{8,10},{9,11},{10,... | collective-permute-start | bytes 392 | tf_op jit(solution)/shard_map/ppermute | solution.py:21
  64.3 0.1 copy.94
  64.3 0.6 copy.100
  65.0 0.9 %collective-permute-done.16 = f32[8,4]{1,0:T(8,128)S(1)} collective-permute-done((f32[8,4]{1,0:T(8,128)S(1)}, f32[8,4]{1,0:T(8,128)S(1)}, u32[]{:S(2)}, u32[]{:S(2)}) %collective-permute-start.16) | collective-permute-done | bytes 160 | tf_op jit(solution)/shard_map/ppermute | solution.py:21
  65.8 2.8 %collective-permute-start.17 = (f32[8,4]{1,0:T(8,128)S(1)}, f32[8,4]{1,0:T(8,128)S(1)}, u32[]{:S(2)}, u32[]{:S(2)}) collective-permute-start(f32[8,4]{1,0:T(8,128)S(1)} %add.552), channel_id=1, source_target_pairs={{0,4},{1,5},{2,6},{3,7},{4,0},{5,1},{6,2},{7,3},{8,12},{9,13},{10,... | collective-permute-start | bytes 392 | tf_op jit(solution)/shard_map/ppermute | solution.py:21
  68.6 0.1 copy.95
  68.7 1.5 %collective-permute-done.17 = f32[8,4]{1,0:T(8,128)S(1)} collective-permute-done((f32[8,4]{1,0:T(8,128)S(1)}, f32[8,4]{1,0:T(8,128)S(1)}, u32[]{:S(2)}, u32[]{:S(2)}) %collective-permute-start.17) | collective-permute-done | bytes 160 | tf_op jit(solution)/shard_map/ppermute | solution.py:21
  70.2 2.0 %collective-permute-start.18 = (f32[8,4]{1,0:T(8,128)S(1)}, f32[8,4]{1,0:T(8,128)S(1)}, u32[]{:S(2)}, u32[]{:S(2)}) collective-permute-start(f32[8,4]{1,0:T(8,128)S(1)} %add.553), channel_id=1, source_target_pairs={{0,8},{1,9},{2,10},{3,11},{4,12},{5,13},{6,14},{7,15},{8,0},{9,1},... | collective-permute-start | bytes 392 | tf_op jit(solution)/shard_map/ppermute | solution.py:21
  72.3 0.1 copy.96
  72.3 2.4 %collective-permute-done.18 = f32[8,4]{1,0:T(8,128)S(1)} collective-permute-done((f32[8,4]{1,0:T(8,128)S(1)}, f32[8,4]{1,0:T(8,128)S(1)}, u32[]{:S(2)}, u32[]{:S(2)}) %collective-permute-start.18) | collective-permute-done | bytes 160 | tf_op jit(solution)/shard_map/ppermute | solution.py:21
  74.8 0.1 copy.97
  74.9 0.1 copy.99
  75.0 0.1 copy.98
  75.3 0.6 copy.101
  75.9 0.7 concatenate.149
  (134 shorter events, 4.6 us)
Async XLA Ops:
  0.6 30.5 %copy-start = (bf16[1,2,4,2,256,256]{5,4,3,2,1,0:T(8,128)(2,1)S(1)}, bf16[1,2,4,2,256,256]{5,4,3,2,1,0:T(8,128)(2,1)}, u32[]{:S(2)}) copy-start(bf16[1,2,4,2,256,256]{5,4,3,2,1,0:T(8,128)(2,1)} %param.9) | copy-start | bytes 6291460
  0.6 30.3 %copy-start.3 = (bf16[1,2,64,512]{3,2,1,0:T(8,128)(2,1)S(1)}, bf16[1,2,64,512]{3,2,1,0:T(8,128)(2,1)}, u32[]{:S(2)}) copy-start(bf16[1,2,64,512]{3,2,1,0:T(8,128)(2,1)} %param.13) | copy-start | bytes 393220
  2.4 6.6 %collective-permute-start = (f32[4100]{0:T(1024)S(1)}, f32[4100]{0:T(1024)S(1)}, u32[]{:S(2)}, u32[]{:S(2)}) collective-permute-start(f32[4100]{0:T(1024)S(1)} %pad_maximum_fusion.1), channel_id=1, source_target_pairs={{0,16},{16,0},{1,17},{17,1},{2,18},{18,2},{3,19},{19,3},{4,20},{20... | collective-permute-start | bytes 49208 | tf_op jit(solution)/shard_map/ppermute | solution.py:44
  9.1 1.2 %collective-permute-start.1 = (f32[516]{0:T(1024)S(1)}, f32[516]{0:T(1024)S(1)}, u32[]{:S(2)}, u32[]{:S(2)}) collective-permute-start(f32[516]{0:T(1024)S(1)} %pad_maximum_fusion.10), channel_id=1, source_target_pairs={{0,1},{1,0},{2,3},{3,2},{4,5},{5,4},{6,7},{7,6},{8,9},{9,8},{10,11... | collective-permute-start | bytes 6200 | tf_op jit(solution)/shard_map/ppermute | solution.py:44
  10.6 3.7 %collective-permute-start.2 = (f32[1028]{0:T(1024)S(1)}, f32[1028]{0:T(1024)S(1)}, u32[]{:S(2)}, u32[]{:S(2)}) collective-permute-start(f32[1028]{0:T(1024)S(1)} %pad_maximum_fusion.7), channel_id=1, source_target_pairs={{0,2},{1,3},{2,0},{3,1},{4,6},{5,7},{6,4},{7,5},{8,10},{9,11},{10,... | collective-permute-start | bytes 12344 | tf_op jit(solution)/shard_map/ppermute | solution.py:44
  14.6 5.0 %collective-permute-start.3 = (f32[2052]{0:T(1024)S(1)}, f32[2052]{0:T(1024)S(1)}, u32[]{:S(2)}, u32[]{:S(2)}) collective-permute-start(f32[2052]{0:T(1024)S(1)} %pad_maximum_fusion.5), channel_id=1, source_target_pairs={{0,4},{1,5},{2,6},{3,7},{4,0},{5,1},{6,2},{7,3},{8,12},{9,13},{10,... | collective-permute-start | bytes 24632 | tf_op jit(solution)/shard_map/ppermute | solution.py:44
  17.0 10.1 %collective-permute-start.5 = (f32[2,4,1,512]{3,2,1,0:T(1,128)}, f32[2,4,1,512]{3,2,1,0:T(1,128)S(1)}, u32[]{:S(2)}, u32[]{:S(2)}) collective-permute-start(f32[2,4,1,512]{3,2,1,0:T(1,128)} %param.8), channel_id=1, source_target_pairs={{0,1},{1,2},{2,3},{3,4},{4,5},{5,6},{6,7},{7,8},{8,9},{9,10},{10,1... | collective-permute-start | bytes 49160 | tf_op jit(solution)/shard_map/ppermute | solution.py:62
  18.3 8.9 %collective-permute-start.6 = (f32[2,4,1,512]{3,2,1,0:T(1,128)}, f32[2,4,1,512]{3,2,1,0:T(1,128)S(1)}, u32[]{:S(2)}, u32[]{:S(2)}) collective-permute-start(f32[2,4,1,512]{3,2,1,0:T(1,128)} %param.8), channel_id=1, source_target_pairs={{1,0},{2,1},{3,2},{4,3},{5,4},{6,5},{7,6},{8,7},{9,8},{10,9},{11,1... | collective-permute-start | bytes 49160 | tf_op jit(solution)/shard_map/ppermute | solution.py:63
  19.9 8.7 %collective-permute-start.4 = (f32[4100]{0:T(1024)S(1)}, f32[4100]{0:T(1024)S(1)}, u32[]{:S(2)}, u32[]{:S(2)}) collective-permute-start(f32[4100]{0:T(1024)S(1)} %pad_maximum_fusion.2), channel_id=1, source_target_pairs={{0,8},{1,9},{2,10},{3,11},{4,12},{5,13},{6,14},{7,15},{8,0},{9,1},... | collective-permute-start | bytes 49208 | tf_op jit(solution)/shard_map/ppermute | solution.py:44
  28.9 2.9 %copy-start.1 = (f32[2,4,1,512]{3,2,1,0:T(1,128)S(1)}, f32[2,4,1,512]{3,2,1,0:T(1,128)}, u32[]{:S(2)}) copy-start(f32[2,4,1,512]{3,2,1,0:T(1,128)} %param.8) | copy-start | bytes 49156
  28.9 3.0 %copy-start.2 = (bf16[1,2,64,512]{3,2,1,0:T(8,128)(2,1)S(1)}, bf16[1,2,64,512]{3,2,1,0:T(8,128)(2,1)}, u32[]{:S(2)}) copy-start(bf16[1,2,64,512]{3,2,1,0:T(8,128)(2,1)} %param.12) | copy-start | bytes 393220
  32.5 1.2 %collective-permute-start.7 = (f32[528]{0:T(1024)S(1)}, f32[528]{0:T(1024)S(1)}, u32[]{:S(2)}, u32[]{:S(2)}) collective-permute-start(f32[528]{0:T(1024)S(1)} %pad_maximum_fusion.12), channel_id=1, source_target_pairs={{0,1},{1,0},{2,3},{3,2},{4,5},{5,4},{6,7},{7,6},{8,9},{9,8},{10,11... | collective-permute-start | bytes 6344 | tf_op jit(solution)/shard_map/ppermute | solution.py:44
  34.0 3.7 %collective-permute-start.8 = (f32[1040]{0:T(1024)S(1)}, f32[1040]{0:T(1024)S(1)}, u32[]{:S(2)}, u32[]{:S(2)}) collective-permute-start(f32[1040]{0:T(1024)S(1)} %pad_maximum_fusion.8), channel_id=1, source_target_pairs={{0,2},{1,3},{2,0},{3,1},{4,6},{5,7},{6,4},{7,5},{8,10},{9,11},{10,... | collective-permute-start | bytes 12488 | tf_op jit(solution)/shard_map/ppermute | solution.py:44
  38.0 3.7 %collective-permute-start.9 = (f32[2064]{0:T(1024)S(1)}, f32[2064]{0:T(1024)S(1)}, u32[]{:S(2)}, u32[]{:S(2)}) collective-permute-start(f32[2064]{0:T(1024)S(1)} %pad_maximum_fusion.6), channel_id=1, source_target_pairs={{0,4},{1,5},{2,6},{3,7},{4,0},{5,1},{6,2},{7,3},{8,12},{9,13},{10,... | collective-permute-start | bytes 24776 | tf_op jit(solution)/shard_map/ppermute | solution.py:44
  42.0 5.4 %collective-permute-start.10 = (f32[4112]{0:T(1024)S(1)}, f32[4112]{0:T(1024)S(1)}, u32[]{:S(2)}, u32[]{:S(2)}) collective-permute-start(f32[4112]{0:T(1024)S(1)} %pad_maximum_fusion.3), channel_id=1, source_target_pairs={{0,8},{1,9},{2,10},{3,11},{4,12},{5,13},{6,14},{7,15},{8,0},{9,1},... | collective-permute-start | bytes 49352 | tf_op jit(solution)/shard_map/ppermute | solution.py:44
  44.6 3.4 %collective-permute-start.12 = (f32[2,4,1,512]{3,1,0,2:T(4,128)S(1)}, f32[2,4,1,512]{3,1,0,2:T(4,128)S(1)}, u32[]{:S(2)}, u32[]{:S(2)}) collective-permute-start(f32[2,4,1,512]{3,1,0,2:T(4,128)S(1)} %get-tuple-element.56), channel_id=1, source_target_pairs={{0,1},{1,2},{2,3},{3,4},{4,5},{5,6},{6,7},{7,8},{8,9},{9,10},{10,1... | collective-permute-start | bytes 49160 | tf_op jit(solution)/shard_map/ppermute | solution.py:62
  45.9 3.9 %collective-permute-start.13 = (f32[2,4,1,512]{3,1,0,2:T(4,128)S(1)}, f32[2,4,1,512]{3,1,0,2:T(4,128)S(1)}, u32[]{:S(2)}, u32[]{:S(2)}) collective-permute-start(f32[2,4,1,512]{3,1,0,2:T(4,128)S(1)} %get-tuple-element.56), channel_id=1, source_target_pairs={{1,0},{2,1},{3,2},{4,3},{5,4},{6,5},{7,6},{8,7},{9,8},{10,9},{11,1... | collective-permute-start | bytes 49160 | tf_op jit(solution)/shard_map/ppermute | solution.py:63
  47.5 3.8 %collective-permute-start.11 = (f32[4112]{0:T(1024)S(1)}, f32[4112]{0:T(1024)S(1)}, u32[]{:S(2)}, u32[]{:S(2)}) collective-permute-start(f32[4112]{0:T(1024)S(1)} %pad_maximum_fusion.4), channel_id=1, source_target_pairs={{0,16},{16,0},{1,17},{17,1},{2,18},{18,2},{3,19},{19,3},{4,20},{20... | collective-permute-start | bytes 49352 | tf_op jit(solution)/shard_map/ppermute | solution.py:44
  55.9 3.7 %collective-permute-start.14 = (f32[8,4]{1,0:T(8,128)S(1)}, f32[8,4]{1,0:T(8,128)S(1)}, u32[]{:S(2)}, u32[]{:S(2)}) collective-permute-start(f32[8,4]{1,0:T(8,128)S(1)} %concatenate.148), channel_id=1, source_target_pairs={{0,16},{16,0},{1,17},{17,1},{2,18},{18,2},{3,19},{19,3},{4,20},{20... | collective-permute-start | bytes 392 | tf_op jit(solution)/shard_map/ppermute | solution.py:21
  59.5 1.5 %collective-permute-start.15 = (f32[8,4]{1,0:T(8,128)S(1)}, f32[8,4]{1,0:T(8,128)S(1)}, u32[]{:S(2)}, u32[]{:S(2)}) collective-permute-start(f32[8,4]{1,0:T(8,128)S(1)} %add.550), channel_id=1, source_target_pairs={{0,1},{1,0},{2,3},{3,2},{4,5},{5,4},{6,7},{7,6},{8,9},{9,8},{10,11... | collective-permute-start | bytes 392 | tf_op jit(solution)/shard_map/ppermute | solution.py:21
  61.0 4.8 %collective-permute-start.16 = (f32[8,4]{1,0:T(8,128)S(1)}, f32[8,4]{1,0:T(8,128)S(1)}, u32[]{:S(2)}, u32[]{:S(2)}) collective-permute-start(f32[8,4]{1,0:T(8,128)S(1)} %add.551), channel_id=1, source_target_pairs={{0,2},{1,3},{2,0},{3,1},{4,6},{5,7},{6,4},{7,5},{8,10},{9,11},{10,... | collective-permute-start | bytes 392 | tf_op jit(solution)/shard_map/ppermute | solution.py:21
  65.8 4.4 %collective-permute-start.17 = (f32[8,4]{1,0:T(8,128)S(1)}, f32[8,4]{1,0:T(8,128)S(1)}, u32[]{:S(2)}, u32[]{:S(2)}) collective-permute-start(f32[8,4]{1,0:T(8,128)S(1)} %add.552), channel_id=1, source_target_pairs={{0,4},{1,5},{2,6},{3,7},{4,0},{5,1},{6,2},{7,3},{8,12},{9,13},{10,... | collective-permute-start | bytes 392 | tf_op jit(solution)/shard_map/ppermute | solution.py:21
  70.2 4.5 %collective-permute-start.18 = (f32[8,4]{1,0:T(8,128)S(1)}, f32[8,4]{1,0:T(8,128)S(1)}, u32[]{:S(2)}, u32[]{:S(2)}) collective-permute-start(f32[8,4]{1,0:T(8,128)S(1)} %add.553), channel_id=1, source_target_pairs={{0,8},{1,9},{2,10},{3,11},{4,12},{5,13},{6,14},{7,15},{8,0},{9,1},... | collective-permute-start | bytes 392 | tf_op jit(solution)/shard_map/ppermute | solution.py:21

commit v14 on v13

--- a/solution.py
+++ b/solution.py
@@ -105,11 +105,15 @@
     return row_coupling * keep[:, None].astype(jnp.float32)
 
 
-def far_field(gathered, weights, target_basis):
-    nrhs = gathered.shape[2]
+def far_inner(gathered, weights):
+    inner = jnp.einsum("sakl,spql->apqk", weights, gathered, precision=lax.Precision.HIGH)
+    return complex_mix(inner)
+
+
+def far_field(far_coef, target_basis):
+    nrhs = far_coef.shape[1]
     rows = target_basis.shape[3]
-    inner = jnp.einsum("sakl,spql->apqk", weights, gathered, precision=lax.Precision.HIGH)
-    rounded_coef = complex_mix(inner).astype(jnp.bfloat16)
+    rounded_coef = far_coef.astype(jnp.bfloat16)
     outward = jnp.einsum(
         "akr,pqk->apqr", target_basis[0], rounded_coef, preferred_element_type=jnp.float32
     )
@@ -175,10 +179,11 @@
     chosen_one = near_tiles(window_rhs, near_blocks, near_cols) / inv_scale
     mates_one = swapped(spread(every_rhs), partner, width) / inv_scale
     coef_one = coef_rhs / beta[None, None, :, None]
+    far_one = far_inner(coef_one, weights)
     image_one = (
         first_vec
         + near_field(chosen_one, near_blocks)
-        + far_field(coef_one, weights, target_basis)
+        + far_field(far_one, target_basis)
         - mates_one.reshape(first_vec.shape)
     )
 
@@ -206,12 +211,13 @@
     chosen_two = (chosen_img - scaled(h_one_one, chosen_one)) / inv_two
     mates_img = swapped(spread(every_img), partner, width)
     mates_two = (mates_img - scaled(h_one_one, mates_one)) / inv_two
-    coef_two = (coef_img - coef_scaled(h_one_one, coef_one)) / h_two_one[None, None, :, None]
+    far_img = far_inner(coef_img, weights)
+    far_two = (far_img - scaled(h_one_one, far_one[:, :, None])[:, :, 0]) / h_two_one[None, :, None]
     early_columns = jnp.stack([beta, h_one_one[0], h_one_one[1], h_two_one], axis=1)
     image_two = (
         second_basis
         + near_field(chosen_two, near_blocks)
-        + far_field(coef_two, weights, target_basis)
+        + far_field(far_two, target_basis)
         - mates_two.reshape(second_basis.shape)
     )
 

time: 77.3 us -> 75.6 us (0.978)
  waiting for transfers between devices: 20.9 us -> 17.6 us
  starting transfers between devices: 31.2 us -> 32.5 us
    ppermute x10, starting transfers between devices: 16.7 us -> 20.2 us  [tree_collect(): got = lax.ppermute(packed, axis, [(i, i ^ k) for i in range(n)])]
    ppermute x5, starting transfers between devices: 9.28 us -> 7.12 us  [tree_sum(): x = x + lax.ppermute(x, axis, [(i, i ^ k) for i in range(n)])]
    ppermute x2, waiting for transfers between devices: 1.75 us -> 0.01 us  [neighbours(): right = lax.ppermute(field, 'blk', [(i + 1, i) for i in range(ends)])]
    ppermute x10, waiting for transfers between devices: 10.5 us -> 9.04 us  [tree_collect(): got = lax.ppermute(packed, axis, [(i, i ^ k) for i in range(n)])]
  transfers between devices with their start and end apart: 19 -> 19, of which waited for: 12 -> 12; matrix products, arithmetic and copies ran while one was open for 13% -> 16% of each run, Pallas kernels for 0% -> 0%
where the time goes in v14:
time: 75.6 us; the launch traced here: 74.9 us
  starting transfers between devices  32.5 us (43%)
  waiting for transfers between devices  17.6 us (23%)
  local copies, waits for them, and re-layouts  9.22 us (12%)
  other arithmetic  7.44 us (10%)
  matrix products  6.91 us (9%)
  between operations  1.21 us (2%)
    ppermute x10, starting transfers between devices, tree_collect(): got = lax.ppermute(packed, axis, [(i, i ^ k) for i in range(n)])  20.2 us
    ppermute x10, waiting for transfers between devices, tree_collect(): got = lax.ppermute(packed, axis, [(i, i ^ k) for i in range(n)])  9.04 us
    ppermute x5, waiting for transfers between devices, tree_sum(): x = x + lax.ppermute(x, axis, [(i, i ^ k) for i in range(n)])  8.55 us
    ppermute x5, starting transfers between devices, tree_sum(): x = x + lax.ppermute(x, axis, [(i, i ^ k) for i in range(n)])  7.12 us
    dot_general x2, matrix products, far_inner(): jnp.einsum('sakl,spql->apqk', weights, gathered, precision=lax.Precision....  3.98 us
    ppermute x2, starting transfers between devices, neighbours(): right = lax.ppermute(field, 'blk', [(i + 1, i) for i in range(ends)])  2.58 us
    ppermute x2, starting transfers between devices, neighbours(): left = lax.ppermute(field, 'blk', [(i, i + 1) for i in range(ends)])  2.57 us
    unnamed x12, local copies, waits for them, and re-layouts  2.01 us
  transfers between devices with their start and end apart: 19, of which 12 were waited for; matrix products, arithmetic and copies ran while one was open for 16% of the time, Pallas kernels for 0%

profile of v14, /device:TPU:0, one launch (start us, length us, event | category | flops | bytes accessed | tf_op | source)
XLA Modules:
  0.0 74.9 jit_solution(7701830476085301617)
XLA Ops:
  0.6 1.0 %add_reduce_fusion.8 = f32[4]{0:T(128)S(1)} fusion(f32[2,4,1,512]{3,2,1,0:T(1,128)} %param.8), kind=kLoop, calls=%fused_computation.121 | loop fusion | flops 8188 | bytes 16400 | tf_op jit(solution)/shard_map/reduce_sum | solution.py:139
  1.6 0.8 %pad_maximum_fusion.1 = f32[4100]{0:T(1024)S(1)} fusion(f32[4096]{0:T(1024)} %bitcast.352, f32[4]{0:T(128)S(1)} %add_reduce_fusion.8), kind=kLoop, calls=%fused_computation.52 | loop fusion | flops 4100 | bytes 32800 | tf_op jit(solution)/shard_map/concatenate | solution.py:40
  2.4 3.0 %collective-permute-start = (f32[4100]{0:T(1024)S(1)}, f32[4100]{0:T(1024)S(1)}, u32[]{:S(2)}, u32[]{:S(2)}) collective-permute-start(f32[4100]{0:T(1024)S(1)} %pad_maximum_fusion.1), channel_id=1, source_target_pairs={{0,16},{16,0},{1,17},{17,1},{2,18},{18,2},{3,19},{19,3},{4,20},{20... | collective-permute-start | bytes 49208 | tf_op jit(solution)/shard_map/ppermute | solution.py:44
  5.4 0.7 convert_element_type.30
  6.1 1.1 %convolution_bitcast_fusion.5 = f32[2,2,4,64]{3,2,1,0:T(4,128)S(1)} fusion(bf16[1,2,64,512]{3,2,1,0:T(8,128)(2,1)} %param.12, bf16[2,4,1,512]{3,2,1,0:T(2,128)(2,1)S(1)} %convert_element_type.30), kind=kOutput, calls=%fused_computation.15 | convolution fusion | flops 1048576 | bytes 143360 | tf_op jit(solution)/shard_map/akr,pqr->apqk/dot_general | solution.py:73
  7.2 0.7 iota_compare_fusion
  8.0 0.2 and_convert_fusion
  8.2 0.8 %reshape_squeeze.4 = s32[8,1]{0,1:T(1,128)S(1)} reshape(s32[1,2,4]{2,1,0:T(2,128)} %param.10) | data formatting | bytes 64 | tf_op jit(solution)/shard_map/reshape;squeeze | solution.py:84
  9.1 0.7 fusion.61
  9.8 0.5 collective-permute-done.1
  10.4 0.1 reshape.1933
  10.7 1.5 %collective-permute-start.2 = (f32[1028]{0:T(1024)S(1)}, f32[1028]{0:T(1024)S(1)}, u32[]{:S(2)}, u32[]{:S(2)}) collective-permute-start(f32[1028]{0:T(1024)S(1)} %pad_maximum_fusion.7), channel_id=1, source_target_pairs={{0,2},{1,3},{2,0},{3,1},{4,6},{5,7},{6,4},{7,5},{8,10},{9,11},{10,... | collective-permute-start | bytes 12344 | tf_op jit(solution)/shard_map/ppermute | solution.py:44
  12.2 2.2 %collective-permute-done.2 = f32[1028]{0:T(1024)S(1)} collective-permute-done((f32[1028]{0:T(1024)S(1)}, f32[1028]{0:T(1024)S(1)}, u32[]{:S(2)}, u32[]{:S(2)}) %collective-permute-start.2) | collective-permute-done | bytes 4144 | tf_op jit(solution)/shard_map/ppermute | solution.py:44
  14.7 1.6 %collective-permute-start.3 = (f32[2052]{0:T(1024)S(1)}, f32[2052]{0:T(1024)S(1)}, u32[]{:S(2)}, u32[]{:S(2)}) collective-permute-start(f32[2052]{0:T(1024)S(1)} %pad_maximum_fusion.5), channel_id=1, source_target_pairs={{0,4},{1,5},{2,6},{3,7},{4,0},{5,1},{6,2},{7,3},{8,12},{9,13},{10,... | collective-permute-start | bytes 24632 | tf_op jit(solution)/shard_map/ppermute | solution.py:44
  16.2 0.7 copy.255
  17.1 1.3 %collective-permute-start.5 = (f32[2,4,1,512]{3,2,1,0:T(1,128)}, f32[2,4,1,512]{3,2,1,0:T(1,128)S(1)}, u32[]{:S(2)}, u32[]{:S(2)}) collective-permute-start(f32[2,4,1,512]{3,2,1,0:T(1,128)} %param.8), channel_id=1, source_target_pairs={{0,1},{1,2},{2,3},{3,4},{4,5},{5,6},{6,7},{7,8},{8,9},{9,10},{10,1... | collective-permute-start | bytes 49160 | tf_op jit(solution)/shard_map/ppermute | solution.py:62
  18.4 1.3 %collective-permute-start.6 = (f32[2,4,1,512]{3,2,1,0:T(1,128)}, f32[2,4,1,512]{3,2,1,0:T(1,128)S(1)}, u32[]{:S(2)}, u32[]{:S(2)}) collective-permute-start(f32[2,4,1,512]{3,2,1,0:T(1,128)} %param.8), channel_id=1, source_target_pairs={{1,0},{2,1},{3,2},{4,3},{5,4},{6,5},{7,6},{8,7},{9,8},{10,9},{11,1... | collective-permute-start | bytes 49160 | tf_op jit(solution)/shard_map/ppermute | solution.py:63
  20.0 6.5 %collective-permute-start.4 = (f32[4100]{0:T(1024)S(1)}, f32[4100]{0:T(1024)S(1)}, u32[]{:S(2)}, u32[]{:S(2)}) collective-permute-start(f32[4100]{0:T(1024)S(1)} %pad_maximum_fusion.2), channel_id=1, source_target_pairs={{0,8},{1,9},{2,10},{3,11},{4,12},{5,13},{6,14},{7,15},{8,0},{9,1},... | collective-permute-start | bytes 49208 | tf_op jit(solution)/shard_map/ppermute | solution.py:44
  26.6 0.6 gather_fusion.1
  27.3 0.9 %maximum_reduce_fusion = f32[2,4,1536]{2,1,0:T(4,128)S(1)} fusion(f32[2,4,1,512]{3,2,1,0:T(1,128)S(1)} %collective-permute-done.6, f32[2,4,1,512]{3,2,1,0:T(1,128)} %param.8, f32[2,4,1,512]{3,2,1,0:T(1,128)S(1)} %collective-permute-done.5), kind=kLoop, calls=%fused_computation.37 | loop fusion | flops 24576 | bytes 98304 | tf_op jit(solution)/shard_map/concatenate | solution.py:64
  28.1 0.6 gather_fusion
  29.0 2.0 %convolution_bitcast_fusion.4 = f32[2,2,4,64]{3,2,0,1:T(4,128)S(1)} fusion(f32[16,2,4,64,1]{3,0,2,1,4:T(8,128)S(1)} %fusion.19, f32[1,1,16,2,64,64]{5,4,3,2,1,0:T(8,128)} %param.14, f32[16,64,64]{2,1,0:T(8,128)S(1)} %and_convert_fusion), kind=kOutput, calls=%fused_computation.14 | convolution fusion | flops 6422528 | bytes 823296 | tf_op jit(solution)/shard_map/sakl,spql->apqk/dot_general | solution.py:109
  31.1 0.1 convolution_bitcast_fusion.1
  31.2 0.7 fusion.4
  32.1 0.1 convolution_bitcast_fusion.3
  32.2 0.2 add_reduce_fusion.7
  32.7 1.2 %collective-permute-done.7 = f32[528]{0:T(1024)S(1)} collective-permute-done((f32[528]{0:T(1024)S(1)}, f32[528]{0:T(1024)S(1)}, u32[]{:S(2)}, u32[]{:S(2)}) %collective-permute-start.7) | collective-permute-done | bytes 2144 | tf_op jit(solution)/shard_map/ppermute | solution.py:44
  33.9 0.1 reshape.1943
  34.2 0.8 %collective-permute-start.8 = (f32[1040]{0:T(1024)S(1)}, f32[1040]{0:T(1024)S(1)}, u32[]{:S(2)}, u32[]{:S(2)}) collective-permute-start(f32[1040]{0:T(1024)S(1)} %pad_maximum_fusion.8), channel_id=1, source_target_pairs={{0,2},{1,3},{2,0},{3,1},{4,6},{5,7},{6,4},{7,5},{8,10},{9,11},{10,... | collective-permute-start | bytes 12488 | tf_op jit(solution)/shard_map/ppermute | solution.py:44
  35.1 2.8 %collective-permute-done.8 = f32[1040]{0:T(1024)S(1)} collective-permute-done((f32[1040]{0:T(1024)S(1)}, f32[1040]{0:T(1024)S(1)}, u32[]{:S(2)}, u32[]{:S(2)}) %collective-permute-start.8) | collective-permute-done | bytes 4192 | tf_op jit(solution)/shard_map/ppermute | solution.py:44
  38.2 0.5 collective-permute-start.9
  38.7 1.3 %collective-permute-start.12 = (f32[2,4,1,512]{3,1,0,2:T(4,128)S(1)}, f32[2,4,1,512]{3,1,0,2:T(4,128)S(1)}, u32[]{:S(2)}, u32[]{:S(2)}) collective-permute-start(f32[2,4,1,512]{3,1,0,2:T(4,128)S(1)} %get-tuple-element.60), channel_id=1, source_target_pairs={{0,1},{1,2},{2,3},{3,4},{4,5},{5,6},{6,7},{7,8},{8,9},{9,10},{10,1... | collective-permute-start | bytes 49160 | tf_op jit(solution)/shard_map/ppermute | solution.py:62
  40.0 1.3 %collective-permute-start.13 = (f32[2,4,1,512]{3,1,0,2:T(4,128)S(1)}, f32[2,4,1,512]{3,1,0,2:T(4,128)S(1)}, u32[]{:S(2)}, u32[]{:S(2)}) collective-permute-start(f32[2,4,1,512]{3,1,0,2:T(4,128)S(1)} %get-tuple-element.60), channel_id=1, source_target_pairs={{1,0},{2,1},{3,2},{4,3},{5,4},{6,5},{7,6},{8,7},{9,8},{10,9},{11,1... | collective-permute-start | bytes 49160 | tf_op jit(solution)/shard_map/ppermute | solution.py:63
  41.5 0.4 collective-permute-done.9
  42.3 5.9 %collective-permute-start.10 = (f32[4112]{0:T(1024)S(1)}, f32[4112]{0:T(1024)S(1)}, u32[]{:S(2)}, u32[]{:S(2)}) collective-permute-start(f32[4112]{0:T(1024)S(1)} %pad_maximum_fusion.3), channel_id=1, source_target_pairs={{0,8},{1,9},{2,10},{3,11},{4,12},{5,13},{6,14},{7,15},{8,0},{9,1},... | collective-permute-start | bytes 49352 | tf_op jit(solution)/shard_map/ppermute | solution.py:44
  48.3 0.6 gather_fusion.2
  48.9 1.0 %collective-permute-done.10 = f32[4112]{0:T(1024)S(1)} collective-permute-done((f32[4112]{0:T(1024)S(1)}, f32[4112]{0:T(1024)S(1)}, u32[]{:S(2)}, u32[]{:S(2)}) %collective-permute-start.10) | collective-permute-done | bytes 16480 | tf_op jit(solution)/shard_map/ppermute | solution.py:44
  50.1 0.5 collective-permute-start.11
  50.8 2.0 %convolution_bitcast_fusion.2 = f32[2,4,2,64]{3,1,2,0:T(4,128)S(1)} fusion(f32[16,2,4,64,1]{3,0,2,1,4:T(8,128)S(1)} %fusion.21, f32[1,1,16,2,64,64]{5,4,3,2,1,0:T(8,128)} %param.14, f32[16,64,64]{2,1,0:T(8,128)S(1)} %and_convert_fusion), kind=kOutput, calls=%fused_computation.12 | convolution fusion | flops 6422528 | bytes 823296 | tf_op jit(solution)/shard_map/sakl,spql->apqk/dot_general | solution.py:109
  52.8 1.0 %collective-permute-done.11 = f32[4112]{0:T(1024)S(1)} collective-permute-done((f32[4112]{0:T(1024)S(1)}, f32[4112]{0:T(1024)S(1)}, u32[]{:S(2)}, u32[]{:S(2)}) %collective-permute-start.11) | collective-permute-done | bytes 16480 | tf_op jit(solution)/shard_map/ppermute | solution.py:44
  53.8 0.1 reshape.1949
  54.4 0.6 gather_fusion.3
  55.0 0.2 convolution_bitcast_fusion
  55.2 0.1 multiply_subtract_fusion
  55.3 0.7 fusion.7
  56.1 0.2 subtract_reduce_fusion
  56.4 0.6 collective-permute-start.14
  57.0 3.1 %collective-permute-done.14 = f32[8,4]{1,0:T(8,128)S(1)} collective-permute-done((f32[8,4]{1,0:T(8,128)S(1)}, f32[8,4]{1,0:T(8,128)S(1)}, u32[]{:S(2)}, u32[]{:S(2)}) %collective-permute-start.14) | collective-permute-done | bytes 160 | tf_op jit(solution)/shard_map/ppermute | solution.py:21
  60.1 1.2 %collective-permute-done.15 = f32[8,4]{1,0:T(8,128)S(1)} collective-permute-done((f32[8,4]{1,0:T(8,128)S(1)}, f32[8,4]{1,0:T(8,128)S(1)}, u32[]{:S(2)}, u32[]{:S(2)}) %collective-permute-start.15) | collective-permute-done | bytes 160 | tf_op jit(solution)/shard_map/ppermute | solution.py:21
  61.2 1.6 %collective-permute-start.16 = (f32[8,4]{1,0:T(8,128)S(1)}, f32[8,4]{1,0:T(8,128)S(1)}, u32[]{:S(2)}, u32[]{:S(2)}) collective-permute-start(f32[8,4]{1,0:T(8,128)S(1)} %add.575), channel_id=1, source_target_pairs={{0,2},{1,3},{2,0},{3,1},{4,6},{5,7},{6,4},{7,5},{8,10},{9,11},{10,... | collective-permute-start | bytes 392 | tf_op jit(solution)/shard_map/ppermute | solution.py:21
  62.8 0.1 copy.179
  62.9 0.6 copy.185
  63.5 1.3 %collective-permute-done.16 = f32[8,4]{1,0:T(8,128)S(1)} collective-permute-done((f32[8,4]{1,0:T(8,128)S(1)}, f32[8,4]{1,0:T(8,128)S(1)}, u32[]{:S(2)}, u32[]{:S(2)}) %collective-permute-start.16) | collective-permute-done | bytes 160 | tf_op jit(solution)/shard_map/ppermute | solution.py:21
  64.9 2.0 %collective-permute-start.17 = (f32[8,4]{1,0:T(8,128)S(1)}, f32[8,4]{1,0:T(8,128)S(1)}, u32[]{:S(2)}, u32[]{:S(2)}) collective-permute-start(f32[8,4]{1,0:T(8,128)S(1)} %add.576), channel_id=1, source_target_pairs={{0,4},{1,5},{2,6},{3,7},{4,0},{5,1},{6,2},{7,3},{8,12},{9,13},{10,... | collective-permute-start | bytes 392 | tf_op jit(solution)/shard_map/ppermute | solution.py:21
  66.9 0.1 copy.180
  67.0 1.5 %collective-permute-done.17 = f32[8,4]{1,0:T(8,128)S(1)} collective-permute-done((f32[8,4]{1,0:T(8,128)S(1)}, f32[8,4]{1,0:T(8,128)S(1)}, u32[]{:S(2)}, u32[]{:S(2)}) %collective-permute-start.17) | collective-permute-done | bytes 160 | tf_op jit(solution)/shard_map/ppermute | solution.py:21
  68.5 2.9 %collective-permute-start.18 = (f32[8,4]{1,0:T(8,128)S(1)}, f32[8,4]{1,0:T(8,128)S(1)}, u32[]{:S(2)}, u32[]{:S(2)}) collective-permute-start(f32[8,4]{1,0:T(8,128)S(1)} %add.577), channel_id=1, source_target_pairs={{0,8},{1,9},{2,10},{3,11},{4,12},{5,13},{6,14},{7,15},{8,0},{9,1},... | collective-permute-start | bytes 392 | tf_op jit(solution)/shard_map/ppermute | solution.py:21
  71.4 0.1 copy.181
  71.5 1.5 %collective-permute-done.18 = f32[8,4]{1,0:T(8,128)S(1)} collective-permute-done((f32[8,4]{1,0:T(8,128)S(1)}, f32[8,4]{1,0:T(8,128)S(1)}, u32[]{:S(2)}, u32[]{:S(2)}) %collective-permute-start.18) | collective-permute-done | bytes 160 | tf_op jit(solution)/shard_map/ppermute | solution.py:21
  73.1 0.1 copy.182
  73.2 0.1 copy.184
  73.3 0.1 copy.183
  73.6 0.6 copy.186
  74.2 0.7 concatenate.156
  (146 shorter events, 4.7 us)
Async XLA Ops:
  0.6 30.6 %copy-start = (bf16[1,2,4,2,256,256]{5,4,3,2,1,0:T(8,128)(2,1)S(1)}, bf16[1,2,4,2,256,256]{5,4,3,2,1,0:T(8,128)(2,1)}, u32[]{:S(2)}) copy-start(bf16[1,2,4,2,256,256]{5,4,3,2,1,0:T(8,128)(2,1)} %param.9) | copy-start | bytes 6291460
  2.4 6.6 %collective-permute-start = (f32[4100]{0:T(1024)S(1)}, f32[4100]{0:T(1024)S(1)}, u32[]{:S(2)}, u32[]{:S(2)}) collective-permute-start(f32[4100]{0:T(1024)S(1)} %pad_maximum_fusion.1), channel_id=1, source_target_pairs={{0,16},{16,0},{1,17},{17,1},{2,18},{18,2},{3,19},{19,3},{4,20},{20... | collective-permute-start | bytes 49208 | tf_op jit(solution)/shard_map/ppermute | solution.py:44
  6.1 25.0 %copy-start.3 = (bf16[1,2,64,512]{3,2,1,0:T(8,128)(2,1)S(1)}, bf16[1,2,64,512]{3,2,1,0:T(8,128)(2,1)}, u32[]{:S(2)}) copy-start(bf16[1,2,64,512]{3,2,1,0:T(8,128)(2,1)} %param.13) | copy-start | bytes 393220
  9.1 1.2 %collective-permute-start.1 = (f32[516]{0:T(1024)S(1)}, f32[516]{0:T(1024)S(1)}, u32[]{:S(2)}, u32[]{:S(2)}) collective-permute-start(f32[516]{0:T(1024)S(1)} %pad_maximum_fusion.10), channel_id=1, source_target_pairs={{0,1},{1,0},{2,3},{3,2},{4,5},{5,4},{6,7},{7,6},{8,9},{9,8},{10,11... | collective-permute-start | bytes 6200 | tf_op jit(solution)/shard_map/ppermute | solution.py:44
  10.7 3.7 %collective-permute-start.2 = (f32[1028]{0:T(1024)S(1)}, f32[1028]{0:T(1024)S(1)}, u32[]{:S(2)}, u32[]{:S(2)}) collective-permute-start(f32[1028]{0:T(1024)S(1)} %pad_maximum_fusion.7), channel_id=1, source_target_pairs={{0,2},{1,3},{2,0},{3,1},{4,6},{5,7},{6,4},{7,5},{8,10},{9,11},{10,... | collective-permute-start | bytes 12344 | tf_op jit(solution)/shard_map/ppermute | solution.py:44
  14.7 5.0 %collective-permute-start.3 = (f32[2052]{0:T(1024)S(1)}, f32[2052]{0:T(1024)S(1)}, u32[]{:S(2)}, u32[]{:S(2)}) collective-permute-start(f32[2052]{0:T(1024)S(1)} %pad_maximum_fusion.5), channel_id=1, source_target_pairs={{0,4},{1,5},{2,6},{3,7},{4,0},{5,1},{6,2},{7,3},{8,12},{9,13},{10,... | collective-permute-start | bytes 24632 | tf_op jit(solution)/shard_map/ppermute | solution.py:44
  17.1 10.2 %collective-permute-start.5 = (f32[2,4,1,512]{3,2,1,0:T(1,128)}, f32[2,4,1,512]{3,2,1,0:T(1,128)S(1)}, u32[]{:S(2)}, u32[]{:S(2)}) collective-permute-start(f32[2,4,1,512]{3,2,1,0:T(1,128)} %param.8), channel_id=1, source_target_pairs={{0,1},{1,2},{2,3},{3,4},{4,5},{5,6},{6,7},{7,8},{8,9},{9,10},{10,1... | collective-permute-start | bytes 49160 | tf_op jit(solution)/shard_map/ppermute | solution.py:62
  18.4 8.9 %collective-permute-start.6 = (f32[2,4,1,512]{3,2,1,0:T(1,128)}, f32[2,4,1,512]{3,2,1,0:T(1,128)S(1)}, u32[]{:S(2)}, u32[]{:S(2)}) collective-permute-start(f32[2,4,1,512]{3,2,1,0:T(1,128)} %param.8), channel_id=1, source_target_pairs={{1,0},{2,1},{3,2},{4,3},{5,4},{6,5},{7,6},{8,7},{9,8},{10,9},{11,1... | collective-permute-start | bytes 49160 | tf_op jit(solution)/shard_map/ppermute | solution.py:63
  20.0 8.7 %collective-permute-start.4 = (f32[4100]{0:T(1024)S(1)}, f32[4100]{0:T(1024)S(1)}, u32[]{:S(2)}, u32[]{:S(2)}) collective-permute-start(f32[4100]{0:T(1024)S(1)} %pad_maximum_fusion.2), channel_id=1, source_target_pairs={{0,8},{1,9},{2,10},{3,11},{4,12},{5,13},{6,14},{7,15},{8,0},{9,1},... | collective-permute-start | bytes 49208 | tf_op jit(solution)/shard_map/ppermute | solution.py:44
  29.0 2.9 %copy-start.1 = (f32[2,4,1,512]{3,2,1,0:T(1,128)S(1)}, f32[2,4,1,512]{3,2,1,0:T(1,128)}, u32[]{:S(2)}) copy-start(f32[2,4,1,512]{3,2,1,0:T(1,128)} %param.8) | copy-start | bytes 49156
  29.0 3.0 %copy-start.2 = (bf16[1,2,64,512]{3,2,1,0:T(8,128)(2,1)S(1)}, bf16[1,2,64,512]{3,2,1,0:T(8,128)(2,1)}, u32[]{:S(2)}) copy-start(bf16[1,2,64,512]{3,2,1,0:T(8,128)(2,1)} %param.12) | copy-start | bytes 393220
  32.7 1.2 %collective-permute-start.7 = (f32[528]{0:T(1024)S(1)}, f32[528]{0:T(1024)S(1)}, u32[]{:S(2)}, u32[]{:S(2)}) collective-permute-start(f32[528]{0:T(1024)S(1)} %pad_maximum_fusion.12), channel_id=1, source_target_pairs={{0,1},{1,0},{2,3},{3,2},{4,5},{5,4},{6,7},{7,6},{8,9},{9,8},{10,11... | collective-permute-start | bytes 6344 | tf_op jit(solution)/shard_map/ppermute | solution.py:44
  34.2 3.7 %collective-permute-start.8 = (f32[1040]{0:T(1024)S(1)}, f32[1040]{0:T(1024)S(1)}, u32[]{:S(2)}, u32[]{:S(2)}) collective-permute-start(f32[1040]{0:T(1024)S(1)} %pad_maximum_fusion.8), channel_id=1, source_target_pairs={{0,2},{1,3},{2,0},{3,1},{4,6},{5,7},{6,4},{7,5},{8,10},{9,11},{10,... | collective-permute-start | bytes 12488 | tf_op jit(solution)/shard_map/ppermute | solution.py:44
  38.2 3.7 %collective-permute-start.9 = (f32[2064]{0:T(1024)S(1)}, f32[2064]{0:T(1024)S(1)}, u32[]{:S(2)}, u32[]{:S(2)}) collective-permute-start(f32[2064]{0:T(1024)S(1)} %pad_maximum_fusion.6), channel_id=1, source_target_pairs={{0,4},{1,5},{2,6},{3,7},{4,0},{5,1},{6,2},{7,3},{8,12},{9,13},{10,... | collective-permute-start | bytes 24776 | tf_op jit(solution)/shard_map/ppermute | solution.py:44
  38.7 9.6 %collective-permute-start.12 = (f32[2,4,1,512]{3,1,0,2:T(4,128)S(1)}, f32[2,4,1,512]{3,1,0,2:T(4,128)S(1)}, u32[]{:S(2)}, u32[]{:S(2)}) collective-permute-start(f32[2,4,1,512]{3,1,0,2:T(4,128)S(1)} %get-tuple-element.60), channel_id=1, source_target_pairs={{0,1},{1,2},{2,3},{3,4},{4,5},{5,6},{6,7},{7,8},{8,9},{9,10},{10,1... | collective-permute-start | bytes 49160 | tf_op jit(solution)/shard_map/ppermute | solution.py:62
  40.0 8.3 %collective-permute-start.13 = (f32[2,4,1,512]{3,1,0,2:T(4,128)S(1)}, f32[2,4,1,512]{3,1,0,2:T(4,128)S(1)}, u32[]{:S(2)}, u32[]{:S(2)}) collective-permute-start(f32[2,4,1,512]{3,1,0,2:T(4,128)S(1)} %get-tuple-element.60), channel_id=1, source_target_pairs={{1,0},{2,1},{3,2},{4,3},{5,4},{6,5},{7,6},{8,7},{9,8},{10,9},{11,1... | collective-permute-start | bytes 49160 | tf_op jit(solution)/shard_map/ppermute | solution.py:63
  42.3 7.7 %collective-permute-start.10 = (f32[4112]{0:T(1024)S(1)}, f32[4112]{0:T(1024)S(1)}, u32[]{:S(2)}, u32[]{:S(2)}) collective-permute-start(f32[4112]{0:T(1024)S(1)} %pad_maximum_fusion.3), channel_id=1, source_target_pairs={{0,8},{1,9},{2,10},{3,11},{4,12},{5,13},{6,14},{7,15},{8,0},{9,1},... | collective-permute-start | bytes 49352 | tf_op jit(solution)/shard_map/ppermute | solution.py:44
  50.1 3.8 %collective-permute-start.11 = (f32[4112]{0:T(1024)S(1)}, f32[4112]{0:T(1024)S(1)}, u32[]{:S(2)}, u32[]{:S(2)}) collective-permute-start(f32[4112]{0:T(1024)S(1)} %pad_maximum_fusion.4), channel_id=1, source_target_pairs={{0,16},{16,0},{1,17},{17,1},{2,18},{18,2},{3,19},{19,3},{4,20},{20... | collective-permute-start | bytes 49352 | tf_op jit(solution)/shard_map/ppermute | solution.py:44
  56.4 3.7 %collective-permute-start.14 = (f32[8,4]{1,0:T(8,128)S(1)}, f32[8,4]{1,0:T(8,128)S(1)}, u32[]{:S(2)}, u32[]{:S(2)}) collective-permute-start(f32[8,4]{1,0:T(8,128)S(1)} %concatenate.155), channel_id=1, source_target_pairs={{0,16},{16,0},{1,17},{17,1},{2,18},{18,2},{3,19},{19,3},{4,20},{20... | collective-permute-start | bytes 392 | tf_op jit(solution)/shard_map/ppermute | solution.py:21
  60.1 1.2 %collective-permute-start.15 = (f32[8,4]{1,0:T(8,128)S(1)}, f32[8,4]{1,0:T(8,128)S(1)}, u32[]{:S(2)}, u32[]{:S(2)}) collective-permute-start(f32[8,4]{1,0:T(8,128)S(1)} %add.574), channel_id=1, source_target_pairs={{0,1},{1,0},{2,3},{3,2},{4,5},{5,4},{6,7},{7,6},{8,9},{9,8},{10,11... | collective-permute-start | bytes 392 | tf_op jit(solution)/shard_map/ppermute | solution.py:21
  61.2 3.6 %collective-permute-start.16 = (f32[8,4]{1,0:T(8,128)S(1)}, f32[8,4]{1,0:T(8,128)S(1)}, u32[]{:S(2)}, u32[]{:S(2)}) collective-permute-start(f32[8,4]{1,0:T(8,128)S(1)} %add.575), channel_id=1, source_target_pairs={{0,2},{1,3},{2,0},{3,1},{4,6},{5,7},{6,4},{7,5},{8,10},{9,11},{10,... | collective-permute-start | bytes 392 | tf_op jit(solution)/shard_map/ppermute | solution.py:21
  64.9 3.6 %collective-permute-start.17 = (f32[8,4]{1,0:T(8,128)S(1)}, f32[8,4]{1,0:T(8,128)S(1)}, u32[]{:S(2)}, u32[]{:S(2)}) collective-permute-start(f32[8,4]{1,0:T(8,128)S(1)} %add.576), channel_id=1, source_target_pairs={{0,4},{1,5},{2,6},{3,7},{4,0},{5,1},{6,2},{7,3},{8,12},{9,13},{10,... | collective-permute-start | bytes 392 | tf_op jit(solution)/shard_map/ppermute | solution.py:21
  68.5 4.5 %collective-permute-start.18 = (f32[8,4]{1,0:T(8,128)S(1)}, f32[8,4]{1,0:T(8,128)S(1)}, u32[]{:S(2)}, u32[]{:S(2)}) collective-permute-start(f32[8,4]{1,0:T(8,128)S(1)} %add.577), channel_id=1, source_target_pairs={{0,8},{1,9},{2,10},{3,11},{4,12},{5,13},{6,14},{7,15},{8,0},{9,1},... | collective-permute-start | bytes 392 | tf_op jit(solution)/shard_map/ppermute | solution.py:21

commit v15 on v14

--- a/solution.py
+++ b/solution.py
@@ -23,7 +23,7 @@
     return x
 
 
-def tree_collect(red, gat_blk, gat_dom, dom_first=False, halo=None):
+def tree_collect(red, gat_blk, gat_dom, dom_first=False, halo=None, weights=None):
     rounds = (("blk", gat_blk), ("dom", gat_dom))
     if dom_first:
         rounds = rounds[::-1]
@@ -44,6 +44,11 @@
                 got = lax.ppermute(packed, axis, [(i, i ^ k) for i in range(n)])
                 red = red + got[: red.size].reshape(red.shape)
                 other = got[red.size :].reshape(buf.shape)
+                if weights is not None and axis == "blk" and 2 * k == n:
+                    base = idx - idx % k
+                    mine = lax.dynamic_slice_in_dim(weights, base, k, axis=0)
+                    theirs = lax.dynamic_slice_in_dim(weights, base ^ k, k, axis=0)
+                    weights = far_inner(buf, mine) + far_inner(other, theirs)
                 low = (idx // k) % 2 == 0
                 buf = jnp.where(low, jnp.concatenate([buf, other]), jnp.concatenate([other, buf]))
                 k *= 2
@@ -51,6 +56,8 @@
             gat_blk = buf
         else:
             gat_dom = buf
+    if weights is not None:
+        return red, gat_blk, gat_dom, halo, weights
     if halo is not None:
         return red, gat_blk, gat_dom, halo
     return red, gat_blk, gat_dom
@@ -166,12 +173,13 @@
     def spread(every):
         return jnp.moveaxis(every, 0, 2)
 
-    start_sum, coef_rhs, every_rhs, window_rhs = tree_collect(
+    start_sum, coef_rhs, every_rhs, window_rhs, far_rhs = tree_collect(
         local_squares(right_side),
         coefficients(right_side, source_basis),
         right_side[:, :, 0],
         dom_first=True,
         halo=right_side,
+        weights=weights,
     )
     beta = jnp.sqrt(start_sum / total + EPSILON)
     inv_scale = beta[None, :, None, None]
@@ -179,7 +187,7 @@
     chosen_one = near_tiles(window_rhs, near_blocks, near_cols) / inv_scale
     mates_one = swapped(spread(every_rhs), partner, width) / inv_scale
     coef_one = coef_rhs / beta[None, None, :, None]
-    far_one = far_inner(coef_one, weights)
+    far_one = far_rhs / beta[None, :, None]
     image_one = (
         first_vec
         + near_field(chosen_one, near_blocks)

time: 75.6 us -> 87.9 us (1.16)
  other arithmetic: 7.44 us -> 17.5 us
  local copies, waits for them, and re-layouts: 9.22 us -> 14.5 us
  starting transfers between devices: 32.5 us -> 28.3 us
  waiting for transfers between devices: 17.6 us -> 18.6 us
    ppermute x10, starting transfers between devices: 20.2 us -> 14.1 us  [tree_collect(): got = lax.ppermute(packed, axis, [(i, i ^ k) for i in range(n)])]
    ppermute x2, starting transfers between devices: 2.57 us -> 6.66 us  [neighbours(): left = lax.ppermute(field, 'blk', [(i, i + 1) for i in range(ends)])]
    ppermute x5, starting transfers between devices: 7.12 us -> 5.04 us  [tree_sum(): x = x + lax.ppermute(x, axis, [(i, i ^ k) for i in range(n)])]
    ppermute x5, waiting for transfers between devices: 8.55 us -> 10.6 us  [tree_sum(): x = x + lax.ppermute(x, axis, [(i, i ^ k) for i in range(n)])]
    reshape x5, local copies, waits for them, and re-layouts: 0.41 us -> 2.15 us  [tree_collect(): red = red + got[:red.size].reshape(red.shape)]
    dot_general x2, matrix products: 1.36 us -> 3.03 us  [near_field(): jnp.einsum('ikarc,pqikc->apqir', near_blocks[0], rounded, preferred_eleme...]
    dot_general x2 -> x3, matrix products: 3.98 us -> 2.37 us  [far_inner(): jnp.einsum('sakl,spql->apqk', weights, gathered, precision=lax.Precision....]
    mul x0 -> x1, other arithmetic: none -> 1.53 us  [far_weights(): return row_coupling * keep[:, None].astype(jnp.float32)]
  transfers between devices with their start and end apart: 19 -> 19, of which waited for: 12 -> 10; matrix products, arithmetic and copies ran while one was open for 16% -> 25% of each run, Pallas kernels for 0% -> 0%
where the time goes in v15:
time: 87.9 us; the launch traced here: 87 us
  starting transfers between devices  28.3 us (32%)
  waiting for transfers between devices  18.6 us (21%)
  other arithmetic  17.5 us (20%)
  local copies, waits for them, and re-layouts  14.5 us (16%)
  matrix products  6.93 us (8%)
  between operations  1.14 us (1%)
    ppermute x10, starting transfers between devices, tree_collect(): got = lax.ppermute(packed, axis, [(i, i ^ k) for i in range(n)])  14.1 us
    ppermute x5, waiting for transfers between devices, tree_sum(): x = x + lax.ppermute(x, axis, [(i, i ^ k) for i in range(n)])  10.6 us
    ppermute x10, waiting for transfers between devices, tree_collect(): got = lax.ppermute(packed, axis, [(i, i ^ k) for i in range(n)])  8.01 us
    ppermute x2, starting transfers between devices, neighbours(): left = lax.ppermute(field, 'blk', [(i, i + 1) for i in range(ends)])  6.66 us
    ppermute x5, starting transfers between devices, tree_sum(): x = x + lax.ppermute(x, axis, [(i, i ^ k) for i in range(n)])  5.04 us
    dot_general x2, matrix products, near_field(): jnp.einsum('ikarc,pqikc->apqir', near_blocks[0], rounded, preferred_eleme...  3.03 us
    gather x4, local copies, waits for them, and re-layouts, near_tiles(): tiles.at[:, :, near_cols[0].reshape(-1)].get(mode='promise_in_bounds')  2.69 us
    concatenate x10, other arithmetic, tree_collect(): packed = jnp.concatenate([red.reshape(-1), buf.reshape(-1)])  2.67 us
  transfers between devices with their start and end apart: 19, of which 10 were waited for; matrix products, arithmetic and copies ran while one was open for 25% of the time, Pallas kernels for 0%

profile of v15, /device:TPU:0, one launch (start us, length us, event | category | flops | bytes accessed | tf_op | source)
XLA Modules:
  0.0 87.0 jit_solution(5005724034798393065)
XLA Ops:
  0.7 1.0 %add_reduce_fusion.8 = f32[4]{0:T(128)S(1)} fusion(f32[2,4,1,512]{3,2,1,0:T(1,128)} %param.8), kind=kLoop, calls=%fused_computation.121 | loop fusion | flops 8188 | bytes 16400 | tf_op jit(solution)/shard_map/reduce_sum | solution.py:146
  1.6 0.8 pad_maximum_fusion.1
  2.4 3.0 %collective-permute-start = (f32[4100]{0:T(1024)S(1)}, f32[4100]{0:T(1024)S(1)}, u32[]{:S(2)}, u32[]{:S(2)}) collective-permute-start(f32[4100]{0:T(1024)S(1)} %pad_maximum_fusion.1), channel_id=1, source_target_pairs={{0,16},{16,0},{1,17},{17,1},{2,18},{18,2},{3,19},{19,3},{4,20},{20... | collective-permute-start | bytes 49208 | tf_op jit(solution)/shard_map/ppermute | solution.py:44
  5.4 0.7 convert_element_type.32
  6.1 1.1 %convolution_bitcast_fusion.4 = f32[2,2,4,64]{3,2,0,1:T(4,128)S(1)} fusion(bf16[1,2,64,512]{3,2,1,0:T(8,128)(2,1)} %param.12, bf16[2,4,1,512]{3,2,1,0:T(2,128)(2,1)S(1)} %convert_element_type.32), kind=kOutput, calls=%fused_computation.14 | convolution fusion | flops 1048576 | bytes 143360 | tf_op jit(solution)/shard_map/akr,pqr->apqk/dot_general | solution.py:80
  7.2 0.7 fusion.66
  7.9 0.7 iota_compare_fusion
  8.6 1.0 %and_convert_fusion = f32[16,64,64]{2,1,0:T(8,128)} fusion(pred[16,64]{1,0:T(8,128)(4,1)S(1)} %iota_compare_fusion), kind=kLoop, calls=%fused_computation.23 | loop fusion | flops 131072 | bytes 263168 | tf_op jit(solution)/shard_map/convert_element_type | solution.py:112
  9.6 0.8 reshape_squeeze.4
  10.4 1.5 %bitcast_multiply_fusion = f32[16,2,64,64]{3,2,0,1:T(8,128)S(1)} fusion(f32[1,1,16,2,64,64]{5,4,3,2,1,0:T(8,128)} %param.14, f32[16,64,64]{2,1,0:T(8,128)} %and_convert_fusion), kind=kLoop, calls=%fused_computation.18 | loop fusion | flops 131072 | bytes 1310720 | tf_op jit(solution)/shard_map/mul | solution.py:112
  13.6 1.5 %collective-permute-start.2 = (f32[1028]{0:T(1024)S(1)}, f32[1028]{0:T(1024)S(1)}, u32[]{:S(2)}, u32[]{:S(2)}) collective-permute-start(f32[1028]{0:T(1024)S(1)} %pad_maximum_fusion.7), channel_id=1, source_target_pairs={{0,2},{1,3},{2,0},{3,1},{4,6},{5,7},{6,4},{7,5},{8,10},{9,11},{10,... | collective-permute-start | bytes 12344 | tf_op jit(solution)/shard_map/ppermute | solution.py:44
  15.2 2.1 %collective-permute-done.2 = f32[1028]{0:T(1024)S(1)} collective-permute-done((f32[1028]{0:T(1024)S(1)}, f32[1028]{0:T(1024)S(1)}, u32[]{:S(2)}, u32[]{:S(2)}) %collective-permute-start.2) | collective-permute-done | bytes 4144 | tf_op jit(solution)/shard_map/ppermute | solution.py:44
  17.6 1.6 %collective-permute-start.3 = (f32[2052]{0:T(1024)S(1)}, f32[2052]{0:T(1024)S(1)}, u32[]{:S(2)}, u32[]{:S(2)}) collective-permute-start(f32[2052]{0:T(1024)S(1)} %pad_maximum_fusion.5), channel_id=1, source_target_pairs={{0,4},{1,5},{2,6},{3,7},{4,0},{5,1},{6,2},{7,3},{8,12},{9,13},{10,... | collective-permute-start | bytes 24632 | tf_op jit(solution)/shard_map/ppermute | solution.py:44
  19.9 0.6 gather.23
  20.5 1.3 %collective-permute-start.6 = (f32[2,4,1,512]{3,2,1,0:T(1,128)S(1)}, f32[2,4,1,512]{3,2,1,0:T(1,128)S(1)}, u32[]{:S(2)}, u32[]{:S(2)}) collective-permute-start(f32[2,4,1,512]{3,2,1,0:T(1,128)S(1)} %copy-done.1), channel_id=1, source_target_pairs={{1,0},{2,1},{3,2},{4,3},{5,4},{6,5},{7,6},{8,7},{9,8},{10,9},{11,1... | collective-permute-start | bytes 49160 | tf_op jit(solution)/shard_map/ppermute | solution.py:70
  21.8 3.6 %collective-permute-start.5 = (f32[2,4,1,512]{3,2,1,0:T(1,128)S(1)}, f32[2,4,1,512]{3,2,1,0:T(1,128)}, u32[]{:S(2)}, u32[]{:S(2)}) collective-permute-start(f32[2,4,1,512]{3,2,1,0:T(1,128)S(1)} %copy-done.1), channel_id=1, source_target_pairs={{0,1},{1,2},{2,3},{3,4},{4,5},{5,6},{6,7},{7,8},{8,9},{9,10},{10,1... | collective-permute-start | bytes 49160 | tf_op jit(solution)/shard_map/ppermute | solution.py:69
  25.7 0.7 pad_maximum_fusion.2
  26.4 2.0 %collective-permute-start.4 = (f32[4100]{0:T(1024)}, f32[4100]{0:T(1024)}, u32[]{:S(2)}, u32[]{:S(2)}) collective-permute-start(f32[4100]{0:T(1024)} %pad_maximum_fusion.2), channel_id=1, source_target_pairs={{0,8},{1,9},{2,10},{3,11},{4,12},{5,13},{6,14},{7,15},{8,0},{9,1},... | collective-permute-start | bytes 49208 | tf_op jit(solution)/shard_map/ppermute | solution.py:44
  28.8 0.6 fusion.55
  29.4 0.6 fusion.57
  30.0 0.9 maximum_reduce_fusion
  30.9 0.7 gather_fusion
  31.6 0.6 copy.68
  32.2 0.8 slice.508
  33.0 0.7 reshape.1877
  33.7 1.2 %convolution_bitcast_fusion.5 = f32[2,2,4,64]{3,2,1,0:T(4,128)S(1)} fusion(f32[16,2,64,64]{3,2,0,1:T(8,128)S(1)} %bitcast_multiply_fusion, s32[]{:T(128)S(6)} %select_n.176, f32[8,2,4,64]{3,2,1,0:T(4,128)} %reshape.1877), kind=kOutput, calls=%fused_computation.15 | convolution fusion | flops 3145728 | bytes 544772 | tf_op jit(solution)/shard_map/sakl,spql->apqk/dot_general | solution.py:116
  34.9 0.7 add_sqrt_fusion.3
  35.6 0.8 fusion.46
  36.6 1.5 %fusion.4 = f32[2,2,4,2,256]{4,2,0,1,3:T(4,128)S(1)} fusion(bf16[1,2,4,2,256,256]{5,4,3,2,1,0:T(8,128)(2,1)S(1)} %copy-done, f32[2,4,2,4,256]{4,1,3,2,0:T(4,128)} %bitcast.364, f32[4]{0:T(128)S(1)} %add_sqrt_fusion.3), kind=kOutput, calls=%fused_computation.8 | convolution fusion | flops 16809984 | bytes 2195472 | tf_op jit(solution)/shard_map/ikarc,pqikc->apqir/dot_general | solution.py:100
  38.1 0.8 copy_divide_fusion
  39.6 0.8 collective-permute-start.7
  40.4 1.3 %collective-permute-start.13 = (f32[2,4,1,512]{3,1,0,2:T(4,128)S(1)}, f32[2,4,1,512]{3,1,0,2:T(4,128)S(1)}, u32[]{:S(2)}, u32[]{:S(2)}) collective-permute-start(f32[2,4,1,512]{3,1,0,2:T(4,128)S(1)} %get-tuple-element.54), channel_id=1, source_target_pairs={{1,0},{2,1},{3,2},{4,3},{5,4},{6,5},{7,6},{8,7},{9,8},{10,9},{11,1... | collective-permute-start | bytes 49160 | tf_op jit(solution)/shard_map/ppermute | solution.py:70
  41.7 3.0 %collective-permute-start.12 = (f32[2,4,1,512]{3,1,0,2:T(4,128)S(1)}, f32[2,4,1,512]{3,1,0,2:T(4,128)S(1)}, u32[]{:S(2)}, u32[]{:S(2)}) collective-permute-start(f32[2,4,1,512]{3,1,0,2:T(4,128)S(1)} %get-tuple-element.54), channel_id=1, source_target_pairs={{0,1},{1,2},{2,3},{3,4},{4,5},{5,6},{6,7},{7,8},{8,9},{9,10},{10,1... | collective-permute-start | bytes 49160 | tf_op jit(solution)/shard_map/ppermute | solution.py:69
  45.1 1.3 %collective-permute-start.8 = (f32[1040]{0:T(1024)S(1)}, f32[1040]{0:T(1024)S(1)}, u32[]{:S(2)}, u32[]{:S(2)}) collective-permute-start(f32[1040]{0:T(1024)S(1)} %pad_maximum_fusion.8), channel_id=1, source_target_pairs={{0,2},{1,3},{2,0},{3,1},{4,6},{5,7},{6,4},{7,5},{8,10},{9,11},{10,... | collective-permute-start | bytes 12488 | tf_op jit(solution)/shard_map/ppermute | solution.py:44
  46.5 2.3 %collective-permute-done.8 = f32[1040]{0:T(1024)S(1)} collective-permute-done((f32[1040]{0:T(1024)S(1)}, f32[1040]{0:T(1024)S(1)}, u32[]{:S(2)}, u32[]{:S(2)}) %collective-permute-start.8) | collective-permute-done | bytes 4192 | tf_op jit(solution)/shard_map/ppermute | solution.py:44
  49.1 1.9 %collective-permute-start.9 = (f32[2064]{0:T(1024)S(1)}, f32[2064]{0:T(1024)S(1)}, u32[]{:S(2)}, u32[]{:S(2)}) collective-permute-start(f32[2064]{0:T(1024)S(1)} %pad_maximum_fusion.6), channel_id=1, source_target_pairs={{0,4},{1,5},{2,6},{3,7},{4,0},{5,1},{6,2},{7,3},{8,12},{9,13},{10,... | collective-permute-start | bytes 24776 | tf_op jit(solution)/shard_map/ppermute | solution.py:44
  51.1 0.7 broadcast_divide_fusion.1
  51.8 0.7 reshape.1882
  52.4 0.7 reshape.1884
  53.3 0.7 pad_maximum_fusion.3
  54.0 1.4 %collective-permute-start.10 = (f32[4112]{0:T(1024)}, f32[4112]{0:T(1024)}, u32[]{:S(2)}, u32[]{:S(2)}) collective-permute-start(f32[4112]{0:T(1024)} %pad_maximum_fusion.3), channel_id=1, source_target_pairs={{0,8},{1,9},{2,10},{3,11},{4,12},{5,13},{6,14},{7,15},{8,0},{9,1},... | collective-permute-start | bytes 49352 | tf_op jit(solution)/shard_map/ppermute | solution.py:44
  55.4 0.7 reshape.1886
  56.1 0.7 gather_fusion.2
  56.8 0.6 copy.84
  57.5 1.5 %collective-permute-done.10 = f32[4112]{0:T(1024)} collective-permute-done((f32[4112]{0:T(1024)}, f32[4112]{0:T(1024)}, u32[]{:S(2)}, u32[]{:S(2)}) %collective-permute-start.10) | collective-permute-done | bytes 16480 | tf_op jit(solution)/shard_map/ppermute | solution.py:44
  59.0 0.7 fusion.86
  60.3 0.8 slice.538
  61.2 0.8 convolution_bitcast_fusion.2
  62.0 1.5 %collective-permute-done.11 = f32[4112]{0:T(1024)S(1)} collective-permute-done((f32[4112]{0:T(1024)S(1)}, f32[4112]{0:T(1024)S(1)}, u32[]{:S(2)}, u32[]{:S(2)}) %collective-permute-start.11) | collective-permute-done | bytes 16480 | tf_op jit(solution)/shard_map/ppermute | solution.py:44
  63.6 0.8 add_multiply_fusion.1
  64.4 0.8 multiply_subtract_fusion.5
  65.4 1.5 %fusion.7 = f32[2,2,4,2,256]{4,2,0,1,3:T(4,128)S(1)} fusion(bf16[1,2,4,2,256,256]{5,4,3,2,1,0:T(8,128)(2,1)S(1)} %copy-done, f32[4]{0:T(128)S(1)} %add_sqrt_fusion.2, f32[2,4,2,4,256]{4,1,3,2,0:T(4,128)} %bitcast.363, f32[1,4,2,4,256]{4,1,3,2,0:T(4,128)S(1)} %bitcast.374, f32[1,4,2,4,256]{4,1,3,2,0:T(4,128)S(1)} %bitcast.373), kind=kOutput, calls=%fused_computation.9 | convolution fusion | flops 16842752 | bytes 2261008 | tf_op jit(solution)/shard_map/ikarc,pqikc->apqir/dot_general | solution.py:100
  67.3 0.7 gather_fusion.3
  69.1 3.1 %collective-permute-done.14 = f32[8,4]{1,0:T(8,128)S(1)} collective-permute-done((f32[8,4]{1,0:T(8,128)S(1)}, f32[8,4]{1,0:T(8,128)S(1)}, u32[]{:S(2)}, u32[]{:S(2)}) %collective-permute-start.14) | collective-permute-done | bytes 160 | tf_op jit(solution)/shard_map/ppermute | solution.py:21
  72.2 1.2 %collective-permute-done.15 = f32[8,4]{1,0:T(8,128)S(1)} collective-permute-done((f32[8,4]{1,0:T(8,128)S(1)}, f32[8,4]{1,0:T(8,128)S(1)}, u32[]{:S(2)}, u32[]{:S(2)}) %collective-permute-start.15) | collective-permute-done | bytes 160 | tf_op jit(solution)/shard_map/ppermute | solution.py:21
  73.3 1.3 %collective-permute-start.16 = (f32[8,4]{1,0:T(8,128)S(1)}, f32[8,4]{1,0:T(8,128)S(1)}, u32[]{:S(2)}, u32[]{:S(2)}) collective-permute-start(f32[8,4]{1,0:T(8,128)S(1)} %add.588), channel_id=1, source_target_pairs={{0,2},{1,3},{2,0},{3,1},{4,6},{5,7},{6,4},{7,5},{8,10},{9,11},{10,... | collective-permute-start | bytes 392 | tf_op jit(solution)/shard_map/ppermute | solution.py:21
  74.7 0.6 copy.99
  75.3 1.6 %collective-permute-done.16 = f32[8,4]{1,0:T(8,128)S(1)} collective-permute-done((f32[8,4]{1,0:T(8,128)S(1)}, f32[8,4]{1,0:T(8,128)S(1)}, u32[]{:S(2)}, u32[]{:S(2)}) %collective-permute-start.16) | collective-permute-done | bytes 160 | tf_op jit(solution)/shard_map/ppermute | solution.py:21
  77.0 1.7 %collective-permute-start.17 = (f32[8,4]{1,0:T(8,128)S(1)}, f32[8,4]{1,0:T(8,128)S(1)}, u32[]{:S(2)}, u32[]{:S(2)}) collective-permute-start(f32[8,4]{1,0:T(8,128)S(1)} %add.589), channel_id=1, source_target_pairs={{0,4},{1,5},{2,6},{3,7},{4,0},{5,1},{6,2},{7,3},{8,12},{9,13},{10,... | collective-permute-start | bytes 392 | tf_op jit(solution)/shard_map/ppermute | solution.py:21
  78.7 1.8 %collective-permute-done.17 = f32[8,4]{1,0:T(8,128)S(1)} collective-permute-done((f32[8,4]{1,0:T(8,128)S(1)}, f32[8,4]{1,0:T(8,128)S(1)}, u32[]{:S(2)}, u32[]{:S(2)}) %collective-permute-start.17) | collective-permute-done | bytes 160 | tf_op jit(solution)/shard_map/ppermute | solution.py:21
  80.6 1.5 %collective-permute-start.18 = (f32[8,4]{1,0:T(8,128)S(1)}, f32[8,4]{1,0:T(8,128)S(1)}, u32[]{:S(2)}, u32[]{:S(2)}) collective-permute-start(f32[8,4]{1,0:T(8,128)S(1)} %add.590), channel_id=1, source_target_pairs={{0,8},{1,9},{2,10},{3,11},{4,12},{5,13},{6,14},{7,15},{8,0},{9,1},... | collective-permute-start | bytes 392 | tf_op jit(solution)/shard_map/ppermute | solution.py:21
  82.2 2.9 %collective-permute-done.18 = f32[8,4]{1,0:T(8,128)S(1)} collective-permute-done((f32[8,4]{1,0:T(8,128)S(1)}, f32[8,4]{1,0:T(8,128)S(1)}, u32[]{:S(2)}, u32[]{:S(2)}) %collective-permute-start.18) | collective-permute-done | bytes 160 | tf_op jit(solution)/shard_map/ppermute | solution.py:21
  85.4 0.6 copy.100
  86.3 0.7 concatenate.148
  (160 shorter events, 8.6 us)
Async XLA Ops:
  0.6 35.9 %copy-start = (bf16[1,2,4,2,256,256]{5,4,3,2,1,0:T(8,128)(2,1)S(1)}, bf16[1,2,4,2,256,256]{5,4,3,2,1,0:T(8,128)(2,1)}, u32[]{:S(2)}) copy-start(bf16[1,2,4,2,256,256]{5,4,3,2,1,0:T(8,128)(2,1)} %param.9) | copy-start | bytes 6291460
  0.6 14.5 %copy-start.1 = (f32[2,4,1,512]{3,2,1,0:T(1,128)S(1)}, f32[2,4,1,512]{3,2,1,0:T(1,128)}, u32[]{:S(2)}) copy-start(f32[2,4,1,512]{3,2,1,0:T(1,128)} %param.8) | copy-start | bytes 49156
  2.4 9.6 %collective-permute-start = (f32[4100]{0:T(1024)S(1)}, f32[4100]{0:T(1024)S(1)}, u32[]{:S(2)}, u32[]{:S(2)}) collective-permute-start(f32[4100]{0:T(1024)S(1)} %pad_maximum_fusion.1), channel_id=1, source_target_pairs={{0,16},{16,0},{1,17},{17,1},{2,18},{18,2},{3,19},{19,3},{4,20},{20... | collective-permute-start | bytes 49208 | tf_op jit(solution)/shard_map/ppermute | solution.py:44
  7.9 20.5 %copy-start.9 = (s32[1024]{0:T(1024)}, s32[1024]{0:T(1024)S(1)}, u32[]{:S(2)}) copy-start(s32[1024]{0:T(1024)S(1)} %pad_clamp_fusion) | copy-start | bytes 12292
  10.4 26.0 %copy-start.3 = (bf16[1,2,64,512]{3,2,1,0:T(8,128)(2,1)S(1)}, bf16[1,2,64,512]{3,2,1,0:T(8,128)(2,1)}, u32[]{:S(2)}) copy-start(bf16[1,2,64,512]{3,2,1,0:T(8,128)(2,1)} %param.13) | copy-start | bytes 393220
  12.1 1.2 %collective-permute-start.1 = (f32[516]{0:T(1024)S(1)}, f32[516]{0:T(1024)S(1)}, u32[]{:S(2)}, u32[]{:S(2)}) collective-permute-start(f32[516]{0:T(1024)S(1)} %pad_maximum_fusion.10), channel_id=1, source_target_pairs={{0,1},{1,0},{2,3},{3,2},{4,5},{5,4},{6,7},{7,6},{8,9},{9,8},{10,11... | collective-permute-start | bytes 6200 | tf_op jit(solution)/shard_map/ppermute | solution.py:44
  13.6 3.7 %collective-permute-start.2 = (f32[1028]{0:T(1024)S(1)}, f32[1028]{0:T(1024)S(1)}, u32[]{:S(2)}, u32[]{:S(2)}) collective-permute-start(f32[1028]{0:T(1024)S(1)} %pad_maximum_fusion.7), channel_id=1, source_target_pairs={{0,2},{1,3},{2,0},{3,1},{4,6},{5,7},{6,4},{7,5},{8,10},{9,11},{10,... | collective-permute-start | bytes 12344 | tf_op jit(solution)/shard_map/ppermute | solution.py:44
  17.6 7.8 %collective-permute-start.3 = (f32[2052]{0:T(1024)S(1)}, f32[2052]{0:T(1024)S(1)}, u32[]{:S(2)}, u32[]{:S(2)}) collective-permute-start(f32[2052]{0:T(1024)S(1)} %pad_maximum_fusion.5), channel_id=1, source_target_pairs={{0,4},{1,5},{2,6},{3,7},{4,0},{5,1},{6,2},{7,3},{8,12},{9,13},{10,... | collective-permute-start | bytes 24632 | tf_op jit(solution)/shard_map/ppermute | solution.py:44
  19.8 5.7 %copy-start.4 = (f32[2,2,4,256]{3,2,1,0:T(4,128)}, f32[2,2,4,256]{3,2,1,0:T(4,128)S(1)}, u32[]{:S(2)}) copy-start(f32[2,2,4,256]{3,2,1,0:T(4,128)S(1)} %gather_fusion.1) | copy-start | bytes 49156
  20.5 9.5 %collective-permute-start.6 = (f32[2,4,1,512]{3,2,1,0:T(1,128)S(1)}, f32[2,4,1,512]{3,2,1,0:T(1,128)S(1)}, u32[]{:S(2)}, u32[]{:S(2)}) collective-permute-start(f32[2,4,1,512]{3,2,1,0:T(1,128)S(1)} %copy-done.1), channel_id=1, source_target_pairs={{1,0},{2,1},{3,2},{4,3},{5,4},{6,5},{7,6},{8,7},{9,8},{10,9},{11,1... | collective-permute-start | bytes 49160 | tf_op jit(solution)/shard_map/ppermute | solution.py:70
  21.8 8.2 %collective-permute-start.5 = (f32[2,4,1,512]{3,2,1,0:T(1,128)S(1)}, f32[2,4,1,512]{3,2,1,0:T(1,128)}, u32[]{:S(2)}, u32[]{:S(2)}) collective-permute-start(f32[2,4,1,512]{3,2,1,0:T(1,128)S(1)} %copy-done.1), channel_id=1, source_target_pairs={{0,1},{1,2},{2,3},{3,4},{4,5},{5,6},{6,7},{7,8},{8,9},{9,10},{10,1... | collective-permute-start | bytes 49160 | tf_op jit(solution)/shard_map/ppermute | solution.py:69
  25.7 5.2 %copy-start.15 = (f32[4]{0:T(128)}, f32[4]{0:T(128)S(1)}, u32[]{:S(2)}) copy-start(f32[4]{0:T(128)S(1)} %slice_add_fusion.9) | copy-start | bytes 52
  26.4 5.9 %collective-permute-start.4 = (f32[4100]{0:T(1024)}, f32[4100]{0:T(1024)}, u32[]{:S(2)}, u32[]{:S(2)}) collective-permute-start(f32[4100]{0:T(1024)} %pad_maximum_fusion.2), channel_id=1, source_target_pairs={{0,8},{1,9},{2,10},{3,11},{4,12},{5,13},{6,14},{7,15},{8,0},{9,1},... | collective-permute-start | bytes 49208 | tf_op jit(solution)/shard_map/ppermute | solution.py:44
  28.8 10.1 %copy-start.2 = (bf16[1,2,64,512]{3,2,1,0:T(8,128)(2,1)S(1)}, bf16[1,2,64,512]{3,2,1,0:T(8,128)(2,1)}, u32[]{:S(2)}) copy-start(bf16[1,2,64,512]{3,2,1,0:T(8,128)(2,1)} %param.12) | copy-start | bytes 393220
  33.0 18.0 %copy-start.5 = (f32[2,2,4,256]{3,2,1,0:T(4,128)S(1)}, f32[2,2,4,256]{3,2,1,0:T(4,128)}, u32[]{:S(2)}) copy-start(f32[2,2,4,256]{3,2,1,0:T(4,128)} %copy-done.4) | copy-start | bytes 49156
  35.6 13.5 %copy-start.7 = (f32[4]{0:T(128)}, f32[4]{0:T(128)S(1)}, u32[]{:S(2)}) copy-start(f32[4]{0:T(128)S(1)} %add_sqrt_fusion.3) | copy-start | bytes 52
  36.4 1.7 %copy-start.6 = (f32[2,4,64]{2,1,0:T(4,128)}, f32[2,4,64]{2,1,0:T(4,128)S(1)}, u32[]{:S(2)}) copy-start(f32[2,4,64]{2,1,0:T(4,128)S(1)} %fusion.46) | copy-start | bytes 6148
  39.4 5.4 %copy-start.10 = (f32[4]{0:T(128)}, f32[4]{0:T(128)S(1)}, u32[]{:S(2)}) copy-start(f32[4]{0:T(128)S(1)} %get-tuple-element.22) | copy-start | bytes 52
  39.4 5.7 %copy-start.11 = (f32[4]{0:T(128)}, f32[4]{0:T(128)S(1)}, u32[]{:S(2)}) copy-start(f32[4]{0:T(128)S(1)} %get-tuple-element.23) | copy-start | bytes 52
  39.4 5.7 %copy-start.12 = (f32[4]{0:T(128)}, f32[4]{0:T(128)S(1)}, u32[]{:S(2)}) copy-start(f32[4]{0:T(128)S(1)} %get-tuple-element.28) | copy-start | bytes 52
  39.4 5.7 %copy-start.13 = (f32[4]{0:T(128)}, f32[4]{0:T(128)S(1)}, u32[]{:S(2)}) copy-start(f32[4]{0:T(128)S(1)} %get-tuple-element.29) | copy-start | bytes 52
  39.6 5.2 %collective-permute-start.7 = (f32[528]{0:T(1024)S(1)}, f32[528]{0:T(1024)S(1)}, u32[]{:S(2)}, u32[]{:S(2)}) collective-permute-start(f32[528]{0:T(1024)S(1)} %pad_maximum_fusion.12), channel_id=1, source_target_pairs={{0,1},{1,0},{2,3},{3,2},{4,5},{5,4},{6,7},{7,6},{8,9},{9,8},{10,11... | collective-permute-start | bytes 6344 | tf_op jit(solution)/shard_map/ppermute | solution.py:44
  40.4 15.7 %collective-permute-start.13 = (f32[2,4,1,512]{3,1,0,2:T(4,128)S(1)}, f32[2,4,1,512]{3,1,0,2:T(4,128)S(1)}, u32[]{:S(2)}, u32[]{:S(2)}) collective-permute-start(f32[2,4,1,512]{3,1,0,2:T(4,128)S(1)} %get-tuple-element.54), channel_id=1, source_target_pairs={{1,0},{2,1},{3,2},{4,3},{5,4},{6,5},{7,6},{8,7},{9,8},{10,9},{11,1... | collective-permute-start | bytes 49160 | tf_op jit(solution)/shard_map/ppermute | solution.py:70
  41.7 14.4 %collective-permute-start.12 = (f32[2,4,1,512]{3,1,0,2:T(4,128)S(1)}, f32[2,4,1,512]{3,1,0,2:T(4,128)S(1)}, u32[]{:S(2)}, u32[]{:S(2)}) collective-permute-start(f32[2,4,1,512]{3,1,0,2:T(4,128)S(1)} %get-tuple-element.54), channel_id=1, source_target_pairs={{0,1},{1,2},{2,3},{3,4},{4,5},{5,6},{6,7},{7,8},{8,9},{9,10},{10,1... | collective-permute-start | bytes 49160 | tf_op jit(solution)/shard_map/ppermute | solution.py:69
  45.1 3.7 %collective-permute-start.8 = (f32[1040]{0:T(1024)S(1)}, f32[1040]{0:T(1024)S(1)}, u32[]{:S(2)}, u32[]{:S(2)}) collective-permute-start(f32[1040]{0:T(1024)S(1)} %pad_maximum_fusion.8), channel_id=1, source_target_pairs={{0,2},{1,3},{2,0},{3,1},{4,6},{5,7},{6,4},{7,5},{8,10},{9,11},{10,... | collective-permute-start | bytes 12488 | tf_op jit(solution)/shard_map/ppermute | solution.py:44
  49.1 4.0 %collective-permute-start.9 = (f32[2064]{0:T(1024)S(1)}, f32[2064]{0:T(1024)S(1)}, u32[]{:S(2)}, u32[]{:S(2)}) collective-permute-start(f32[2064]{0:T(1024)S(1)} %pad_maximum_fusion.6), channel_id=1, source_target_pairs={{0,4},{1,5},{2,6},{3,7},{4,0},{5,1},{6,2},{7,3},{8,12},{9,13},{10,... | collective-permute-start | bytes 24776 | tf_op jit(solution)/shard_map/ppermute | solution.py:44
  53.3 2.8 %copy-start.14 = (f32[16]{0:T(128)}, f32[16]{0:T(128)S(1)}, u32[]{:S(2)}) copy-start(f32[16]{0:T(128)S(1)} %get-tuple-element.56) | copy-start | bytes 196
  54.0 5.0 %collective-permute-start.10 = (f32[4112]{0:T(1024)}, f32[4112]{0:T(1024)}, u32[]{:S(2)}, u32[]{:S(2)}) collective-permute-start(f32[4112]{0:T(1024)} %pad_maximum_fusion.3), channel_id=1, source_target_pairs={{0,8},{1,9},{2,10},{3,11},{4,12},{5,13},{6,14},{7,15},{8,0},{9,1},... | collective-permute-start | bytes 49352 | tf_op jit(solution)/shard_map/ppermute | solution.py:44
  59.8 3.8 %collective-permute-start.11 = (f32[4112]{0:T(1024)S(1)}, f32[4112]{0:T(1024)S(1)}, u32[]{:S(2)}, u32[]{:S(2)}) collective-permute-start(f32[4112]{0:T(1024)S(1)} %pad_maximum_fusion.4), channel_id=1, source_target_pairs={{0,16},{16,0},{1,17},{17,1},{2,18},{18,2},{3,19},{19,3},{4,20},{20... | collective-permute-start | bytes 49352 | tf_op jit(solution)/shard_map/ppermute | solution.py:44
  61.9 12.7 %copy-start.8 = (f32[4]{0:T(128)S(1)}, f32[4]{0:T(128)}, u32[]{:S(2)}) copy-start(f32[4]{0:T(128)} %copy-done.7) | copy-start | bytes 52
  68.5 3.7 %collective-permute-start.14 = (f32[8,4]{1,0:T(8,128)S(1)}, f32[8,4]{1,0:T(8,128)S(1)}, u32[]{:S(2)}, u32[]{:S(2)}) collective-permute-start(f32[8,4]{1,0:T(8,128)S(1)} %concatenate.147), channel_id=1, source_target_pairs={{0,16},{16,0},{1,17},{17,1},{2,18},{18,2},{3,19},{19,3},{4,20},{20... | collective-permute-start | bytes 392 | tf_op jit(solution)/shard_map/ppermute | solution.py:21
  72.2 1.2 %collective-permute-start.15 = (f32[8,4]{1,0:T(8,128)S(1)}, f32[8,4]{1,0:T(8,128)S(1)}, u32[]{:S(2)}, u32[]{:S(2)}) collective-permute-start(f32[8,4]{1,0:T(8,128)S(1)} %add.587), channel_id=1, source_target_pairs={{0,1},{1,0},{2,3},{3,2},{4,5},{5,4},{6,7},{7,6},{8,9},{9,8},{10,11... | collective-permute-start | bytes 392 | tf_op jit(solution)/shard_map/ppermute | solution.py:21
  73.3 3.6 %collective-permute-start.16 = (f32[8,4]{1,0:T(8,128)S(1)}, f32[8,4]{1,0:T(8,128)S(1)}, u32[]{:S(2)}, u32[]{:S(2)}) collective-permute-start(f32[8,4]{1,0:T(8,128)S(1)} %add.588), channel_id=1, source_target_pairs={{0,2},{1,3},{2,0},{3,1},{4,6},{5,7},{6,4},{7,5},{8,10},{9,11},{10,... | collective-permute-start | bytes 392 | tf_op jit(solution)/shard_map/ppermute | solution.py:21
  77.0 3.6 %collective-permute-start.17 = (f32[8,4]{1,0:T(8,128)S(1)}, f32[8,4]{1,0:T(8,128)S(1)}, u32[]{:S(2)}, u32[]{:S(2)}) collective-permute-start(f32[8,4]{1,0:T(8,128)S(1)} %add.589), channel_id=1, source_target_pairs={{0,4},{1,5},{2,6},{3,7},{4,0},{5,1},{6,2},{7,3},{8,12},{9,13},{10,... | collective-permute-start | bytes 392 | tf_op jit(solution)/shard_map/ppermute | solution.py:21
  80.6 4.5 %collective-permute-start.18 = (f32[8,4]{1,0:T(8,128)S(1)}, f32[8,4]{1,0:T(8,128)S(1)}, u32[]{:S(2)}, u32[]{:S(2)}) collective-permute-start(f32[8,4]{1,0:T(8,128)S(1)} %add.590), channel_id=1, source_target_pairs={{0,8},{1,9},{2,10},{3,11},{4,12},{5,13},{6,14},{7,15},{8,0},{9,1},... | collective-permute-start | bytes 392 | tf_op jit(solution)/shard_map/ppermute | solution.py:21

commit v16 on v14

--- a/solution.py
+++ b/solution.py
@@ -187,7 +187,6 @@
         - mates_one.reshape(first_vec.shape)
     )
 
-    window_img = neighbours(image_one)
     parts = jnp.concatenate(
         [
             local_products([first_vec], image_one)[0],
@@ -195,8 +194,8 @@
             local_squares(first_vec)[None],
         ]
     )
-    one, coef_img, every_img = tree_collect(
-        parts, coefficients(image_one, source_basis), image_one[:, :, 0]
+    one, coef_img, every_img, window_img = tree_collect(
+        parts, coefficients(image_one, source_basis), image_one[:, :, 0], halo=image_one
     )
     one = one / total
     h_one_one = one[0:2]

time: 75.6 us -> 75.6 us (level)
  no operation moved by 1% of the time
where the time goes in v16:
time: 75.6 us; the launch traced here: 74.9 us
  starting transfers between devices  32.5 us (43%)
  waiting for transfers between devices  17.6 us (23%)
  local copies, waits for them, and re-layouts  9.22 us (12%)
  other arithmetic  7.44 us (10%)
  matrix products  6.91 us (9%)
  between operations  1.21 us (2%)
    ppermute x10, starting transfers between devices, tree_collect(): got = lax.ppermute(packed, axis, [(i, i ^ k) for i in range(n)])  20.2 us
    ppermute x10, waiting for transfers between devices, tree_collect(): got = lax.ppermute(packed, axis, [(i, i ^ k) for i in range(n)])  9.04 us
    ppermute x5, waiting for transfers between devices, tree_sum(): x = x + lax.ppermute(x, axis, [(i, i ^ k) for i in range(n)])  8.55 us
    ppermute x5, starting transfers between devices, tree_sum(): x = x + lax.ppermute(x, axis, [(i, i ^ k) for i in range(n)])  7.12 us
    dot_general x2, matrix products, far_inner(): jnp.einsum('sakl,spql->apqk', weights, gathered, precision=lax.Precision....  3.98 us
    ppermute x2, starting transfers between devices, neighbours(): right = lax.ppermute(field, 'blk', [(i + 1, i) for i in range(ends)])  2.58 us
    ppermute x2, starting transfers between devices, neighbours(): left = lax.ppermute(field, 'blk', [(i, i + 1) for i in range(ends)])  2.58 us
    unnamed x12, local copies, waits for them, and re-layouts  2 us
  transfers between devices with their start and end apart: 19, of which 12 were waited for; matrix products, arithmetic and copies ran while one was open for 16% of the time, Pallas kernels for 0%

profile of v16, /device:TPU:0, one launch (start us, length us, event | category | flops | bytes accessed | tf_op | source)
XLA Modules:
  0.0 74.9 jit_solution(16044390774839156034)
XLA Ops:
  0.6 1.0 %add_reduce_fusion.8 = f32[4]{0:T(128)S(1)} fusion(f32[2,4,1,512]{3,2,1,0:T(1,128)} %param.8), kind=kLoop, calls=%fused_computation.121 | loop fusion | flops 8188 | bytes 16400 | tf_op jit(solution)/shard_map/reduce_sum | solution.py:139
  1.6 0.8 %pad_maximum_fusion.1 = f32[4100]{0:T(1024)S(1)} fusion(f32[4096]{0:T(1024)} %bitcast.352, f32[4]{0:T(128)S(1)} %add_reduce_fusion.8), kind=kLoop, calls=%fused_computation.52 | loop fusion | flops 4100 | bytes 32800 | tf_op jit(solution)/shard_map/concatenate | solution.py:40
  2.4 3.0 %collective-permute-start = (f32[4100]{0:T(1024)S(1)}, f32[4100]{0:T(1024)S(1)}, u32[]{:S(2)}, u32[]{:S(2)}) collective-permute-start(f32[4100]{0:T(1024)S(1)} %pad_maximum_fusion.1), channel_id=1, source_target_pairs={{0,16},{16,0},{1,17},{17,1},{2,18},{18,2},{3,19},{19,3},{4,20},{20... | collective-permute-start | bytes 49208 | tf_op jit(solution)/shard_map/ppermute | solution.py:44
  5.4 0.7 convert_element_type.30
  6.1 1.1 %convolution_bitcast_fusion.5 = f32[2,2,4,64]{3,2,1,0:T(4,128)S(1)} fusion(bf16[1,2,64,512]{3,2,1,0:T(8,128)(2,1)} %param.12, bf16[2,4,1,512]{3,2,1,0:T(2,128)(2,1)S(1)} %convert_element_type.30), kind=kOutput, calls=%fused_computation.15 | convolution fusion | flops 1048576 | bytes 143360 | tf_op jit(solution)/shard_map/akr,pqr->apqk/dot_general | solution.py:73
  7.2 0.7 iota_compare_fusion
  8.0 0.2 and_convert_fusion
  8.2 0.8 %reshape_squeeze.4 = s32[8,1]{0,1:T(1,128)S(1)} reshape(s32[1,2,4]{2,1,0:T(2,128)} %param.10) | data formatting | bytes 64 | tf_op jit(solution)/shard_map/reshape;squeeze | solution.py:84
  9.1 0.7 fusion.61
  9.8 0.5 collective-permute-done.1
  10.4 0.1 reshape.1933
  10.7 1.5 %collective-permute-start.2 = (f32[1028]{0:T(1024)S(1)}, f32[1028]{0:T(1024)S(1)}, u32[]{:S(2)}, u32[]{:S(2)}) collective-permute-start(f32[1028]{0:T(1024)S(1)} %pad_maximum_fusion.7), channel_id=1, source_target_pairs={{0,2},{1,3},{2,0},{3,1},{4,6},{5,7},{6,4},{7,5},{8,10},{9,11},{10,... | collective-permute-start | bytes 12344 | tf_op jit(solution)/shard_map/ppermute | solution.py:44
  12.2 2.2 %collective-permute-done.2 = f32[1028]{0:T(1024)S(1)} collective-permute-done((f32[1028]{0:T(1024)S(1)}, f32[1028]{0:T(1024)S(1)}, u32[]{:S(2)}, u32[]{:S(2)}) %collective-permute-start.2) | collective-permute-done | bytes 4144 | tf_op jit(solution)/shard_map/ppermute | solution.py:44
  14.7 1.6 %collective-permute-start.3 = (f32[2052]{0:T(1024)S(1)}, f32[2052]{0:T(1024)S(1)}, u32[]{:S(2)}, u32[]{:S(2)}) collective-permute-start(f32[2052]{0:T(1024)S(1)} %pad_maximum_fusion.5), channel_id=1, source_target_pairs={{0,4},{1,5},{2,6},{3,7},{4,0},{5,1},{6,2},{7,3},{8,12},{9,13},{10,... | collective-permute-start | bytes 24632 | tf_op jit(solution)/shard_map/ppermute | solution.py:44
  16.2 0.7 copy.255
  17.1 1.3 %collective-permute-start.5 = (f32[2,4,1,512]{3,2,1,0:T(1,128)}, f32[2,4,1,512]{3,2,1,0:T(1,128)S(1)}, u32[]{:S(2)}, u32[]{:S(2)}) collective-permute-start(f32[2,4,1,512]{3,2,1,0:T(1,128)} %param.8), channel_id=1, source_target_pairs={{0,1},{1,2},{2,3},{3,4},{4,5},{5,6},{6,7},{7,8},{8,9},{9,10},{10,1... | collective-permute-start | bytes 49160 | tf_op jit(solution)/shard_map/ppermute | solution.py:62
  18.4 1.3 %collective-permute-start.6 = (f32[2,4,1,512]{3,2,1,0:T(1,128)}, f32[2,4,1,512]{3,2,1,0:T(1,128)S(1)}, u32[]{:S(2)}, u32[]{:S(2)}) collective-permute-start(f32[2,4,1,512]{3,2,1,0:T(1,128)} %param.8), channel_id=1, source_target_pairs={{1,0},{2,1},{3,2},{4,3},{5,4},{6,5},{7,6},{8,7},{9,8},{10,9},{11,1... | collective-permute-start | bytes 49160 | tf_op jit(solution)/shard_map/ppermute | solution.py:63
  20.0 6.5 %collective-permute-start.4 = (f32[4100]{0:T(1024)S(1)}, f32[4100]{0:T(1024)S(1)}, u32[]{:S(2)}, u32[]{:S(2)}) collective-permute-start(f32[4100]{0:T(1024)S(1)} %pad_maximum_fusion.2), channel_id=1, source_target_pairs={{0,8},{1,9},{2,10},{3,11},{4,12},{5,13},{6,14},{7,15},{8,0},{9,1},... | collective-permute-start | bytes 49208 | tf_op jit(solution)/shard_map/ppermute | solution.py:44
  26.6 0.6 gather_fusion.1
  27.3 0.9 %maximum_reduce_fusion = f32[2,4,1536]{2,1,0:T(4,128)S(1)} fusion(f32[2,4,1,512]{3,2,1,0:T(1,128)S(1)} %collective-permute-done.6, f32[2,4,1,512]{3,2,1,0:T(1,128)} %param.8, f32[2,4,1,512]{3,2,1,0:T(1,128)S(1)} %collective-permute-done.5), kind=kLoop, calls=%fused_computation.37 | loop fusion | flops 24576 | bytes 98304 | tf_op jit(solution)/shard_map/concatenate | solution.py:64
  28.1 0.6 gather_fusion
  29.0 2.0 %convolution_bitcast_fusion.4 = f32[2,2,4,64]{3,2,0,1:T(4,128)S(1)} fusion(f32[16,2,4,64,1]{3,0,2,1,4:T(8,128)S(1)} %fusion.19, f32[1,1,16,2,64,64]{5,4,3,2,1,0:T(8,128)} %param.14, f32[16,64,64]{2,1,0:T(8,128)S(1)} %and_convert_fusion), kind=kOutput, calls=%fused_computation.14 | convolution fusion | flops 6422528 | bytes 823296 | tf_op jit(solution)/shard_map/sakl,spql->apqk/dot_general | solution.py:109
  31.1 0.1 convolution_bitcast_fusion.1
  31.2 0.7 fusion.4
  32.1 0.1 convolution_bitcast_fusion.3
  32.2 0.2 add_reduce_fusion.7
  32.7 1.2 %collective-permute-done.7 = f32[528]{0:T(1024)S(1)} collective-permute-done((f32[528]{0:T(1024)S(1)}, f32[528]{0:T(1024)S(1)}, u32[]{:S(2)}, u32[]{:S(2)}) %collective-permute-start.7) | collective-permute-done | bytes 2144 | tf_op jit(solution)/shard_map/ppermute | solution.py:44
  33.9 0.1 reshape.1943
  34.2 0.8 %collective-permute-start.8 = (f32[1040]{0:T(1024)S(1)}, f32[1040]{0:T(1024)S(1)}, u32[]{:S(2)}, u32[]{:S(2)}) collective-permute-start(f32[1040]{0:T(1024)S(1)} %pad_maximum_fusion.8), channel_id=1, source_target_pairs={{0,2},{1,3},{2,0},{3,1},{4,6},{5,7},{6,4},{7,5},{8,10},{9,11},{10,... | collective-permute-start | bytes 12488 | tf_op jit(solution)/shard_map/ppermute | solution.py:44
  35.1 2.8 %collective-permute-done.8 = f32[1040]{0:T(1024)S(1)} collective-permute-done((f32[1040]{0:T(1024)S(1)}, f32[1040]{0:T(1024)S(1)}, u32[]{:S(2)}, u32[]{:S(2)}) %collective-permute-start.8) | collective-permute-done | bytes 4192 | tf_op jit(solution)/shard_map/ppermute | solution.py:44
  38.2 0.5 collective-permute-start.9
  38.7 1.3 %collective-permute-start.12 = (f32[2,4,1,512]{3,1,0,2:T(4,128)S(1)}, f32[2,4,1,512]{3,1,0,2:T(4,128)S(1)}, u32[]{:S(2)}, u32[]{:S(2)}) collective-permute-start(f32[2,4,1,512]{3,1,0,2:T(4,128)S(1)} %get-tuple-element.10), channel_id=1, source_target_pairs={{0,1},{1,2},{2,3},{3,4},{4,5},{5,6},{6,7},{7,8},{8,9},{9,10},{10,1... | collective-permute-start | bytes 49160 | tf_op jit(solution)/shard_map/ppermute | solution.py:62
  40.0 1.3 %collective-permute-start.13 = (f32[2,4,1,512]{3,1,0,2:T(4,128)S(1)}, f32[2,4,1,512]{3,1,0,2:T(4,128)S(1)}, u32[]{:S(2)}, u32[]{:S(2)}) collective-permute-start(f32[2,4,1,512]{3,1,0,2:T(4,128)S(1)} %get-tuple-element.10), channel_id=1, source_target_pairs={{1,0},{2,1},{3,2},{4,3},{5,4},{6,5},{7,6},{8,7},{9,8},{10,9},{11,1... | collective-permute-start | bytes 49160 | tf_op jit(solution)/shard_map/ppermute | solution.py:63
  41.5 0.4 collective-permute-done.9
  42.3 5.9 %collective-permute-start.10 = (f32[4112]{0:T(1024)S(1)}, f32[4112]{0:T(1024)S(1)}, u32[]{:S(2)}, u32[]{:S(2)}) collective-permute-start(f32[4112]{0:T(1024)S(1)} %pad_maximum_fusion.3), channel_id=1, source_target_pairs={{0,8},{1,9},{2,10},{3,11},{4,12},{5,13},{6,14},{7,15},{8,0},{9,1},... | collective-permute-start | bytes 49352 | tf_op jit(solution)/shard_map/ppermute | solution.py:44
  48.3 0.6 gather_fusion.2
  48.9 1.0 %collective-permute-done.10 = f32[4112]{0:T(1024)S(1)} collective-permute-done((f32[4112]{0:T(1024)S(1)}, f32[4112]{0:T(1024)S(1)}, u32[]{:S(2)}, u32[]{:S(2)}) %collective-permute-start.10) | collective-permute-done | bytes 16480 | tf_op jit(solution)/shard_map/ppermute | solution.py:44
  50.1 0.5 collective-permute-start.11
  50.8 2.0 %convolution_bitcast_fusion.2 = f32[2,4,2,64]{3,1,2,0:T(4,128)S(1)} fusion(f32[16,2,4,64,1]{3,0,2,1,4:T(8,128)S(1)} %fusion.21, f32[1,1,16,2,64,64]{5,4,3,2,1,0:T(8,128)} %param.14, f32[16,64,64]{2,1,0:T(8,128)S(1)} %and_convert_fusion), kind=kOutput, calls=%fused_computation.12 | convolution fusion | flops 6422528 | bytes 823296 | tf_op jit(solution)/shard_map/sakl,spql->apqk/dot_general | solution.py:109
  52.8 1.0 %collective-permute-done.11 = f32[4112]{0:T(1024)S(1)} collective-permute-done((f32[4112]{0:T(1024)S(1)}, f32[4112]{0:T(1024)S(1)}, u32[]{:S(2)}, u32[]{:S(2)}) %collective-permute-start.11) | collective-permute-done | bytes 16480 | tf_op jit(solution)/shard_map/ppermute | solution.py:44
  53.8 0.1 reshape.1949
  54.4 0.6 gather_fusion.3
  55.0 0.2 convolution_bitcast_fusion
  55.2 0.1 multiply_subtract_fusion
  55.3 0.7 fusion.7
  56.1 0.2 subtract_reduce_fusion
  56.4 0.6 collective-permute-start.14
  57.0 3.1 %collective-permute-done.14 = f32[8,4]{1,0:T(8,128)S(1)} collective-permute-done((f32[8,4]{1,0:T(8,128)S(1)}, f32[8,4]{1,0:T(8,128)S(1)}, u32[]{:S(2)}, u32[]{:S(2)}) %collective-permute-start.14) | collective-permute-done | bytes 160 | tf_op jit(solution)/shard_map/ppermute | solution.py:21
  60.1 1.2 %collective-permute-done.15 = f32[8,4]{1,0:T(8,128)S(1)} collective-permute-done((f32[8,4]{1,0:T(8,128)S(1)}, f32[8,4]{1,0:T(8,128)S(1)}, u32[]{:S(2)}, u32[]{:S(2)}) %collective-permute-start.15) | collective-permute-done | bytes 160 | tf_op jit(solution)/shard_map/ppermute | solution.py:21
  61.2 1.6 %collective-permute-start.16 = (f32[8,4]{1,0:T(8,128)S(1)}, f32[8,4]{1,0:T(8,128)S(1)}, u32[]{:S(2)}, u32[]{:S(2)}) collective-permute-start(f32[8,4]{1,0:T(8,128)S(1)} %add.575), channel_id=1, source_target_pairs={{0,2},{1,3},{2,0},{3,1},{4,6},{5,7},{6,4},{7,5},{8,10},{9,11},{10,... | collective-permute-start | bytes 392 | tf_op jit(solution)/shard_map/ppermute | solution.py:21
  62.8 0.1 copy.179
  62.9 0.6 copy.185
  63.5 1.3 %collective-permute-done.16 = f32[8,4]{1,0:T(8,128)S(1)} collective-permute-done((f32[8,4]{1,0:T(8,128)S(1)}, f32[8,4]{1,0:T(8,128)S(1)}, u32[]{:S(2)}, u32[]{:S(2)}) %collective-permute-start.16) | collective-permute-done | bytes 160 | tf_op jit(solution)/shard_map/ppermute | solution.py:21
  64.9 2.0 %collective-permute-start.17 = (f32[8,4]{1,0:T(8,128)S(1)}, f32[8,4]{1,0:T(8,128)S(1)}, u32[]{:S(2)}, u32[]{:S(2)}) collective-permute-start(f32[8,4]{1,0:T(8,128)S(1)} %add.576), channel_id=1, source_target_pairs={{0,4},{1,5},{2,6},{3,7},{4,0},{5,1},{6,2},{7,3},{8,12},{9,13},{10,... | collective-permute-start | bytes 392 | tf_op jit(solution)/shard_map/ppermute | solution.py:21
  66.9 0.1 copy.180
  67.0 1.5 %collective-permute-done.17 = f32[8,4]{1,0:T(8,128)S(1)} collective-permute-done((f32[8,4]{1,0:T(8,128)S(1)}, f32[8,4]{1,0:T(8,128)S(1)}, u32[]{:S(2)}, u32[]{:S(2)}) %collective-permute-start.17) | collective-permute-done | bytes 160 | tf_op jit(solution)/shard_map/ppermute | solution.py:21
  68.5 2.9 %collective-permute-start.18 = (f32[8,4]{1,0:T(8,128)S(1)}, f32[8,4]{1,0:T(8,128)S(1)}, u32[]{:S(2)}, u32[]{:S(2)}) collective-permute-start(f32[8,4]{1,0:T(8,128)S(1)} %add.577), channel_id=1, source_target_pairs={{0,8},{1,9},{2,10},{3,11},{4,12},{5,13},{6,14},{7,15},{8,0},{9,1},... | collective-permute-start | bytes 392 | tf_op jit(solution)/shard_map/ppermute | solution.py:21
  71.4 0.1 copy.181
  71.5 1.5 %collective-permute-done.18 = f32[8,4]{1,0:T(8,128)S(1)} collective-permute-done((f32[8,4]{1,0:T(8,128)S(1)}, f32[8,4]{1,0:T(8,128)S(1)}, u32[]{:S(2)}, u32[]{:S(2)}) %collective-permute-start.18) | collective-permute-done | bytes 160 | tf_op jit(solution)/shard_map/ppermute | solution.py:21
  73.1 0.1 copy.182
  73.2 0.1 copy.184
  73.3 0.1 copy.183
  73.6 0.6 copy.186
  74.2 0.7 concatenate.156
  (146 shorter events, 4.7 us)
Async XLA Ops:
  0.6 30.6 %copy-start = (bf16[1,2,4,2,256,256]{5,4,3,2,1,0:T(8,128)(2,1)S(1)}, bf16[1,2,4,2,256,256]{5,4,3,2,1,0:T(8,128)(2,1)}, u32[]{:S(2)}) copy-start(bf16[1,2,4,2,256,256]{5,4,3,2,1,0:T(8,128)(2,1)} %param.9) | copy-start | bytes 6291460
  2.4 6.6 %collective-permute-start = (f32[4100]{0:T(1024)S(1)}, f32[4100]{0:T(1024)S(1)}, u32[]{:S(2)}, u32[]{:S(2)}) collective-permute-start(f32[4100]{0:T(1024)S(1)} %pad_maximum_fusion.1), channel_id=1, source_target_pairs={{0,16},{16,0},{1,17},{17,1},{2,18},{18,2},{3,19},{19,3},{4,20},{20... | collective-permute-start | bytes 49208 | tf_op jit(solution)/shard_map/ppermute | solution.py:44
  6.1 25.0 %copy-start.3 = (bf16[1,2,64,512]{3,2,1,0:T(8,128)(2,1)S(1)}, bf16[1,2,64,512]{3,2,1,0:T(8,128)(2,1)}, u32[]{:S(2)}) copy-start(bf16[1,2,64,512]{3,2,1,0:T(8,128)(2,1)} %param.13) | copy-start | bytes 393220
  9.1 1.2 %collective-permute-start.1 = (f32[516]{0:T(1024)S(1)}, f32[516]{0:T(1024)S(1)}, u32[]{:S(2)}, u32[]{:S(2)}) collective-permute-start(f32[516]{0:T(1024)S(1)} %pad_maximum_fusion.10), channel_id=1, source_target_pairs={{0,1},{1,0},{2,3},{3,2},{4,5},{5,4},{6,7},{7,6},{8,9},{9,8},{10,11... | collective-permute-start | bytes 6200 | tf_op jit(solution)/shard_map/ppermute | solution.py:44
  10.7 3.7 %collective-permute-start.2 = (f32[1028]{0:T(1024)S(1)}, f32[1028]{0:T(1024)S(1)}, u32[]{:S(2)}, u32[]{:S(2)}) collective-permute-start(f32[1028]{0:T(1024)S(1)} %pad_maximum_fusion.7), channel_id=1, source_target_pairs={{0,2},{1,3},{2,0},{3,1},{4,6},{5,7},{6,4},{7,5},{8,10},{9,11},{10,... | collective-permute-start | bytes 12344 | tf_op jit(solution)/shard_map/ppermute | solution.py:44
  14.7 5.0 %collective-permute-start.3 = (f32[2052]{0:T(1024)S(1)}, f32[2052]{0:T(1024)S(1)}, u32[]{:S(2)}, u32[]{:S(2)}) collective-permute-start(f32[2052]{0:T(1024)S(1)} %pad_maximum_fusion.5), channel_id=1, source_target_pairs={{0,4},{1,5},{2,6},{3,7},{4,0},{5,1},{6,2},{7,3},{8,12},{9,13},{10,... | collective-permute-start | bytes 24632 | tf_op jit(solution)/shard_map/ppermute | solution.py:44
  17.1 10.2 %collective-permute-start.5 = (f32[2,4,1,512]{3,2,1,0:T(1,128)}, f32[2,4,1,512]{3,2,1,0:T(1,128)S(1)}, u32[]{:S(2)}, u32[]{:S(2)}) collective-permute-start(f32[2,4,1,512]{3,2,1,0:T(1,128)} %param.8), channel_id=1, source_target_pairs={{0,1},{1,2},{2,3},{3,4},{4,5},{5,6},{6,7},{7,8},{8,9},{9,10},{10,1... | collective-permute-start | bytes 49160 | tf_op jit(solution)/shard_map/ppermute | solution.py:62
  18.4 8.9 %collective-permute-start.6 = (f32[2,4,1,512]{3,2,1,0:T(1,128)}, f32[2,4,1,512]{3,2,1,0:T(1,128)S(1)}, u32[]{:S(2)}, u32[]{:S(2)}) collective-permute-start(f32[2,4,1,512]{3,2,1,0:T(1,128)} %param.8), channel_id=1, source_target_pairs={{1,0},{2,1},{3,2},{4,3},{5,4},{6,5},{7,6},{8,7},{9,8},{10,9},{11,1... | collective-permute-start | bytes 49160 | tf_op jit(solution)/shard_map/ppermute | solution.py:63
  20.0 8.7 %collective-permute-start.4 = (f32[4100]{0:T(1024)S(1)}, f32[4100]{0:T(1024)S(1)}, u32[]{:S(2)}, u32[]{:S(2)}) collective-permute-start(f32[4100]{0:T(1024)S(1)} %pad_maximum_fusion.2), channel_id=1, source_target_pairs={{0,8},{1,9},{2,10},{3,11},{4,12},{5,13},{6,14},{7,15},{8,0},{9,1},... | collective-permute-start | bytes 49208 | tf_op jit(solution)/shard_map/ppermute | solution.py:44
  29.0 2.9 %copy-start.1 = (f32[2,4,1,512]{3,2,1,0:T(1,128)S(1)}, f32[2,4,1,512]{3,2,1,0:T(1,128)}, u32[]{:S(2)}) copy-start(f32[2,4,1,512]{3,2,1,0:T(1,128)} %param.8) | copy-start | bytes 49156
  29.0 3.0 %copy-start.2 = (bf16[1,2,64,512]{3,2,1,0:T(8,128)(2,1)S(1)}, bf16[1,2,64,512]{3,2,1,0:T(8,128)(2,1)}, u32[]{:S(2)}) copy-start(bf16[1,2,64,512]{3,2,1,0:T(8,128)(2,1)} %param.12) | copy-start | bytes 393220
  32.7 1.2 %collective-permute-start.7 = (f32[528]{0:T(1024)S(1)}, f32[528]{0:T(1024)S(1)}, u32[]{:S(2)}, u32[]{:S(2)}) collective-permute-start(f32[528]{0:T(1024)S(1)} %pad_maximum_fusion.12), channel_id=1, source_target_pairs={{0,1},{1,0},{2,3},{3,2},{4,5},{5,4},{6,7},{7,6},{8,9},{9,8},{10,11... | collective-permute-start | bytes 6344 | tf_op jit(solution)/shard_map/ppermute | solution.py:44
  34.2 3.7 %collective-permute-start.8 = (f32[1040]{0:T(1024)S(1)}, f32[1040]{0:T(1024)S(1)}, u32[]{:S(2)}, u32[]{:S(2)}) collective-permute-start(f32[1040]{0:T(1024)S(1)} %pad_maximum_fusion.8), channel_id=1, source_target_pairs={{0,2},{1,3},{2,0},{3,1},{4,6},{5,7},{6,4},{7,5},{8,10},{9,11},{10,... | collective-permute-start | bytes 12488 | tf_op jit(solution)/shard_map/ppermute | solution.py:44
  38.2 3.7 %collective-permute-start.9 = (f32[2064]{0:T(1024)S(1)}, f32[2064]{0:T(1024)S(1)}, u32[]{:S(2)}, u32[]{:S(2)}) collective-permute-start(f32[2064]{0:T(1024)S(1)} %pad_maximum_fusion.6), channel_id=1, source_target_pairs={{0,4},{1,5},{2,6},{3,7},{4,0},{5,1},{6,2},{7,3},{8,12},{9,13},{10,... | collective-permute-start | bytes 24776 | tf_op jit(solution)/shard_map/ppermute | solution.py:44
  38.7 9.6 %collective-permute-start.12 = (f32[2,4,1,512]{3,1,0,2:T(4,128)S(1)}, f32[2,4,1,512]{3,1,0,2:T(4,128)S(1)}, u32[]{:S(2)}, u32[]{:S(2)}) collective-permute-start(f32[2,4,1,512]{3,1,0,2:T(4,128)S(1)} %get-tuple-element.10), channel_id=1, source_target_pairs={{0,1},{1,2},{2,3},{3,4},{4,5},{5,6},{6,7},{7,8},{8,9},{9,10},{10,1... | collective-permute-start | bytes 49160 | tf_op jit(solution)/shard_map/ppermute | solution.py:62
  40.0 8.3 %collective-permute-start.13 = (f32[2,4,1,512]{3,1,0,2:T(4,128)S(1)}, f32[2,4,1,512]{3,1,0,2:T(4,128)S(1)}, u32[]{:S(2)}, u32[]{:S(2)}) collective-permute-start(f32[2,4,1,512]{3,1,0,2:T(4,128)S(1)} %get-tuple-element.10), channel_id=1, source_target_pairs={{1,0},{2,1},{3,2},{4,3},{5,4},{6,5},{7,6},{8,7},{9,8},{10,9},{11,1... | collective-permute-start | bytes 49160 | tf_op jit(solution)/shard_map/ppermute | solution.py:63
  42.3 7.7 %collective-permute-start.10 = (f32[4112]{0:T(1024)S(1)}, f32[4112]{0:T(1024)S(1)}, u32[]{:S(2)}, u32[]{:S(2)}) collective-permute-start(f32[4112]{0:T(1024)S(1)} %pad_maximum_fusion.3), channel_id=1, source_target_pairs={{0,8},{1,9},{2,10},{3,11},{4,12},{5,13},{6,14},{7,15},{8,0},{9,1},... | collective-permute-start | bytes 49352 | tf_op jit(solution)/shard_map/ppermute | solution.py:44
  50.1 3.8 %collective-permute-start.11 = (f32[4112]{0:T(1024)S(1)}, f32[4112]{0:T(1024)S(1)}, u32[]{:S(2)}, u32[]{:S(2)}) collective-permute-start(f32[4112]{0:T(1024)S(1)} %pad_maximum_fusion.4), channel_id=1, source_target_pairs={{0,16},{16,0},{1,17},{17,1},{2,18},{18,2},{3,19},{19,3},{4,20},{20... | collective-permute-start | bytes 49352 | tf_op jit(solution)/shard_map/ppermute | solution.py:44
  56.4 3.7 %collective-permute-start.14 = (f32[8,4]{1,0:T(8,128)S(1)}, f32[8,4]{1,0:T(8,128)S(1)}, u32[]{:S(2)}, u32[]{:S(2)}) collective-permute-start(f32[8,4]{1,0:T(8,128)S(1)} %concatenate.155), channel_id=1, source_target_pairs={{0,16},{16,0},{1,17},{17,1},{2,18},{18,2},{3,19},{19,3},{4,20},{20... | collective-permute-start | bytes 392 | tf_op jit(solution)/shard_map/ppermute | solution.py:21
  60.1 1.2 %collective-permute-start.15 = (f32[8,4]{1,0:T(8,128)S(1)}, f32[8,4]{1,0:T(8,128)S(1)}, u32[]{:S(2)}, u32[]{:S(2)}) collective-permute-start(f32[8,4]{1,0:T(8,128)S(1)} %add.574), channel_id=1, source_target_pairs={{0,1},{1,0},{2,3},{3,2},{4,5},{5,4},{6,7},{7,6},{8,9},{9,8},{10,11... | collective-permute-start | bytes 392 | tf_op jit(solution)/shard_map/ppermute | solution.py:21
  61.2 3.6 %collective-permute-start.16 = (f32[8,4]{1,0:T(8,128)S(1)}, f32[8,4]{1,0:T(8,128)S(1)}, u32[]{:S(2)}, u32[]{:S(2)}) collective-permute-start(f32[8,4]{1,0:T(8,128)S(1)} %add.575), channel_id=1, source_target_pairs={{0,2},{1,3},{2,0},{3,1},{4,6},{5,7},{6,4},{7,5},{8,10},{9,11},{10,... | collective-permute-start | bytes 392 | tf_op jit(solution)/shard_map/ppermute | solution.py:21
  64.9 3.6 %collective-permute-start.17 = (f32[8,4]{1,0:T(8,128)S(1)}, f32[8,4]{1,0:T(8,128)S(1)}, u32[]{:S(2)}, u32[]{:S(2)}) collective-permute-start(f32[8,4]{1,0:T(8,128)S(1)} %add.576), channel_id=1, source_target_pairs={{0,4},{1,5},{2,6},{3,7},{4,0},{5,1},{6,2},{7,3},{8,12},{9,13},{10,... | collective-permute-start | bytes 392 | tf_op jit(solution)/shard_map/ppermute | solution.py:21
  68.5 4.5 %collective-permute-start.18 = (f32[8,4]{1,0:T(8,128)S(1)}, f32[8,4]{1,0:T(8,128)S(1)}, u32[]{:S(2)}, u32[]{:S(2)}) collective-permute-start(f32[8,4]{1,0:T(8,128)S(1)} %add.577), channel_id=1, source_target_pairs={{0,8},{1,9},{2,10},{3,11},{4,12},{5,13},{6,14},{7,15},{8,0},{9,1},... | collective-permute-start | bytes 392 | tf_op jit(solution)/shard_map/ppermute | solution.py:21

commit v17 on v14

--- a/solution.py
+++ b/solution.py
@@ -37,13 +37,18 @@
             buf = gat[None]
             k = 1
             while k < n:
-                packed = jnp.concatenate([red.reshape(-1), buf.reshape(-1)])
+                packed = buf.reshape(-1)
+                if red is not None:
+                    packed = jnp.concatenate([red.reshape(-1), packed])
                 if halo is not None and axis == "blk" and k == 2:
                     packed, halo = lax.optimization_barrier((packed, halo))
                     halo = neighbours(halo)
                 got = lax.ppermute(packed, axis, [(i, i ^ k) for i in range(n)])
-                red = red + got[: red.size].reshape(red.shape)
-                other = got[red.size :].reshape(buf.shape)
+                skip = 0
+                if red is not None:
+                    red = red + got[: red.size].reshape(red.shape)
+                    skip = red.size
+                other = got[skip:].reshape(buf.shape)
                 low = (idx // k) % 2 == 0
                 buf = jnp.where(low, jnp.concatenate([buf, other]), jnp.concatenate([other, buf]))
                 k *= 2
@@ -51,6 +56,11 @@
             gat_blk = buf
         else:
             gat_dom = buf
+            if red is None:
+                squares = jnp.sum(buf[:, 0] * buf[:, 0] + buf[:, 1] * buf[:, 1], axis=-1)
+                red = squares[0]
+                for d in range(1, squares.shape[0]):
+                    red = red + squares[d]
     if halo is not None:
         return red, gat_blk, gat_dom, halo
     return red, gat_blk, gat_dom
@@ -167,7 +177,7 @@
         return jnp.moveaxis(every, 0, 2)
 
     start_sum, coef_rhs, every_rhs, window_rhs = tree_collect(
-        local_squares(right_side),
+        None,
         coefficients(right_side, source_basis),
         right_side[:, :, 0],
         dom_first=True,

time: 75.6 us -> 73.7 us (0.975)
  other arithmetic: 7.44 us -> 5.84 us
    reduce_sum x1, other arithmetic: 0.98 us -> 0.09 us  [tree_collect(): squares = jnp.sum(buf[:, 0] * buf[:, 0] + buf[:, 1] * buf[:, 1], axis=-1)]
    concatenate x10 -> x9, other arithmetic: 1.47 us -> 0.68 us  [tree_collect(): packed = jnp.concatenate([red.reshape(-1), packed])]
where the time goes in v17:
time: 73.7 us; the launch traced here: 73.2 us
  starting transfers between devices  32.6 us (44%)
  waiting for transfers between devices  17.6 us (24%)
  local copies, waits for them, and re-layouts  9.15 us (12%)
  matrix products  6.87 us (9%)
  other arithmetic  5.84 us (8%)
  between operations  1.23 us (2%)
    ppermute x10, starting transfers between devices, tree_collect(): got = lax.ppermute(packed, axis, [(i, i ^ k) for i in range(n)])  20.3 us
    ppermute x10, waiting for transfers between devices, tree_collect(): got = lax.ppermute(packed, axis, [(i, i ^ k) for i in range(n)])  9.01 us
    ppermute x5, waiting for transfers between devices, tree_sum(): x = x + lax.ppermute(x, axis, [(i, i ^ k) for i in range(n)])  8.53 us
    ppermute x5, starting transfers between devices, tree_sum(): x = x + lax.ppermute(x, axis, [(i, i ^ k) for i in range(n)])  7.14 us
    dot_general x2, matrix products, far_inner(): jnp.einsum('sakl,spql->apqk', weights, gathered, precision=lax.Precision....  3.98 us
    ppermute x2, starting transfers between devices, neighbours(): right = lax.ppermute(field, 'blk', [(i + 1, i) for i in range(ends)])  2.58 us
    ppermute x2, starting transfers between devices, neighbours(): left = lax.ppermute(field, 'blk', [(i, i + 1) for i in range(ends)])  2.56 us
    unnamed x12, local copies, waits for them, and re-layouts  2.01 us
  transfers between devices with their start and end apart: 19, of which 12 were waited for; matrix products, arithmetic and copies ran while one was open for 16% of the time, Pallas kernels for 0%

profile of v17, /device:TPU:0, one launch (start us, length us, event | category | flops | bytes accessed | tf_op | source)
XLA Modules:
  0.0 73.2 jit_solution(14503695160052756329)
XLA Ops:
  0.6 3.0 %collective-permute-start = (f32[4096]{0:T(1024)}, f32[4096]{0:T(1024)S(1)}, u32[]{:S(2)}, u32[]{:S(2)}) collective-permute-start(f32[4096]{0:T(1024)} %bitcast.359), channel_id=1, source_target_pairs={{0,16},{16,0},{1,17},{17,1},{2,18},{18,2},{3,19},{19,3},{4,20},{20... | collective-permute-start | bytes 49160 | tf_op jit(solution)/shard_map/ppermute | solution.py:46
  3.7 0.8 %convert_element_type.30 = bf16[2,4,1,512]{3,2,1,0:T(2,128)(2,1)S(1)} convert(f32[2,4,1,512]{3,2,1,0:T(1,128)} %param.8) | non-fusion elementwise | flops 4096 | bytes 24576 | tf_op jit(solution)/shard_map/convert_element_type | solution.py:82
  4.4 1.1 %convolution_bitcast_fusion.5 = f32[2,2,4,64]{3,2,1,0:T(4,128)S(1)} fusion(bf16[1,2,64,512]{3,2,1,0:T(8,128)(2,1)} %param.12, bf16[2,4,1,512]{3,2,1,0:T(2,128)(2,1)S(1)} %convert_element_type.30), kind=kOutput, calls=%fused_computation.15 | convolution fusion | flops 1048576 | bytes 143360 | tf_op jit(solution)/shard_map/akr,pqr->apqk/dot_general | solution.py:83
  5.5 0.8 %iota_compare_fusion = pred[16,64]{1,0:T(8,128)(4,1)S(1)} fusion(s32[16]{0:T(128)} %bitcast.396), kind=kLoop, calls=%fused_computation.122 | loop fusion | flops 1024 | bytes 1088 | tf_op jit(solution)/shard_map/lt | solution.py:114
  6.3 0.2 and_convert_fusion
  6.5 0.8 %reshape_squeeze.4 = s32[8,1]{0,1:T(1,128)S(1)} reshape(s32[1,2,4]{2,1,0:T(2,128)} %param.10) | data formatting | bytes 64 | tf_op jit(solution)/shard_map/reshape;squeeze | solution.py:94
  7.3 0.7 copy.255
  8.1 0.1 fusion.31
  8.3 0.7 fusion.62
  9.0 0.5 collective-permute-done.1
  9.5 0.1 reshape.1907
  9.8 1.5 %collective-permute-start.2 = (f32[1028]{0:T(1024)S(1)}, f32[1028]{0:T(1024)S(1)}, u32[]{:S(2)}, u32[]{:S(2)}) collective-permute-start(f32[1028]{0:T(1024)S(1)} %pad_maximum_fusion.6), channel_id=1, source_target_pairs={{0,2},{1,3},{2,0},{3,1},{4,6},{5,7},{6,4},{7,5},{8,10},{9,11},{10,... | collective-permute-start | bytes 12344 | tf_op jit(solution)/shard_map/ppermute | solution.py:46
  11.3 2.2 %collective-permute-done.2 = f32[1028]{0:T(1024)S(1)} collective-permute-done((f32[1028]{0:T(1024)S(1)}, f32[1028]{0:T(1024)S(1)}, u32[]{:S(2)}, u32[]{:S(2)}) %collective-permute-start.2) | collective-permute-done | bytes 4144 | tf_op jit(solution)/shard_map/ppermute | solution.py:46
  13.8 1.6 %collective-permute-start.3 = (f32[2052]{0:T(1024)S(1)}, f32[2052]{0:T(1024)S(1)}, u32[]{:S(2)}, u32[]{:S(2)}) collective-permute-start(f32[2052]{0:T(1024)S(1)} %pad_maximum_fusion.4), channel_id=1, source_target_pairs={{0,4},{1,5},{2,6},{3,7},{4,0},{5,1},{6,2},{7,3},{8,12},{9,13},{10,... | collective-permute-start | bytes 24632 | tf_op jit(solution)/shard_map/ppermute | solution.py:46
  15.4 1.3 %collective-permute-start.5 = (f32[2,4,1,512]{3,2,1,0:T(1,128)}, f32[2,4,1,512]{3,2,1,0:T(1,128)S(1)}, u32[]{:S(2)}, u32[]{:S(2)}) collective-permute-start(f32[2,4,1,512]{3,2,1,0:T(1,128)} %param.8), channel_id=1, source_target_pairs={{0,1},{1,2},{2,3},{3,4},{4,5},{5,6},{6,7},{7,8},{8,9},{9,10},{10,1... | collective-permute-start | bytes 49160 | tf_op jit(solution)/shard_map/ppermute | solution.py:72
  16.7 1.3 %collective-permute-start.6 = (f32[2,4,1,512]{3,2,1,0:T(1,128)}, f32[2,4,1,512]{3,2,1,0:T(1,128)S(1)}, u32[]{:S(2)}, u32[]{:S(2)}) collective-permute-start(f32[2,4,1,512]{3,2,1,0:T(1,128)} %param.8), channel_id=1, source_target_pairs={{1,0},{2,1},{3,2},{4,3},{5,4},{6,5},{7,6},{8,7},{9,8},{10,9},{11,1... | collective-permute-start | bytes 49160 | tf_op jit(solution)/shard_map/ppermute | solution.py:73
  18.4 6.5 %collective-permute-start.4 = (f32[4100]{0:T(1024)S(1)}, f32[4100]{0:T(1024)S(1)}, u32[]{:S(2)}, u32[]{:S(2)}) collective-permute-start(f32[4100]{0:T(1024)S(1)} %pad_maximum_fusion.1), channel_id=1, source_target_pairs={{0,8},{1,9},{2,10},{3,11},{4,12},{5,13},{6,14},{7,15},{8,0},{9,1},... | collective-permute-start | bytes 49208 | tf_op jit(solution)/shard_map/ppermute | solution.py:46
  25.0 0.6 gather_fusion.1
  25.6 0.9 %maximum_reduce_fusion = f32[2,4,1536]{2,1,0:T(4,128)S(1)} fusion(f32[2,4,1,512]{3,2,1,0:T(1,128)S(1)} %collective-permute-done.6, f32[2,4,1,512]{3,2,1,0:T(1,128)} %param.8, f32[2,4,1,512]{3,2,1,0:T(1,128)S(1)} %collective-permute-done.5), kind=kLoop, calls=%fused_computation.37 | loop fusion | flops 24576 | bytes 98304 | tf_op jit(solution)/shard_map/concatenate | solution.py:74
  26.5 0.6 gather_fusion
  27.4 2.0 %convolution_bitcast_fusion.4 = f32[2,2,4,64]{3,2,0,1:T(4,128)S(1)} fusion(f32[16,2,4,64,1]{3,0,2,1,4:T(8,128)S(1)} %fusion.19, f32[1,1,16,2,64,64]{5,4,3,2,1,0:T(8,128)} %param.14, f32[16,64,64]{2,1,0:T(8,128)S(1)} %and_convert_fusion), kind=kOutput, calls=%fused_computation.14 | convolution fusion | flops 6422528 | bytes 823296 | tf_op jit(solution)/shard_map/sakl,spql->apqk/dot_general | solution.py:119
  29.4 0.1 convolution_bitcast_fusion.1
  29.6 0.7 fusion.4
  30.4 0.1 convolution_bitcast_fusion.3
  30.6 0.2 add_reduce_fusion.7
  30.9 0.1 reshape_broadcast_in_dim.7
  31.0 1.2 %collective-permute-done.7 = f32[528]{0:T(1024)S(1)} collective-permute-done((f32[528]{0:T(1024)S(1)}, f32[528]{0:T(1024)S(1)}, u32[]{:S(2)}, u32[]{:S(2)}) %collective-permute-start.7) | collective-permute-done | bytes 2144 | tf_op jit(solution)/shard_map/ppermute | solution.py:46
  32.3 0.1 reshape.1916
  32.5 0.8 %collective-permute-start.8 = (f32[1040]{0:T(1024)S(1)}, f32[1040]{0:T(1024)S(1)}, u32[]{:S(2)}, u32[]{:S(2)}) collective-permute-start(f32[1040]{0:T(1024)S(1)} %pad_maximum_fusion.7), channel_id=1, source_target_pairs={{0,2},{1,3},{2,0},{3,1},{4,6},{5,7},{6,4},{7,5},{8,10},{9,11},{10,... | collective-permute-start | bytes 12488 | tf_op jit(solution)/shard_map/ppermute | solution.py:46
  33.4 2.8 %collective-permute-done.8 = f32[1040]{0:T(1024)S(1)} collective-permute-done((f32[1040]{0:T(1024)S(1)}, f32[1040]{0:T(1024)S(1)}, u32[]{:S(2)}, u32[]{:S(2)}) %collective-permute-start.8) | collective-permute-done | bytes 4192 | tf_op jit(solution)/shard_map/ppermute | solution.py:46
  36.6 0.5 collective-permute-start.9
  37.1 1.3 %collective-permute-start.12 = (f32[2,4,1,512]{3,1,0,2:T(4,128)S(1)}, f32[2,4,1,512]{3,1,0,2:T(4,128)S(1)}, u32[]{:S(2)}, u32[]{:S(2)}) collective-permute-start(f32[2,4,1,512]{3,1,0,2:T(4,128)S(1)} %get-tuple-element.60), channel_id=1, source_target_pairs={{0,1},{1,2},{2,3},{3,4},{4,5},{5,6},{6,7},{7,8},{8,9},{9,10},{10,1... | collective-permute-start | bytes 49160 | tf_op jit(solution)/shard_map/ppermute | solution.py:72
  38.4 1.3 %collective-permute-start.13 = (f32[2,4,1,512]{3,1,0,2:T(4,128)S(1)}, f32[2,4,1,512]{3,1,0,2:T(4,128)S(1)}, u32[]{:S(2)}, u32[]{:S(2)}) collective-permute-start(f32[2,4,1,512]{3,1,0,2:T(4,128)S(1)} %get-tuple-element.60), channel_id=1, source_target_pairs={{1,0},{2,1},{3,2},{4,3},{5,4},{6,5},{7,6},{8,7},{9,8},{10,9},{11,1... | collective-permute-start | bytes 49160 | tf_op jit(solution)/shard_map/ppermute | solution.py:73
  39.8 0.4 collective-permute-done.9
  40.6 5.9 %collective-permute-start.10 = (f32[4112]{0:T(1024)S(1)}, f32[4112]{0:T(1024)S(1)}, u32[]{:S(2)}, u32[]{:S(2)}) collective-permute-start(f32[4112]{0:T(1024)S(1)} %pad_maximum_fusion.2), channel_id=1, source_target_pairs={{0,8},{1,9},{2,10},{3,11},{4,12},{5,13},{6,14},{7,15},{8,0},{9,1},... | collective-permute-start | bytes 49352 | tf_op jit(solution)/shard_map/ppermute | solution.py:46
  46.7 0.6 gather_fusion.2
  47.3 1.0 %collective-permute-done.10 = f32[4112]{0:T(1024)S(1)} collective-permute-done((f32[4112]{0:T(1024)S(1)}, f32[4112]{0:T(1024)S(1)}, u32[]{:S(2)}, u32[]{:S(2)}) %collective-permute-start.10) | collective-permute-done | bytes 16480 | tf_op jit(solution)/shard_map/ppermute | solution.py:46
  48.4 0.5 collective-permute-start.11
  49.2 2.0 %convolution_bitcast_fusion.2 = f32[2,4,2,64]{3,1,2,0:T(4,128)S(1)} fusion(f32[16,2,4,64,1]{3,0,2,1,4:T(8,128)S(1)} %fusion.21, f32[1,1,16,2,64,64]{5,4,3,2,1,0:T(8,128)} %param.14, f32[16,64,64]{2,1,0:T(8,128)S(1)} %and_convert_fusion), kind=kOutput, calls=%fused_computation.12 | convolution fusion | flops 6422528 | bytes 823296 | tf_op jit(solution)/shard_map/sakl,spql->apqk/dot_general | solution.py:119
  51.2 1.0 %collective-permute-done.11 = f32[4112]{0:T(1024)S(1)} collective-permute-done((f32[4112]{0:T(1024)S(1)}, f32[4112]{0:T(1024)S(1)}, u32[]{:S(2)}, u32[]{:S(2)}) %collective-permute-start.11) | collective-permute-done | bytes 16480 | tf_op jit(solution)/shard_map/ppermute | solution.py:46
  52.2 0.1 reshape.1922
  52.8 0.6 gather_fusion.3
  53.4 0.2 convolution_bitcast_fusion
  53.6 0.1 multiply_subtract_fusion
  53.7 0.7 fusion.7
  54.5 0.2 subtract_reduce_fusion
  54.8 0.6 collective-permute-start.14
  55.4 3.1 %collective-permute-done.14 = f32[8,4]{1,0:T(8,128)S(1)} collective-permute-done((f32[8,4]{1,0:T(8,128)S(1)}, f32[8,4]{1,0:T(8,128)S(1)}, u32[]{:S(2)}, u32[]{:S(2)}) %collective-permute-start.14) | collective-permute-done | bytes 160 | tf_op jit(solution)/shard_map/ppermute | solution.py:21
  58.4 1.2 %collective-permute-done.15 = f32[8,4]{1,0:T(8,128)S(1)} collective-permute-done((f32[8,4]{1,0:T(8,128)S(1)}, f32[8,4]{1,0:T(8,128)S(1)}, u32[]{:S(2)}, u32[]{:S(2)}) %collective-permute-start.15) | collective-permute-done | bytes 160 | tf_op jit(solution)/shard_map/ppermute | solution.py:21
  59.6 1.6 %collective-permute-start.16 = (f32[8,4]{1,0:T(8,128)S(1)}, f32[8,4]{1,0:T(8,128)S(1)}, u32[]{:S(2)}, u32[]{:S(2)}) collective-permute-start(f32[8,4]{1,0:T(8,128)S(1)} %add.571), channel_id=1, source_target_pairs={{0,2},{1,3},{2,0},{3,1},{4,6},{5,7},{6,4},{7,5},{8,10},{9,11},{10,... | collective-permute-start | bytes 392 | tf_op jit(solution)/shard_map/ppermute | solution.py:21
  61.2 0.1 copy.179
  61.3 0.6 copy.185
  61.9 1.3 %collective-permute-done.16 = f32[8,4]{1,0:T(8,128)S(1)} collective-permute-done((f32[8,4]{1,0:T(8,128)S(1)}, f32[8,4]{1,0:T(8,128)S(1)}, u32[]{:S(2)}, u32[]{:S(2)}) %collective-permute-start.16) | collective-permute-done | bytes 160 | tf_op jit(solution)/shard_map/ppermute | solution.py:21
  63.2 2.0 %collective-permute-start.17 = (f32[8,4]{1,0:T(8,128)S(1)}, f32[8,4]{1,0:T(8,128)S(1)}, u32[]{:S(2)}, u32[]{:S(2)}) collective-permute-start(f32[8,4]{1,0:T(8,128)S(1)} %add.572), channel_id=1, source_target_pairs={{0,4},{1,5},{2,6},{3,7},{4,0},{5,1},{6,2},{7,3},{8,12},{9,13},{10,... | collective-permute-start | bytes 392 | tf_op jit(solution)/shard_map/ppermute | solution.py:21
  65.3 0.1 copy.180
  65.3 1.5 %collective-permute-done.17 = f32[8,4]{1,0:T(8,128)S(1)} collective-permute-done((f32[8,4]{1,0:T(8,128)S(1)}, f32[8,4]{1,0:T(8,128)S(1)}, u32[]{:S(2)}, u32[]{:S(2)}) %collective-permute-start.17) | collective-permute-done | bytes 160 | tf_op jit(solution)/shard_map/ppermute | solution.py:21
  66.8 2.9 %collective-permute-start.18 = (f32[8,4]{1,0:T(8,128)S(1)}, f32[8,4]{1,0:T(8,128)S(1)}, u32[]{:S(2)}, u32[]{:S(2)}) collective-permute-start(f32[8,4]{1,0:T(8,128)S(1)} %add.573), channel_id=1, source_target_pairs={{0,8},{1,9},{2,10},{3,11},{4,12},{5,13},{6,14},{7,15},{8,0},{9,1},... | collective-permute-start | bytes 392 | tf_op jit(solution)/shard_map/ppermute | solution.py:21
  69.7 0.1 copy.181
  69.8 1.5 %collective-permute-done.18 = f32[8,4]{1,0:T(8,128)S(1)} collective-permute-done((f32[8,4]{1,0:T(8,128)S(1)}, f32[8,4]{1,0:T(8,128)S(1)}, u32[]{:S(2)}, u32[]{:S(2)}) %collective-permute-start.18) | collective-permute-done | bytes 160 | tf_op jit(solution)/shard_map/ppermute | solution.py:21
  71.4 0.1 copy.182
  71.5 0.1 copy.184
  71.6 0.1 copy.183
  71.9 0.6 copy.186
  72.6 0.7 concatenate.152
  (145 shorter events, 4.5 us)
Async XLA Ops:
  0.6 29.0 %copy-start = (bf16[1,2,4,2,256,256]{5,4,3,2,1,0:T(8,128)(2,1)S(1)}, bf16[1,2,4,2,256,256]{5,4,3,2,1,0:T(8,128)(2,1)}, u32[]{:S(2)}) copy-start(bf16[1,2,4,2,256,256]{5,4,3,2,1,0:T(8,128)(2,1)} %param.9) | copy-start | bytes 6291460
  0.6 7.4 %collective-permute-start = (f32[4096]{0:T(1024)}, f32[4096]{0:T(1024)S(1)}, u32[]{:S(2)}, u32[]{:S(2)}) collective-permute-start(f32[4096]{0:T(1024)} %bitcast.359), channel_id=1, source_target_pairs={{0,16},{16,0},{1,17},{17,1},{2,18},{18,2},{3,19},{19,3},{4,20},{20... | collective-permute-start | bytes 49160 | tf_op jit(solution)/shard_map/ppermute | solution.py:46
  5.5 23.9 %copy-start.2 = (bf16[1,2,64,512]{3,2,1,0:T(8,128)(2,1)S(1)}, bf16[1,2,64,512]{3,2,1,0:T(8,128)(2,1)}, u32[]{:S(2)}) copy-start(bf16[1,2,64,512]{3,2,1,0:T(8,128)(2,1)} %param.13) | copy-start | bytes 393220
  8.3 1.2 %collective-permute-start.1 = (f32[516]{0:T(1024)S(1)}, f32[516]{0:T(1024)S(1)}, u32[]{:S(2)}, u32[]{:S(2)}) collective-permute-start(f32[516]{0:T(1024)S(1)} %pad_maximum_fusion.9), channel_id=1, source_target_pairs={{0,1},{1,0},{2,3},{3,2},{4,5},{5,4},{6,7},{7,6},{8,9},{9,8},{10,11... | collective-permute-start | bytes 6200 | tf_op jit(solution)/shard_map/ppermute | solution.py:46
  9.8 3.7 %collective-permute-start.2 = (f32[1028]{0:T(1024)S(1)}, f32[1028]{0:T(1024)S(1)}, u32[]{:S(2)}, u32[]{:S(2)}) collective-permute-start(f32[1028]{0:T(1024)S(1)} %pad_maximum_fusion.6), channel_id=1, source_target_pairs={{0,2},{1,3},{2,0},{3,1},{4,6},{5,7},{6,4},{7,5},{8,10},{9,11},{10,... | collective-permute-start | bytes 12344 | tf_op jit(solution)/shard_map/ppermute | solution.py:46
  13.8 4.2 %collective-permute-start.3 = (f32[2052]{0:T(1024)S(1)}, f32[2052]{0:T(1024)S(1)}, u32[]{:S(2)}, u32[]{:S(2)}) collective-permute-start(f32[2052]{0:T(1024)S(1)} %pad_maximum_fusion.4), channel_id=1, source_target_pairs={{0,4},{1,5},{2,6},{3,7},{4,0},{5,1},{6,2},{7,3},{8,12},{9,13},{10,... | collective-permute-start | bytes 24632 | tf_op jit(solution)/shard_map/ppermute | solution.py:46
  15.4 10.2 %collective-permute-start.5 = (f32[2,4,1,512]{3,2,1,0:T(1,128)}, f32[2,4,1,512]{3,2,1,0:T(1,128)S(1)}, u32[]{:S(2)}, u32[]{:S(2)}) collective-permute-start(f32[2,4,1,512]{3,2,1,0:T(1,128)} %param.8), channel_id=1, source_target_pairs={{0,1},{1,2},{2,3},{3,4},{4,5},{5,6},{6,7},{7,8},{8,9},{9,10},{10,1... | collective-permute-start | bytes 49160 | tf_op jit(solution)/shard_map/ppermute | solution.py:72
  16.7 8.9 %collective-permute-start.6 = (f32[2,4,1,512]{3,2,1,0:T(1,128)}, f32[2,4,1,512]{3,2,1,0:T(1,128)S(1)}, u32[]{:S(2)}, u32[]{:S(2)}) collective-permute-start(f32[2,4,1,512]{3,2,1,0:T(1,128)} %param.8), channel_id=1, source_target_pairs={{1,0},{2,1},{3,2},{4,3},{5,4},{6,5},{7,6},{8,7},{9,8},{10,9},{11,1... | collective-permute-start | bytes 49160 | tf_op jit(solution)/shard_map/ppermute | solution.py:73
  18.4 8.7 %collective-permute-start.4 = (f32[4100]{0:T(1024)S(1)}, f32[4100]{0:T(1024)S(1)}, u32[]{:S(2)}, u32[]{:S(2)}) collective-permute-start(f32[4100]{0:T(1024)S(1)} %pad_maximum_fusion.1), channel_id=1, source_target_pairs={{0,8},{1,9},{2,10},{3,11},{4,12},{5,13},{6,14},{7,15},{8,0},{9,1},... | collective-permute-start | bytes 49208 | tf_op jit(solution)/shard_map/ppermute | solution.py:46
  27.4 2.9 %copy-start.3 = (f32[2,4,1,512]{3,2,1,0:T(1,128)S(1)}, f32[2,4,1,512]{3,2,1,0:T(1,128)}, u32[]{:S(2)}) copy-start(f32[2,4,1,512]{3,2,1,0:T(1,128)} %param.8) | copy-start | bytes 49156
  27.4 3.0 %copy-start.1 = (bf16[1,2,64,512]{3,2,1,0:T(8,128)(2,1)S(1)}, bf16[1,2,64,512]{3,2,1,0:T(8,128)(2,1)}, u32[]{:S(2)}) copy-start(bf16[1,2,64,512]{3,2,1,0:T(8,128)(2,1)} %param.12) | copy-start | bytes 393220
  31.0 1.2 %collective-permute-start.7 = (f32[528]{0:T(1024)S(1)}, f32[528]{0:T(1024)S(1)}, u32[]{:S(2)}, u32[]{:S(2)}) collective-permute-start(f32[528]{0:T(1024)S(1)} %pad_maximum_fusion.11), channel_id=1, source_target_pairs={{0,1},{1,0},{2,3},{3,2},{4,5},{5,4},{6,7},{7,6},{8,9},{9,8},{10,11... | collective-permute-start | bytes 6344 | tf_op jit(solution)/shard_map/ppermute | solution.py:46
  32.5 3.7 %collective-permute-start.8 = (f32[1040]{0:T(1024)S(1)}, f32[1040]{0:T(1024)S(1)}, u32[]{:S(2)}, u32[]{:S(2)}) collective-permute-start(f32[1040]{0:T(1024)S(1)} %pad_maximum_fusion.7), channel_id=1, source_target_pairs={{0,2},{1,3},{2,0},{3,1},{4,6},{5,7},{6,4},{7,5},{8,10},{9,11},{10,... | collective-permute-start | bytes 12488 | tf_op jit(solution)/shard_map/ppermute | solution.py:46
  36.6 3.7 %collective-permute-start.9 = (f32[2064]{0:T(1024)S(1)}, f32[2064]{0:T(1024)S(1)}, u32[]{:S(2)}, u32[]{:S(2)}) collective-permute-start(f32[2064]{0:T(1024)S(1)} %pad_maximum_fusion.5), channel_id=1, source_target_pairs={{0,4},{1,5},{2,6},{3,7},{4,0},{5,1},{6,2},{7,3},{8,12},{9,13},{10,... | collective-permute-start | bytes 24776 | tf_op jit(solution)/shard_map/ppermute | solution.py:46
  37.1 9.6 %collective-permute-start.12 = (f32[2,4,1,512]{3,1,0,2:T(4,128)S(1)}, f32[2,4,1,512]{3,1,0,2:T(4,128)S(1)}, u32[]{:S(2)}, u32[]{:S(2)}) collective-permute-start(f32[2,4,1,512]{3,1,0,2:T(4,128)S(1)} %get-tuple-element.60), channel_id=1, source_target_pairs={{0,1},{1,2},{2,3},{3,4},{4,5},{5,6},{6,7},{7,8},{8,9},{9,10},{10,1... | collective-permute-start | bytes 49160 | tf_op jit(solution)/shard_map/ppermute | solution.py:72
  38.4 8.3 %collective-permute-start.13 = (f32[2,4,1,512]{3,1,0,2:T(4,128)S(1)}, f32[2,4,1,512]{3,1,0,2:T(4,128)S(1)}, u32[]{:S(2)}, u32[]{:S(2)}) collective-permute-start(f32[2,4,1,512]{3,1,0,2:T(4,128)S(1)} %get-tuple-element.60), channel_id=1, source_target_pairs={{1,0},{2,1},{3,2},{4,3},{5,4},{6,5},{7,6},{8,7},{9,8},{10,9},{11,1... | collective-permute-start | bytes 49160 | tf_op jit(solution)/shard_map/ppermute | solution.py:73
  40.6 7.7 %collective-permute-start.10 = (f32[4112]{0:T(1024)S(1)}, f32[4112]{0:T(1024)S(1)}, u32[]{:S(2)}, u32[]{:S(2)}) collective-permute-start(f32[4112]{0:T(1024)S(1)} %pad_maximum_fusion.2), channel_id=1, source_target_pairs={{0,8},{1,9},{2,10},{3,11},{4,12},{5,13},{6,14},{7,15},{8,0},{9,1},... | collective-permute-start | bytes 49352 | tf_op jit(solution)/shard_map/ppermute | solution.py:46
  48.4 3.8 %collective-permute-start.11 = (f32[4112]{0:T(1024)S(1)}, f32[4112]{0:T(1024)S(1)}, u32[]{:S(2)}, u32[]{:S(2)}) collective-permute-start(f32[4112]{0:T(1024)S(1)} %pad_maximum_fusion.3), channel_id=1, source_target_pairs={{0,16},{16,0},{1,17},{17,1},{2,18},{18,2},{3,19},{19,3},{4,20},{20... | collective-permute-start | bytes 49352 | tf_op jit(solution)/shard_map/ppermute | solution.py:46
  54.8 3.7 %collective-permute-start.14 = (f32[8,4]{1,0:T(8,128)S(1)}, f32[8,4]{1,0:T(8,128)S(1)}, u32[]{:S(2)}, u32[]{:S(2)}) collective-permute-start(f32[8,4]{1,0:T(8,128)S(1)} %concatenate.151), channel_id=1, source_target_pairs={{0,16},{16,0},{1,17},{17,1},{2,18},{18,2},{3,19},{19,3},{4,20},{20... | collective-permute-start | bytes 392 | tf_op jit(solution)/shard_map/ppermute | solution.py:21
  58.4 1.2 %collective-permute-start.15 = (f32[8,4]{1,0:T(8,128)S(1)}, f32[8,4]{1,0:T(8,128)S(1)}, u32[]{:S(2)}, u32[]{:S(2)}) collective-permute-start(f32[8,4]{1,0:T(8,128)S(1)} %add.570), channel_id=1, source_target_pairs={{0,1},{1,0},{2,3},{3,2},{4,5},{5,4},{6,7},{7,6},{8,9},{9,8},{10,11... | collective-permute-start | bytes 392 | tf_op jit(solution)/shard_map/ppermute | solution.py:21
  59.6 3.6 %collective-permute-start.16 = (f32[8,4]{1,0:T(8,128)S(1)}, f32[8,4]{1,0:T(8,128)S(1)}, u32[]{:S(2)}, u32[]{:S(2)}) collective-permute-start(f32[8,4]{1,0:T(8,128)S(1)} %add.571), channel_id=1, source_target_pairs={{0,2},{1,3},{2,0},{3,1},{4,6},{5,7},{6,4},{7,5},{8,10},{9,11},{10,... | collective-permute-start | bytes 392 | tf_op jit(solution)/shard_map/ppermute | solution.py:21
  63.2 3.6 %collective-permute-start.17 = (f32[8,4]{1,0:T(8,128)S(1)}, f32[8,4]{1,0:T(8,128)S(1)}, u32[]{:S(2)}, u32[]{:S(2)}) collective-permute-start(f32[8,4]{1,0:T(8,128)S(1)} %add.572), channel_id=1, source_target_pairs={{0,4},{1,5},{2,6},{3,7},{4,0},{5,1},{6,2},{7,3},{8,12},{9,13},{10,... | collective-permute-start | bytes 392 | tf_op jit(solution)/shard_map/ppermute | solution.py:21
  66.8 4.5 %collective-permute-start.18 = (f32[8,4]{1,0:T(8,128)S(1)}, f32[8,4]{1,0:T(8,128)S(1)}, u32[]{:S(2)}, u32[]{:S(2)}) collective-permute-start(f32[8,4]{1,0:T(8,128)S(1)} %add.573), channel_id=1, source_target_pairs={{0,8},{1,9},{2,10},{3,11},{4,12},{5,13},{6,14},{7,15},{8,0},{9,1},... | collective-permute-start | bytes 392 | tf_op jit(solution)/shard_map/ppermute | solution.py:21

commit v18 on v17

--- a/solution.py
+++ b/solution.py
@@ -91,7 +91,7 @@
     blocks_dev = near_blocks.shape[1]
     width = near_blocks.shape[4]
     tiles = window.reshape(2, nrhs, 3 * blocks_dev, width)
-    return tiles.at[:, :, near_cols[0].reshape(-1)].get(mode="promise_in_bounds")
+    return tiles.at[:, :, near_cols[0].reshape(-1)].get(mode="promise_in_bounds", wrap_negative_indices=False)
 
 
 def near_field(chosen, near_blocks):
@@ -133,7 +133,7 @@
 def swapped(every, partner, width):
     nrhs = every.shape[1]
     tiles = every.reshape(2, nrhs, -1, width)
-    return tiles.at[:, :, partner[0]].get(mode="promise_in_bounds")
+    return tiles.at[:, :, partner[0]].get(mode="promise_in_bounds", wrap_negative_indices=False)
 
 
 def local_products(vectors, image):

time: 73.7 us -> 73.4 us (level)
  transfers between devices with their start and end apart: 19 -> 19, of which waited for: 12 -> 12; matrix products, arithmetic and copies ran while one was open for 16% -> 17% of each run, Pallas kernels for 0% -> 0%
where the time goes in v18:
time: 73.4 us; the launch traced here: 72.9 us
  starting transfers between devices  32.6 us (44%)
  waiting for transfers between devices  17.2 us (23%)
  local copies, waits for them, and re-layouts  9.15 us (12%)
  matrix products  6.87 us (9%)
  other arithmetic  5.82 us (8%)
  between operations  1.25 us (2%)
    ppermute x10, starting transfers between devices, tree_collect(): got = lax.ppermute(packed, axis, [(i, i ^ k) for i in range(n)])  20.3 us
    ppermute x10, waiting for transfers between devices, tree_collect(): got = lax.ppermute(packed, axis, [(i, i ^ k) for i in range(n)])  8.68 us
    ppermute x5, waiting for transfers between devices, tree_sum(): x = x + lax.ppermute(x, axis, [(i, i ^ k) for i in range(n)])  8.53 us
    ppermute x5, starting transfers between devices, tree_sum(): x = x + lax.ppermute(x, axis, [(i, i ^ k) for i in range(n)])  7.14 us
    dot_general x2, matrix products, far_inner(): jnp.einsum('sakl,spql->apqk', weights, gathered, precision=lax.Precision....  3.98 us
    ppermute x2, starting transfers between devices, neighbours(): right = lax.ppermute(field, 'blk', [(i + 1, i) for i in range(ends)])  2.58 us
    ppermute x2, starting transfers between devices, neighbours(): left = lax.ppermute(field, 'blk', [(i, i + 1) for i in range(ends)])  2.56 us
    unnamed x12, local copies, waits for them, and re-layouts  2.01 us
  transfers between devices with their start and end apart: 19, of which 12 were waited for; matrix products, arithmetic and copies ran while one was open for 17% of the time, Pallas kernels for 0%

profile of v18, /device:TPU:0, one launch (start us, length us, event | category | flops | bytes accessed | tf_op | source)
XLA Modules:
  0.0 72.9 jit_solution(2690278006321789994)
XLA Ops:
  0.6 3.0 %collective-permute-start = (f32[4096]{0:T(1024)}, f32[4096]{0:T(1024)S(1)}, u32[]{:S(2)}, u32[]{:S(2)}) collective-permute-start(f32[4096]{0:T(1024)} %bitcast.354), channel_id=1, source_target_pairs={{0,16},{16,0},{1,17},{17,1},{2,18},{18,2},{3,19},{19,3},{4,20},{20... | collective-permute-start | bytes 49160 | tf_op jit(solution)/shard_map/ppermute | solution.py:46
  3.7 0.8 %convert_element_type.30 = bf16[2,4,1,512]{3,2,1,0:T(2,128)(2,1)S(1)} convert(f32[2,4,1,512]{3,2,1,0:T(1,128)} %param.8) | non-fusion elementwise | flops 4096 | bytes 24576 | tf_op jit(solution)/shard_map/convert_element_type | solution.py:82
  4.4 1.1 %convolution_bitcast_fusion.5 = f32[2,2,4,64]{3,2,1,0:T(4,128)S(1)} fusion(bf16[1,2,64,512]{3,2,1,0:T(8,128)(2,1)} %param.12, bf16[2,4,1,512]{3,2,1,0:T(2,128)(2,1)S(1)} %convert_element_type.30), kind=kOutput, calls=%fused_computation.15 | convolution fusion | flops 1048576 | bytes 143360 | tf_op jit(solution)/shard_map/akr,pqr->apqk/dot_general | solution.py:83
  5.5 0.8 %iota_compare_fusion = pred[16,64]{1,0:T(8,128)(4,1)S(1)} fusion(s32[16]{0:T(128)} %bitcast.391), kind=kLoop, calls=%fused_computation.122 | loop fusion | flops 1024 | bytes 1088 | tf_op jit(solution)/shard_map/lt | solution.py:114
  6.3 0.7 copy.255
  7.2 0.1 fusion.31
  7.3 0.2 and_convert_fusion
  7.6 0.8 %reshape.1877 = s32[8]{0:T(128)S(1)} reshape(s32[1,2,4]{2,1,0:T(2,128)} %param.10) | data formatting | bytes 64 | tf_op jit(solution)/shard_map/broadcast_in_dim;reshape;squeeze | solution.py:94
  8.3 0.2 collective-permute-done.1
  8.6 0.1 reshape.1851
  8.9 1.5 %collective-permute-start.2 = (f32[1028]{0:T(1024)S(1)}, f32[1028]{0:T(1024)S(1)}, u32[]{:S(2)}, u32[]{:S(2)}) collective-permute-start(f32[1028]{0:T(1024)S(1)} %pad_maximum_fusion.6), channel_id=1, source_target_pairs={{0,2},{1,3},{2,0},{3,1},{4,6},{5,7},{6,4},{7,5},{8,10},{9,11},{10,... | collective-permute-start | bytes 12344 | tf_op jit(solution)/shard_map/ppermute | solution.py:46
  10.4 2.2 %collective-permute-done.2 = f32[1028]{0:T(1024)S(1)} collective-permute-done((f32[1028]{0:T(1024)S(1)}, f32[1028]{0:T(1024)S(1)}, u32[]{:S(2)}, u32[]{:S(2)}) %collective-permute-start.2) | collective-permute-done | bytes 4144 | tf_op jit(solution)/shard_map/ppermute | solution.py:46
  12.9 1.6 %collective-permute-start.3 = (f32[2052]{0:T(1024)S(1)}, f32[2052]{0:T(1024)S(1)}, u32[]{:S(2)}, u32[]{:S(2)}) collective-permute-start(f32[2052]{0:T(1024)S(1)} %pad_maximum_fusion.4), channel_id=1, source_target_pairs={{0,4},{1,5},{2,6},{3,7},{4,0},{5,1},{6,2},{7,3},{8,12},{9,13},{10,... | collective-permute-start | bytes 24632 | tf_op jit(solution)/shard_map/ppermute | solution.py:46
  14.4 0.7 pad_clamp_fusion
  15.1 1.3 %collective-permute-start.5 = (f32[2,4,1,512]{3,2,1,0:T(1,128)}, f32[2,4,1,512]{3,2,1,0:T(1,128)S(1)}, u32[]{:S(2)}, u32[]{:S(2)}) collective-permute-start(f32[2,4,1,512]{3,2,1,0:T(1,128)} %param.8), channel_id=1, source_target_pairs={{0,1},{1,2},{2,3},{3,4},{4,5},{5,6},{6,7},{7,8},{8,9},{9,10},{10,1... | collective-permute-start | bytes 49160 | tf_op jit(solution)/shard_map/ppermute | solution.py:72
  16.4 1.3 %collective-permute-start.6 = (f32[2,4,1,512]{3,2,1,0:T(1,128)}, f32[2,4,1,512]{3,2,1,0:T(1,128)S(1)}, u32[]{:S(2)}, u32[]{:S(2)}) collective-permute-start(f32[2,4,1,512]{3,2,1,0:T(1,128)} %param.8), channel_id=1, source_target_pairs={{1,0},{2,1},{3,2},{4,3},{5,4},{6,5},{7,6},{8,7},{9,8},{10,9},{11,1... | collective-permute-start | bytes 49160 | tf_op jit(solution)/shard_map/ppermute | solution.py:73
  18.1 6.5 %collective-permute-start.4 = (f32[4100]{0:T(1024)S(1)}, f32[4100]{0:T(1024)S(1)}, u32[]{:S(2)}, u32[]{:S(2)}) collective-permute-start(f32[4100]{0:T(1024)S(1)} %pad_maximum_fusion.1), channel_id=1, source_target_pairs={{0,8},{1,9},{2,10},{3,11},{4,12},{5,13},{6,14},{7,15},{8,0},{9,1},... | collective-permute-start | bytes 49208 | tf_op jit(solution)/shard_map/ppermute | solution.py:46
  24.7 0.6 gather_fusion.1
  25.3 0.9 %maximum_reduce_fusion = f32[2,4,1536]{2,1,0:T(4,128)S(1)} fusion(f32[2,4,1,512]{3,2,1,0:T(1,128)S(1)} %collective-permute-done.6, f32[2,4,1,512]{3,2,1,0:T(1,128)} %param.8, f32[2,4,1,512]{3,2,1,0:T(1,128)S(1)} %collective-permute-done.5), kind=kLoop, calls=%fused_computation.37 | loop fusion | flops 24576 | bytes 98304 | tf_op jit(solution)/shard_map/concatenate | solution.py:74
  26.2 0.6 gather_fusion
  27.1 2.0 %convolution_bitcast_fusion.4 = f32[2,2,4,64]{3,2,0,1:T(4,128)S(1)} fusion(f32[16,2,4,64,1]{3,0,2,1,4:T(8,128)S(1)} %fusion.19, f32[1,1,16,2,64,64]{5,4,3,2,1,0:T(8,128)} %param.14, f32[16,64,64]{2,1,0:T(8,128)S(1)} %and_convert_fusion), kind=kOutput, calls=%fused_computation.14 | convolution fusion | flops 6422528 | bytes 823296 | tf_op jit(solution)/shard_map/sakl,spql->apqk/dot_general | solution.py:119
  29.1 0.1 convolution_bitcast_fusion.1
  29.3 0.7 fusion.4
  30.1 0.1 convolution_bitcast_fusion.3
  30.2 0.2 add_reduce_fusion.7
  30.5 0.1 reshape_broadcast_in_dim.7
  30.7 1.2 %collective-permute-done.7 = f32[528]{0:T(1024)S(1)} collective-permute-done((f32[528]{0:T(1024)S(1)}, f32[528]{0:T(1024)S(1)}, u32[]{:S(2)}, u32[]{:S(2)}) %collective-permute-start.7) | collective-permute-done | bytes 2144 | tf_op jit(solution)/shard_map/ppermute | solution.py:46
  31.9 0.1 reshape.1860
  32.2 0.8 %collective-permute-start.8 = (f32[1040]{0:T(1024)S(1)}, f32[1040]{0:T(1024)S(1)}, u32[]{:S(2)}, u32[]{:S(2)}) collective-permute-start(f32[1040]{0:T(1024)S(1)} %pad_maximum_fusion.7), channel_id=1, source_target_pairs={{0,2},{1,3},{2,0},{3,1},{4,6},{5,7},{6,4},{7,5},{8,10},{9,11},{10,... | collective-permute-start | bytes 12488 | tf_op jit(solution)/shard_map/ppermute | solution.py:46
  33.1 2.8 %collective-permute-done.8 = f32[1040]{0:T(1024)S(1)} collective-permute-done((f32[1040]{0:T(1024)S(1)}, f32[1040]{0:T(1024)S(1)}, u32[]{:S(2)}, u32[]{:S(2)}) %collective-permute-start.8) | collective-permute-done | bytes 4192 | tf_op jit(solution)/shard_map/ppermute | solution.py:46
  36.2 0.5 collective-permute-start.9
  36.8 1.3 %collective-permute-start.12 = (f32[2,4,1,512]{3,1,0,2:T(4,128)S(1)}, f32[2,4,1,512]{3,1,0,2:T(4,128)S(1)}, u32[]{:S(2)}, u32[]{:S(2)}) collective-permute-start(f32[2,4,1,512]{3,1,0,2:T(4,128)S(1)} %get-tuple-element.60), channel_id=1, source_target_pairs={{0,1},{1,2},{2,3},{3,4},{4,5},{5,6},{6,7},{7,8},{8,9},{9,10},{10,1... | collective-permute-start | bytes 49160 | tf_op jit(solution)/shard_map/ppermute | solution.py:72
  38.1 1.3 %collective-permute-start.13 = (f32[2,4,1,512]{3,1,0,2:T(4,128)S(1)}, f32[2,4,1,512]{3,1,0,2:T(4,128)S(1)}, u32[]{:S(2)}, u32[]{:S(2)}) collective-permute-start(f32[2,4,1,512]{3,1,0,2:T(4,128)S(1)} %get-tuple-element.60), channel_id=1, source_target_pairs={{1,0},{2,1},{3,2},{4,3},{5,4},{6,5},{7,6},{8,7},{9,8},{10,9},{11,1... | collective-permute-start | bytes 49160 | tf_op jit(solution)/shard_map/ppermute | solution.py:73
  39.5 0.4 collective-permute-done.9
  40.3 5.9 %collective-permute-start.10 = (f32[4112]{0:T(1024)S(1)}, f32[4112]{0:T(1024)S(1)}, u32[]{:S(2)}, u32[]{:S(2)}) collective-permute-start(f32[4112]{0:T(1024)S(1)} %pad_maximum_fusion.2), channel_id=1, source_target_pairs={{0,8},{1,9},{2,10},{3,11},{4,12},{5,13},{6,14},{7,15},{8,0},{9,1},... | collective-permute-start | bytes 49352 | tf_op jit(solution)/shard_map/ppermute | solution.py:46
  46.4 0.6 gather_fusion.2
  47.0 1.0 %collective-permute-done.10 = f32[4112]{0:T(1024)S(1)} collective-permute-done((f32[4112]{0:T(1024)S(1)}, f32[4112]{0:T(1024)S(1)}, u32[]{:S(2)}, u32[]{:S(2)}) %collective-permute-start.10) | collective-permute-done | bytes 16480 | tf_op jit(solution)/shard_map/ppermute | solution.py:46
  48.1 0.5 collective-permute-start.11
  48.8 2.0 %convolution_bitcast_fusion.2 = f32[2,4,2,64]{3,1,2,0:T(4,128)S(1)} fusion(f32[16,2,4,64,1]{3,0,2,1,4:T(8,128)S(1)} %fusion.21, f32[1,1,16,2,64,64]{5,4,3,2,1,0:T(8,128)} %param.14, f32[16,64,64]{2,1,0:T(8,128)S(1)} %and_convert_fusion), kind=kOutput, calls=%fused_computation.12 | convolution fusion | flops 6422528 | bytes 823296 | tf_op jit(solution)/shard_map/sakl,spql->apqk/dot_general | solution.py:119
  50.9 1.0 %collective-permute-done.11 = f32[4112]{0:T(1024)S(1)} collective-permute-done((f32[4112]{0:T(1024)S(1)}, f32[4112]{0:T(1024)S(1)}, u32[]{:S(2)}, u32[]{:S(2)}) %collective-permute-start.11) | collective-permute-done | bytes 16480 | tf_op jit(solution)/shard_map/ppermute | solution.py:46
  51.9 0.1 reshape.1866
  52.4 0.6 gather_fusion.3
  53.1 0.2 convolution_bitcast_fusion
  53.3 0.1 multiply_subtract_fusion
  53.4 0.7 fusion.7
  54.1 0.2 subtract_reduce_fusion
  54.4 0.6 collective-permute-start.14
  55.0 3.1 %collective-permute-done.14 = f32[8,4]{1,0:T(8,128)S(1)} collective-permute-done((f32[8,4]{1,0:T(8,128)S(1)}, f32[8,4]{1,0:T(8,128)S(1)}, u32[]{:S(2)}, u32[]{:S(2)}) %collective-permute-start.14) | collective-permute-done | bytes 160 | tf_op jit(solution)/shard_map/ppermute | solution.py:21
  58.1 1.2 %collective-permute-done.15 = f32[8,4]{1,0:T(8,128)S(1)} collective-permute-done((f32[8,4]{1,0:T(8,128)S(1)}, f32[8,4]{1,0:T(8,128)S(1)}, u32[]{:S(2)}, u32[]{:S(2)}) %collective-permute-start.15) | collective-permute-done | bytes 160 | tf_op jit(solution)/shard_map/ppermute | solution.py:21
  59.3 1.6 %collective-permute-start.16 = (f32[8,4]{1,0:T(8,128)S(1)}, f32[8,4]{1,0:T(8,128)S(1)}, u32[]{:S(2)}, u32[]{:S(2)}) collective-permute-start(f32[8,4]{1,0:T(8,128)S(1)} %add.547), channel_id=1, source_target_pairs={{0,2},{1,3},{2,0},{3,1},{4,6},{5,7},{6,4},{7,5},{8,10},{9,11},{10,... | collective-permute-start | bytes 392 | tf_op jit(solution)/shard_map/ppermute | solution.py:21
  60.9 0.1 copy.179
  61.0 0.6 copy.185
  61.6 1.3 %collective-permute-done.16 = f32[8,4]{1,0:T(8,128)S(1)} collective-permute-done((f32[8,4]{1,0:T(8,128)S(1)}, f32[8,4]{1,0:T(8,128)S(1)}, u32[]{:S(2)}, u32[]{:S(2)}) %collective-permute-start.16) | collective-permute-done | bytes 160 | tf_op jit(solution)/shard_map/ppermute | solution.py:21
  62.9 2.0 %collective-permute-start.17 = (f32[8,4]{1,0:T(8,128)S(1)}, f32[8,4]{1,0:T(8,128)S(1)}, u32[]{:S(2)}, u32[]{:S(2)}) collective-permute-start(f32[8,4]{1,0:T(8,128)S(1)} %add.548), channel_id=1, source_target_pairs={{0,4},{1,5},{2,6},{3,7},{4,0},{5,1},{6,2},{7,3},{8,12},{9,13},{10,... | collective-permute-start | bytes 392 | tf_op jit(solution)/shard_map/ppermute | solution.py:21
  64.9 0.1 copy.180
  65.0 1.5 %collective-permute-done.17 = f32[8,4]{1,0:T(8,128)S(1)} collective-permute-done((f32[8,4]{1,0:T(8,128)S(1)}, f32[8,4]{1,0:T(8,128)S(1)}, u32[]{:S(2)}, u32[]{:S(2)}) %collective-permute-start.17) | collective-permute-done | bytes 160 | tf_op jit(solution)/shard_map/ppermute | solution.py:21
  66.5 2.9 %collective-permute-start.18 = (f32[8,4]{1,0:T(8,128)S(1)}, f32[8,4]{1,0:T(8,128)S(1)}, u32[]{:S(2)}, u32[]{:S(2)}) collective-permute-start(f32[8,4]{1,0:T(8,128)S(1)} %add.549), channel_id=1, source_target_pairs={{0,8},{1,9},{2,10},{3,11},{4,12},{5,13},{6,14},{7,15},{8,0},{9,1},... | collective-permute-start | bytes 392 | tf_op jit(solution)/shard_map/ppermute | solution.py:21
  69.4 0.1 copy.181
  69.5 1.5 %collective-permute-done.18 = f32[8,4]{1,0:T(8,128)S(1)} collective-permute-done((f32[8,4]{1,0:T(8,128)S(1)}, f32[8,4]{1,0:T(8,128)S(1)}, u32[]{:S(2)}, u32[]{:S(2)}) %collective-permute-start.18) | collective-permute-done | bytes 160 | tf_op jit(solution)/shard_map/ppermute | solution.py:21
  71.1 0.1 copy.182
  71.2 0.1 copy.184
  71.3 0.1 copy.183
  71.6 0.6 copy.186
  72.2 0.7 concatenate.152
  (143 shorter events, 4.5 us)
Async XLA Ops:
  0.6 28.6 %copy-start = (bf16[1,2,4,2,256,256]{5,4,3,2,1,0:T(8,128)(2,1)S(1)}, bf16[1,2,4,2,256,256]{5,4,3,2,1,0:T(8,128)(2,1)}, u32[]{:S(2)}) copy-start(bf16[1,2,4,2,256,256]{5,4,3,2,1,0:T(8,128)(2,1)} %param.9) | copy-start | bytes 6291460
  0.6 6.5 %collective-permute-start = (f32[4096]{0:T(1024)}, f32[4096]{0:T(1024)S(1)}, u32[]{:S(2)}, u32[]{:S(2)}) collective-permute-start(f32[4096]{0:T(1024)} %bitcast.354), channel_id=1, source_target_pairs={{0,16},{16,0},{1,17},{17,1},{2,18},{18,2},{3,19},{19,3},{4,20},{20... | collective-permute-start | bytes 49160 | tf_op jit(solution)/shard_map/ppermute | solution.py:46
  5.5 23.6 %copy-start.2 = (bf16[1,2,64,512]{3,2,1,0:T(8,128)(2,1)S(1)}, bf16[1,2,64,512]{3,2,1,0:T(8,128)(2,1)}, u32[]{:S(2)}) copy-start(bf16[1,2,64,512]{3,2,1,0:T(8,128)(2,1)} %param.13) | copy-start | bytes 393220
  7.3 1.2 %collective-permute-start.1 = (f32[516]{0:T(1024)S(1)}, f32[516]{0:T(1024)S(1)}, u32[]{:S(2)}, u32[]{:S(2)}) collective-permute-start(f32[516]{0:T(1024)S(1)} %pad_maximum_fusion.9), channel_id=1, source_target_pairs={{0,1},{1,0},{2,3},{3,2},{4,5},{5,4},{6,7},{7,6},{8,9},{9,8},{10,11... | collective-permute-start | bytes 6200 | tf_op jit(solution)/shard_map/ppermute | solution.py:46
  8.9 3.7 %collective-permute-start.2 = (f32[1028]{0:T(1024)S(1)}, f32[1028]{0:T(1024)S(1)}, u32[]{:S(2)}, u32[]{:S(2)}) collective-permute-start(f32[1028]{0:T(1024)S(1)} %pad_maximum_fusion.6), channel_id=1, source_target_pairs={{0,2},{1,3},{2,0},{3,1},{4,6},{5,7},{6,4},{7,5},{8,10},{9,11},{10,... | collective-permute-start | bytes 12344 | tf_op jit(solution)/shard_map/ppermute | solution.py:46
  12.9 4.8 %collective-permute-start.3 = (f32[2052]{0:T(1024)S(1)}, f32[2052]{0:T(1024)S(1)}, u32[]{:S(2)}, u32[]{:S(2)}) collective-permute-start(f32[2052]{0:T(1024)S(1)} %pad_maximum_fusion.4), channel_id=1, source_target_pairs={{0,4},{1,5},{2,6},{3,7},{4,0},{5,1},{6,2},{7,3},{8,12},{9,13},{10,... | collective-permute-start | bytes 24632 | tf_op jit(solution)/shard_map/ppermute | solution.py:46
  15.1 10.2 %collective-permute-start.5 = (f32[2,4,1,512]{3,2,1,0:T(1,128)}, f32[2,4,1,512]{3,2,1,0:T(1,128)S(1)}, u32[]{:S(2)}, u32[]{:S(2)}) collective-permute-start(f32[2,4,1,512]{3,2,1,0:T(1,128)} %param.8), channel_id=1, source_target_pairs={{0,1},{1,2},{2,3},{3,4},{4,5},{5,6},{6,7},{7,8},{8,9},{9,10},{10,1... | collective-permute-start | bytes 49160 | tf_op jit(solution)/shard_map/ppermute | solution.py:72
  16.4 8.9 %collective-permute-start.6 = (f32[2,4,1,512]{3,2,1,0:T(1,128)}, f32[2,4,1,512]{3,2,1,0:T(1,128)S(1)}, u32[]{:S(2)}, u32[]{:S(2)}) collective-permute-start(f32[2,4,1,512]{3,2,1,0:T(1,128)} %param.8), channel_id=1, source_target_pairs={{1,0},{2,1},{3,2},{4,3},{5,4},{6,5},{7,6},{8,7},{9,8},{10,9},{11,1... | collective-permute-start | bytes 49160 | tf_op jit(solution)/shard_map/ppermute | solution.py:73
  18.1 8.7 %collective-permute-start.4 = (f32[4100]{0:T(1024)S(1)}, f32[4100]{0:T(1024)S(1)}, u32[]{:S(2)}, u32[]{:S(2)}) collective-permute-start(f32[4100]{0:T(1024)S(1)} %pad_maximum_fusion.1), channel_id=1, source_target_pairs={{0,8},{1,9},{2,10},{3,11},{4,12},{5,13},{6,14},{7,15},{8,0},{9,1},... | collective-permute-start | bytes 49208 | tf_op jit(solution)/shard_map/ppermute | solution.py:46
  27.1 2.9 %copy-start.3 = (f32[2,4,1,512]{3,2,1,0:T(1,128)S(1)}, f32[2,4,1,512]{3,2,1,0:T(1,128)}, u32[]{:S(2)}) copy-start(f32[2,4,1,512]{3,2,1,0:T(1,128)} %param.8) | copy-start | bytes 49156
  27.1 3.0 %copy-start.1 = (bf16[1,2,64,512]{3,2,1,0:T(8,128)(2,1)S(1)}, bf16[1,2,64,512]{3,2,1,0:T(8,128)(2,1)}, u32[]{:S(2)}) copy-start(bf16[1,2,64,512]{3,2,1,0:T(8,128)(2,1)} %param.12) | copy-start | bytes 393220
  30.7 1.2 %collective-permute-start.7 = (f32[528]{0:T(1024)S(1)}, f32[528]{0:T(1024)S(1)}, u32[]{:S(2)}, u32[]{:S(2)}) collective-permute-start(f32[528]{0:T(1024)S(1)} %pad_maximum_fusion.11), channel_id=1, source_target_pairs={{0,1},{1,0},{2,3},{3,2},{4,5},{5,4},{6,7},{7,6},{8,9},{9,8},{10,11... | collective-permute-start | bytes 6344 | tf_op jit(solution)/shard_map/ppermute | solution.py:46
  32.2 3.7 %collective-permute-start.8 = (f32[1040]{0:T(1024)S(1)}, f32[1040]{0:T(1024)S(1)}, u32[]{:S(2)}, u32[]{:S(2)}) collective-permute-start(f32[1040]{0:T(1024)S(1)} %pad_maximum_fusion.7), channel_id=1, source_target_pairs={{0,2},{1,3},{2,0},{3,1},{4,6},{5,7},{6,4},{7,5},{8,10},{9,11},{10,... | collective-permute-start | bytes 12488 | tf_op jit(solution)/shard_map/ppermute | solution.py:46
  36.2 3.7 %collective-permute-start.9 = (f32[2064]{0:T(1024)S(1)}, f32[2064]{0:T(1024)S(1)}, u32[]{:S(2)}, u32[]{:S(2)}) collective-permute-start(f32[2064]{0:T(1024)S(1)} %pad_maximum_fusion.5), channel_id=1, source_target_pairs={{0,4},{1,5},{2,6},{3,7},{4,0},{5,1},{6,2},{7,3},{8,12},{9,13},{10,... | collective-permute-start | bytes 24776 | tf_op jit(solution)/shard_map/ppermute | solution.py:46
  36.8 9.6 %collective-permute-start.12 = (f32[2,4,1,512]{3,1,0,2:T(4,128)S(1)}, f32[2,4,1,512]{3,1,0,2:T(4,128)S(1)}, u32[]{:S(2)}, u32[]{:S(2)}) collective-permute-start(f32[2,4,1,512]{3,1,0,2:T(4,128)S(1)} %get-tuple-element.60), channel_id=1, source_target_pairs={{0,1},{1,2},{2,3},{3,4},{4,5},{5,6},{6,7},{7,8},{8,9},{9,10},{10,1... | collective-permute-start | bytes 49160 | tf_op jit(solution)/shard_map/ppermute | solution.py:72
  38.1 8.3 %collective-permute-start.13 = (f32[2,4,1,512]{3,1,0,2:T(4,128)S(1)}, f32[2,4,1,512]{3,1,0,2:T(4,128)S(1)}, u32[]{:S(2)}, u32[]{:S(2)}) collective-permute-start(f32[2,4,1,512]{3,1,0,2:T(4,128)S(1)} %get-tuple-element.60), channel_id=1, source_target_pairs={{1,0},{2,1},{3,2},{4,3},{5,4},{6,5},{7,6},{8,7},{9,8},{10,9},{11,1... | collective-permute-start | bytes 49160 | tf_op jit(solution)/shard_map/ppermute | solution.py:73
  40.3 7.7 %collective-permute-start.10 = (f32[4112]{0:T(1024)S(1)}, f32[4112]{0:T(1024)S(1)}, u32[]{:S(2)}, u32[]{:S(2)}) collective-permute-start(f32[4112]{0:T(1024)S(1)} %pad_maximum_fusion.2), channel_id=1, source_target_pairs={{0,8},{1,9},{2,10},{3,11},{4,12},{5,13},{6,14},{7,15},{8,0},{9,1},... | collective-permute-start | bytes 49352 | tf_op jit(solution)/shard_map/ppermute | solution.py:46
  48.1 3.8 %collective-permute-start.11 = (f32[4112]{0:T(1024)S(1)}, f32[4112]{0:T(1024)S(1)}, u32[]{:S(2)}, u32[]{:S(2)}) collective-permute-start(f32[4112]{0:T(1024)S(1)} %pad_maximum_fusion.3), channel_id=1, source_target_pairs={{0,16},{16,0},{1,17},{17,1},{2,18},{18,2},{3,19},{19,3},{4,20},{20... | collective-permute-start | bytes 49352 | tf_op jit(solution)/shard_map/ppermute | solution.py:46
  54.4 3.7 %collective-permute-start.14 = (f32[8,4]{1,0:T(8,128)S(1)}, f32[8,4]{1,0:T(8,128)S(1)}, u32[]{:S(2)}, u32[]{:S(2)}) collective-permute-start(f32[8,4]{1,0:T(8,128)S(1)} %concatenate.151), channel_id=1, source_target_pairs={{0,16},{16,0},{1,17},{17,1},{2,18},{18,2},{3,19},{19,3},{4,20},{20... | collective-permute-start | bytes 392 | tf_op jit(solution)/shard_map/ppermute | solution.py:21
  58.1 1.2 %collective-permute-start.15 = (f32[8,4]{1,0:T(8,128)S(1)}, f32[8,4]{1,0:T(8,128)S(1)}, u32[]{:S(2)}, u32[]{:S(2)}) collective-permute-start(f32[8,4]{1,0:T(8,128)S(1)} %add.546), channel_id=1, source_target_pairs={{0,1},{1,0},{2,3},{3,2},{4,5},{5,4},{6,7},{7,6},{8,9},{9,8},{10,11... | collective-permute-start | bytes 392 | tf_op jit(solution)/shard_map/ppermute | solution.py:21
  59.3 3.6 %collective-permute-start.16 = (f32[8,4]{1,0:T(8,128)S(1)}, f32[8,4]{1,0:T(8,128)S(1)}, u32[]{:S(2)}, u32[]{:S(2)}) collective-permute-start(f32[8,4]{1,0:T(8,128)S(1)} %add.547), channel_id=1, source_target_pairs={{0,2},{1,3},{2,0},{3,1},{4,6},{5,7},{6,4},{7,5},{8,10},{9,11},{10,... | collective-permute-start | bytes 392 | tf_op jit(solution)/shard_map/ppermute | solution.py:21
  62.9 3.6 %collective-permute-start.17 = (f32[8,4]{1,0:T(8,128)S(1)}, f32[8,4]{1,0:T(8,128)S(1)}, u32[]{:S(2)}, u32[]{:S(2)}) collective-permute-start(f32[8,4]{1,0:T(8,128)S(1)} %add.548), channel_id=1, source_target_pairs={{0,4},{1,5},{2,6},{3,7},{4,0},{5,1},{6,2},{7,3},{8,12},{9,13},{10,... | collective-permute-start | bytes 392 | tf_op jit(solution)/shard_map/ppermute | solution.py:21
  66.5 4.5 %collective-permute-start.18 = (f32[8,4]{1,0:T(8,128)S(1)}, f32[8,4]{1,0:T(8,128)S(1)}, u32[]{:S(2)}, u32[]{:S(2)}) collective-permute-start(f32[8,4]{1,0:T(8,128)S(1)} %add.549), channel_id=1, source_target_pairs={{0,8},{1,9},{2,10},{3,11},{4,12},{5,13},{6,14},{7,15},{8,0},{9,1},... | collective-permute-start | bytes 392 | tf_op jit(solution)/shard_map/ppermute | solution.py:21

commit v19 on v18

--- a/solution.py
+++ b/solution.py
@@ -20,6 +20,30 @@
         while k < n:
             x = x + lax.ppermute(x, axis, [(i, i ^ k) for i in range(n)])
             k *= 2
+    return x
+
+
+def radix_sum(x, axis):
+    n = lax.axis_size(axis)
+    if not _pow2(n):
+        return lax.psum(x, axis)
+    idx = lax.axis_index(axis)
+    k = 1
+    while k < n:
+        if 4 * k > n:
+            x = x + lax.ppermute(x, axis, [(i, i ^ k) for i in range(n)])
+            k *= 2
+            continue
+        got = [x] + [lax.ppermute(x, axis, [(i, i ^ (j * k)) for i in range(n)]) for j in (1, 2, 3)]
+        digit = (idx // k) % 4
+        total = None
+        for m in range(4):
+            member = got[0]
+            for j in range(1, 4):
+                member = jnp.where((digit ^ j) == m, got[j], member)
+            total = member if total is None else total + member
+        x = total
+        k *= 4
     return x
 
 
@@ -232,7 +256,7 @@
     )
 
     two = (
-        tree_sum(
+        radix_sum(tree_sum(
             jnp.concatenate(
                 [
                     local_products([first_vec, second_basis], image_two).reshape(4, -1),
@@ -241,8 +265,8 @@
                     local_squares(second_basis)[None],
                 ]
             ),
-            everyone,
-        )
+            ("dom",),
+        ), "blk")
         / total
     )
     h_one_two = two[0:2]

time: 73.4 us -> 73.5 us (level)
    ppermute x0 -> x6, starting transfers between devices: none -> 6.61 us  [radix_sum(): lax.ppermute(x, axis, [(i, i ^ j * k) for i in range(n)])]
    ppermute x5 -> x1, starting transfers between devices: 7.14 us -> 0.61 us  [tree_sum(): x = x + lax.ppermute(x, axis, [(i, i ^ k) for i in range(n)])]
    ppermute x5 -> x1, waiting for transfers between devices: 8.53 us -> 2.88 us  [tree_sum(): x = x + lax.ppermute(x, axis, [(i, i ^ k) for i in range(n)])]
    ppermute x0 -> x6, waiting for transfers between devices: none -> 5.65 us  [radix_sum(): lax.ppermute(x, axis, [(i, i ^ j * k) for i in range(n)])]
  transfers between devices with their start and end apart: 19 -> 21, of which waited for: 12 -> 12; matrix products, arithmetic and copies ran while one was open for 17% -> 16% of each run, Pallas kernels for 0% -> 0%
where the time goes in v19:
time: 73.5 us; the launch traced here: 73 us
  starting transfers between devices  32.8 us (45%)
  waiting for transfers between devices  17 us (23%)
  local copies, waits for them, and re-layouts  9.15 us (12%)
  matrix products  6.87 us (9%)
  other arithmetic  5.83 us (8%)
  between operations  1.34 us (2%)
    ppermute x10, starting transfers between devices, tree_collect(): got = lax.ppermute(packed, axis, [(i, i ^ k) for i in range(n)])  20.4 us
    ppermute x10, waiting for transfers between devices, tree_collect(): got = lax.ppermute(packed, axis, [(i, i ^ k) for i in range(n)])  8.51 us
    ppermute x6, starting transfers between devices, radix_sum(): lax.ppermute(x, axis, [(i, i ^ j * k) for i in range(n)])  6.61 us
    ppermute x6, waiting for transfers between devices, radix_sum(): lax.ppermute(x, axis, [(i, i ^ j * k) for i in range(n)])  5.65 us
    dot_general x2, matrix products, far_inner(): jnp.einsum('sakl,spql->apqk', weights, gathered, precision=lax.Precision....  3.98 us
    ppermute x1, waiting for transfers between devices, tree_sum(): x = x + lax.ppermute(x, axis, [(i, i ^ k) for i in range(n)])  2.88 us
    ppermute x2, starting transfers between devices, neighbours(): right = lax.ppermute(field, 'blk', [(i + 1, i) for i in range(ends)])  2.58 us
    ppermute x2, starting transfers between devices, neighbours(): left = lax.ppermute(field, 'blk', [(i, i + 1) for i in range(ends)])  2.56 us
  transfers between devices with their start and end apart: 21, of which 12 were waited for; matrix products, arithmetic and copies ran while one was open for 16% of the time, Pallas kernels for 0%

profile of v19, /device:TPU:0, one launch (start us, length us, event | category | flops | bytes accessed | tf_op | source)
XLA Modules:
  0.0 73.0 jit_solution(11839309420164736311)
XLA Ops:
  0.6 3.0 %collective-permute-start = (f32[4096]{0:T(1024)}, f32[4096]{0:T(1024)S(1)}, u32[]{:S(2)}, u32[]{:S(2)}) collective-permute-start(f32[4096]{0:T(1024)} %bitcast.354), channel_id=1, source_target_pairs={{0,16},{16,0},{1,17},{17,1},{2,18},{18,2},{3,19},{19,3},{4,20},{20... | collective-permute-start | bytes 49160 | tf_op jit(solution)/shard_map/ppermute | solution.py:70
  3.7 0.8 %convert_element_type.30 = bf16[2,4,1,512]{3,2,1,0:T(2,128)(2,1)S(1)} convert(f32[2,4,1,512]{3,2,1,0:T(1,128)} %param.8) | non-fusion elementwise | flops 4096 | bytes 24576 | tf_op jit(solution)/shard_map/convert_element_type | solution.py:106
  4.4 1.1 %convolution_bitcast_fusion.5 = f32[2,2,4,64]{3,2,1,0:T(4,128)S(1)} fusion(bf16[1,2,64,512]{3,2,1,0:T(8,128)(2,1)} %param.12, bf16[2,4,1,512]{3,2,1,0:T(2,128)(2,1)S(1)} %convert_element_type.30), kind=kOutput, calls=%fused_computation.15 | convolution fusion | flops 1048576 | bytes 143360 | tf_op jit(solution)/shard_map/akr,pqr->apqk/dot_general | solution.py:107
  5.5 0.8 %iota_compare_fusion = pred[16,64]{1,0:T(8,128)(4,1)S(1)} fusion(s32[16]{0:T(128)} %bitcast.391), kind=kLoop, calls=%fused_computation.122 | loop fusion | flops 1024 | bytes 1088 | tf_op jit(solution)/shard_map/lt | solution.py:138
  6.3 0.7 copy.255
  7.2 0.1 fusion.31
  7.3 0.2 and_convert_fusion
  7.6 0.8 %reshape.1877 = s32[8]{0:T(128)S(1)} reshape(s32[1,2,4]{2,1,0:T(2,128)} %param.10) | data formatting | bytes 64 | tf_op jit(solution)/shard_map/broadcast_in_dim;reshape;squeeze | solution.py:118
  8.3 0.2 collective-permute-done.1
  8.6 0.1 reshape.1851
  8.9 1.5 %collective-permute-start.2 = (f32[1028]{0:T(1024)S(1)}, f32[1028]{0:T(1024)S(1)}, u32[]{:S(2)}, u32[]{:S(2)}) collective-permute-start(f32[1028]{0:T(1024)S(1)} %pad_maximum_fusion.6), channel_id=1, source_target_pairs={{0,2},{1,3},{2,0},{3,1},{4,6},{5,7},{6,4},{7,5},{8,10},{9,11},{10,... | collective-permute-start | bytes 12344 | tf_op jit(solution)/shard_map/ppermute | solution.py:70
  10.4 2.2 %collective-permute-done.2 = f32[1028]{0:T(1024)S(1)} collective-permute-done((f32[1028]{0:T(1024)S(1)}, f32[1028]{0:T(1024)S(1)}, u32[]{:S(2)}, u32[]{:S(2)}) %collective-permute-start.2) | collective-permute-done | bytes 4144 | tf_op jit(solution)/shard_map/ppermute | solution.py:70
  12.9 1.6 %collective-permute-start.3 = (f32[2052]{0:T(1024)S(1)}, f32[2052]{0:T(1024)S(1)}, u32[]{:S(2)}, u32[]{:S(2)}) collective-permute-start(f32[2052]{0:T(1024)S(1)} %pad_maximum_fusion.4), channel_id=1, source_target_pairs={{0,4},{1,5},{2,6},{3,7},{4,0},{5,1},{6,2},{7,3},{8,12},{9,13},{10,... | collective-permute-start | bytes 24632 | tf_op jit(solution)/shard_map/ppermute | solution.py:70
  14.4 0.7 pad_clamp_fusion
  15.1 1.3 %collective-permute-start.5 = (f32[2,4,1,512]{3,2,1,0:T(1,128)}, f32[2,4,1,512]{3,2,1,0:T(1,128)S(1)}, u32[]{:S(2)}, u32[]{:S(2)}) collective-permute-start(f32[2,4,1,512]{3,2,1,0:T(1,128)} %param.8), channel_id=1, source_target_pairs={{0,1},{1,2},{2,3},{3,4},{4,5},{5,6},{6,7},{7,8},{8,9},{9,10},{10,1... | collective-permute-start | bytes 49160 | tf_op jit(solution)/shard_map/ppermute | solution.py:96
  16.4 1.3 %collective-permute-start.6 = (f32[2,4,1,512]{3,2,1,0:T(1,128)}, f32[2,4,1,512]{3,2,1,0:T(1,128)S(1)}, u32[]{:S(2)}, u32[]{:S(2)}) collective-permute-start(f32[2,4,1,512]{3,2,1,0:T(1,128)} %param.8), channel_id=1, source_target_pairs={{1,0},{2,1},{3,2},{4,3},{5,4},{6,5},{7,6},{8,7},{9,8},{10,9},{11,1... | collective-permute-start | bytes 49160 | tf_op jit(solution)/shard_map/ppermute | solution.py:97
  18.1 6.5 %collective-permute-start.4 = (f32[4100]{0:T(1024)S(1)}, f32[4100]{0:T(1024)S(1)}, u32[]{:S(2)}, u32[]{:S(2)}) collective-permute-start(f32[4100]{0:T(1024)S(1)} %pad_maximum_fusion.1), channel_id=1, source_target_pairs={{0,8},{1,9},{2,10},{3,11},{4,12},{5,13},{6,14},{7,15},{8,0},{9,1},... | collective-permute-start | bytes 49208 | tf_op jit(solution)/shard_map/ppermute | solution.py:70
  24.7 0.6 gather_fusion.1
  25.3 0.9 %maximum_reduce_fusion = f32[2,4,1536]{2,1,0:T(4,128)S(1)} fusion(f32[2,4,1,512]{3,2,1,0:T(1,128)S(1)} %collective-permute-done.6, f32[2,4,1,512]{3,2,1,0:T(1,128)} %param.8, f32[2,4,1,512]{3,2,1,0:T(1,128)S(1)} %collective-permute-done.5), kind=kLoop, calls=%fused_computation.37 | loop fusion | flops 24576 | bytes 98304 | tf_op jit(solution)/shard_map/concatenate | solution.py:98
  26.2 0.6 gather_fusion
  27.1 2.0 %convolution_bitcast_fusion.4 = f32[2,2,4,64]{3,2,0,1:T(4,128)S(1)} fusion(f32[16,2,4,64,1]{3,0,2,1,4:T(8,128)S(1)} %fusion.19, f32[1,1,16,2,64,64]{5,4,3,2,1,0:T(8,128)} %param.14, f32[16,64,64]{2,1,0:T(8,128)S(1)} %and_convert_fusion), kind=kOutput, calls=%fused_computation.14 | convolution fusion | flops 6422528 | bytes 823296 | tf_op jit(solution)/shard_map/sakl,spql->apqk/dot_general | solution.py:143
  29.1 0.1 convolution_bitcast_fusion.1
  29.3 0.7 fusion.4
  30.1 0.1 convolution_bitcast_fusion.3
  30.2 0.2 add_reduce_fusion.7
  30.8 1.1 %collective-permute-done.7 = f32[528]{0:T(1024)S(1)} collective-permute-done((f32[528]{0:T(1024)S(1)}, f32[528]{0:T(1024)S(1)}, u32[]{:S(2)}, u32[]{:S(2)}) %collective-permute-start.7) | collective-permute-done | bytes 2144 | tf_op jit(solution)/shard_map/ppermute | solution.py:70
  31.9 0.1 reshape.1860
  32.2 0.8 %collective-permute-start.8 = (f32[1040]{0:T(1024)S(1)}, f32[1040]{0:T(1024)S(1)}, u32[]{:S(2)}, u32[]{:S(2)}) collective-permute-start(f32[1040]{0:T(1024)S(1)} %pad_maximum_fusion.7), channel_id=1, source_target_pairs={{0,2},{1,3},{2,0},{3,1},{4,6},{5,7},{6,4},{7,5},{8,10},{9,11},{10,... | collective-permute-start | bytes 12488 | tf_op jit(solution)/shard_map/ppermute | solution.py:70
  33.1 2.8 %collective-permute-done.8 = f32[1040]{0:T(1024)S(1)} collective-permute-done((f32[1040]{0:T(1024)S(1)}, f32[1040]{0:T(1024)S(1)}, u32[]{:S(2)}, u32[]{:S(2)}) %collective-permute-start.8) | collective-permute-done | bytes 4192 | tf_op jit(solution)/shard_map/ppermute | solution.py:70
  36.2 0.5 collective-permute-start.9
  36.8 1.3 %collective-permute-start.12 = (f32[2,4,1,512]{3,1,0,2:T(4,128)S(1)}, f32[2,4,1,512]{3,1,0,2:T(4,128)S(1)}, u32[]{:S(2)}, u32[]{:S(2)}) collective-permute-start(f32[2,4,1,512]{3,1,0,2:T(4,128)S(1)} %get-tuple-element.60), channel_id=1, source_target_pairs={{0,1},{1,2},{2,3},{3,4},{4,5},{5,6},{6,7},{7,8},{8,9},{9,10},{10,1... | collective-permute-start | bytes 49160 | tf_op jit(solution)/shard_map/ppermute | solution.py:96
  38.1 1.3 %collective-permute-start.13 = (f32[2,4,1,512]{3,1,0,2:T(4,128)S(1)}, f32[2,4,1,512]{3,1,0,2:T(4,128)S(1)}, u32[]{:S(2)}, u32[]{:S(2)}) collective-permute-start(f32[2,4,1,512]{3,1,0,2:T(4,128)S(1)} %get-tuple-element.60), channel_id=1, source_target_pairs={{1,0},{2,1},{3,2},{4,3},{5,4},{6,5},{7,6},{8,7},{9,8},{10,9},{11,1... | collective-permute-start | bytes 49160 | tf_op jit(solution)/shard_map/ppermute | solution.py:97
  39.4 0.1 copy.179
  39.6 0.3 collective-permute-done.9
  40.3 6.0 %collective-permute-start.10 = (f32[4112]{0:T(1024)S(1)}, f32[4112]{0:T(1024)S(1)}, u32[]{:S(2)}, u32[]{:S(2)}) collective-permute-start(f32[4112]{0:T(1024)S(1)} %pad_maximum_fusion.2), channel_id=1, source_target_pairs={{0,8},{1,9},{2,10},{3,11},{4,12},{5,13},{6,14},{7,15},{8,0},{9,1},... | collective-permute-start | bytes 49352 | tf_op jit(solution)/shard_map/ppermute | solution.py:70
  46.5 0.6 gather_fusion.2
  47.1 1.0 %collective-permute-done.10 = f32[4112]{0:T(1024)S(1)} collective-permute-done((f32[4112]{0:T(1024)S(1)}, f32[4112]{0:T(1024)S(1)}, u32[]{:S(2)}, u32[]{:S(2)}) %collective-permute-start.10) | collective-permute-done | bytes 16480 | tf_op jit(solution)/shard_map/ppermute | solution.py:70
  48.2 0.5 collective-permute-start.11
  48.9 2.0 %convolution_bitcast_fusion.2 = f32[2,4,2,64]{3,1,2,0:T(4,128)S(1)} fusion(f32[16,2,4,64,1]{3,0,2,1,4:T(8,128)S(1)} %fusion.21, f32[1,1,16,2,64,64]{5,4,3,2,1,0:T(8,128)} %param.14, f32[16,64,64]{2,1,0:T(8,128)S(1)} %and_convert_fusion), kind=kOutput, calls=%fused_computation.12 | convolution fusion | flops 6422528 | bytes 823296 | tf_op jit(solution)/shard_map/sakl,spql->apqk/dot_general | solution.py:143
  51.0 1.0 %collective-permute-done.11 = f32[4112]{0:T(1024)S(1)} collective-permute-done((f32[4112]{0:T(1024)S(1)}, f32[4112]{0:T(1024)S(1)}, u32[]{:S(2)}, u32[]{:S(2)}) %collective-permute-start.11) | collective-permute-done | bytes 16480 | tf_op jit(solution)/shard_map/ppermute | solution.py:70
  52.0 0.1 reshape.1866
  52.5 0.6 gather_fusion.3
  53.1 0.2 convolution_bitcast_fusion
  53.4 0.1 multiply_subtract_fusion
  53.5 0.7 fusion.7
  54.2 0.6 copy.185
  54.9 0.2 subtract_reduce_fusion
  55.2 0.6 collective-permute-start.14
  55.8 0.1 copy.180
  55.9 0.1 copy.181
  55.9 2.9 %collective-permute-done.14 = f32[8,4]{1,0:T(8,128)S(1)} collective-permute-done((f32[8,4]{1,0:T(8,128)S(1)}, f32[8,4]{1,0:T(8,128)S(1)}, u32[]{:S(2)}, u32[]{:S(2)}) %collective-permute-start.14) | collective-permute-done | bytes 160 | tf_op jit(solution)/shard_map/ppermute | solution.py:21
  58.8 1.6 %collective-permute-start.16 = (f32[8,4]{1,0:T(8,128)S(1)}, f32[8,4]{1,0:T(8,128)S(1)}, u32[]{:S(2)}, u32[]{:S(2)}) collective-permute-start(f32[8,4]{1,0:T(8,128)S(1)} %add.560), channel_id=1, source_target_pairs={{0,2},{1,3},{2,0},{3,1},{4,6},{5,7},{6,4},{7,5},{8,10},{9,11},{10,... | collective-permute-start | bytes 392 | tf_op jit(solution)/shard_map/ppermute | solution.py:37
  60.4 0.2 collective-permute-start.17
  60.7 1.2 %collective-permute-done.15 = f32[8,4]{1,0:T(8,128)S(1)} collective-permute-done((f32[8,4]{1,0:T(8,128)S(1)}, f32[8,4]{1,0:T(8,128)S(1)}, u32[]{:S(2)}, u32[]{:S(2)}) %collective-permute-start.15) | collective-permute-done | bytes 160 | tf_op jit(solution)/shard_map/ppermute | solution.py:37
  61.9 0.6 collective-permute-done.16
  62.5 4.1 %collective-permute-start.18 = (f32[8,4]{1,0:T(8,128)S(1)}, f32[8,4]{1,0:T(8,128)S(1)}, u32[]{:S(2)}, u32[]{:S(2)}) collective-permute-start(f32[8,4]{1,0:T(8,128)S(1)} %select_add_fusion), channel_id=1, source_target_pairs={{0,12},{1,13},{2,14},{3,15},{4,8},{5,9},{6,10},{7,11},{8,4},{9,5},... | collective-permute-start | bytes 392 | tf_op jit(solution)/shard_map/ppermute | solution.py:37
  66.6 0.6 collective-permute-start.20
  67.2 0.9 %collective-permute-done.18 = f32[8,4]{1,0:T(8,128)S(1)} collective-permute-done((f32[8,4]{1,0:T(8,128)S(1)}, f32[8,4]{1,0:T(8,128)S(1)}, u32[]{:S(2)}, u32[]{:S(2)}) %collective-permute-start.18) | collective-permute-done | bytes 160 | tf_op jit(solution)/shard_map/ppermute | solution.py:37
  68.2 2.9 %collective-permute-done.19 = f32[8,4]{1,0:T(8,128)S(1)} collective-permute-done((f32[8,4]{1,0:T(8,128)S(1)}, f32[8,4]{1,0:T(8,128)S(1)}, u32[]{:S(2)}, u32[]{:S(2)}) %collective-permute-start.19) | collective-permute-done | bytes 160 | tf_op jit(solution)/shard_map/ppermute | solution.py:37
  71.2 0.1 copy.182
  71.3 0.1 copy.184
  71.4 0.1 copy.183
  71.7 0.6 copy.186
  72.3 0.7 concatenate.152
  (145 shorter events, 4.6 us)
Async XLA Ops:
  0.6 28.6 %copy-start = (bf16[1,2,4,2,256,256]{5,4,3,2,1,0:T(8,128)(2,1)S(1)}, bf16[1,2,4,2,256,256]{5,4,3,2,1,0:T(8,128)(2,1)}, u32[]{:S(2)}) copy-start(bf16[1,2,4,2,256,256]{5,4,3,2,1,0:T(8,128)(2,1)} %param.9) | copy-start | bytes 6291460
  0.6 6.5 %collective-permute-start = (f32[4096]{0:T(1024)}, f32[4096]{0:T(1024)S(1)}, u32[]{:S(2)}, u32[]{:S(2)}) collective-permute-start(f32[4096]{0:T(1024)} %bitcast.354), channel_id=1, source_target_pairs={{0,16},{16,0},{1,17},{17,1},{2,18},{18,2},{3,19},{19,3},{4,20},{20... | collective-permute-start | bytes 49160 | tf_op jit(solution)/shard_map/ppermute | solution.py:70
  5.5 23.6 %copy-start.2 = (bf16[1,2,64,512]{3,2,1,0:T(8,128)(2,1)S(1)}, bf16[1,2,64,512]{3,2,1,0:T(8,128)(2,1)}, u32[]{:S(2)}) copy-start(bf16[1,2,64,512]{3,2,1,0:T(8,128)(2,1)} %param.13) | copy-start | bytes 393220
  7.3 1.2 %collective-permute-start.1 = (f32[516]{0:T(1024)S(1)}, f32[516]{0:T(1024)S(1)}, u32[]{:S(2)}, u32[]{:S(2)}) collective-permute-start(f32[516]{0:T(1024)S(1)} %pad_maximum_fusion.9), channel_id=1, source_target_pairs={{0,1},{1,0},{2,3},{3,2},{4,5},{5,4},{6,7},{7,6},{8,9},{9,8},{10,11... | collective-permute-start | bytes 6200 | tf_op jit(solution)/shard_map/ppermute | solution.py:70
  8.9 3.7 %collective-permute-start.2 = (f32[1028]{0:T(1024)S(1)}, f32[1028]{0:T(1024)S(1)}, u32[]{:S(2)}, u32[]{:S(2)}) collective-permute-start(f32[1028]{0:T(1024)S(1)} %pad_maximum_fusion.6), channel_id=1, source_target_pairs={{0,2},{1,3},{2,0},{3,1},{4,6},{5,7},{6,4},{7,5},{8,10},{9,11},{10,... | collective-permute-start | bytes 12344 | tf_op jit(solution)/shard_map/ppermute | solution.py:70
  12.9 4.8 %collective-permute-start.3 = (f32[2052]{0:T(1024)S(1)}, f32[2052]{0:T(1024)S(1)}, u32[]{:S(2)}, u32[]{:S(2)}) collective-permute-start(f32[2052]{0:T(1024)S(1)} %pad_maximum_fusion.4), channel_id=1, source_target_pairs={{0,4},{1,5},{2,6},{3,7},{4,0},{5,1},{6,2},{7,3},{8,12},{9,13},{10,... | collective-permute-start | bytes 24632 | tf_op jit(solution)/shard_map/ppermute | solution.py:70
  15.1 10.2 %collective-permute-start.5 = (f32[2,4,1,512]{3,2,1,0:T(1,128)}, f32[2,4,1,512]{3,2,1,0:T(1,128)S(1)}, u32[]{:S(2)}, u32[]{:S(2)}) collective-permute-start(f32[2,4,1,512]{3,2,1,0:T(1,128)} %param.8), channel_id=1, source_target_pairs={{0,1},{1,2},{2,3},{3,4},{4,5},{5,6},{6,7},{7,8},{8,9},{9,10},{10,1... | collective-permute-start | bytes 49160 | tf_op jit(solution)/shard_map/ppermute | solution.py:96
  16.4 8.9 %collective-permute-start.6 = (f32[2,4,1,512]{3,2,1,0:T(1,128)}, f32[2,4,1,512]{3,2,1,0:T(1,128)S(1)}, u32[]{:S(2)}, u32[]{:S(2)}) collective-permute-start(f32[2,4,1,512]{3,2,1,0:T(1,128)} %param.8), channel_id=1, source_target_pairs={{1,0},{2,1},{3,2},{4,3},{5,4},{6,5},{7,6},{8,7},{9,8},{10,9},{11,1... | collective-permute-start | bytes 49160 | tf_op jit(solution)/shard_map/ppermute | solution.py:97
  18.1 8.7 %collective-permute-start.4 = (f32[4100]{0:T(1024)S(1)}, f32[4100]{0:T(1024)S(1)}, u32[]{:S(2)}, u32[]{:S(2)}) collective-permute-start(f32[4100]{0:T(1024)S(1)} %pad_maximum_fusion.1), channel_id=1, source_target_pairs={{0,8},{1,9},{2,10},{3,11},{4,12},{5,13},{6,14},{7,15},{8,0},{9,1},... | collective-permute-start | bytes 49208 | tf_op jit(solution)/shard_map/ppermute | solution.py:70
  27.1 2.9 %copy-start.3 = (f32[2,4,1,512]{3,2,1,0:T(1,128)S(1)}, f32[2,4,1,512]{3,2,1,0:T(1,128)}, u32[]{:S(2)}) copy-start(f32[2,4,1,512]{3,2,1,0:T(1,128)} %param.8) | copy-start | bytes 49156
  27.1 3.0 %copy-start.1 = (bf16[1,2,64,512]{3,2,1,0:T(8,128)(2,1)S(1)}, bf16[1,2,64,512]{3,2,1,0:T(8,128)(2,1)}, u32[]{:S(2)}) copy-start(bf16[1,2,64,512]{3,2,1,0:T(8,128)(2,1)} %param.12) | copy-start | bytes 393220
  30.7 1.2 %collective-permute-start.7 = (f32[528]{0:T(1024)S(1)}, f32[528]{0:T(1024)S(1)}, u32[]{:S(2)}, u32[]{:S(2)}) collective-permute-start(f32[528]{0:T(1024)S(1)} %pad_maximum_fusion.11), channel_id=1, source_target_pairs={{0,1},{1,0},{2,3},{3,2},{4,5},{5,4},{6,7},{7,6},{8,9},{9,8},{10,11... | collective-permute-start | bytes 6344 | tf_op jit(solution)/shard_map/ppermute | solution.py:70
  32.2 3.7 %collective-permute-start.8 = (f32[1040]{0:T(1024)S(1)}, f32[1040]{0:T(1024)S(1)}, u32[]{:S(2)}, u32[]{:S(2)}) collective-permute-start(f32[1040]{0:T(1024)S(1)} %pad_maximum_fusion.7), channel_id=1, source_target_pairs={{0,2},{1,3},{2,0},{3,1},{4,6},{5,7},{6,4},{7,5},{8,10},{9,11},{10,... | collective-permute-start | bytes 12488 | tf_op jit(solution)/shard_map/ppermute | solution.py:70
  36.2 3.7 %collective-permute-start.9 = (f32[2064]{0:T(1024)S(1)}, f32[2064]{0:T(1024)S(1)}, u32[]{:S(2)}, u32[]{:S(2)}) collective-permute-start(f32[2064]{0:T(1024)S(1)} %pad_maximum_fusion.5), channel_id=1, source_target_pairs={{0,4},{1,5},{2,6},{3,7},{4,0},{5,1},{6,2},{7,3},{8,12},{9,13},{10,... | collective-permute-start | bytes 24776 | tf_op jit(solution)/shard_map/ppermute | solution.py:70
  36.8 9.7 %collective-permute-start.12 = (f32[2,4,1,512]{3,1,0,2:T(4,128)S(1)}, f32[2,4,1,512]{3,1,0,2:T(4,128)S(1)}, u32[]{:S(2)}, u32[]{:S(2)}) collective-permute-start(f32[2,4,1,512]{3,1,0,2:T(4,128)S(1)} %get-tuple-element.60), channel_id=1, source_target_pairs={{0,1},{1,2},{2,3},{3,4},{4,5},{5,6},{6,7},{7,8},{8,9},{9,10},{10,1... | collective-permute-start | bytes 49160 | tf_op jit(solution)/shard_map/ppermute | solution.py:96
  38.1 8.4 %collective-permute-start.13 = (f32[2,4,1,512]{3,1,0,2:T(4,128)S(1)}, f32[2,4,1,512]{3,1,0,2:T(4,128)S(1)}, u32[]{:S(2)}, u32[]{:S(2)}) collective-permute-start(f32[2,4,1,512]{3,1,0,2:T(4,128)S(1)} %get-tuple-element.60), channel_id=1, source_target_pairs={{1,0},{2,1},{3,2},{4,3},{5,4},{6,5},{7,6},{8,7},{9,8},{10,9},{11,1... | collective-permute-start | bytes 49160 | tf_op jit(solution)/shard_map/ppermute | solution.py:97
  40.3 7.8 %collective-permute-start.10 = (f32[4112]{0:T(1024)S(1)}, f32[4112]{0:T(1024)S(1)}, u32[]{:S(2)}, u32[]{:S(2)}) collective-permute-start(f32[4112]{0:T(1024)S(1)} %pad_maximum_fusion.2), channel_id=1, source_target_pairs={{0,8},{1,9},{2,10},{3,11},{4,12},{5,13},{6,14},{7,15},{8,0},{9,1},... | collective-permute-start | bytes 49352 | tf_op jit(solution)/shard_map/ppermute | solution.py:70
  48.2 3.8 %collective-permute-start.11 = (f32[4112]{0:T(1024)S(1)}, f32[4112]{0:T(1024)S(1)}, u32[]{:S(2)}, u32[]{:S(2)}) collective-permute-start(f32[4112]{0:T(1024)S(1)} %pad_maximum_fusion.3), channel_id=1, source_target_pairs={{0,16},{16,0},{1,17},{17,1},{2,18},{18,2},{3,19},{19,3},{4,20},{20... | collective-permute-start | bytes 49352 | tf_op jit(solution)/shard_map/ppermute | solution.py:70
  55.2 3.7 %collective-permute-start.14 = (f32[8,4]{1,0:T(8,128)S(1)}, f32[8,4]{1,0:T(8,128)S(1)}, u32[]{:S(2)}, u32[]{:S(2)}) collective-permute-start(f32[8,4]{1,0:T(8,128)S(1)} %concatenate.151), channel_id=1, source_target_pairs={{0,16},{16,0},{1,17},{17,1},{2,18},{18,2},{3,19},{19,3},{4,20},{20... | collective-permute-start | bytes 392 | tf_op jit(solution)/shard_map/ppermute | solution.py:21
  58.8 3.0 %collective-permute-start.15 = (f32[8,4]{1,0:T(8,128)S(1)}, f32[8,4]{1,0:T(8,128)S(1)}, u32[]{:S(2)}, u32[]{:S(2)}) collective-permute-start(f32[8,4]{1,0:T(8,128)S(1)} %add.560), channel_id=1, source_target_pairs={{0,3},{1,2},{2,1},{3,0},{4,7},{5,6},{6,5},{7,4},{8,11},{9,10},{10,... | collective-permute-start | bytes 392 | tf_op jit(solution)/shard_map/ppermute | solution.py:37
  58.8 3.6 %collective-permute-start.16 = (f32[8,4]{1,0:T(8,128)S(1)}, f32[8,4]{1,0:T(8,128)S(1)}, u32[]{:S(2)}, u32[]{:S(2)}) collective-permute-start(f32[8,4]{1,0:T(8,128)S(1)} %add.560), channel_id=1, source_target_pairs={{0,2},{1,3},{2,0},{3,1},{4,6},{5,7},{6,4},{7,5},{8,10},{9,11},{10,... | collective-permute-start | bytes 392 | tf_op jit(solution)/shard_map/ppermute | solution.py:37
  60.4 2.0 %collective-permute-start.17 = (f32[8,4]{1,0:T(8,128)S(1)}, f32[8,4]{1,0:T(8,128)S(1)}, u32[]{:S(2)}, u32[]{:S(2)}) collective-permute-start(f32[8,4]{1,0:T(8,128)S(1)} %add.560), channel_id=1, source_target_pairs={{0,1},{1,0},{2,3},{3,2},{4,5},{5,4},{6,7},{7,6},{8,9},{9,8},{10,11... | collective-permute-start | bytes 392 | tf_op jit(solution)/shard_map/ppermute | solution.py:37
  62.5 5.7 %collective-permute-start.18 = (f32[8,4]{1,0:T(8,128)S(1)}, f32[8,4]{1,0:T(8,128)S(1)}, u32[]{:S(2)}, u32[]{:S(2)}) collective-permute-start(f32[8,4]{1,0:T(8,128)S(1)} %select_add_fusion), channel_id=1, source_target_pairs={{0,12},{1,13},{2,14},{3,15},{4,8},{5,9},{6,10},{7,11},{8,4},{9,5},... | collective-permute-start | bytes 392 | tf_op jit(solution)/shard_map/ppermute | solution.py:37
  66.6 4.5 %collective-permute-start.19 = (f32[8,4]{1,0:T(8,128)S(1)}, f32[8,4]{1,0:T(8,128)S(1)}, u32[]{:S(2)}, u32[]{:S(2)}) collective-permute-start(f32[8,4]{1,0:T(8,128)S(1)} %select_add_fusion), channel_id=1, source_target_pairs={{0,8},{1,9},{2,10},{3,11},{4,12},{5,13},{6,14},{7,15},{8,0},{9,1},... | collective-permute-start | bytes 392 | tf_op jit(solution)/shard_map/ppermute | solution.py:37
  66.6 4.5 %collective-permute-start.20 = (f32[8,4]{1,0:T(8,128)S(1)}, f32[8,4]{1,0:T(8,128)S(1)}, u32[]{:S(2)}, u32[]{:S(2)}) collective-permute-start(f32[8,4]{1,0:T(8,128)S(1)} %select_add_fusion), channel_id=1, source_target_pairs={{0,4},{1,5},{2,6},{3,7},{4,0},{5,1},{6,2},{7,3},{8,12},{9,13},{10,... | collective-permute-start | bytes 392 | tf_op jit(solution)/shard_map/ppermute | solution.py:37
